TPU v7x, 32 devices: a whole 2x2x4 slice. The times are simulated.
32 devices in a mesh: dp: 8 (over y, x, core), tensor: 4 (over z).
Axes of the slice: x: 2, y: 2, z: 4, core: 2. Of those that a mesh axis runs over, the one named last changes fastest.
Arguments:
- glu_input: bfloat16 [16, 256, 3072], P('dp', 'tensor'), may hold values from -12 to 12
- depth_kernel: float32 [31, 1536], replicated, may hold values from -1 to 1
- norm_scale: float32 [1536], replicated, may hold values from 0.5 to 1.5
- norm_shift: float32 [1536], replicated, may hold values from -3 to 3
- proj_weight: bfloat16 [1536, 1536], P('tensor'), may hold values from -0.15625 to 0.15625
- out_grad: bfloat16 [16, 256, 1536], P('dp', 'tensor'), may hold values from -6 to 6
Outputs:
- conv_output: bfloat16 [16, 256, 1536], P('dp', 'tensor')
- input_grad: bfloat16 [16, 256, 3072], P('dp', 'tensor')
- weight_grad: float32 [1536, 1536], P('tensor')
- kernel_grad: float32 [31, 1536], replicated
- scale_grad: float32 [1536], replicated
- shift_grad: float32 [1536], replicated
All inputs are finite; a program needn't handle non-finite values.
Results may differ from a plain program's by a relative error of at most 0.0057.
Values may be sent and summed in bfloat16 or wider, within the bound.
No kernel may reach another device: no remote copies, remote signals or barrier semaphores. Data moves between devices by JAX's collectives and lax.ppermute only.
A program may use at most 128 MiB of HBM per device.

v0:
```python
import jax
import jax.numpy as jnp
from jax import lax
from jax.sharding import PartitionSpec as P

epsilon = 1e-05


def extended(array, sides, width):
    for axis, dim in sides:
        peers, length = (lax.axis_size(axis), array.shape[dim])
        up = [(i, (i + 1) % peers) for i in range(peers - 1)]
        down = [(j, i) for i, j in up]
        last = lax.slice_in_dim(array, length - width, length, axis=dim)
        leading = lax.slice_in_dim(array, 0, width, axis=dim)
        before = lax.ppermute(last, axis, up)
        after = lax.ppermute(leading, axis, down)
        array = jnp.concatenate([before, array, after], axis=dim)
    return array


def on_device(glu_input, depth_kernel, norm_scale, norm_shift, proj_weight, out_grad):
    width = proj_weight.shape[1]
    frames = glu_input.shape[1]
    taps = depth_kernel.shape[0]
    radius = (taps - 1) // 2
    everyone = glu_input.shape[0] * frames * lax.axis_size("dp") * lax.axis_size("tensor")
    values = glu_input[..., :width].astype(jnp.float32)
    gates = jax.nn.sigmoid(glu_input[..., width:].astype(jnp.float32))
    gated = (values * gates).astype(jnp.bfloat16)
    padded = extended(gated, (("tensor", 1),), radius)
    conv_out = jnp.zeros(gated.shape, jnp.float32)
    for offset in range(taps):
        conv_out = conv_out + depth_kernel[offset] * padded[:, offset : offset + frames, :]
    average = lax.psum(jnp.sum(conv_out, axis=(0, 1)), ("dp", "tensor")) / everyone
    centred = conv_out - average
    variance = lax.psum(jnp.sum(centred * centred, axis=(0, 1)), ("dp", "tensor")) / everyone
    inverse = lax.rsqrt(variance + epsilon)
    normed = centred * inverse
    affine = norm_scale * normed + norm_shift
    sig_affine = jax.nn.sigmoid(affine)
    activated = (affine * sig_affine).astype(jnp.bfloat16)
    full_weight = lax.all_gather(proj_weight, "tensor", axis=0, tiled=True)
    conv_output = jnp.einsum(
        "btc,cd->btd", activated, full_weight, preferred_element_type=jnp.float32
    ).astype(jnp.bfloat16)
    grad_act = jnp.einsum("btd,cd->btc", out_grad, full_weight, preferred_element_type=jnp.float32)
    grad_affine = grad_act * (sig_affine + affine * sig_affine * (1.0 - sig_affine))
    shift_grad, scale_grad = lax.psum(
        (jnp.sum(grad_affine, axis=(0, 1)), jnp.sum(grad_affine * normed, axis=(0, 1))),
        ("dp", "tensor"),
    )
    grad_conv = (
        norm_scale
        * inverse
        * (grad_affine - shift_grad / everyone - normed * scale_grad / everyone)
    ).astype(jnp.bfloat16)
    grad_pad = extended(grad_conv, (("tensor", 1),), radius)
    grad_gated = jnp.zeros(gated.shape, jnp.float32)
    for offset in range(taps):
        begin = 2 * radius - offset
        grad_gated = grad_gated + depth_kernel[offset] * grad_pad[:, begin : begin + frames, :]
    grad_wide = grad_conv.astype(jnp.float32)
    kernel_terms = jnp.stack(
        [
            jnp.sum(
                padded[:, offset : offset + frames, :].astype(jnp.float32) * grad_wide, axis=(0, 1)
            )
            for offset in range(taps)
        ]
    )
    kernel_grad = lax.psum(kernel_terms, ("dp", "tensor"))
    input_grad = jnp.concatenate(
        [grad_gated * gates, grad_gated * values * gates * (1.0 - gates)], axis=-1
    ).astype(jnp.bfloat16)
    partial_sum = jnp.einsum("btc,btd->cd", activated, out_grad, preferred_element_type=jnp.float32)
    received = lax.all_to_all(partial_sum[None], "tensor", split_axis=1, concat_axis=0, tiled=True)
    local_grad = jnp.sum(received, axis=0)
    weight_grad = lax.psum(local_grad, "dp")
    return (conv_output, input_grad, weight_grad, kernel_grad, scale_grad, shift_grad)


def solution(mesh):
    in_specs = (P("dp", "tensor", None), P(), P(), P(), P("tensor", None), P("dp", "tensor", None))
    out_specs = (P("dp", "tensor", None), P("dp", "tensor", None), P("tensor", None), P(), P(), P())
    return jax.shard_map(
        on_device, mesh=mesh, in_specs=in_specs, out_specs=out_specs, check_vma=False
    )
```

profile of v0, /device:TPU:0, one launch (start us, length us, event | category | flops | bytes accessed | tf_op | source)
XLA Modules:
  0.0 659.3 jit_solution(2058861156043940140)
XLA Ops:
  7.2 1.4 fusion.10
  8.6 4.9 collective-permute-start
  13.5 1.3 collective-permute-start.1
  14.8 1.8 slice_reduce_fusion.30
  16.6 1.4 slice_reduce_fusion.29
  18.0 2.0 collective-permute-done.1
  20.0 3.8 fusion.154
  23.9 40.6 %psum.42 = f32[1536]{0:T(1024)S(1)} all-reduce(f32[1536]{0:T(1024)S(1)} %get-tuple-element.75), channel_id=1, replica_groups=mesh['dp'=8,'tensor'=4] {'dp','tensor'}, use_global_device_ids=true, to_apply=%region_1.0 | all-reduce | flops 1536 | bytes 12288 | tf_op jit(solution)/shard_map/psum | solution.py:35
  64.6 39.4 %psum.43 = f32[1536]{0:T(1024)S(1)} all-reduce(f32[1536]{0:T(1024)S(1)} %multiply_reduce_fusion.1), channel_id=1, replica_groups=mesh['dp'=8,'tensor'=4] {'dp','tensor'}, use_global_device_ids=true, to_apply=%region_3.0 | all-reduce | flops 1536 | bytes 12288 | tf_op jit(solution)/shard_map/psum | solution.py:37
  104.0 0.7 fusion.149
  104.7 2.2 convolution_bitcast_fusion
  106.8 35.9 %copy.12 = f32[1,1536,1536]{2,0,1:T(1,128)} copy(f32[1,1536,1536]{2,1,0:T(8,128)S(1)} %convolution_bitcast_fusion) | data formatting | bytes 18874368 | tf_op jit(solution)/shard_map/broadcast_in_dim | solution.py:77
  142.8 5.9 all-to-all-start
  148.8 0.7 all-gather.2.cloned.1.call-update
  149.5 167.6 %all-gather.2.cloned.1.call-done = bf16[1536,1536]{1,0:T(8,128)(2,1)} async-done(((bf16[384,1536]{1,0:T(8,128)(2,1)}), bf16[1536,1536]{1,0:T(8,128)(2,1)}) %all-gather.2.cloned.1.call-update) | async-done | bytes 4718608 | tf_op jit(solution)/shard_map/all_gather | solution.py:43
  317.1 4.1 fusion.152
  321.2 128.5 %all-reduce = (f32[1536]{0:T(1024)S(1)}, f32[1536]{0:T(1024)S(1)}) all-reduce(f32[1536]{0:T(1024)S(1)} %get-tuple-element.38, f32[1536]{0:T(1024)S(1)} %get-tuple-element.37), channel_id=1, replica_groups=mesh['dp'=8,'tensor'=4] {'dp','tensor'}, use_global_device_ids=true, to_apply=%region_7.0 | all-reduce | flops 3072 | bytes 24576 | tf_op jit(solution)/shard_map/psum | solution.py:49
  449.7 1.5 fusion.90
  451.3 0.9 fusion.89
  452.4 1.2 fusion.74
  453.6 0.8 fusion.73
  454.6 2.8 stack.127
  457.4 1.3 collective-permute-start.2
  458.7 4.6 collective-permute-start.3
  463.3 4.0 fusion.7
  467.3 8.2 %copy.13 = f32[1,1536,1536]{2,1,0:T(8,128)} copy(f32[1,1536,1536]{2,0,1:T(1,128)} %all-to-all-done) | data formatting | bytes 18874368
  475.5 6.5 reduce_sum.328
  482.0 4.1 multiply_convert_fusion
  486.4 1.0 pad_maximum_fusion
  487.4 93.8 %all-reduce.6.cloned.1.call-done = f32[31,1536]{1,0:T(8,128)} async-done(((f32[31,1536]{1,0:T(8,128)}), f32[31,1536]{1,0:T(8,128)}) %all-reduce.6.cloned.1.call-update) | async-done | bytes 190480 | tf_op jit(solution)/shard_map/psum | solution.py:72
  581.2 67.7 %all-reduce.4.cloned.1.call-done = f32[384,1536]{1,0:T(8,128)} async-done(((f32[384,1536]{1,0:T(8,128)}), f32[384,1536]{1,0:T(8,128)}) %all-reduce.4.cloned.1.call-update) | async-done | bytes 2359312 | tf_op jit(solution)/shard_map/psum | solution.py:79
  648.9 3.2 copy.16
  (61 shorter events, 1.5 us)
Async XLA Ops:
  7.2 97.5 %copy-start = (bf16[2,64,1536]{2,1,0:T(8,128)(2,1)S(1)}, bf16[2,64,1536]{2,1,0:T(8,128)(2,1)}, u32[]{:S(2)}) copy-start(bf16[2,64,1536]{2,1,0:T(8,128)(2,1)} %param.11) | copy-start | bytes 1179652
  8.6 9.4 %collective-permute-start = (bf16[2,15,1536]{2,1,0:T(8,128)(2,1)S(1)}, bf16[2,15,1536]{2,1,0:T(8,128)(2,1)S(1)}, u32[]{:S(2)}, u32[]{:S(2)}) collective-permute-start(bf16[2,15,1536]{2,1,0:T(8,128)(2,1)S(1)} %get-tuple-element.79), channel_id=1, source_target_pairs={{0,1},{1,2},{2,3},{4,5},{5,6},{6,7},{8,9},{9,10},{10,11},{12,13},{... | collective-permute-start | bytes 276488 | tf_op jit(solution)/shard_map/ppermute | solution.py:16
  13.5 6.5 collective-permute-start.1
  142.8 174.4 %copy-start.3 = (f32[1536]{0:T(1024)S(1)}, f32[1536]{0:T(1024)}, u32[]{:S(2)}) copy-start(f32[1536]{0:T(1024)} %param.8) | copy-start | bytes 18436
  142.8 174.4 %copy-start.4 = (f32[1536]{0:T(1024)S(1)}, f32[1536]{0:T(1024)}, u32[]{:S(2)}) copy-start(f32[1536]{0:T(1024)} %param.9) | copy-start | bytes 18436
  142.8 324.5 %all-to-all-start = ((f32[1,1536,1536]{2,0,1:T(1,128)}), f32[1,1536,1536]{2,0,1:T(1,128)}, u32[]{:S(2)}, u32[]{:S(2)}) async-start(f32[1,1536,1536]{2,0,1:T(1,128)} %copy.12), calls=%async_computation | async-start | bytes 18874368 | tf_op jit(solution)/shard_map/all_to_all | solution.py:77
  148.7 168.4 %all-gather.2.cloned.1.call-start = ((), (), s32[]{:S(2)}) async-start(), calls=%async_computation.1 | async-start | bytes 5898240 | tf_op jit(solution)/shard_map/all_gather | solution.py:43
  149.4 431.7 %all-reduce.6.cloned.1.call-start = ((), (), s32[]{:S(2)}) async-start(), calls=%async_computation.3 | async-start | bytes 393216 | tf_op jit(solution)/shard_map/psum | solution.py:72
  449.7 17.6 %copy-start.5 = (f32[1536]{0:T(1024)}, f32[1536]{0:T(1024)S(1)}, u32[]{:S(2)}) copy-start(f32[1536]{0:T(1024)S(1)} %get-tuple-element.88) | copy-start | bytes 18436
  449.7 17.6 %copy-start.6 = (f32[1536]{0:T(1024)}, f32[1536]{0:T(1024)S(1)}, u32[]{:S(2)}) copy-start(f32[1536]{0:T(1024)S(1)} %get-tuple-element.89) | copy-start | bytes 18436
  457.3 191.6 %all-reduce.4.cloned.1.call-start = ((), (), s32[]{:S(2)}) async-start(), calls=%async_computation.2 | async-start | bytes 4718592 | tf_op jit(solution)/shard_map/psum | solution.py:79
  457.4 24.6 %collective-permute-start.2 = (bf16[2,15,1536]{2,1,0:T(8,128)(2,1)S(1)}, bf16[2,15,1536]{2,1,0:T(8,128)(2,1)S(1)}, u32[]{:S(2)}, u32[]{:S(2)}) collective-permute-start(bf16[2,15,1536]{2,1,0:T(8,128)(2,1)S(1)} %get-tuple-element.77), channel_id=1, source_target_pairs={{1,0},{2,1},{3,2},{5,4},{6,5},{7,6},{9,8},{10,9},{11,10},{13,12},{... | collective-permute-start | bytes 276488 | tf_op jit(solution)/shard_map/ppermute | solution.py:17
  458.7 23.3 %collective-permute-start.3 = (bf16[2,15,1536]{2,1,0:T(8,128)(2,1)S(1)}, bf16[2,15,1536]{2,1,0:T(8,128)(2,1)S(1)}, u32[]{:S(2)}, u32[]{:S(2)}) collective-permute-start(bf16[2,15,1536]{2,1,0:T(8,128)(2,1)S(1)} %get-tuple-element.78), channel_id=1, source_target_pairs={{0,1},{1,2},{2,3},{4,5},{5,6},{6,7},{8,9},{9,10},{10,11},{12,13},{... | collective-permute-start | bytes 276488 | tf_op jit(solution)/shard_map/ppermute | solution.py:16
  475.5 6.5 copy-start.1
  581.2 70.9 %copy-start.2 = (f32[31,1536]{1,0:T(8,128)S(1)}, f32[31,1536]{1,0:T(8,128)}, u32[]{:S(2)}) copy-start(f32[31,1536]{1,0:T(8,128)} %all-reduce.6.cloned.1.call-done) | copy-start | bytes 571396
Sparse Core Ops, SparseCore 0:
  151.1 165.9 all-gather.1
  457.5 123.6 all-reduce.5
  585.0 63.8 all-reduce.3
where the time goes:
time: 660 us; the launch traced here: 659 us
  waiting for transfers between devices  332 us (50%)
  blocking collectives  208 us (32%)
  local copies, waits for them, and re-layouts  54.2 us (8%)
  other arithmetic  22.2 us (3%)
  starting transfers between devices  18.1 us (3%)
  between operations  14.2 us (2%)
  matrix products  10.2 us (2%)
    all_gather x1, waiting for transfers between devices, on_device(): full_weight = lax.all_gather(proj_weight, 'tensor', axis=0, tiled=True)  168 us
    psum x1, blocking collectives, on_device(): lax.psum((jnp.sum(grad_affine, axis=(0, 1)), jnp.sum(grad_affine * normed...  129 us
    psum x1, waiting for transfers between devices, on_device(): kernel_grad = lax.psum(kernel_terms, ('dp', 'tensor'))  93.8 us
    psum x1, waiting for transfers between devices, on_device(): weight_grad = lax.psum(local_grad, 'dp')  67.7 us
    psum x1, blocking collectives, on_device(): lax.psum(jnp.sum(conv_out, axis=(0, 1)), ('dp', 'tensor')) / everyone  40.6 us
    psum x1, blocking collectives, on_device(): lax.psum(jnp.sum(centred * centred, axis=(0, 1)), ('dp', 'tensor'))  39.4 us
    broadcast_in_dim x1, local copies, waits for them, and re-layouts, on_device(): partial_sum[None]  35.9 us
  transfers between devices with their start and end apart: 8, of which 4 were waited for; matrix products, arithmetic and copies ran while one was open for 6% of the time, Pallas kernels for 0%

commit v1 on v0

--- a/solution.py
+++ b/solution.py
@@ -19,12 +19,53 @@
     return array
 
 
+def is_power_of_two(n):
+    return n > 0 and (n & (n - 1)) == 0
+
+
+def all_sum(x, axes):
+    for axis in axes:
+        peers = lax.axis_size(axis)
+        if not is_power_of_two(peers):
+            x = lax.psum(x, axis)
+            continue
+        step = 1
+        while step < peers:
+            x = x + lax.ppermute(x, axis, [(i, i ^ step) for i in range(peers)])
+            step *= 2
+    return x
+
+
+def all_moments(mean, spread, count, axes):
+    for axis in axes:
+        peers = lax.axis_size(axis)
+        step = 1
+        while step < peers:
+            other = lax.ppermute(jnp.stack([mean, spread]), axis, [(i, i ^ step) for i in range(peers)])
+            delta = other[0] - mean
+            mean = (mean + other[0]) * 0.5
+            spread = (spread + other[1]) + delta * delta * (count * 0.5)
+            count = count * 2
+            step *= 2
+    return mean, spread
+
+
+def shifted(x, axis, shift):
+    peers = lax.axis_size(axis)
+    return lax.ppermute(x, axis, [(i, (i + shift) % peers) for i in range(peers)])
+
+
 def on_device(glu_input, depth_kernel, norm_scale, norm_shift, proj_weight, out_grad):
     width = proj_weight.shape[1]
+    rows = proj_weight.shape[0]
     frames = glu_input.shape[1]
     taps = depth_kernel.shape[0]
     radius = (taps - 1) // 2
-    everyone = glu_input.shape[0] * frames * lax.axis_size("dp") * lax.axis_size("tensor")
+    peers = lax.axis_size("tensor")
+    me = lax.axis_index("tensor")
+    local = glu_input.shape[0] * frames
+    everyone = local * lax.axis_size("dp") * peers
+    full_weight = lax.all_gather(proj_weight, "tensor", axis=0, tiled=True)
     values = glu_input[..., :width].astype(jnp.float32)
     gates = jax.nn.sigmoid(glu_input[..., width:].astype(jnp.float32))
     gated = (values * gates).astype(jnp.bfloat16)
@@ -32,24 +73,32 @@
     conv_out = jnp.zeros(gated.shape, jnp.float32)
     for offset in range(taps):
         conv_out = conv_out + depth_kernel[offset] * padded[:, offset : offset + frames, :]
-    average = lax.psum(jnp.sum(conv_out, axis=(0, 1)), ("dp", "tensor")) / everyone
+    mean_local = jnp.sum(conv_out, axis=(0, 1)) / local
+    dev_local = conv_out - mean_local
+    spread_local = jnp.sum(dev_local * dev_local, axis=(0, 1))
+    if all(is_power_of_two(lax.axis_size(a)) for a in ("dp", "tensor")):
+        average, spread = all_moments(mean_local, spread_local, float(local), ("dp", "tensor"))
+        variance = spread / everyone
+    else:
+        average = lax.psum(jnp.sum(conv_out, axis=(0, 1)), ("dp", "tensor")) / everyone
+        centred0 = conv_out - average
+        variance = lax.psum(jnp.sum(centred0 * centred0, axis=(0, 1)), ("dp", "tensor")) / everyone
     centred = conv_out - average
-    variance = lax.psum(jnp.sum(centred * centred, axis=(0, 1)), ("dp", "tensor")) / everyone
     inverse = lax.rsqrt(variance + epsilon)
     normed = centred * inverse
     affine = norm_scale * normed + norm_shift
     sig_affine = jax.nn.sigmoid(affine)
     activated = (affine * sig_affine).astype(jnp.bfloat16)
-    full_weight = lax.all_gather(proj_weight, "tensor", axis=0, tiled=True)
     conv_output = jnp.einsum(
         "btc,cd->btd", activated, full_weight, preferred_element_type=jnp.float32
     ).astype(jnp.bfloat16)
     grad_act = jnp.einsum("btd,cd->btc", out_grad, full_weight, preferred_element_type=jnp.float32)
     grad_affine = grad_act * (sig_affine + affine * sig_affine * (1.0 - sig_affine))
-    shift_grad, scale_grad = lax.psum(
-        (jnp.sum(grad_affine, axis=(0, 1)), jnp.sum(grad_affine * normed, axis=(0, 1))),
+    sums = all_sum(
+        jnp.stack([jnp.sum(grad_affine, axis=(0, 1)), jnp.sum(grad_affine * normed, axis=(0, 1))]),
         ("dp", "tensor"),
     )
+    shift_grad, scale_grad = sums[0], sums[1]
     grad_conv = (
         norm_scale
         * inverse
@@ -69,13 +118,25 @@
             for offset in range(taps)
         ]
     )
-    kernel_grad = lax.psum(kernel_terms, ("dp", "tensor"))
+    kernel_grad = all_sum(kernel_terms, ("dp", "tensor"))
     input_grad = jnp.concatenate(
         [grad_gated * gates, grad_gated * values * gates * (1.0 - gates)], axis=-1
     ).astype(jnp.bfloat16)
-    partial_sum = jnp.einsum("btc,btd->cd", activated, out_grad, preferred_element_type=jnp.float32)
-    received = lax.all_to_all(partial_sum[None], "tensor", split_axis=1, concat_axis=0, tiled=True)
-    local_grad = jnp.sum(received, axis=0)
+    flat_act = activated.reshape(-1, width)
+    flat_grad = out_grad.reshape(-1, width)
+    act_parts = [lax.dynamic_slice_in_dim(flat_act, me * rows, rows, axis=1)]
+    grad_parts = [flat_grad]
+    for shift in range(1, peers):
+        owner = lax.rem(me + shift, peers)
+        block = lax.dynamic_slice_in_dim(flat_act, owner * rows, rows, axis=1)
+        act_parts.append(shifted(block, "tensor", shift))
+        grad_parts.append(shifted(flat_grad, "tensor", shift))
+    local_grad = jnp.einsum(
+        "fc,fd->cd",
+        jnp.concatenate(act_parts, axis=0),
+        jnp.concatenate(grad_parts, axis=0),
+        preferred_element_type=jnp.float32,
+    )
     weight_grad = lax.psum(local_grad, "dp")
     return (conv_output, input_grad, weight_grad, kernel_grad, scale_grad, shift_grad)
 

time: 660 us -> 249 us (0.38)
  blocking collectives: 208 us -> 0 us
  waiting for transfers between devices: 332 us -> 158 us
  local copies, waits for them, and re-layouts: 54.2 us -> 7.79 us
  starting transfers between devices: 18.1 us -> 38.6 us
    psum x3 -> x0, blocking collectives: 208 us -> none  [the longest x1 129 us: on_device(): lax.psum((jnp.sum(grad_affine, axis=(0, 1)), jnp.sum(grad_affine * normed...]
    all_gather x1, waiting for transfers between devices: 168 us -> 57.9 us  [on_device(): full_weight = lax.all_gather(proj_weight, 'tensor', axis=0, tiled=True)]
    psum x1 -> x0, waiting for transfers between devices: 93.8 us -> none  [on_device(): kernel_grad = lax.psum(kernel_terms, ('dp', 'tensor'))]
    ppermute x0 -> x21, waiting for transfers between devices: none -> 63.1 us  [the longest x10 48.6 us: all_sum(): x = x + lax.ppermute(x, axis, [(i, i ^ step) for i in range(peers)])]
    broadcast_in_dim x1 -> x0, local copies, waits for them, and re-layouts: 35.9 us -> none  [on_device(): partial_sum[None]]
    psum x1, waiting for transfers between devices: 67.7 us -> 36.5 us  [on_device(): weight_grad = lax.psum(local_grad, 'dp')]
    ppermute x0 -> x21, starting transfers between devices: none -> 28.3 us  [the longest x6 11.9 us: shifted(): lax.ppermute(x, axis, [(i, (i + shift) % peers) for i in range(peers)])]
    unnamed x17 -> x35, local copies, waits for them, and re-layouts: 12.1 us -> 3.86 us
  transfers between devices with their start and end apart: 8 -> 27, of which waited for: 4 -> 16; matrix products, arithmetic and copies ran while one was open for 6% -> 12% of each run, Pallas kernels for 0% -> 0%
where the time goes in v1:
time: 249 us
  waiting for transfers between devices  158 us (63%)
  starting transfers between devices  38.6 us (16%)
  other arithmetic  17.5 us (7%)
  between operations  14.9 us (6%)
  matrix products  11.7 us (5%)
  local copies, waits for them, and re-layouts  7.79 us (3%)
    all_gather x1, waiting for transfers between devices, on_device(): full_weight = lax.all_gather(proj_weight, 'tensor', axis=0, tiled=True)  57.9 us
    ppermute x10, waiting for transfers between devices, all_sum(): x = x + lax.ppermute(x, axis, [(i, i ^ step) for i in range(peers)])  48.6 us
    psum x1, waiting for transfers between devices, on_device(): weight_grad = lax.psum(local_grad, 'dp')  36.5 us
    ppermute x5, waiting for transfers between devices, all_moments(): lax.ppermute(jnp.stack([mean, spread]), axis, [(i, i ^ step) for i in ran...  12.6 us
    ppermute x6, starting transfers between devices, shifted(): lax.ppermute(x, axis, [(i, (i + shift) % peers) for i in range(peers)])  11.9 us
    ppermute x10, starting transfers between devices, all_sum(): x = x + lax.ppermute(x, axis, [(i, i ^ step) for i in range(peers)])  9.19 us
    ppermute x2, starting transfers between devices, extended(): before = lax.ppermute(last, axis, up)  7.47 us
    ppermute x5, starting transfers between devices, all_moments(): lax.ppermute(jnp.stack([mean, spread]), axis, [(i, i ^ step) for i in ran...  7.18 us
  transfers between devices with their start and end apart: 27, of which 16 were waited for; matrix products, arithmetic and copies ran while one was open for 12% of the time, Pallas kernels for 0%

profile of v1, /device:TPU:0, one launch (start us, length us, event | category | flops | bytes accessed | tf_op | source)
XLA Modules:
  0.0 248.7 jit_solution(13282721406135225623)
XLA Ops:
  10.6 5.6 %collective-permute-start = (bf16[2,15,1536]{2,1,0:T(8,128)(2,1)S(1)}, bf16[2,15,1536]{2,1,0:T(8,128)(2,1)S(1)}, u32[]{:S(2)}, u32[]{:S(2)}) collective-permute-start(bf16[2,15,1536]{2,1,0:T(8,128)(2,1)S(1)} %get-tuple-element.96), channel_id=1, source_target_pairs={{0,1},{1,2},{2,3},{4,5},{5,6},{6,7},{8,9},{9,10},{10,11},{12,13},{... | collective-permute-start | bytes 276488 | tf_op jit(solution)/shard_map/ppermute | solution.py:16
  16.2 1.8 slice_reduce_fusion.34
  19.5 3.9 %fusion.169 = (f32[1536]{0:T(1024)S(1)}, f32[2,64,1536]{2,1,0:T(8,128)S(1)}) fusion(bf16[2,15,1536]{2,1,0:T(8,128)(2,1)S(1)} %collective-permute-done.1, bf16[2,64,1536]{2,1,0:T(8,128)(2,1)S(1)} %fusion.18, f32[1536]{0:T(1024)S(1)} %get-tuple-element.68, f32[1536]{0:T(1024)S(1)} %get-tuple-element.69, f32[1536]{0:T(1024)S(1)} %get-tuple-element.40, ...), kind=kLoop, calls=%fused_computation.391 | loop fusion | flops 35977728 | bytes 1560576 | tf_op jit(solution)/shard_map/reduce_sum | solution.py:76
  24.9 2.0 collective-permute-start.3
  26.9 1.8 collective-permute-done.3
  28.8 2.0 collective-permute-start.4
  30.8 1.7 collective-permute-done.4
  32.6 2.1 collective-permute-start.5
  34.7 4.0 %collective-permute-done.5 = f32[2,1536]{1,0:T(2,128)S(1)} collective-permute-done((f32[2,1536]{1,0:T(2,128)S(1)}, f32[2,1536]{1,0:T(2,128)S(1)}, u32[]{:S(2)}, u32[]{:S(2)}) %collective-permute-start.5) | collective-permute-done | bytes 12320 | tf_op jit(solution)/shard_map/ppermute | solution.py:44
  39.8 3.9 %collective-permute-done.6 = f32[2,1536]{1,0:T(2,128)S(1)} collective-permute-done((f32[2,1536]{1,0:T(2,128)S(1)}, f32[2,1536]{1,0:T(2,128)S(1)}, u32[]{:S(2)}, u32[]{:S(2)}) %collective-permute-start.6) | collective-permute-done | bytes 12320 | tf_op jit(solution)/shard_map/ppermute | solution.py:44
  44.4 57.9 %all-gather.2.cloned.1.call-done = bf16[1536,1536]{1,0:T(8,128)(2,1)} async-done(((bf16[384,1536]{1,0:T(8,128)(2,1)}), bf16[1536,1536]{1,0:T(8,128)(2,1)}) %all-gather.2.cloned.1.call-update) | async-done | bytes 4718608 | tf_op jit(solution)/shard_map/all_gather | solution.py:68
  102.2 4.2 %fusion.166 = (f32[1536]{0:T(1024)S(1)}, f32[1536]{0:T(1024)S(1)}, bf16[2,64,1536]{2,1,0:T(8,128)(2,1)S(1)}, f32[2,64,1536]{2,1,0:T(8,128)S(1)}) fusion(f32[1536]{0:T(1024)S(1)} %get-tuple-element.86, f32[2,64,1536]{2,1,0:T(8,128)S(1)} %get-tuple-element.88, f32[1536]{0:T(1024)S(1)} %get-tuple-element.98, f32[1536]{0:T(1024)S(1)} %copy-done.16, ...), kind=kOutput, calls=%fused_computation.389 | convolution fusion | flops 607122432 | bytes 7114752 | tf_op jit(solution)/shard_map/btd,cd->btc/dot_general | solution.py:95
  107.8 1.6 collective-permute-start.8
  109.4 2.2 collective-permute-done.8
  111.6 1.6 collective-permute-start.9
  113.1 2.2 collective-permute-done.9
  115.4 2.3 collective-permute-start.19
  120.8 4.9 %collective-permute-start.16 = (bf16[128,384]{1,0:T(8,128)(2,1)S(1)}, bf16[128,384]{1,0:T(8,128)(2,1)}, u32[]{:S(2)}, u32[]{:S(2)}) collective-permute-start(bf16[128,384]{1,0:T(8,128)(2,1)S(1)} %get-tuple-element.91), channel_id=1, source_target_pairs={{0,3},{1,0},{2,1},{3,2},{4,7},{5,4},{6,5},{7,6},{8,11},{9,8},{10,9... | collective-permute-start | bytes 294920 | tf_op jit(solution)/shard_map/ppermute | solution.py:55
  125.7 26.8 %collective-permute-done.11 = f32[2,1536]{1,0:T(2,128)S(1)} collective-permute-done((f32[2,1536]{1,0:T(2,128)S(1)}, f32[2,1536]{1,0:T(2,128)S(1)}, u32[]{:S(2)}, u32[]{:S(2)}) %collective-permute-start.11) | collective-permute-done | bytes 12320 | tf_op jit(solution)/shard_map/ppermute | solution.py:34
  153.2 2.3 fusion.98
  159.2 3.9 %fusion.7 = bf16[2,64,1536]{2,1,0:T(8,128)(2,1)} fusion(bf16[2,64,1536]{2,1,0:T(8,128)(2,1)S(1)} %get-tuple-element.89, bf16[1536,1536]{1,0:T(8,128)(2,1)} %all-gather.2.cloned.1.call-done), kind=kOutput, calls=%fused_computation.37 | convolution fusion | flops 604176384 | bytes 5505024 | tf_op jit(solution)/shard_map/btc,cd->btd/dot_general | solution.py:92
  163.1 3.5 %collective-permute-start.14 = (bf16[128,384]{1,0:T(8,128)(2,1)S(1)}, bf16[128,384]{1,0:T(8,128)(2,1)S(1)}, u32[]{:S(2)}, u32[]{:S(2)}) collective-permute-start(bf16[128,384]{1,0:T(8,128)(2,1)S(1)} %get-tuple-element.93), channel_id=1, source_target_pairs={{0,1},{1,2},{2,3},{3,0},{4,5},{5,6},{6,7},{7,4},{8,9},{9,10},{10,1... | collective-permute-start | bytes 294920 | tf_op jit(solution)/shard_map/ppermute | solution.py:55
  166.7 1.9 collective-permute-start.13
  170.1 1.6 collective-permute-start.21
  171.7 1.9 collective-permute-done.15
  173.6 3.7 %fusion.10 = f32[384,1536]{1,0:T(8,128)} fusion(bf16[128,1536]{1,0:T(8,128)(2,1)} %collective-permute-done.19, bf16[128,1536]{1,0:T(8,128)(2,1)} %collective-permute-done.18, bf16[128,1536]{1,0:T(8,128)(2,1)} %collective-permute-done.17, bf16[128,1536]{1,0:T(8,128)(2,1)} %bitcast.2, bf16[128,384]{1,0:T(8,128)(2,1)} %collective-permute-done.16, ...), kind=kOutput, calls=%fused_computation.94 | convolution fusion | flops 611844096 | bytes 4325376 | tf_op jit(solution)/shard_map/fc,fd->cd/dot_general | solution.py:134
  178.9 4.1 %multiply_convert_fusion = (bf16[2,64,1536]{2,1,0:T(8,128)(2,1)S(1)}, f32[2,64,1536]{2,1,0:T(8,128)S(1)}) fusion(bf16[2,64,3072]{2,1,0:T(8,128)(2,1)S(1)} %copy-done, bf16[2,64,1536]{2,1,0:T(8,128)(2,1)S(1)} %get-tuple-element.82, bf16[2,15,1536]{2,1,0:T(8,128)(2,1)S(1)} %collective-permute-done.13, f32[1536]{0:T(1024)S(1)} %copy-done.8, ...), kind=kLoop, calls=%fused_computation.217 | loop fusion | flops 36962304 | bytes 2340864 | tf_op jit(solution)/shard_map/convert
  183.0 3.1 %collective-permute-done.22 = f32[31,1536]{1,0:T(8,128)S(1)} collective-permute-done((f32[31,1536]{1,0:T(8,128)S(1)}, f32[31,1536]{1,0:T(8,128)S(1)}, u32[]{:S(2)}, u32[]{:S(2)}) %collective-permute-start.22) | collective-permute-done | bytes 190496 | tf_op jit(solution)/shard_map/ppermute | solution.py:34
  187.6 5.0 %collective-permute-done.23 = f32[31,1536]{1,0:T(8,128)S(1)} collective-permute-done((f32[31,1536]{1,0:T(8,128)S(1)}, f32[31,1536]{1,0:T(8,128)S(1)}, u32[]{:S(2)}, u32[]{:S(2)}) %collective-permute-start.23) | collective-permute-done | bytes 190496 | tf_op jit(solution)/shard_map/ppermute | solution.py:34
  193.7 7.7 %collective-permute-done.24 = f32[31,1536]{1,0:T(8,128)S(1)} collective-permute-done((f32[31,1536]{1,0:T(8,128)S(1)}, f32[31,1536]{1,0:T(8,128)S(1)}, u32[]{:S(2)}, u32[]{:S(2)}) %collective-permute-start.24) | collective-permute-done | bytes 190496 | tf_op jit(solution)/shard_map/ppermute | solution.py:34
  202.1 36.5 %all-reduce.2.cloned.1.call-done = f32[384,1536]{1,0:T(8,128)} async-done(((f32[384,1536]{1,0:T(8,128)}), f32[384,1536]{1,0:T(8,128)}) %all-reduce.2.cloned.1.call-update) | async-done | bytes 2359312 | tf_op jit(solution)/shard_map/psum | solution.py:140
  238.6 3.2 %copy.13 = f32[384,1536]{1,0:T(8,128)} copy(f32[384,1536]{1,0:T(8,128)} %all-reduce.2.cloned.1.call-done) | data formatting | bytes 4718592
  (138 shorter events, 23.0 us)
Async XLA Ops:
  7.2 95.0 %copy-start.16 = (f32[1536]{0:T(1024)S(1)}, f32[1536]{0:T(1024)}, u32[]{:S(2)}) copy-start(f32[1536]{0:T(1024)} %param.9) | copy-start | bytes 18436
  7.2 95.0 %all-gather.2.cloned.1.call-start = ((), (), s32[]{:S(2)}) async-start(), calls=%async_computation | async-start | bytes 5898240 | tf_op jit(solution)/shard_map/all_gather | solution.py:68
  7.9 230.7 %all-reduce.2.cloned.1.call-start = ((), (), s32[]{:S(2)}) async-start(), calls=%async_computation.1 | async-start | bytes 4718592 | tf_op jit(solution)/shard_map/psum | solution.py:140
  9.3 10.2 %collective-permute-start.1 = (bf16[2,15,1536]{2,1,0:T(8,128)(2,1)S(1)}, bf16[2,15,1536]{2,1,0:T(8,128)(2,1)S(1)}, u32[]{:S(2)}, u32[]{:S(2)}) collective-permute-start(bf16[2,15,1536]{2,1,0:T(8,128)(2,1)S(1)} %get-tuple-element.97), channel_id=1, source_target_pairs={{1,0},{2,1},{3,2},{5,4},{6,5},{7,6},{9,8},{10,9},{11,10},{13,12},{... | collective-permute-start | bytes 276488 | tf_op jit(solution)/shard_map/ppermute | solution.py:17
  10.6 8.9 %collective-permute-start = (bf16[2,15,1536]{2,1,0:T(8,128)(2,1)S(1)}, bf16[2,15,1536]{2,1,0:T(8,128)(2,1)S(1)}, u32[]{:S(2)}, u32[]{:S(2)}) collective-permute-start(bf16[2,15,1536]{2,1,0:T(8,128)(2,1)S(1)} %get-tuple-element.96), channel_id=1, source_target_pairs={{0,1},{1,2},{2,3},{4,5},{5,6},{6,7},{8,9},{9,10},{10,11},{12,13},{... | collective-permute-start | bytes 276488 | tf_op jit(solution)/shard_map/ppermute | solution.py:16
  19.5 87.0 %copy-start.5 = (f32[1536]{0:T(1024)}, f32[1536]{0:T(1024)S(1)}, u32[]{:S(2)}) copy-start(f32[1536]{0:T(1024)S(1)} %get-tuple-element.67) | copy-start | bytes 18436
  19.5 87.0 %copy-start.7 = (f32[1536]{0:T(1024)}, f32[1536]{0:T(1024)S(1)}, u32[]{:S(2)}) copy-start(f32[1536]{0:T(1024)S(1)} %get-tuple-element.68) | copy-start | bytes 18436
  19.5 87.0 %copy-start.9 = (f32[1536]{0:T(1024)}, f32[1536]{0:T(1024)S(1)}, u32[]{:S(2)}) copy-start(f32[1536]{0:T(1024)S(1)} %get-tuple-element.69) | copy-start | bytes 18436
  23.6 1.2 collective-permute-start.2
  24.9 3.8 %collective-permute-start.3 = (f32[2,1536]{1,0:T(2,128)S(1)}, f32[2,1536]{1,0:T(2,128)S(1)}, u32[]{:S(2)}, u32[]{:S(2)}) collective-permute-start(f32[2,1536]{1,0:T(2,128)S(1)} %pad_maximum_fusion.6), channel_id=1, source_target_pairs={{0,8},{4,12},{8,0},{12,4},{16,24},{20,28},{24,16},{28,20},{1,9},{5... | collective-permute-start | bytes 36872 | tf_op jit(solution)/shard_map/ppermute | solution.py:44
  28.8 3.8 %collective-permute-start.4 = (f32[2,1536]{1,0:T(2,128)S(1)}, f32[2,1536]{1,0:T(2,128)S(1)}, u32[]{:S(2)}, u32[]{:S(2)}) collective-permute-start(f32[2,1536]{1,0:T(2,128)S(1)} %pad_maximum_fusion.7), channel_id=1, source_target_pairs={{0,16},{4,20},{8,24},{12,28},{16,0},{20,4},{24,8},{28,12},{1,17},{... | collective-permute-start | bytes 36872 | tf_op jit(solution)/shard_map/ppermute | solution.py:44
  32.6 6.1 %collective-permute-start.5 = (f32[2,1536]{1,0:T(2,128)S(1)}, f32[2,1536]{1,0:T(2,128)S(1)}, u32[]{:S(2)}, u32[]{:S(2)}) collective-permute-start(f32[2,1536]{1,0:T(2,128)S(1)} %pad_maximum_fusion.8), channel_id=1, source_target_pairs={{0,1},{1,0},{2,3},{3,2},{4,5},{5,4},{6,7},{7,6},{8,9},{9,8},{10,11... | collective-permute-start | bytes 36872 | tf_op jit(solution)/shard_map/ppermute | solution.py:44
  38.7 4.9 %collective-permute-start.6 = (f32[2,1536]{1,0:T(2,128)S(1)}, f32[2,1536]{1,0:T(2,128)S(1)}, u32[]{:S(2)}, u32[]{:S(2)}) collective-permute-start(f32[2,1536]{1,0:T(2,128)S(1)} %pad_maximum_fusion.9), channel_id=1, source_target_pairs={{0,2},{1,3},{2,0},{3,1},{4,6},{5,7},{6,4},{7,5},{8,10},{9,11},{10,... | collective-permute-start | bytes 36872 | tf_op jit(solution)/shard_map/ppermute | solution.py:44
  44.4 62.1 %copy-start.13 = (f32[1536]{0:T(1024)}, f32[1536]{0:T(1024)S(1)}, u32[]{:S(2)}) copy-start(f32[1536]{0:T(1024)S(1)} %get-tuple-element.98) | copy-start | bytes 18436
  106.5 1.2 collective-permute-start.7
  107.8 3.8 %collective-permute-start.8 = (f32[2,1536]{1,0:T(2,128)S(1)}, f32[2,1536]{1,0:T(2,128)S(1)}, u32[]{:S(2)}, u32[]{:S(2)}) collective-permute-start(f32[2,1536]{1,0:T(2,128)S(1)} %fusion.165), channel_id=1, source_target_pairs={{0,8},{4,12},{8,0},{12,4},{16,24},{20,28},{24,16},{28,20},{1,9},{5... | collective-permute-start | bytes 36872 | tf_op jit(solution)/shard_map/ppermute | solution.py:34
  111.6 3.8 %collective-permute-start.9 = (f32[2,1536]{1,0:T(2,128)S(1)}, f32[2,1536]{1,0:T(2,128)S(1)}, u32[]{:S(2)}, u32[]{:S(2)}) collective-permute-start(f32[2,1536]{1,0:T(2,128)S(1)} %fusion.175), channel_id=1, source_target_pairs={{0,16},{4,20},{8,24},{12,28},{16,0},{20,4},{24,8},{28,12},{1,17},{... | collective-permute-start | bytes 36872 | tf_op jit(solution)/shard_map/ppermute | solution.py:34
  115.3 4.0 %collective-permute-start.10 = (f32[2,1536]{1,0:T(2,128)S(1)}, f32[2,1536]{1,0:T(2,128)S(1)}, u32[]{:S(2)}, u32[]{:S(2)}) collective-permute-start(f32[2,1536]{1,0:T(2,128)S(1)} %add.503), channel_id=1, source_target_pairs={{0,1},{1,0},{2,3},{3,2},{4,5},{5,4},{6,7},{7,6},{8,9},{9,8},{10,11... | collective-permute-start | bytes 36872 | tf_op jit(solution)/shard_map/ppermute | solution.py:34
  115.4 47.6 %collective-permute-start.19 = (bf16[128,1536]{1,0:T(8,128)(2,1)}, bf16[128,1536]{1,0:T(8,128)(2,1)}, u32[]{:S(2)}, u32[]{:S(2)}) collective-permute-start(bf16[128,1536]{1,0:T(8,128)(2,1)} %bitcast.2), channel_id=1, source_target_pairs={{0,3},{1,0},{2,1},{3,2},{4,7},{5,4},{6,5},{7,6},{8,11},{9,8},{10,9... | collective-permute-start | bytes 1179656 | tf_op jit(solution)/shard_map/ppermute | solution.py:55
  117.7 48.9 %collective-permute-start.18 = (bf16[128,1536]{1,0:T(8,128)(2,1)}, bf16[128,1536]{1,0:T(8,128)(2,1)}, u32[]{:S(2)}, u32[]{:S(2)}) collective-permute-start(bf16[128,1536]{1,0:T(8,128)(2,1)} %bitcast.2), channel_id=1, source_target_pairs={{0,2},{1,3},{2,0},{3,1},{4,6},{5,7},{6,4},{7,5},{8,10},{9,11},{10,... | collective-permute-start | bytes 1179656 | tf_op jit(solution)/shard_map/ppermute | solution.py:55
  118.9 49.7 %collective-permute-start.17 = (bf16[128,1536]{1,0:T(8,128)(2,1)}, bf16[128,1536]{1,0:T(8,128)(2,1)}, u32[]{:S(2)}, u32[]{:S(2)}) collective-permute-start(bf16[128,1536]{1,0:T(8,128)(2,1)} %bitcast.2), channel_id=1, source_target_pairs={{0,1},{1,2},{2,3},{3,0},{4,5},{5,6},{6,7},{7,4},{8,9},{9,10},{10,1... | collective-permute-start | bytes 1179656 | tf_op jit(solution)/shard_map/ppermute | solution.py:55
  119.3 33.2 %collective-permute-start.11 = (f32[2,1536]{1,0:T(2,128)S(1)}, f32[2,1536]{1,0:T(2,128)S(1)}, u32[]{:S(2)}, u32[]{:S(2)}) collective-permute-start(f32[2,1536]{1,0:T(2,128)S(1)} %add.504), channel_id=1, source_target_pairs={{0,2},{1,3},{2,0},{3,1},{4,6},{5,7},{6,4},{7,5},{8,10},{9,11},{10,... | collective-permute-start | bytes 36872 | tf_op jit(solution)/shard_map/ppermute | solution.py:34
  120.8 49.3 %collective-permute-start.16 = (bf16[128,384]{1,0:T(8,128)(2,1)S(1)}, bf16[128,384]{1,0:T(8,128)(2,1)}, u32[]{:S(2)}, u32[]{:S(2)}) collective-permute-start(bf16[128,384]{1,0:T(8,128)(2,1)S(1)} %get-tuple-element.91), channel_id=1, source_target_pairs={{0,3},{1,0},{2,1},{3,2},{4,7},{5,4},{6,5},{7,6},{8,11},{9,8},{10,9... | collective-permute-start | bytes 294920 | tf_op jit(solution)/shard_map/ppermute | solution.py:55
  159.1 4.0 %collective-permute-start.20 = (f32[31,1536]{1,0:T(8,128)S(1)}, f32[31,1536]{1,0:T(8,128)S(1)}, u32[]{:S(2)}, u32[]{:S(2)}) collective-permute-start(f32[31,1536]{1,0:T(8,128)S(1)} %stack.172), channel_id=1, source_target_pairs={{0,4},{4,0},{8,12},{12,8},{16,20},{20,16},{24,28},{28,24},{1,5},{5... | collective-permute-start | bytes 571400 | tf_op jit(solution)/shard_map/ppermute | solution.py:34
  163.1 10.5 %collective-permute-start.15 = (bf16[128,384]{1,0:T(8,128)(2,1)S(1)}, bf16[128,384]{1,0:T(8,128)(2,1)S(1)}, u32[]{:S(2)}, u32[]{:S(2)}) collective-permute-start(bf16[128,384]{1,0:T(8,128)(2,1)S(1)} %get-tuple-element.92), channel_id=1, source_target_pairs={{0,2},{1,3},{2,0},{3,1},{4,6},{5,7},{6,4},{7,5},{8,10},{9,11},{10,... | collective-permute-start | bytes 294920 | tf_op jit(solution)/shard_map/ppermute | solution.py:55
  163.1 10.5 %collective-permute-start.14 = (bf16[128,384]{1,0:T(8,128)(2,1)S(1)}, bf16[128,384]{1,0:T(8,128)(2,1)S(1)}, u32[]{:S(2)}, u32[]{:S(2)}) collective-permute-start(bf16[128,384]{1,0:T(8,128)(2,1)S(1)} %get-tuple-element.93), channel_id=1, source_target_pairs={{0,1},{1,2},{2,3},{3,0},{4,5},{5,6},{6,7},{7,4},{8,9},{9,10},{10,1... | collective-permute-start | bytes 294920 | tf_op jit(solution)/shard_map/ppermute | solution.py:55
  166.7 12.2 %collective-permute-start.13 = (bf16[2,15,1536]{2,1,0:T(8,128)(2,1)S(1)}, bf16[2,15,1536]{2,1,0:T(8,128)(2,1)S(1)}, u32[]{:S(2)}, u32[]{:S(2)}) collective-permute-start(bf16[2,15,1536]{2,1,0:T(8,128)(2,1)S(1)} %get-tuple-element.95), channel_id=1, source_target_pairs={{0,1},{1,2},{2,3},{4,5},{5,6},{6,7},{8,9},{9,10},{10,11},{12,13},{... | collective-permute-start | bytes 276488 | tf_op jit(solution)/shard_map/ppermute | solution.py:16
  168.6 10.2 %collective-permute-start.12 = (bf16[2,15,1536]{2,1,0:T(8,128)(2,1)S(1)}, bf16[2,15,1536]{2,1,0:T(8,128)(2,1)S(1)}, u32[]{:S(2)}, u32[]{:S(2)}) collective-permute-start(bf16[2,15,1536]{2,1,0:T(8,128)(2,1)S(1)} %get-tuple-element.94), channel_id=1, source_target_pairs={{1,0},{2,1},{3,2},{5,4},{6,5},{7,6},{9,8},{10,9},{11,10},{13,12},{... | collective-permute-start | bytes 276488 | tf_op jit(solution)/shard_map/ppermute | solution.py:17
  170.1 7.2 %collective-permute-start.21 = (f32[31,1536]{1,0:T(8,128)S(1)}, f32[31,1536]{1,0:T(8,128)S(1)}, u32[]{:S(2)}, u32[]{:S(2)}) collective-permute-start(f32[31,1536]{1,0:T(8,128)S(1)} %add.543), channel_id=1, source_target_pairs={{0,8},{4,12},{8,0},{12,4},{16,24},{20,28},{24,16},{28,20},{1,9},{5... | collective-permute-start | bytes 571400 | tf_op jit(solution)/shard_map/ppermute | solution.py:34
  177.4 8.7 %collective-permute-start.22 = (f32[31,1536]{1,0:T(8,128)S(1)}, f32[31,1536]{1,0:T(8,128)S(1)}, u32[]{:S(2)}, u32[]{:S(2)}) collective-permute-start(f32[31,1536]{1,0:T(8,128)S(1)} %add.544), channel_id=1, source_target_pairs={{0,16},{4,20},{8,24},{12,28},{16,0},{20,4},{24,8},{28,12},{1,17},{... | collective-permute-start | bytes 571400 | tf_op jit(solution)/shard_map/ppermute | solution.py:34
  186.1 6.5 %collective-permute-start.23 = (f32[31,1536]{1,0:T(8,128)S(1)}, f32[31,1536]{1,0:T(8,128)S(1)}, u32[]{:S(2)}, u32[]{:S(2)}) collective-permute-start(f32[31,1536]{1,0:T(8,128)S(1)} %add.545), channel_id=1, source_target_pairs={{0,1},{1,0},{2,3},{3,2},{4,5},{5,4},{6,7},{7,6},{8,9},{9,8},{10,11... | collective-permute-start | bytes 571400 | tf_op jit(solution)/shard_map/ppermute | solution.py:34
  192.7 8.7 %collective-permute-start.24 = (f32[31,1536]{1,0:T(8,128)S(1)}, f32[31,1536]{1,0:T(8,128)S(1)}, u32[]{:S(2)}, u32[]{:S(2)}) collective-permute-start(f32[31,1536]{1,0:T(8,128)S(1)} %add.546), channel_id=1, source_target_pairs={{0,2},{1,3},{2,0},{3,1},{4,6},{5,7},{6,4},{7,5},{8,10},{9,11},{10,... | collective-permute-start | bytes 571400 | tf_op jit(solution)/shard_map/ppermute | solution.py:34
  (12 other events, 138.1 us)
Sparse Core Ops, SparseCore 0:
  9.6 92.5 all-gather.1
  177.4 61.1 all-reduce.1

commit v2 on v1

--- a/solution.py
+++ b/solution.py
@@ -50,9 +50,32 @@
     return mean, spread
 
 
-def shifted(x, axis, shift):
-    peers = lax.axis_size(axis)
-    return lax.ppermute(x, axis, [(i, (i + shift) % peers) for i in range(peers)])
+def gather_weight(block):
+    peers = lax.axis_size("tensor")
+    me = lax.axis_index("tensor")
+    pairs = lax.axis_size("dp") % 2 == 0
+    if pairs:
+        half = block.shape[0] // 2
+        core = lax.rem(lax.axis_index("dp"), 2)
+        mine = lax.dynamic_slice_in_dim(block, core * half, half, axis=0)
+    else:
+        mine = block
+    right = [(i, i + 1) for i in range(peers - 1)]
+    left = [(i + 1, i) for i in range(peers - 1)]
+    index = lax.broadcasted_iota(jnp.int32, (peers, 1, 1), 0)
+    held = jnp.where(index == me, mine[None], jnp.zeros_like(mine)[None])
+    going_right, going_left = mine, mine
+    for hop in range(1, peers):
+        going_right = lax.ppermute(going_right, "tensor", right)
+        going_left = lax.ppermute(going_left, "tensor", left)
+        held = jnp.where(index == me - hop, going_right[None], held)
+        held = jnp.where(index == me + hop, going_left[None], held)
+    if pairs:
+        other = lax.ppermute(held, "dp", [(i, i ^ 1) for i in range(lax.axis_size("dp"))])
+        first = jnp.where(core == 0, held, other)
+        second = jnp.where(core == 0, other, held)
+        held = jnp.concatenate([first, second], axis=1)
+    return held.reshape(peers * block.shape[0], block.shape[1])
 
 
 def on_device(glu_input, depth_kernel, norm_scale, norm_shift, proj_weight, out_grad):
@@ -65,7 +88,7 @@
     me = lax.axis_index("tensor")
     local = glu_input.shape[0] * frames
     everyone = local * lax.axis_size("dp") * peers
-    full_weight = lax.all_gather(proj_weight, "tensor", axis=0, tiled=True)
+    full_weight = gather_weight(proj_weight)
     values = glu_input[..., :width].astype(jnp.float32)
     gates = jax.nn.sigmoid(glu_input[..., width:].astype(jnp.float32))
     gated = (values * gates).astype(jnp.bfloat16)
@@ -124,19 +147,9 @@
     ).astype(jnp.bfloat16)
     flat_act = activated.reshape(-1, width)
     flat_grad = out_grad.reshape(-1, width)
-    act_parts = [lax.dynamic_slice_in_dim(flat_act, me * rows, rows, axis=1)]
-    grad_parts = [flat_grad]
-    for shift in range(1, peers):
-        owner = lax.rem(me + shift, peers)
-        block = lax.dynamic_slice_in_dim(flat_act, owner * rows, rows, axis=1)
-        act_parts.append(shifted(block, "tensor", shift))
-        grad_parts.append(shifted(flat_grad, "tensor", shift))
-    local_grad = jnp.einsum(
-        "fc,fd->cd",
-        jnp.concatenate(act_parts, axis=0),
-        jnp.concatenate(grad_parts, axis=0),
-        preferred_element_type=jnp.float32,
-    )
+    group_grad = lax.all_gather(flat_grad, "tensor", axis=0, tiled=True)
+    group_act = lax.all_to_all(flat_act, "tensor", split_axis=1, concat_axis=0, tiled=True)
+    local_grad = jnp.einsum("fc,fd->cd", group_act, group_grad, preferred_element_type=jnp.float32)
     weight_grad = lax.psum(local_grad, "dp")
     return (conv_output, input_grad, weight_grad, kernel_grad, scale_grad, shift_grad)
 

time: 249 us -> 231 us (0.928)
  waiting for transfers between devices: 158 us -> 94.1 us
  other arithmetic: 17.5 us -> 42.8 us
  starting transfers between devices: 38.6 us -> 53 us
  local copies, waits for them, and re-layouts: 7.79 us -> 13.9 us
    all_gather x1, waiting for transfers between devices: 57.9 us -> 11.3 us  [on_device(): group_grad = lax.all_gather(flat_grad, 'tensor', axis=0, tiled=True)]
    ppermute x10, waiting for transfers between devices: 48.6 us -> 23.8 us  [all_sum(): x = x + lax.ppermute(x, axis, [(i, i ^ step) for i in range(peers)])]
    ppermute x6 -> x7, waiting for transfers between devices: 1.88 us -> 12.5 us  [the longest x3 8.27 us: gather_weight(): going_right = lax.ppermute(going_right, 'tensor', right)]
    select_n x0 -> x2, other arithmetic: none -> 6.08 us  [the longest x1 3.15 us: gather_weight(): first = jnp.where(core == 0, held, other)]
    ppermute x6 -> x7, starting transfers between devices: 11.9 us -> 17.7 us  [the longest x3 13.8 us: gather_weight(): going_right = lax.ppermute(going_right, 'tensor', right)]
    unnamed x35 -> x109, local copies, waits for them, and re-layouts: 3.86 us -> 7.58 us
    reduce_sum x4, other arithmetic: 5.1 us -> 8.65 us  [on_device(): jnp.sum(padded[:, offset:offset + frames, :].astype(jnp.float32) * grad_w...]
    all_to_all x0 -> x1, starting transfers between devices: none -> 3.46 us  [on_device(): lax.all_to_all(flat_act, 'tensor', split_axis=1, concat_axis=0, tiled=True)]
  transfers between devices with their start and end apart: 27 -> 29, of which waited for: 16 -> 17; matrix products, arithmetic and copies ran while one was open for 12% -> 22% of each run, Pallas kernels for 0% -> 0%
where the time goes in v2:
time: 231 us; the launch traced here: 229 us
  waiting for transfers between devices  94.1 us (41%)
  starting transfers between devices  53 us (23%)
  other arithmetic  42.8 us (19%)
  between operations  15.2 us (7%)
  local copies, waits for them, and re-layouts  13.9 us (6%)
  matrix products  10.1 us (4%)
    psum x1, waiting for transfers between devices, on_device(): weight_grad = lax.psum(local_grad, 'dp')  34 us
    ppermute x10, waiting for transfers between devices, all_sum(): x = x + lax.ppermute(x, axis, [(i, i ^ step) for i in range(peers)])  23.8 us
    ppermute x3, starting transfers between devices, gather_weight(): going_right = lax.ppermute(going_right, 'tensor', right)  13.8 us
    ppermute x5, waiting for transfers between devices, all_moments(): lax.ppermute(jnp.stack([mean, spread]), axis, [(i, i ^ step) for i in ran...  12.5 us
    ppermute x10, starting transfers between devices, all_sum(): x = x + lax.ppermute(x, axis, [(i, i ^ step) for i in range(peers)])  11.4 us
    all_gather x1, waiting for transfers between devices, on_device(): group_grad = lax.all_gather(flat_grad, 'tensor', axis=0, tiled=True)  11.3 us
    ppermute x2, starting transfers between devices, extended(): before = lax.ppermute(last, axis, up)  9.73 us
    reduce_sum x4, other arithmetic, on_device(): jnp.sum(padded[:, offset:offset + frames, :].astype(jnp.float32) * grad_w...  8.65 us
  transfers between devices with their start and end apart: 29, of which 17 were waited for; matrix products, arithmetic and copies ran while one was open for 22% of the time, Pallas kernels for 0%

profile of v2, /device:TPU:0, one launch (start us, length us, event | category | flops | bytes accessed | tf_op | source)
XLA Modules:
  0.0 229.2 jit_solution(2860157548396607766)
XLA Ops:
  8.5 5.0 %collective-permute-start.10 = (bf16[192,1536]{1,0:T(8,128)(2,1)S(1)}, bf16[192,1536]{1,0:T(8,128)(2,1)S(1)}, u32[]{:S(2)}, u32[]{:S(2)}) collective-permute-start(bf16[192,1536]{1,0:T(8,128)(2,1)S(1)} %constant_dynamic-slice_fusion), channel_id=1, source_target_pairs={{0,1},{1,2},{2,3},{4,5},{5,6},{6,7},{8,9},{9,10},{10,11},{12,13},{... | collective-permute-start | bytes 1769480 | tf_op jit(solution)/shard_map/ppermute | solution.py:69
  16.8 4.5 %collective-permute-start = (bf16[2,15,1536]{2,1,0:T(8,128)(2,1)}, bf16[2,15,1536]{2,1,0:T(8,128)(2,1)S(1)}, u32[]{:S(2)}, u32[]{:S(2)}) collective-permute-start(bf16[2,15,1536]{2,1,0:T(8,128)(2,1)} %get-tuple-element.94), channel_id=1, source_target_pairs={{0,1},{1,2},{2,3},{4,5},{5,6},{6,7},{8,9},{9,10},{10,11},{12,13},{... | collective-permute-start | bytes 276488 | tf_op jit(solution)/shard_map/ppermute | solution.py:16
  23.2 3.8 %collective-permute-done.10 = bf16[192,1536]{1,0:T(8,128)(2,1)S(1)} collective-permute-done((bf16[192,1536]{1,0:T(8,128)(2,1)S(1)}, bf16[192,1536]{1,0:T(8,128)(2,1)S(1)}, u32[]{:S(2)}, u32[]{:S(2)}) %collective-permute-start.10) | collective-permute-done | bytes 589856 | tf_op jit(solution)/shard_map/ppermute | solution.py:69
  27.0 4.4 %collective-permute-start.11 = (bf16[192,1536]{1,0:T(8,128)(2,1)S(1)}, bf16[192,1536]{1,0:T(8,128)(2,1)S(1)}, u32[]{:S(2)}, u32[]{:S(2)}) collective-permute-start(bf16[192,1536]{1,0:T(8,128)(2,1)S(1)} %collective-permute-done.10), channel_id=1, source_target_pairs={{0,1},{1,2},{2,3},{4,5},{5,6},{6,7},{8,9},{9,10},{10,11},{12,13},{... | collective-permute-start | bytes 1769480 | tf_op jit(solution)/shard_map/ppermute | solution.py:69
  38.1 3.9 %collective-permute-done.11 = bf16[192,1536]{1,0:T(8,128)(2,1)S(1)} collective-permute-done((bf16[192,1536]{1,0:T(8,128)(2,1)S(1)}, bf16[192,1536]{1,0:T(8,128)(2,1)S(1)}, u32[]{:S(2)}, u32[]{:S(2)}) %collective-permute-start.11) | collective-permute-done | bytes 589856 | tf_op jit(solution)/shard_map/ppermute | solution.py:69
  42.1 4.4 %collective-permute-start.12 = (bf16[192,1536]{1,0:T(8,128)(2,1)S(1)}, bf16[192,1536]{1,0:T(8,128)(2,1)S(1)}, u32[]{:S(2)}, u32[]{:S(2)}) collective-permute-start(bf16[192,1536]{1,0:T(8,128)(2,1)S(1)} %collective-permute-done.11), channel_id=1, source_target_pairs={{0,1},{1,2},{2,3},{4,5},{5,6},{6,7},{8,9},{9,10},{10,11},{12,13},{... | collective-permute-start | bytes 1769480 | tf_op jit(solution)/shard_map/ppermute | solution.py:69
  48.5 7.0 %fusion.144 = (f32[1536]{0:T(1024)S(1)}, f32[2,64,1536]{2,1,0:T(8,128)S(1)}) fusion(bf16[2,15,1536]{2,1,0:T(8,128)(2,1)} %copy-done.9, bf16[2,64,1536]{2,1,0:T(8,128)(2,1)S(1)} %fusion.1, f32[1536]{0:T(1024)S(1)} %get-tuple-element.68, f32[1536]{0:T(1024)S(1)} %get-tuple-element.69, f32[1536]{0:T(1024)S(1)} %get-tuple-element.40, ...), kind=kLoop, calls=%fused_computation.380 | loop fusion | flops 35977728 | bytes 1560576 | tf_op jit(solution)/shard_map/reduce_sum | solution.py:99
  56.2 4.2 %collective-permute-done.9 = bf16[192,1536]{1,0:T(8,128)(2,1)S(1)} collective-permute-done((bf16[192,1536]{1,0:T(8,128)(2,1)S(1)}, bf16[192,1536]{1,0:T(8,128)(2,1)S(1)}, u32[]{:S(2)}, u32[]{:S(2)}) %collective-permute-start.9) | collective-permute-done | bytes 589856 | tf_op jit(solution)/shard_map/ppermute | solution.py:70
  60.4 2.9 %select_select_fusion = bf16[4,192,1536]{2,1,0:T(8,128)(2,1)} fusion(pred[4]{0:T(512)(128)(4,1)S(1)} %get-tuple-element.114, pred[4]{0:T(512)(128)(4,1)} %get-tuple-element.115, pred[4]{0:T(512)(128)(4,1)} %get-tuple-element.116, pred[4]{0:T(512)(128)(4,1)} %get-tuple-element.117, pred[4]{0:T(512)(128)(4,1)} %get-tuple-element.118, ...), kind=kLoop, calls=%fused_computation.36 | loop fusion | flops 8257536 | bytes 6488092 | tf_op jit(solution)/shard_map/jit(_where)/select_n | solution.py:72
  64.1 3.6 %collective-permute-done.2 = f32[2,1536]{1,0:T(2,128)S(1)} collective-permute-done((f32[2,1536]{1,0:T(2,128)S(1)}, f32[2,1536]{1,0:T(2,128)S(1)}, u32[]{:S(2)}, u32[]{:S(2)}) %collective-permute-start.2) | collective-permute-done | bytes 12320 | tf_op jit(solution)/shard_map/ppermute | solution.py:44
  69.9 2.2 collective-permute-done.3
  74.4 2.2 collective-permute-done.4
  82.3 2.6 %collective-permute-start.6 = (f32[2,1536]{1,0:T(2,128)}, f32[2,1536]{1,0:T(2,128)}, u32[]{:S(2)}, u32[]{:S(2)}) collective-permute-start(f32[2,1536]{1,0:T(2,128)} %pad_maximum_fusion.10), channel_id=1, source_target_pairs={{0,2},{1,3},{2,0},{3,1},{4,6},{5,7},{6,4},{7,5},{8,10},{9,11},{10,... | collective-permute-start | bytes 36872 | tf_op jit(solution)/shard_map/ppermute | solution.py:44
  84.8 2.4 %collective-permute-done.6 = f32[2,1536]{1,0:T(2,128)} collective-permute-done((f32[2,1536]{1,0:T(2,128)}, f32[2,1536]{1,0:T(2,128)}, u32[]{:S(2)}, u32[]{:S(2)}) %collective-permute-start.6) | collective-permute-done | bytes 12320 | tf_op jit(solution)/shard_map/ppermute | solution.py:44
  89.5 3.1 %broadcast_select_fusion.1 = (bf16[4,192,1536]{2,1,0:T(8,128)(2,1)S(1)}, bf16[4,192,1536]{2,1,0:T(8,128)(2,1)S(1)}) fusion(bf16[4,192,1536]{2,1,0:T(8,128)(2,1)} %collective-permute-done.13, pred[]{:T(512)S(6)} %eq.81, bf16[192,1536]{1,0:T(8,128)(2,1)S(1)} %constant_dynamic-slice_fusion, pred[4]{0:T(512)(128)(4,1)} %copy-done.52, ...), kind=kLoop, calls=%fused_computation.38 | loop fusion | flops 10616832 | bytes 11206685 | tf_op jit(solution)/shard_map/jit(_where)/select_n | solution.py:75
  93.6 2.6 %fusion.141 = (f32[1536]{0:T(1024)S(1)}, f32[1536]{0:T(1024)S(1)}, bf16[2,64,1536]{2,1,0:T(8,128)(2,1)S(1)}, f32[2,64,1536]{2,1,0:T(8,128)}) fusion(f32[1536]{0:T(1024)S(1)} %get-tuple-element.86, f32[2,64,1536]{2,1,0:T(8,128)S(1)} %get-tuple-element.88, f32[1536]{0:T(1024)S(1)} %get-tuple-element.96, f32[1536]{0:T(1024)S(1)} %copy-done.53, ...), kind=kOutput, calls=%fused_computation.378 | convolution fusion | flops 607122432 | bytes 7114752 | tf_op jit(solution)/shard_map/btd,cd->btc/dot_general | solution.py:118
  99.1 2.2 collective-permute-done.15
  103.0 2.2 collective-permute-done.16
  109.5 2.5 %collective-permute-start.18 = (f32[2,1536]{1,0:T(2,128)}, f32[2,1536]{1,0:T(2,128)}, u32[]{:S(2)}, u32[]{:S(2)}) collective-permute-start(f32[2,1536]{1,0:T(2,128)} %add.502), channel_id=1, source_target_pairs={{0,2},{1,3},{2,0},{3,1},{4,6},{5,7},{6,4},{7,5},{8,10},{9,11},{10,... | collective-permute-start | bytes 36872 | tf_op jit(solution)/shard_map/ppermute | solution.py:34
  113.0 3.5 %all-to-all-start = ((bf16[128,4,384]{2,0,1:T(8,128)(2,1)}), bf16[128,4,384]{2,0,1:T(8,128)(2,1)S(1)}, u32[]{:S(2)}, u32[]{:S(2)}) async-start(bf16[128,4,384]{2,0,1:T(8,128)(2,1)} %copy.12), calls=%async_computation | async-start | bytes 786432 | tf_op jit(solution)/shard_map/all_to_all | solution.py:151
  118.1 3.1 %fusion.81 = (f32[1536]{0:T(1024)S(1)}, f32[1536]{0:T(1024)S(1)}, f32[1536]{0:T(1024)S(1)}, f32[1536]{0:T(1024)S(1)}, f32[1536]{0:T(1024)S(1)}, /*index=5*/f32[1...) fusion(bf16[2,15,1536]{2,1,0:T(8,128)(2,1)} %copy-done.9, ...), kind=kLoop, calls=%fused_computation.208 | loop fusion | flops 12372480 | bytes 2537472 | tf_op jit(solution)/shard_map/reduce_sum | solution.py:138
  121.1 2.6 %fusion.65 = (f32[1536]{0:T(1024)S(1)}, f32[1536]{0:T(1024)S(1)}, f32[1536]{0:T(1024)S(1)}, f32[1536]{0:T(1024)S(1)}, f32[1536]{0:T(1024)S(1)}, /*index=5*/f32[1...) fusion(bf16[2,64,1536]{2,1,0:T(8,128)(2,1)S(1)} %get-tuple-element.82, ...), kind=kLoop, calls=%fused_computation.192 | loop fusion | flops 10799616 | bytes 933888 | tf_op jit(solution)/shard_map/reduce_sum | solution.py:138
  123.9 2.2 fusion.80
  127.6 3.9 %convolution_convert_fusion = bf16[2,64,1536]{2,1,0:T(8,128)(2,1)} fusion(bf16[2,64,1536]{2,1,0:T(8,128)(2,1)S(1)} %get-tuple-element.91, bf16[1536,1536,1]{1,0,2:T(8,128)(2,1)} %bitcast.18), kind=kOutput, calls=%fused_computation.35 | convolution fusion | flops 604176384 | bytes 5505024 | tf_op jit(solution)/shard_map/btc,cd->btd/dot_general | solution.py:115
  134.4 5.2 %collective-permute-start.20 = (bf16[2,15,1536]{2,1,0:T(8,128)(2,1)S(1)}, bf16[2,15,1536]{2,1,0:T(8,128)(2,1)}, u32[]{:S(2)}, u32[]{:S(2)}) collective-permute-start(bf16[2,15,1536]{2,1,0:T(8,128)(2,1)S(1)} %get-tuple-element.93), channel_id=1, source_target_pairs={{0,1},{1,2},{2,3},{4,5},{5,6},{6,7},{8,9},{9,10},{10,11},{12,13},{... | collective-permute-start | bytes 276488 | tf_op jit(solution)/shard_map/ppermute | solution.py:16
  141.8 11.3 %all-gather.2.cloned.1.call-done = bf16[512,1536]{1,0:T(8,128)(2,1)} async-done(((bf16[128,1536]{1,0:T(8,128)(2,1)}), bf16[512,1536]{1,0:T(8,128)(2,1)}) %all-gather.2.cloned.1.call-update) | async-done | bytes 1572880 | tf_op jit(solution)/shard_map/all_gather | solution.py:150
  153.2 3.6 %fusion.148 = f32[384,1536]{1,0:T(8,128)} fusion(bf16[512,384]{1,0:T(8,128)(2,1)S(1)} %bitcast.19, bf16[512,1536]{1,0:T(8,128)(2,1)} %all-gather.2.cloned.1.call-done), kind=kOutput, calls=%fused_computation.383 | convolution fusion | flops 603979776 | bytes 4325376 | tf_op jit(solution)/shard_map/fc,fd->cd/dot_general | solution.py:152
  158.0 7.2 %multiply_convert_fusion = (bf16[2,64,1536]{2,1,0:T(8,128)(2,1)S(1)}, f32[2,64,1536]{2,1,0:T(8,128)S(1)}) fusion(bf16[2,64,3072]{2,1,0:T(8,128)(2,1)S(1)} %copy-done.2, bf16[2,64,1536]{2,1,0:T(8,128)(2,1)S(1)} %get-tuple-element.82, bf16[2,15,1536]{2,1,0:T(8,128)(2,1)} %collective-permute-done.20, f32[1536]{0:T(1024)} %copy-done.43, f32[1536]{0:T(1024)} %copy-done.44, ...), kind=kLoop, calls=%fused_computation.210 | loop fusion | flops 36962304 | bytes 2340864 | tf_op jit(solution)/shard_map/convert
  166.6 6.6 %collective-permute-done.24 = f32[31,1536]{1,0:T(8,128)S(1)} collective-permute-done((f32[31,1536]{1,0:T(8,128)S(1)}, f32[31,1536]{1,0:T(8,128)S(1)}, u32[]{:S(2)}, u32[]{:S(2)}) %collective-permute-start.24) | collective-permute-done | bytes 190496 | tf_op jit(solution)/shard_map/ppermute | solution.py:34
  174.9 9.6 %collective-permute-done.25 = f32[31,1536]{1,0:T(8,128)S(1)} collective-permute-done((f32[31,1536]{1,0:T(8,128)S(1)}, f32[31,1536]{1,0:T(8,128)S(1)}, u32[]{:S(2)}, u32[]{:S(2)}) %collective-permute-start.25) | collective-permute-done | bytes 190496 | tf_op jit(solution)/shard_map/ppermute | solution.py:34
  185.2 34.0 %all-reduce.2.cloned.1.call-done = f32[384,1536]{1,0:T(8,128)} async-done(((f32[384,1536]{1,0:T(8,128)}), f32[384,1536]{1,0:T(8,128)}) %all-reduce.2.cloned.1.call-update) | async-done | bytes 2359312 | tf_op jit(solution)/shard_map/psum | solution.py:153
  219.2 3.2 %copy.14 = f32[384,1536]{1,0:T(8,128)} copy(f32[384,1536]{1,0:T(8,128)} %all-reduce.2.cloned.1.call-done) | data formatting | bytes 4718592
  (225 shorter events, 52.4 us)
Async XLA Ops:
  7.2 146.0 %all-gather.2.cloned.1.call-start = ((), (), s32[]{:S(2)}) async-start(), calls=%async_computation.1 | async-start | bytes 1966080 | tf_op jit(solution)/shard_map/all_gather | solution.py:150
  8.5 18.6 %collective-permute-start.10 = (bf16[192,1536]{1,0:T(8,128)(2,1)S(1)}, bf16[192,1536]{1,0:T(8,128)(2,1)S(1)}, u32[]{:S(2)}, u32[]{:S(2)}) collective-permute-start(bf16[192,1536]{1,0:T(8,128)(2,1)S(1)} %constant_dynamic-slice_fusion), channel_id=1, source_target_pairs={{0,1},{1,2},{2,3},{4,5},{5,6},{6,7},{8,9},{9,10},{10,11},{12,13},{... | collective-permute-start | bytes 1769480 | tf_op jit(solution)/shard_map/ppermute | solution.py:69
  13.5 18.0 %collective-permute-start.7 = (bf16[192,1536]{1,0:T(8,128)(2,1)S(1)}, bf16[192,1536]{1,0:T(8,128)(2,1)S(1)}, u32[]{:S(2)}, u32[]{:S(2)}) collective-permute-start(bf16[192,1536]{1,0:T(8,128)(2,1)S(1)} %constant_dynamic-slice_fusion), channel_id=1, source_target_pairs={{1,0},{2,1},{3,2},{5,4},{6,5},{7,6},{9,8},{10,9},{11,10},{13,12},{... | collective-permute-start | bytes 1769480 | tf_op jit(solution)/shard_map/ppermute | solution.py:70
  16.8 31.0 %collective-permute-start = (bf16[2,15,1536]{2,1,0:T(8,128)(2,1)}, bf16[2,15,1536]{2,1,0:T(8,128)(2,1)S(1)}, u32[]{:S(2)}, u32[]{:S(2)}) collective-permute-start(bf16[2,15,1536]{2,1,0:T(8,128)(2,1)} %get-tuple-element.94), channel_id=1, source_target_pairs={{0,1},{1,2},{2,3},{4,5},{5,6},{6,7},{8,9},{9,10},{10,11},{12,13},{... | collective-permute-start | bytes 276488 | tf_op jit(solution)/shard_map/ppermute | solution.py:16
  21.3 26.5 %collective-permute-start.1 = (bf16[2,15,1536]{2,1,0:T(8,128)(2,1)}, bf16[2,15,1536]{2,1,0:T(8,128)(2,1)S(1)}, u32[]{:S(2)}, u32[]{:S(2)}) collective-permute-start(bf16[2,15,1536]{2,1,0:T(8,128)(2,1)} %get-tuple-element.95), channel_id=1, source_target_pairs={{1,0},{2,1},{3,2},{5,4},{6,5},{7,6},{9,8},{10,9},{11,10},{13,12},{... | collective-permute-start | bytes 276488 | tf_op jit(solution)/shard_map/ppermute | solution.py:17
  23.2 40.1 %copy-start.52 = (pred[4]{0:T(512)(128)(4,1)}, pred[4]{0:T(512)(128)(4,1)S(1)}, u32[]{:S(2)}) copy-start(pred[4]{0:T(512)(128)(4,1)S(1)} %get-tuple-element.114) | copy-start | bytes 16
  27.0 15.0 %collective-permute-start.11 = (bf16[192,1536]{1,0:T(8,128)(2,1)S(1)}, bf16[192,1536]{1,0:T(8,128)(2,1)S(1)}, u32[]{:S(2)}, u32[]{:S(2)}) collective-permute-start(bf16[192,1536]{1,0:T(8,128)(2,1)S(1)} %collective-permute-done.10), channel_id=1, source_target_pairs={{0,1},{1,2},{2,3},{4,5},{5,6},{6,7},{8,9},{9,10},{10,11},{12,13},{... | collective-permute-start | bytes 1769480 | tf_op jit(solution)/shard_map/ppermute | solution.py:69
  31.5 15.0 %collective-permute-start.8 = (bf16[192,1536]{1,0:T(8,128)(2,1)S(1)}, bf16[192,1536]{1,0:T(8,128)(2,1)S(1)}, u32[]{:S(2)}, u32[]{:S(2)}) collective-permute-start(bf16[192,1536]{1,0:T(8,128)(2,1)S(1)} %collective-permute-done.7), channel_id=1, source_target_pairs={{1,0},{2,1},{3,2},{5,4},{6,5},{7,6},{9,8},{10,9},{11,10},{13,12},{... | collective-permute-start | bytes 1769480 | tf_op jit(solution)/shard_map/ppermute | solution.py:70
  37.5 41.4 %copy-start.31 = (f32[1536]{0:T(1024)}, f32[1536]{0:T(1024)S(1)}, u32[]{:S(2)}) copy-start(f32[1536]{0:T(1024)S(1)} %get-tuple-element.56) | copy-start | bytes 18436
  37.5 43.5 %copy-start.32 = (f32[1536]{0:T(1024)}, f32[1536]{0:T(1024)S(1)}, u32[]{:S(2)}) copy-start(f32[1536]{0:T(1024)S(1)} %get-tuple-element.57) | copy-start | bytes 18436
  42.1 14.1 %collective-permute-start.12 = (bf16[192,1536]{1,0:T(8,128)(2,1)S(1)}, bf16[192,1536]{1,0:T(8,128)(2,1)S(1)}, u32[]{:S(2)}, u32[]{:S(2)}) collective-permute-start(bf16[192,1536]{1,0:T(8,128)(2,1)S(1)} %collective-permute-done.11), channel_id=1, source_target_pairs={{0,1},{1,2},{2,3},{4,5},{5,6},{6,7},{8,9},{9,10},{10,11},{12,13},{... | collective-permute-start | bytes 1769480 | tf_op jit(solution)/shard_map/ppermute | solution.py:69
  46.5 13.8 %collective-permute-start.9 = (bf16[192,1536]{1,0:T(8,128)(2,1)S(1)}, bf16[192,1536]{1,0:T(8,128)(2,1)S(1)}, u32[]{:S(2)}, u32[]{:S(2)}) collective-permute-start(bf16[192,1536]{1,0:T(8,128)(2,1)S(1)} %collective-permute-done.8), channel_id=1, source_target_pairs={{1,0},{2,1},{3,2},{5,4},{6,5},{7,6},{9,8},{10,9},{11,10},{13,12},{... | collective-permute-start | bytes 1769480 | tf_op jit(solution)/shard_map/ppermute | solution.py:70
  63.4 26.0 %collective-permute-start.13 = (bf16[4,192,1536]{2,1,0:T(8,128)(2,1)}, bf16[4,192,1536]{2,1,0:T(8,128)(2,1)}, u32[]{:S(2)}, u32[]{:S(2)}) collective-permute-start(bf16[4,192,1536]{2,1,0:T(8,128)(2,1)} %select_select_fusion), channel_id=1, source_target_pairs={{0,4},{4,0},{8,12},{12,8},{16,20},{20,16},{24,28},{28,24},{1,5},{5... | collective-permute-start | bytes 7077896 | tf_op jit(solution)/shard_map/ppermute | solution.py:74
  63.5 4.1 %collective-permute-start.2 = (f32[2,1536]{1,0:T(2,128)S(1)}, f32[2,1536]{1,0:T(2,128)S(1)}, u32[]{:S(2)}, u32[]{:S(2)}) collective-permute-start(f32[2,1536]{1,0:T(2,128)S(1)} %pad_maximum_fusion.6), channel_id=1, source_target_pairs={{0,4},{4,0},{8,12},{12,8},{16,20},{20,16},{24,28},{28,24},{1,5},{5... | collective-permute-start | bytes 36872 | tf_op jit(solution)/shard_map/ppermute | solution.py:44
  68.4 3.8 %collective-permute-start.3 = (f32[2,1536]{1,0:T(2,128)S(1)}, f32[2,1536]{1,0:T(2,128)S(1)}, u32[]{:S(2)}, u32[]{:S(2)}) collective-permute-start(f32[2,1536]{1,0:T(2,128)S(1)} %pad_maximum_fusion.7), channel_id=1, source_target_pairs={{0,8},{4,12},{8,0},{12,4},{16,24},{20,28},{24,16},{28,20},{1,9},{5... | collective-permute-start | bytes 36872 | tf_op jit(solution)/shard_map/ppermute | solution.py:44
  72.8 3.8 %collective-permute-start.4 = (f32[2,1536]{1,0:T(2,128)S(1)}, f32[2,1536]{1,0:T(2,128)S(1)}, u32[]{:S(2)}, u32[]{:S(2)}) collective-permute-start(f32[2,1536]{1,0:T(2,128)S(1)} %pad_maximum_fusion.8), channel_id=1, source_target_pairs={{0,16},{4,20},{8,24},{12,28},{16,0},{20,4},{24,8},{28,12},{1,17},{... | collective-permute-start | bytes 36872 | tf_op jit(solution)/shard_map/ppermute | solution.py:44
  77.3 3.8 %collective-permute-start.5 = (f32[2,1536]{1,0:T(2,128)S(1)}, f32[2,1536]{1,0:T(2,128)S(1)}, u32[]{:S(2)}, u32[]{:S(2)}) collective-permute-start(f32[2,1536]{1,0:T(2,128)S(1)} %pad_maximum_fusion.9), channel_id=1, source_target_pairs={{0,1},{1,0},{2,3},{3,2},{4,5},{5,4},{6,7},{7,6},{8,9},{9,8},{10,11... | collective-permute-start | bytes 36872 | tf_op jit(solution)/shard_map/ppermute | solution.py:44
  82.3 4.9 %collective-permute-start.6 = (f32[2,1536]{1,0:T(2,128)}, f32[2,1536]{1,0:T(2,128)}, u32[]{:S(2)}, u32[]{:S(2)}) collective-permute-start(f32[2,1536]{1,0:T(2,128)} %pad_maximum_fusion.10), channel_id=1, source_target_pairs={{0,2},{1,3},{2,0},{3,1},{4,6},{5,7},{6,4},{7,5},{8,10},{9,11},{10,... | collective-permute-start | bytes 36872 | tf_op jit(solution)/shard_map/ppermute | solution.py:44
  96.3 1.2 collective-permute-start.14
  97.6 3.8 %collective-permute-start.15 = (f32[2,1536]{1,0:T(2,128)S(1)}, f32[2,1536]{1,0:T(2,128)S(1)}, u32[]{:S(2)}, u32[]{:S(2)}) collective-permute-start(f32[2,1536]{1,0:T(2,128)S(1)} %fusion.140), channel_id=1, source_target_pairs={{0,8},{4,12},{8,0},{12,4},{16,24},{20,28},{24,16},{28,20},{1,9},{5... | collective-permute-start | bytes 36872 | tf_op jit(solution)/shard_map/ppermute | solution.py:34
  101.4 3.8 %collective-permute-start.16 = (f32[2,1536]{1,0:T(2,128)S(1)}, f32[2,1536]{1,0:T(2,128)S(1)}, u32[]{:S(2)}, u32[]{:S(2)}) collective-permute-start(f32[2,1536]{1,0:T(2,128)S(1)} %fusion.155), channel_id=1, source_target_pairs={{0,16},{4,20},{8,24},{12,28},{16,0},{20,4},{24,8},{28,12},{1,17},{... | collective-permute-start | bytes 36872 | tf_op jit(solution)/shard_map/ppermute | solution.py:34
  105.1 3.8 %collective-permute-start.17 = (f32[2,1536]{1,0:T(2,128)S(1)}, f32[2,1536]{1,0:T(2,128)S(1)}, u32[]{:S(2)}, u32[]{:S(2)}) collective-permute-start(f32[2,1536]{1,0:T(2,128)S(1)} %add.501), channel_id=1, source_target_pairs={{0,1},{1,0},{2,3},{3,2},{4,5},{5,4},{6,7},{7,6},{8,9},{9,8},{10,11... | collective-permute-start | bytes 36872 | tf_op jit(solution)/shard_map/ppermute | solution.py:34
  109.5 7.2 %collective-permute-start.18 = (f32[2,1536]{1,0:T(2,128)}, f32[2,1536]{1,0:T(2,128)}, u32[]{:S(2)}, u32[]{:S(2)}) collective-permute-start(f32[2,1536]{1,0:T(2,128)} %add.502), channel_id=1, source_target_pairs={{0,2},{1,3},{2,0},{3,1},{4,6},{5,7},{6,4},{7,5},{8,10},{9,11},{10,... | collective-permute-start | bytes 36872 | tf_op jit(solution)/shard_map/ppermute | solution.py:34
  113.0 40.2 %all-to-all-start = ((bf16[128,4,384]{2,0,1:T(8,128)(2,1)}), bf16[128,4,384]{2,0,1:T(8,128)(2,1)S(1)}, u32[]{:S(2)}, u32[]{:S(2)}) async-start(bf16[128,4,384]{2,0,1:T(8,128)(2,1)} %copy.12), calls=%async_computation | async-start | bytes 786432 | tf_op jit(solution)/shard_map/all_to_all | solution.py:151
  116.4 102.7 %all-reduce.2.cloned.1.call-start = ((), (), s32[]{:S(2)}) async-start(), calls=%async_computation.2 | async-start | bytes 4718592 | tf_op jit(solution)/shard_map/psum | solution.py:153
  127.5 4.0 %collective-permute-start.21 = (f32[31,1536]{1,0:T(8,128)S(1)}, f32[31,1536]{1,0:T(8,128)S(1)}, u32[]{:S(2)}, u32[]{:S(2)}) collective-permute-start(f32[31,1536]{1,0:T(8,128)S(1)} %stack.172), channel_id=1, source_target_pairs={{0,4},{4,0},{8,12},{12,8},{16,20},{20,16},{24,28},{28,24},{1,5},{5... | collective-permute-start | bytes 571400 | tf_op jit(solution)/shard_map/ppermute | solution.py:34
  131.5 8.1 %collective-permute-start.22 = (f32[31,1536]{1,0:T(8,128)S(1)}, f32[31,1536]{1,0:T(8,128)S(1)}, u32[]{:S(2)}, u32[]{:S(2)}) collective-permute-start(f32[31,1536]{1,0:T(8,128)S(1)} %add.534), channel_id=1, source_target_pairs={{0,8},{4,12},{8,0},{12,4},{16,24},{20,28},{24,16},{28,20},{1,9},{5... | collective-permute-start | bytes 571400 | tf_op jit(solution)/shard_map/ppermute | solution.py:34
  133.1 23.7 %collective-permute-start.19 = (bf16[2,15,1536]{2,1,0:T(8,128)(2,1)S(1)}, bf16[2,15,1536]{2,1,0:T(8,128)(2,1)S(1)}, u32[]{:S(2)}, u32[]{:S(2)}) collective-permute-start(bf16[2,15,1536]{2,1,0:T(8,128)(2,1)S(1)} %get-tuple-element.92), channel_id=1, source_target_pairs={{1,0},{2,1},{3,2},{5,4},{6,5},{7,6},{9,8},{10,9},{11,10},{13,12},{... | collective-permute-start | bytes 276488 | tf_op jit(solution)/shard_map/ppermute | solution.py:17
  134.4 23.1 %collective-permute-start.20 = (bf16[2,15,1536]{2,1,0:T(8,128)(2,1)S(1)}, bf16[2,15,1536]{2,1,0:T(8,128)(2,1)}, u32[]{:S(2)}, u32[]{:S(2)}) collective-permute-start(bf16[2,15,1536]{2,1,0:T(8,128)(2,1)S(1)} %get-tuple-element.93), channel_id=1, source_target_pairs={{0,1},{1,2},{2,3},{4,5},{5,6},{6,7},{8,9},{9,10},{10,11},{12,13},{... | collective-permute-start | bytes 276488 | tf_op jit(solution)/shard_map/ppermute | solution.py:16
  140.3 24.8 %collective-permute-start.23 = (f32[31,1536]{1,0:T(8,128)}, f32[31,1536]{1,0:T(8,128)}, u32[]{:S(2)}, u32[]{:S(2)}) collective-permute-start(f32[31,1536]{1,0:T(8,128)} %add.535), channel_id=1, source_target_pairs={{0,16},{4,20},{8,24},{12,28},{16,0},{20,4},{24,8},{28,12},{1,17},{... | collective-permute-start | bytes 571400 | tf_op jit(solution)/shard_map/ppermute | solution.py:34
  166.2 6.9 %collective-permute-start.24 = (f32[31,1536]{1,0:T(8,128)S(1)}, f32[31,1536]{1,0:T(8,128)S(1)}, u32[]{:S(2)}, u32[]{:S(2)}) collective-permute-start(f32[31,1536]{1,0:T(8,128)S(1)} %add.536), channel_id=1, source_target_pairs={{0,1},{1,0},{2,3},{3,2},{4,5},{5,4},{6,7},{7,6},{8,9},{9,8},{10,11... | collective-permute-start | bytes 571400 | tf_op jit(solution)/shard_map/ppermute | solution.py:34
  173.2 11.3 %collective-permute-start.25 = (f32[31,1536]{1,0:T(8,128)S(1)}, f32[31,1536]{1,0:T(8,128)S(1)}, u32[]{:S(2)}, u32[]{:S(2)}) collective-permute-start(f32[31,1536]{1,0:T(8,128)S(1)} %add.537), channel_id=1, source_target_pairs={{0,2},{1,3},{2,0},{3,1},{4,6},{5,7},{6,4},{7,5},{8,10},{9,11},{10,... | collective-permute-start | bytes 571400 | tf_op jit(solution)/shard_map/ppermute | solution.py:34
  (51 other events, 1040.0 us)
Sparse Core Ops, SparseCore 0:
  112.2 40.9 all-gather.1
  157.0 62.0 all-reduce.1

commit v3 on v2

--- a/solution.py
+++ b/solution.py
@@ -50,6 +50,27 @@
     return mean, spread
 
 
+def rows_sum(x, axis):
+    peers = lax.axis_size(axis)
+    if not is_power_of_two(peers) or x.shape[0] % peers:
+        return lax.psum(x, axis)
+    me = lax.axis_index(axis)
+    bits = []
+    step = 1
+    while step < peers:
+        bit = lax.rem(me // step, 2)
+        half = x.shape[0] // 2
+        keep = lax.dynamic_slice_in_dim(x, bit * half, half, axis=0)
+        give = lax.dynamic_slice_in_dim(x, (1 - bit) * half, half, axis=0)
+        x = keep + lax.ppermute(give, axis, [(i, i ^ step) for i in range(peers)])
+        bits.append((step, bit))
+        step *= 2
+    for step, bit in reversed(bits):
+        other = lax.ppermute(x, axis, [(i, i ^ step) for i in range(peers)])
+        x = jnp.where(bit == 0, jnp.concatenate([x, other]), jnp.concatenate([other, x]))
+    return x
+
+
 def gather_weight(block):
     peers = lax.axis_size("tensor")
     me = lax.axis_index("tensor")
@@ -89,6 +110,8 @@
     local = glu_input.shape[0] * frames
     everyone = local * lax.axis_size("dp") * peers
     full_weight = gather_weight(proj_weight)
+    flat_grad = out_grad.reshape(-1, width)
+    group_grad = lax.all_gather(flat_grad, "tensor", axis=0, tiled=True)
     values = glu_input[..., :width].astype(jnp.float32)
     gates = jax.nn.sigmoid(glu_input[..., width:].astype(jnp.float32))
     gated = (values * gates).astype(jnp.bfloat16)
@@ -112,15 +135,19 @@
     affine = norm_scale * normed + norm_shift
     sig_affine = jax.nn.sigmoid(affine)
     activated = (affine * sig_affine).astype(jnp.bfloat16)
+    full_weight, group_grad = lax.optimization_barrier((full_weight, group_grad))
+    flat_act = activated.reshape(-1, width)
+    group_act = lax.all_to_all(flat_act, "tensor", split_axis=1, concat_axis=0, tiled=True)
+    local_grad = jnp.einsum("fc,fd->cd", group_act, group_grad, preferred_element_type=jnp.float32)
     conv_output = jnp.einsum(
         "btc,cd->btd", activated, full_weight, preferred_element_type=jnp.float32
     ).astype(jnp.bfloat16)
     grad_act = jnp.einsum("btd,cd->btc", out_grad, full_weight, preferred_element_type=jnp.float32)
     grad_affine = grad_act * (sig_affine + affine * sig_affine * (1.0 - sig_affine))
-    sums = all_sum(
-        jnp.stack([jnp.sum(grad_affine, axis=(0, 1)), jnp.sum(grad_affine * normed, axis=(0, 1))]),
-        ("dp", "tensor"),
-    )
+    sums = jnp.stack([jnp.sum(grad_affine, axis=(0, 1)), jnp.sum(grad_affine * normed, axis=(0, 1))])
+    local_grad, sums = lax.optimization_barrier((local_grad, sums))
+    weight_grad = rows_sum(local_grad, "dp")
+    sums = all_sum(sums, ("dp", "tensor"))
     shift_grad, scale_grad = sums[0], sums[1]
     grad_conv = (
         norm_scale
@@ -145,12 +172,6 @@
     input_grad = jnp.concatenate(
         [grad_gated * gates, grad_gated * values * gates * (1.0 - gates)], axis=-1
     ).astype(jnp.bfloat16)
-    flat_act = activated.reshape(-1, width)
-    flat_grad = out_grad.reshape(-1, width)
-    group_grad = lax.all_gather(flat_grad, "tensor", axis=0, tiled=True)
-    group_act = lax.all_to_all(flat_act, "tensor", split_axis=1, concat_axis=0, tiled=True)
-    local_grad = jnp.einsum("fc,fd->cd", group_act, group_grad, preferred_element_type=jnp.float32)
-    weight_grad = lax.psum(local_grad, "dp")
     return (conv_output, input_grad, weight_grad, kernel_grad, scale_grad, shift_grad)
 
 

time: 231 us -> 236 us (1.022)
  waiting for transfers between devices: 94.1 us -> 104 us
  other arithmetic: 42.8 us -> 39.6 us
  local copies, waits for them, and re-layouts: 13.9 us -> 11.1 us
    psum x1 -> x0, waiting for transfers between devices: 34 us -> none  [on_device(): weight_grad = lax.psum(local_grad, 'dp')]
    ppermute x0 -> x6, waiting for transfers between devices: none -> 17.5 us  [the longest x3 13.6 us: rows_sum(): x = keep + lax.ppermute(give, axis, [(i, i ^ step) for i in range(peers)])]
    all_to_all x1, waiting for transfers between devices: 0.01 us -> 11.7 us  [on_device(): lax.all_to_all(flat_act, 'tensor', split_axis=1, concat_axis=0, tiled=True)]
    ppermute x10, waiting for transfers between devices: 23.8 us -> 34.2 us  [all_sum(): x = x + lax.ppermute(x, axis, [(i, i ^ step) for i in range(peers)])]
    ppermute x0 -> x6, starting transfers between devices: none -> 6.25 us  [the longest x3 3.16 us: rows_sum(): other = lax.ppermute(x, axis, [(i, i ^ step) for i in range(peers)])]
    ppermute x10, starting transfers between devices: 11.4 us -> 6.43 us  [all_sum(): x = x + lax.ppermute(x, axis, [(i, i ^ step) for i in range(peers)])]
    reduce_sum x4, other arithmetic: 8.65 us -> 4.37 us  [on_device(): jnp.sum(padded[:, offset:offset + frames, :].astype(jnp.float32) * grad_w...]
    unnamed x109 -> x172, local copies, waits for them, and re-layouts: 7.58 us -> 3.61 us
  transfers between devices with their start and end apart: 29 -> 34, of which waited for: 17 -> 23; matrix products, arithmetic and copies ran while one was open for 22% -> 18% of each run, Pallas kernels for 0% -> 0%
where the time goes in v3:
time: 236 us; the launch traced here: 235 us
  waiting for transfers between devices  104 us (44%)
  starting transfers between devices  53.6 us (23%)
  other arithmetic  39.6 us (17%)
  between operations  15.9 us (7%)
  local copies, waits for them, and re-layouts  11.1 us (5%)
  matrix products  11 us (5%)
    ppermute x10, waiting for transfers between devices, all_sum(): x = x + lax.ppermute(x, axis, [(i, i ^ step) for i in range(peers)])  34.2 us
    ppermute x5, waiting for transfers between devices, all_moments(): lax.ppermute(jnp.stack([mean, spread]), axis, [(i, i ^ step) for i in ran...  14 us
    ppermute x3, starting transfers between devices, gather_weight(): going_right = lax.ppermute(going_right, 'tensor', right)  13.8 us
    all_gather x1, waiting for transfers between devices, on_device(): group_grad = lax.all_gather(flat_grad, 'tensor', axis=0, tiled=True)  13.7 us
    ppermute x3, waiting for transfers between devices, rows_sum(): x = keep + lax.ppermute(give, axis, [(i, i ^ step) for i in range(peers)])  13.6 us
    all_to_all x1, waiting for transfers between devices, on_device(): lax.all_to_all(flat_act, 'tensor', split_axis=1, concat_axis=0, tiled=True)  11.7 us
    ppermute x2, starting transfers between devices, extended(): before = lax.ppermute(last, axis, up)  9.09 us
    ppermute x3, waiting for transfers between devices, gather_weight(): going_right = lax.ppermute(going_right, 'tensor', right)  8.28 us
  transfers between devices with their start and end apart: 34, of which 23 were waited for; matrix products, arithmetic and copies ran while one was open for 18% of the time, Pallas kernels for 0%

profile of v3, /device:TPU:0, one launch (start us, length us, event | category | flops | bytes accessed | tf_op | source)
XLA Modules:
  0.0 234.8 jit_solution(1433902232327334667)
XLA Ops:
  8.5 5.0 %collective-permute-start.10 = (bf16[192,1536]{1,0:T(8,128)(2,1)S(1)}, bf16[192,1536]{1,0:T(8,128)(2,1)S(1)}, u32[]{:S(2)}, u32[]{:S(2)}) collective-permute-start(bf16[192,1536]{1,0:T(8,128)(2,1)S(1)} %constant_dynamic-slice_fusion.3), channel_id=1, source_target_pairs={{0,1},{1,2},{2,3},{4,5},{5,6},{6,7},{8,9},{9,10},{10,11},{12,13},{... | collective-permute-start | bytes 1769480 | tf_op jit(solution)/shard_map/ppermute | solution.py:90
  16.8 4.5 %collective-permute-start = (bf16[2,15,1536]{2,1,0:T(8,128)(2,1)}, bf16[2,15,1536]{2,1,0:T(8,128)(2,1)S(1)}, u32[]{:S(2)}, u32[]{:S(2)}) collective-permute-start(bf16[2,15,1536]{2,1,0:T(8,128)(2,1)} %get-tuple-element.102), channel_id=1, source_target_pairs={{0,1},{1,2},{2,3},{4,5},{5,6},{6,7},{8,9},{9,10},{10,11},{12,13},{... | collective-permute-start | bytes 276488 | tf_op jit(solution)/shard_map/ppermute | solution.py:16
  23.1 3.9 %collective-permute-done.10 = bf16[192,1536]{1,0:T(8,128)(2,1)S(1)} collective-permute-done((bf16[192,1536]{1,0:T(8,128)(2,1)S(1)}, bf16[192,1536]{1,0:T(8,128)(2,1)S(1)}, u32[]{:S(2)}, u32[]{:S(2)}) %collective-permute-start.10) | collective-permute-done | bytes 589856 | tf_op jit(solution)/shard_map/ppermute | solution.py:90
  27.0 4.4 %collective-permute-start.11 = (bf16[192,1536]{1,0:T(8,128)(2,1)S(1)}, bf16[192,1536]{1,0:T(8,128)(2,1)S(1)}, u32[]{:S(2)}, u32[]{:S(2)}) collective-permute-start(bf16[192,1536]{1,0:T(8,128)(2,1)S(1)} %collective-permute-done.10), channel_id=1, source_target_pairs={{0,1},{1,2},{2,3},{4,5},{5,6},{6,7},{8,9},{9,10},{10,11},{12,13},{... | collective-permute-start | bytes 1769480 | tf_op jit(solution)/shard_map/ppermute | solution.py:90
  38.1 4.0 %collective-permute-done.11 = bf16[192,1536]{1,0:T(8,128)(2,1)S(1)} collective-permute-done((bf16[192,1536]{1,0:T(8,128)(2,1)S(1)}, bf16[192,1536]{1,0:T(8,128)(2,1)S(1)}, u32[]{:S(2)}, u32[]{:S(2)}) %collective-permute-start.11) | collective-permute-done | bytes 589856 | tf_op jit(solution)/shard_map/ppermute | solution.py:90
  42.1 4.4 %collective-permute-start.12 = (bf16[192,1536]{1,0:T(8,128)(2,1)S(1)}, bf16[192,1536]{1,0:T(8,128)(2,1)S(1)}, u32[]{:S(2)}, u32[]{:S(2)}) collective-permute-start(bf16[192,1536]{1,0:T(8,128)(2,1)S(1)} %collective-permute-done.11), channel_id=1, source_target_pairs={{0,1},{1,2},{2,3},{4,5},{5,6},{6,7},{8,9},{9,10},{10,11},{12,13},{... | collective-permute-start | bytes 1769480 | tf_op jit(solution)/shard_map/ppermute | solution.py:90
  48.5 7.1 %fusion.155 = (f32[1536]{0:T(1024)S(1)}, f32[2,64,1536]{2,1,0:T(8,128)S(1)}) fusion(bf16[2,15,1536]{2,1,0:T(8,128)(2,1)} %copy-done.9, bf16[2,64,1536]{2,1,0:T(8,128)(2,1)S(1)} %fusion.13, f32[1536]{0:T(1024)S(1)} %get-tuple-element.76, f32[1536]{0:T(1024)S(1)} %get-tuple-element.77, f32[1536]{0:T(1024)S(1)} %get-tuple-element.48, ...), kind=kLoop, calls=%fused_computation.392 | loop fusion | flops 35977728 | bytes 1560576 | tf_op jit(solution)/shard_map/reduce_sum | solution.py:122
  56.2 4.2 %collective-permute-done.9 = bf16[192,1536]{1,0:T(8,128)(2,1)S(1)} collective-permute-done((bf16[192,1536]{1,0:T(8,128)(2,1)S(1)}, bf16[192,1536]{1,0:T(8,128)(2,1)S(1)}, u32[]{:S(2)}, u32[]{:S(2)}) %collective-permute-start.9) | collective-permute-done | bytes 589856 | tf_op jit(solution)/shard_map/ppermute | solution.py:91
  60.4 2.9 %select_select_fusion = bf16[4,192,1536]{2,1,0:T(8,128)(2,1)} fusion(pred[4]{0:T(512)(128)(4,1)S(1)} %get-tuple-element.122, pred[4]{0:T(512)(128)(4,1)} %get-tuple-element.123, pred[4]{0:T(512)(128)(4,1)} %get-tuple-element.124, pred[4]{0:T(512)(128)(4,1)} %get-tuple-element.125, pred[4]{0:T(512)(128)(4,1)} %get-tuple-element.126, ...), kind=kLoop, calls=%fused_computation.41 | loop fusion | flops 8257536 | bytes 6488092 | tf_op jit(solution)/shard_map/jit(_where)/select_n | solution.py:93
  64.1 3.6 %collective-permute-done.2 = f32[2,1536]{1,0:T(2,128)S(1)} collective-permute-done((f32[2,1536]{1,0:T(2,128)S(1)}, f32[2,1536]{1,0:T(2,128)S(1)}, u32[]{:S(2)}, u32[]{:S(2)}) %collective-permute-start.2) | collective-permute-done | bytes 12320 | tf_op jit(solution)/shard_map/ppermute | solution.py:44
  75.0 2.4 %collective-permute-done.4 = f32[2,1536]{1,0:T(2,128)} collective-permute-done((f32[2,1536]{1,0:T(2,128)}, f32[2,1536]{1,0:T(2,128)}, u32[]{:S(2)}, u32[]{:S(2)}) %collective-permute-start.4) | collective-permute-done | bytes 12320 | tf_op jit(solution)/shard_map/ppermute | solution.py:44
  83.9 2.6 %collective-permute-start.6 = (f32[2,1536]{1,0:T(2,128)}, f32[2,1536]{1,0:T(2,128)}, u32[]{:S(2)}, u32[]{:S(2)}) collective-permute-start(f32[2,1536]{1,0:T(2,128)} %pad_maximum_fusion.10), channel_id=1, source_target_pairs={{0,2},{1,3},{2,0},{3,1},{4,6},{5,7},{6,4},{7,5},{8,10},{9,11},{10,... | collective-permute-start | bytes 36872 | tf_op jit(solution)/shard_map/ppermute | solution.py:44
  86.4 3.7 %collective-permute-done.6 = f32[2,1536]{1,0:T(2,128)} collective-permute-done((f32[2,1536]{1,0:T(2,128)}, f32[2,1536]{1,0:T(2,128)}, u32[]{:S(2)}, u32[]{:S(2)}) %collective-permute-start.6) | collective-permute-done | bytes 12320 | tf_op jit(solution)/shard_map/ppermute | solution.py:44
  92.4 3.2 %broadcast_select_fusion.1 = (bf16[4,192,1536]{2,1,0:T(8,128)(2,1)S(1)}, bf16[4,192,1536]{2,1,0:T(8,128)(2,1)S(1)}) fusion(bf16[4,192,1536]{2,1,0:T(8,128)(2,1)} %collective-permute-done.13, pred[]{:T(512)S(6)} %eq.88, bf16[192,1536]{1,0:T(8,128)(2,1)S(1)} %constant_dynamic-slice_fusion.3, pred[4]{0:T(512)(128)(4,1)} %copy-done.84, ...), kind=kLoop, calls=%fused_computation.43 | loop fusion | flops 10616832 | bytes 11206685 | tf_op jit(solution)/shard_map/jit(_where)/select_n | solution.py:96
  95.7 2.4 %pad_maximum_fusion = bf16[4,384,1536]{2,1,0:T(8,128)(2,1)} fusion(bf16[4,192,1536]{2,1,0:T(8,128)(2,1)S(1)} %get-tuple-element.98, bf16[4,192,1536]{2,1,0:T(8,128)(2,1)S(1)} %get-tuple-element.97), kind=kLoop, calls=%fused_computation.32 | loop fusion | flops 9437184 | bytes 9437184 | tf_op jit(solution)/shard_map/concatenate | solution.py:98
  98.1 13.7 %all-gather.2.cloned.1.call-done = bf16[512,1536]{1,0:T(8,128)(2,1)} async-done(((bf16[128,1536]{1,0:T(8,128)(2,1)}), bf16[512,1536]{1,0:T(8,128)(2,1)}) %all-gather.2.cloned.1.call-update) | async-done | bytes 1572880 | tf_op jit(solution)/shard_map/all_gather | solution.py:114
  111.8 4.9 %fusion.152 = (f32[1536]{0:T(1024)S(1)}, f32[1536]{0:T(1024)S(1)}, bf16[2,64,1536]{2,1,0:T(8,128)(2,1)S(1)}, f32[2,64,1536]{2,1,0:T(8,128)}) fusion(f32[1536]{0:T(1024)S(1)} %copy-done.80, f32[2,64,1536]{2,1,0:T(8,128)S(1)} %get-tuple-element.96, f32[1536]{0:T(1024)S(1)} %copy-done.81, f32[1536]{0:T(1024)S(1)} %copy-done.85, f32[1536]{0:T(1024)S(1)} %copy-done.83, ...), kind=kOutput, calls=%fused_computation.390 | convolution fusion | flops 607122432 | bytes 7114752 | tf_op jit(solution)/shard_map/btd,cd->btc/dot_general | solution.py:145
  117.6 3.6 %all-to-all-start = ((bf16[128,4,384]{2,0,1:T(8,128)(2,1)}), bf16[128,4,384]{2,0,1:T(8,128)(2,1)S(1)}, u32[]{:S(2)}, u32[]{:S(2)}) async-start(bf16[128,4,384]{2,0,1:T(8,128)(2,1)} %copy.12), calls=%async_computation | async-start | bytes 786432 | tf_op jit(solution)/shard_map/all_to_all | solution.py:140
  121.4 11.7 %all-to-all-done = bf16[128,4,384]{2,0,1:T(8,128)(2,1)S(1)} async-done(((bf16[128,4,384]{2,0,1:T(8,128)(2,1)}), bf16[128,4,384]{2,0,1:T(8,128)(2,1)S(1)}, u32[]{:S(2)}, u32[]{:S(2)}) %all-to-all-start) | async-done | bytes 393248 | tf_op jit(solution)/shard_map/all_to_all | solution.py:140
  141.8 2.2 collective-permute-done.15
  145.6 2.2 collective-permute-done.16
  147.9 3.7 %collective-permute-done.17 = f32[2,1536]{1,0:T(2,128)S(1)} collective-permute-done((f32[2,1536]{1,0:T(2,128)S(1)}, f32[2,1536]{1,0:T(2,128)S(1)}, u32[]{:S(2)}, u32[]{:S(2)}) %collective-permute-start.17) | collective-permute-done | bytes 12320 | tf_op jit(solution)/shard_map/ppermute | solution.py:34
  151.7 4.5 %collective-permute-done.18 = f32[2,1536]{1,0:T(2,128)S(1)} collective-permute-done((f32[2,1536]{1,0:T(2,128)S(1)}, f32[2,1536]{1,0:T(2,128)S(1)}, u32[]{:S(2)}, u32[]{:S(2)}) %collective-permute-start.18) | collective-permute-done | bytes 12320 | tf_op jit(solution)/shard_map/ppermute | solution.py:34
  162.8 6.6 %collective-permute-done.22 = f32[96,1536]{1,0:T(8,128)S(1)} collective-permute-done((f32[96,1536]{1,0:T(8,128)S(1)}, f32[96,1536]{1,0:T(8,128)S(1)}, u32[]{:S(2)}, u32[]{:S(2)}) %collective-permute-start.22) | collective-permute-done | bytes 589856 | tf_op jit(solution)/shard_map/ppermute | solution.py:65
  172.0 7.0 %collective-permute-done.23 = f32[48,1536]{1,0:T(8,128)S(1)} collective-permute-done((f32[48,1536]{1,0:T(8,128)S(1)}, f32[48,1536]{1,0:T(8,128)S(1)}, u32[]{:S(2)}, u32[]{:S(2)}) %collective-permute-start.23) | collective-permute-done | bytes 294944 | tf_op jit(solution)/shard_map/ppermute | solution.py:65
  182.0 3.8 %collective-permute-done.24 = f32[48,1536]{1,0:T(8,128)S(1)} collective-permute-done((f32[48,1536]{1,0:T(8,128)S(1)}, f32[48,1536]{1,0:T(8,128)S(1)}, u32[]{:S(2)}, u32[]{:S(2)}) %collective-permute-start.24) | collective-permute-done | bytes 294944 | tf_op jit(solution)/shard_map/ppermute | solution.py:69
  187.4 3.9 %fusion.10 = bf16[2,64,1536]{2,1,0:T(8,128)(2,1)} fusion(bf16[2,64,1536]{2,1,0:T(8,128)(2,1)S(1)} %get-tuple-element.99, bf16[1536,1536]{1,0:T(8,128)(2,1)} %bitcast.27), kind=kOutput, calls=%fused_computation.39 | convolution fusion | flops 604176384 | bytes 5505024 | tf_op jit(solution)/shard_map/btc,cd->btd/dot_general | solution.py:142
  193.6 4.6 %collective-permute-start.20 = (bf16[2,15,1536]{2,1,0:T(8,128)(2,1)S(1)}, bf16[2,15,1536]{2,1,0:T(8,128)(2,1)S(1)}, u32[]{:S(2)}, u32[]{:S(2)}) collective-permute-start(bf16[2,15,1536]{2,1,0:T(8,128)(2,1)S(1)} %get-tuple-element.101), channel_id=1, source_target_pairs={{0,1},{1,2},{2,3},{4,5},{5,6},{6,7},{8,9},{9,10},{10,11},{12,13},{... | collective-permute-start | bytes 276488 | tf_op jit(solution)/shard_map/ppermute | solution.py:16
  198.1 3.9 %collective-permute-done.28 = f32[31,1536]{1,0:T(8,128)S(1)} collective-permute-done((f32[31,1536]{1,0:T(8,128)S(1)}, f32[31,1536]{1,0:T(8,128)S(1)}, u32[]{:S(2)}, u32[]{:S(2)}) %collective-permute-start.28) | collective-permute-done | bytes 190496 | tf_op jit(solution)/shard_map/ppermute | solution.py:34
  203.2 4.1 %multiply_convert_fusion = (bf16[2,64,1536]{2,1,0:T(8,128)(2,1)S(1)}, f32[2,64,1536]{2,1,0:T(8,128)S(1)}) fusion(bf16[2,64,3072]{2,1,0:T(8,128)(2,1)S(1)} %copy-done.2, bf16[2,64,1536]{2,1,0:T(8,128)(2,1)S(1)} %get-tuple-element.90, bf16[2,15,1536]{2,1,0:T(8,128)(2,1)S(1)} %collective-permute-done.20, f32[1536]{0:T(1024)S(1)} %copy-done.72, ...), kind=kLoop, calls=%fused_computation.217 | loop fusion | flops 36962304 | bytes 2340864 | tf_op jit(solution)/shard_map/convert
  208.6 6.0 %collective-permute-done.30 = f32[31,1536]{1,0:T(8,128)S(1)} collective-permute-done((f32[31,1536]{1,0:T(8,128)S(1)}, f32[31,1536]{1,0:T(8,128)S(1)}, u32[]{:S(2)}, u32[]{:S(2)}) %collective-permute-start.30) | collective-permute-done | bytes 190496 | tf_op jit(solution)/shard_map/ppermute | solution.py:34
  216.5 9.1 %collective-permute-done.31 = f32[31,1536]{1,0:T(8,128)S(1)} collective-permute-done((f32[31,1536]{1,0:T(8,128)S(1)}, f32[31,1536]{1,0:T(8,128)S(1)}, u32[]{:S(2)}, u32[]{:S(2)}) %collective-permute-start.31) | collective-permute-done | bytes 190496 | tf_op jit(solution)/shard_map/ppermute | solution.py:34
  (306 shorter events, 65.0 us)
Async XLA Ops:
  7.2 104.6 %all-gather.2.cloned.1.call-start = ((), (), s32[]{:S(2)}) async-start(), calls=%async_computation.1 | async-start | bytes 1966080 | tf_op jit(solution)/shard_map/all_gather | solution.py:114
  8.5 18.6 %collective-permute-start.10 = (bf16[192,1536]{1,0:T(8,128)(2,1)S(1)}, bf16[192,1536]{1,0:T(8,128)(2,1)S(1)}, u32[]{:S(2)}, u32[]{:S(2)}) collective-permute-start(bf16[192,1536]{1,0:T(8,128)(2,1)S(1)} %constant_dynamic-slice_fusion.3), channel_id=1, source_target_pairs={{0,1},{1,2},{2,3},{4,5},{5,6},{6,7},{8,9},{9,10},{10,11},{12,13},{... | collective-permute-start | bytes 1769480 | tf_op jit(solution)/shard_map/ppermute | solution.py:90
  13.5 18.0 %collective-permute-start.7 = (bf16[192,1536]{1,0:T(8,128)(2,1)S(1)}, bf16[192,1536]{1,0:T(8,128)(2,1)S(1)}, u32[]{:S(2)}, u32[]{:S(2)}) collective-permute-start(bf16[192,1536]{1,0:T(8,128)(2,1)S(1)} %constant_dynamic-slice_fusion.3), channel_id=1, source_target_pairs={{1,0},{2,1},{3,2},{5,4},{6,5},{7,6},{9,8},{10,9},{11,10},{13,12},{... | collective-permute-start | bytes 1769480 | tf_op jit(solution)/shard_map/ppermute | solution.py:91
  16.8 31.0 %collective-permute-start = (bf16[2,15,1536]{2,1,0:T(8,128)(2,1)}, bf16[2,15,1536]{2,1,0:T(8,128)(2,1)S(1)}, u32[]{:S(2)}, u32[]{:S(2)}) collective-permute-start(bf16[2,15,1536]{2,1,0:T(8,128)(2,1)} %get-tuple-element.102), channel_id=1, source_target_pairs={{0,1},{1,2},{2,3},{4,5},{5,6},{6,7},{8,9},{9,10},{10,11},{12,13},{... | collective-permute-start | bytes 276488 | tf_op jit(solution)/shard_map/ppermute | solution.py:16
  21.3 26.5 %collective-permute-start.1 = (bf16[2,15,1536]{2,1,0:T(8,128)(2,1)}, bf16[2,15,1536]{2,1,0:T(8,128)(2,1)S(1)}, u32[]{:S(2)}, u32[]{:S(2)}) collective-permute-start(bf16[2,15,1536]{2,1,0:T(8,128)(2,1)} %get-tuple-element.103), channel_id=1, source_target_pairs={{1,0},{2,1},{3,2},{5,4},{6,5},{7,6},{9,8},{10,9},{11,10},{13,12},{... | collective-permute-start | bytes 276488 | tf_op jit(solution)/shard_map/ppermute | solution.py:17
  27.0 15.0 %collective-permute-start.11 = (bf16[192,1536]{1,0:T(8,128)(2,1)S(1)}, bf16[192,1536]{1,0:T(8,128)(2,1)S(1)}, u32[]{:S(2)}, u32[]{:S(2)}) collective-permute-start(bf16[192,1536]{1,0:T(8,128)(2,1)S(1)} %collective-permute-done.10), channel_id=1, source_target_pairs={{0,1},{1,2},{2,3},{4,5},{5,6},{6,7},{8,9},{9,10},{10,11},{12,13},{... | collective-permute-start | bytes 1769480 | tf_op jit(solution)/shard_map/ppermute | solution.py:90
  31.5 15.0 %collective-permute-start.8 = (bf16[192,1536]{1,0:T(8,128)(2,1)S(1)}, bf16[192,1536]{1,0:T(8,128)(2,1)S(1)}, u32[]{:S(2)}, u32[]{:S(2)}) collective-permute-start(bf16[192,1536]{1,0:T(8,128)(2,1)S(1)} %collective-permute-done.7), channel_id=1, source_target_pairs={{1,0},{2,1},{3,2},{5,4},{6,5},{7,6},{9,8},{10,9},{11,10},{13,12},{... | collective-permute-start | bytes 1769480 | tf_op jit(solution)/shard_map/ppermute | solution.py:91
  42.1 14.1 %collective-permute-start.12 = (bf16[192,1536]{1,0:T(8,128)(2,1)S(1)}, bf16[192,1536]{1,0:T(8,128)(2,1)S(1)}, u32[]{:S(2)}, u32[]{:S(2)}) collective-permute-start(bf16[192,1536]{1,0:T(8,128)(2,1)S(1)} %collective-permute-done.11), channel_id=1, source_target_pairs={{0,1},{1,2},{2,3},{4,5},{5,6},{6,7},{8,9},{9,10},{10,11},{12,13},{... | collective-permute-start | bytes 1769480 | tf_op jit(solution)/shard_map/ppermute | solution.py:90
  46.5 13.8 %collective-permute-start.9 = (bf16[192,1536]{1,0:T(8,128)(2,1)S(1)}, bf16[192,1536]{1,0:T(8,128)(2,1)S(1)}, u32[]{:S(2)}, u32[]{:S(2)}) collective-permute-start(bf16[192,1536]{1,0:T(8,128)(2,1)S(1)} %collective-permute-done.8), channel_id=1, source_target_pairs={{1,0},{2,1},{3,2},{5,4},{6,5},{7,6},{9,8},{10,9},{11,10},{13,12},{... | collective-permute-start | bytes 1769480 | tf_op jit(solution)/shard_map/ppermute | solution.py:91
  63.4 29.0 %collective-permute-start.13 = (bf16[4,192,1536]{2,1,0:T(8,128)(2,1)}, bf16[4,192,1536]{2,1,0:T(8,128)(2,1)}, u32[]{:S(2)}, u32[]{:S(2)}) collective-permute-start(bf16[4,192,1536]{2,1,0:T(8,128)(2,1)} %select_select_fusion), channel_id=1, source_target_pairs={{0,4},{4,0},{8,12},{12,8},{16,20},{20,16},{24,28},{28,24},{1,5},{5... | collective-permute-start | bytes 7077896 | tf_op jit(solution)/shard_map/ppermute | solution.py:95
  63.5 4.1 %collective-permute-start.2 = (f32[2,1536]{1,0:T(2,128)S(1)}, f32[2,1536]{1,0:T(2,128)S(1)}, u32[]{:S(2)}, u32[]{:S(2)}) collective-permute-start(f32[2,1536]{1,0:T(2,128)S(1)} %pad_maximum_fusion.6), channel_id=1, source_target_pairs={{0,4},{4,0},{8,12},{12,8},{16,20},{20,16},{24,28},{28,24},{1,5},{5... | collective-permute-start | bytes 36872 | tf_op jit(solution)/shard_map/ppermute | solution.py:44
  68.4 3.8 %collective-permute-start.3 = (f32[2,1536]{1,0:T(2,128)S(1)}, f32[2,1536]{1,0:T(2,128)S(1)}, u32[]{:S(2)}, u32[]{:S(2)}) collective-permute-start(f32[2,1536]{1,0:T(2,128)S(1)} %pad_maximum_fusion.7), channel_id=1, source_target_pairs={{0,8},{4,12},{8,0},{12,4},{16,24},{20,28},{24,16},{28,20},{1,9},{5... | collective-permute-start | bytes 36872 | tf_op jit(solution)/shard_map/ppermute | solution.py:44
  73.4 4.0 %collective-permute-start.4 = (f32[2,1536]{1,0:T(2,128)}, f32[2,1536]{1,0:T(2,128)}, u32[]{:S(2)}, u32[]{:S(2)}) collective-permute-start(f32[2,1536]{1,0:T(2,128)} %pad_maximum_fusion.8), channel_id=1, source_target_pairs={{0,16},{4,20},{8,24},{12,28},{16,0},{20,4},{24,8},{28,12},{1,17},{... | collective-permute-start | bytes 36872 | tf_op jit(solution)/shard_map/ppermute | solution.py:44
  78.9 3.8 %collective-permute-start.5 = (f32[2,1536]{1,0:T(2,128)S(1)}, f32[2,1536]{1,0:T(2,128)S(1)}, u32[]{:S(2)}, u32[]{:S(2)}) collective-permute-start(f32[2,1536]{1,0:T(2,128)S(1)} %pad_maximum_fusion.9), channel_id=1, source_target_pairs={{0,1},{1,0},{2,3},{3,2},{4,5},{5,4},{6,7},{7,6},{8,9},{9,8},{10,11... | collective-permute-start | bytes 36872 | tf_op jit(solution)/shard_map/ppermute | solution.py:44
  83.9 6.2 %collective-permute-start.6 = (f32[2,1536]{1,0:T(2,128)}, f32[2,1536]{1,0:T(2,128)}, u32[]{:S(2)}, u32[]{:S(2)}) collective-permute-start(f32[2,1536]{1,0:T(2,128)} %pad_maximum_fusion.10), channel_id=1, source_target_pairs={{0,2},{1,3},{2,0},{3,1},{4,6},{5,7},{6,4},{7,5},{8,10},{9,11},{10,... | collective-permute-start | bytes 36872 | tf_op jit(solution)/shard_map/ppermute | solution.py:44
  117.6 15.4 %all-to-all-start = ((bf16[128,4,384]{2,0,1:T(8,128)(2,1)}), bf16[128,4,384]{2,0,1:T(8,128)(2,1)S(1)}, u32[]{:S(2)}, u32[]{:S(2)}) async-start(bf16[128,4,384]{2,0,1:T(8,128)(2,1)} %copy.12), calls=%async_computation | async-start | bytes 786432 | tf_op jit(solution)/shard_map/all_to_all | solution.py:140
  137.8 18.6 %collective-permute-start.21 = (f32[192,1536]{1,0:T(8,128)}, f32[192,1536]{1,0:T(8,128)}, u32[]{:S(2)}, u32[]{:S(2)}) collective-permute-start(f32[192,1536]{1,0:T(8,128)} %constant_dynamic-slice_fusion.2), channel_id=1, source_target_pairs={{0,4},{4,0},{8,12},{12,8},{16,20},{20,16},{24,28},{28,24},{1,5},{5... | collective-permute-start | bytes 3538952 | tf_op jit(solution)/shard_map/ppermute | solution.py:65
  140.3 3.8 %collective-permute-start.15 = (f32[2,1536]{1,0:T(2,128)S(1)}, f32[2,1536]{1,0:T(2,128)S(1)}, u32[]{:S(2)}, u32[]{:S(2)}) collective-permute-start(f32[2,1536]{1,0:T(2,128)S(1)} %add.525), channel_id=1, source_target_pairs={{0,8},{4,12},{8,0},{12,4},{16,24},{20,28},{24,16},{28,20},{1,9},{5... | collective-permute-start | bytes 36872 | tf_op jit(solution)/shard_map/ppermute | solution.py:34
  144.1 3.8 %collective-permute-start.16 = (f32[2,1536]{1,0:T(2,128)S(1)}, f32[2,1536]{1,0:T(2,128)S(1)}, u32[]{:S(2)}, u32[]{:S(2)}) collective-permute-start(f32[2,1536]{1,0:T(2,128)S(1)} %add.526), channel_id=1, source_target_pairs={{0,16},{4,20},{8,24},{12,28},{16,0},{20,4},{24,8},{28,12},{1,17},{... | collective-permute-start | bytes 36872 | tf_op jit(solution)/shard_map/ppermute | solution.py:34
  151.6 4.7 %collective-permute-start.18 = (f32[2,1536]{1,0:T(2,128)S(1)}, f32[2,1536]{1,0:T(2,128)S(1)}, u32[]{:S(2)}, u32[]{:S(2)}) collective-permute-start(f32[2,1536]{1,0:T(2,128)S(1)} %add.528), channel_id=1, source_target_pairs={{0,2},{1,3},{2,0},{3,1},{4,6},{5,7},{6,4},{7,5},{8,10},{9,11},{10,... | collective-permute-start | bytes 36872 | tf_op jit(solution)/shard_map/ppermute | solution.py:34
  158.3 11.1 %collective-permute-start.22 = (f32[96,1536]{1,0:T(8,128)S(1)}, f32[96,1536]{1,0:T(8,128)S(1)}, u32[]{:S(2)}, u32[]{:S(2)}) collective-permute-start(f32[96,1536]{1,0:T(8,128)S(1)} %constant_dynamic-slice_fusion.1), channel_id=1, source_target_pairs={{0,8},{4,12},{8,0},{12,4},{16,24},{20,28},{24,16},{28,20},{1,9},{5... | collective-permute-start | bytes 1769480 | tf_op jit(solution)/shard_map/ppermute | solution.py:65
  169.5 9.5 %collective-permute-start.23 = (f32[48,1536]{1,0:T(8,128)S(1)}, f32[48,1536]{1,0:T(8,128)S(1)}, u32[]{:S(2)}, u32[]{:S(2)}) collective-permute-start(f32[48,1536]{1,0:T(8,128)S(1)} %constant_dynamic-slice_fusion), channel_id=1, source_target_pairs={{0,16},{4,20},{8,24},{12,28},{16,0},{20,4},{24,8},{28,12},{1,17},{... | collective-permute-start | bytes 884744 | tf_op jit(solution)/shard_map/ppermute | solution.py:65
  179.0 6.8 %collective-permute-start.24 = (f32[48,1536]{1,0:T(8,128)S(1)}, f32[48,1536]{1,0:T(8,128)S(1)}, u32[]{:S(2)}, u32[]{:S(2)}) collective-permute-start(f32[48,1536]{1,0:T(8,128)S(1)} %dynamic-slice_add_fusion.2), channel_id=1, source_target_pairs={{0,16},{4,20},{8,24},{12,28},{16,0},{20,4},{24,8},{28,12},{1,17},{... | collective-permute-start | bytes 884744 | tf_op jit(solution)/shard_map/ppermute | solution.py:69
  181.9 9.7 %collective-permute-start.27 = (f32[31,1536]{1,0:T(8,128)S(1)}, f32[31,1536]{1,0:T(8,128)S(1)}, u32[]{:S(2)}, u32[]{:S(2)}) collective-permute-start(f32[31,1536]{1,0:T(8,128)S(1)} %stack.172), channel_id=1, source_target_pairs={{0,4},{4,0},{8,12},{12,8},{16,20},{20,16},{24,28},{28,24},{1,5},{5... | collective-permute-start | bytes 571400 | tf_op jit(solution)/shard_map/ppermute | solution.py:34
  185.9 16.8 %collective-permute-start.25 = (f32[96,1536]{1,0:T(8,128)S(1)}, f32[96,1536]{1,0:T(8,128)S(1)}, u32[]{:S(2)}, u32[]{:S(2)}) collective-permute-start(f32[96,1536]{1,0:T(8,128)S(1)} %maximum_select_fusion.2), channel_id=1, source_target_pairs={{0,8},{4,12},{8,0},{12,4},{16,24},{20,28},{24,16},{28,20},{1,9},{5... | collective-permute-start | bytes 1769480 | tf_op jit(solution)/shard_map/ppermute | solution.py:69
  191.6 10.4 %collective-permute-start.28 = (f32[31,1536]{1,0:T(8,128)S(1)}, f32[31,1536]{1,0:T(8,128)S(1)}, u32[]{:S(2)}, u32[]{:S(2)}) collective-permute-start(f32[31,1536]{1,0:T(8,128)S(1)} %add.568), channel_id=1, source_target_pairs={{0,8},{4,12},{8,0},{12,4},{16,24},{20,28},{24,16},{28,20},{1,9},{5... | collective-permute-start | bytes 571400 | tf_op jit(solution)/shard_map/ppermute | solution.py:34
  192.3 10.6 %collective-permute-start.19 = (bf16[2,15,1536]{2,1,0:T(8,128)(2,1)S(1)}, bf16[2,15,1536]{2,1,0:T(8,128)(2,1)S(1)}, u32[]{:S(2)}, u32[]{:S(2)}) collective-permute-start(bf16[2,15,1536]{2,1,0:T(8,128)(2,1)S(1)} %get-tuple-element.100), channel_id=1, source_target_pairs={{1,0},{2,1},{3,2},{5,4},{6,5},{7,6},{9,8},{10,9},{11,10},{13,12},{... | collective-permute-start | bytes 276488 | tf_op jit(solution)/shard_map/ppermute | solution.py:17
  193.6 9.3 %collective-permute-start.20 = (bf16[2,15,1536]{2,1,0:T(8,128)(2,1)S(1)}, bf16[2,15,1536]{2,1,0:T(8,128)(2,1)S(1)}, u32[]{:S(2)}, u32[]{:S(2)}) collective-permute-start(bf16[2,15,1536]{2,1,0:T(8,128)(2,1)S(1)} %get-tuple-element.101), channel_id=1, source_target_pairs={{0,1},{1,2},{2,3},{4,5},{5,6},{6,7},{8,9},{9,10},{10,11},{12,13},{... | collective-permute-start | bytes 276488 | tf_op jit(solution)/shard_map/ppermute | solution.py:16
  202.1 5.7 %collective-permute-start.29 = (f32[31,1536]{1,0:T(8,128)S(1)}, f32[31,1536]{1,0:T(8,128)S(1)}, u32[]{:S(2)}, u32[]{:S(2)}) collective-permute-start(f32[31,1536]{1,0:T(8,128)S(1)} %add.569), channel_id=1, source_target_pairs={{0,16},{4,20},{8,24},{12,28},{16,0},{20,4},{24,8},{28,12},{1,17},{... | collective-permute-start | bytes 571400 | tf_op jit(solution)/shard_map/ppermute | solution.py:34
  202.8 23.6 %collective-permute-start.26 = (f32[192,1536]{1,0:T(8,128)S(1)}, f32[192,1536]{1,0:T(8,128)S(1)}, u32[]{:S(2)}, u32[]{:S(2)}) collective-permute-start(f32[192,1536]{1,0:T(8,128)S(1)} %maximum_select_fusion.1), channel_id=1, source_target_pairs={{0,4},{4,0},{8,12},{12,8},{16,20},{20,16},{24,28},{28,24},{1,5},{5... | collective-permute-start | bytes 3538952 | tf_op jit(solution)/shard_map/ppermute | solution.py:69
  207.8 6.8 %collective-permute-start.30 = (f32[31,1536]{1,0:T(8,128)S(1)}, f32[31,1536]{1,0:T(8,128)S(1)}, u32[]{:S(2)}, u32[]{:S(2)}) collective-permute-start(f32[31,1536]{1,0:T(8,128)S(1)} %add.570), channel_id=1, source_target_pairs={{0,1},{1,0},{2,3},{3,2},{4,5},{5,4},{6,7},{7,6},{8,9},{9,8},{10,11... | collective-permute-start | bytes 571400 | tf_op jit(solution)/shard_map/ppermute | solution.py:34
  214.7 10.9 %collective-permute-start.31 = (f32[31,1536]{1,0:T(8,128)S(1)}, f32[31,1536]{1,0:T(8,128)S(1)}, u32[]{:S(2)}, u32[]{:S(2)}) collective-permute-start(f32[31,1536]{1,0:T(8,128)S(1)} %add.571), channel_id=1, source_target_pairs={{0,2},{1,3},{2,0},{3,1},{4,6},{5,7},{6,4},{7,5},{8,10},{9,11},{10,... | collective-permute-start | bytes 571400 | tf_op jit(solution)/shard_map/ppermute | solution.py:34
  (88 other events, 1549.0 us)
Sparse Core Ops, SparseCore 0:
  75.1 36.5 all-gather.1

commit v4 on v3

--- a/solution.py
+++ b/solution.py
@@ -72,31 +72,17 @@
 
 
 def gather_weight(block):
+    if lax.axis_size("dp") % 2:
+        return lax.all_gather(block, "tensor", axis=0, tiled=True)
     peers = lax.axis_size("tensor")
-    me = lax.axis_index("tensor")
-    pairs = lax.axis_size("dp") % 2 == 0
-    if pairs:
-        half = block.shape[0] // 2
-        core = lax.rem(lax.axis_index("dp"), 2)
-        mine = lax.dynamic_slice_in_dim(block, core * half, half, axis=0)
-    else:
-        mine = block
-    right = [(i, i + 1) for i in range(peers - 1)]
-    left = [(i + 1, i) for i in range(peers - 1)]
-    index = lax.broadcasted_iota(jnp.int32, (peers, 1, 1), 0)
-    held = jnp.where(index == me, mine[None], jnp.zeros_like(mine)[None])
-    going_right, going_left = mine, mine
-    for hop in range(1, peers):
-        going_right = lax.ppermute(going_right, "tensor", right)
-        going_left = lax.ppermute(going_left, "tensor", left)
-        held = jnp.where(index == me - hop, going_right[None], held)
-        held = jnp.where(index == me + hop, going_left[None], held)
-    if pairs:
-        other = lax.ppermute(held, "dp", [(i, i ^ 1) for i in range(lax.axis_size("dp"))])
-        first = jnp.where(core == 0, held, other)
-        second = jnp.where(core == 0, other, held)
-        held = jnp.concatenate([first, second], axis=1)
-    return held.reshape(peers * block.shape[0], block.shape[1])
+    half = block.shape[0] // 2
+    core = lax.rem(lax.axis_index("dp"), 2)
+    mine = lax.dynamic_slice_in_dim(block, core * half, half, axis=0)
+    held = lax.all_gather(mine, "tensor", axis=0, tiled=False)
+    other = lax.ppermute(held, "dp", [(i, i ^ 1) for i in range(lax.axis_size("dp"))])
+    first = jnp.where(core == 0, held, other)
+    second = jnp.where(core == 0, other, held)
+    return jnp.concatenate([first, second], axis=1).reshape(peers * block.shape[0], block.shape[1])
 
 
 def on_device(glu_input, depth_kernel, norm_scale, norm_shift, proj_weight, out_grad):
@@ -135,7 +121,6 @@
     affine = norm_scale * normed + norm_shift
     sig_affine = jax.nn.sigmoid(affine)
     activated = (affine * sig_affine).astype(jnp.bfloat16)
-    full_weight, group_grad = lax.optimization_barrier((full_weight, group_grad))
     flat_act = activated.reshape(-1, width)
     group_act = lax.all_to_all(flat_act, "tensor", split_axis=1, concat_axis=0, tiled=True)
     local_grad = jnp.einsum("fc,fd->cd", group_act, group_grad, preferred_element_type=jnp.float32)
@@ -145,8 +130,6 @@
     grad_act = jnp.einsum("btd,cd->btc", out_grad, full_weight, preferred_element_type=jnp.float32)
     grad_affine = grad_act * (sig_affine + affine * sig_affine * (1.0 - sig_affine))
     sums = jnp.stack([jnp.sum(grad_affine, axis=(0, 1)), jnp.sum(grad_affine * normed, axis=(0, 1))])
-    local_grad, sums = lax.optimization_barrier((local_grad, sums))
-    weight_grad = rows_sum(local_grad, "dp")
     sums = all_sum(sums, ("dp", "tensor"))
     shift_grad, scale_grad = sums[0], sums[1]
     grad_conv = (
@@ -168,6 +151,8 @@
             for offset in range(taps)
         ]
     )
+    local_grad, kernel_terms = lax.optimization_barrier((local_grad, kernel_terms))
+    weight_grad = rows_sum(local_grad, "dp")
     kernel_grad = all_sum(kernel_terms, ("dp", "tensor"))
     input_grad = jnp.concatenate(
         [grad_gated * gates, grad_gated * values * gates * (1.0 - gates)], axis=-1

time: 236 us -> 233 us (0.987)
  waiting for transfers between devices: 104 us -> 137 us
  starting transfers between devices: 53.6 us -> 33.9 us
  other arithmetic: 39.6 us -> 26.1 us
    all_gather x0 -> x1, waiting for transfers between devices: none -> 37.2 us  [gather_weight(): held = lax.all_gather(mine, 'tensor', axis=0, tiled=False)]
    ppermute x6 -> x0, starting transfers between devices: 17.7 us -> none  [the longest x3 13.8 us: gather_weight(): going_right = lax.ppermute(going_right, 'tensor', right)]
    ppermute x6 -> x0, waiting for transfers between devices: 12.5 us -> none  [the longest x3 8.28 us: gather_weight(): going_right = lax.ppermute(going_right, 'tensor', right)]
    all_to_all x1, waiting for transfers between devices: 11.7 us -> 0.01 us  [on_device(): lax.all_to_all(flat_act, 'tensor', split_axis=1, concat_axis=0, tiled=True)]
    ppermute x3, waiting for transfers between devices: 13.6 us -> 23.8 us  [rows_sum(): x = keep + lax.ppermute(give, axis, [(i, i ^ step) for i in range(peers)])]
    all_gather x1, waiting for transfers between devices: 13.7 us -> 18.5 us  [on_device(): group_grad = lax.all_gather(flat_grad, 'tensor', axis=0, tiled=True)]
    ppermute x2, waiting for transfers between devices: 0.01 us -> 4.32 us  [extended(): after = lax.ppermute(leading, axis, down)]
    reduce_sum x1, other arithmetic: 7.13 us -> 3.85 us  [on_device(): mean_local = jnp.sum(conv_out, axis=(0, 1)) / local]
  transfers between devices with their start and end apart: 34 -> 29, of which waited for: 23 -> 20; matrix products, arithmetic and copies ran while one was open for 18% -> 11% of each run, Pallas kernels for 0% -> 0%
where the time goes in v4:
time: 233 us; the launch traced here: 232 us
  waiting for transfers between devices  137 us (59%)
  starting transfers between devices  33.9 us (15%)
  other arithmetic  26.1 us (11%)
  between operations  15.8 us (7%)
  local copies, waits for them, and re-layouts  10.3 us (4%)
  matrix products  8.83 us (4%)
    all_gather x1, waiting for transfers between devices, gather_weight(): held = lax.all_gather(mine, 'tensor', axis=0, tiled=False)  37.2 us
    ppermute x10, waiting for transfers between devices, all_sum(): x = x + lax.ppermute(x, axis, [(i, i ^ step) for i in range(peers)])  32.2 us
    ppermute x3, waiting for transfers between devices, rows_sum(): x = keep + lax.ppermute(give, axis, [(i, i ^ step) for i in range(peers)])  23.8 us
    all_gather x1, waiting for transfers between devices, on_device(): group_grad = lax.all_gather(flat_grad, 'tensor', axis=0, tiled=True)  18.5 us
    ppermute x5, waiting for transfers between devices, all_moments(): lax.ppermute(jnp.stack([mean, spread]), axis, [(i, i ^ step) for i in ran...  15.1 us
    ppermute x2, starting transfers between devices, extended(): before = lax.ppermute(last, axis, up)  9.48 us
    ppermute x10, starting transfers between devices, all_sum(): x = x + lax.ppermute(x, axis, [(i, i ^ step) for i in range(peers)])  6.23 us
    ppermute x3, waiting for transfers between devices, rows_sum(): other = lax.ppermute(x, axis, [(i, i ^ step) for i in range(peers)])  5.83 us
  transfers between devices with their start and end apart: 29, of which 20 were waited for; matrix products, arithmetic and copies ran while one was open for 11% of the time, Pallas kernels for 0%

profile of v4, /device:TPU:0, one launch (start us, length us, event | category | flops | bytes accessed | tf_op | source)
XLA Modules:
  0.0 232.0 jit_solution(10656756062917724202)
XLA Ops:
  10.8 4.9 %collective-permute-start = (bf16[2,15,1536]{2,1,0:T(8,128)(2,1)S(1)}, bf16[2,15,1536]{2,1,0:T(8,128)(2,1)S(1)}, u32[]{:S(2)}, u32[]{:S(2)}) collective-permute-start(bf16[2,15,1536]{2,1,0:T(8,128)(2,1)S(1)} %get-tuple-element.98), channel_id=1, source_target_pairs={{0,1},{1,2},{2,3},{4,5},{5,6},{6,7},{8,9},{9,10},{10,11},{12,13},{... | collective-permute-start | bytes 276488 | tf_op jit(solution)/shard_map/ppermute | solution.py:16
  17.9 4.3 %collective-permute-done.1 = bf16[2,15,1536]{2,1,0:T(8,128)(2,1)S(1)} collective-permute-done((bf16[2,15,1536]{2,1,0:T(8,128)(2,1)S(1)}, bf16[2,15,1536]{2,1,0:T(8,128)(2,1)S(1)}, u32[]{:S(2)}, u32[]{:S(2)}) %collective-permute-start.1) | collective-permute-done | bytes 92192 | tf_op jit(solution)/shard_map/ppermute | solution.py:17
  22.2 3.8 %fusion.144 = (f32[1536]{0:T(1024)S(1)}, f32[2,64,1536]{2,1,0:T(8,128)S(1)}) fusion(bf16[2,15,1536]{2,1,0:T(8,128)(2,1)S(1)} %collective-permute-done.1, bf16[2,64,1536]{2,1,0:T(8,128)(2,1)S(1)} %fusion.1, f32[1536]{0:T(1024)S(1)} %get-tuple-element.72, f32[1536]{0:T(1024)S(1)} %get-tuple-element.73, f32[1536]{0:T(1024)S(1)} %get-tuple-element.44, ...), kind=kLoop, calls=%fused_computation.381 | loop fusion | flops 35977728 | bytes 1560576 | tf_op jit(solution)/shard_map/reduce_sum | solution.py:108
  26.2 37.2 %all-gather.6.cloned.1.call-done = bf16[768,1536]{1,0:T(8,128)(2,1)} async-done(((bf16[192,1536]{1,0:T(8,128)(2,1)}), bf16[768,1536]{1,0:T(8,128)(2,1)}) %all-gather.6.cloned.1.call-update) | async-done | bytes 2359312 | tf_op jit(solution)/shard_map/all_gather | solution.py:81
  64.0 3.6 %collective-permute-done.2 = f32[2,1536]{1,0:T(2,128)S(1)} collective-permute-done((f32[2,1536]{1,0:T(2,128)S(1)}, f32[2,1536]{1,0:T(2,128)S(1)}, u32[]{:S(2)}, u32[]{:S(2)}) %collective-permute-start.2) | collective-permute-done | bytes 12320 | tf_op jit(solution)/shard_map/ppermute | solution.py:44
  69.2 2.2 collective-permute-done.3
  73.0 2.2 collective-permute-done.4
  75.4 3.7 %collective-permute-done.5 = f32[2,1536]{1,0:T(2,128)S(1)} collective-permute-done((f32[2,1536]{1,0:T(2,128)S(1)}, f32[2,1536]{1,0:T(2,128)S(1)}, u32[]{:S(2)}, u32[]{:S(2)}) %collective-permute-start.5) | collective-permute-done | bytes 12320 | tf_op jit(solution)/shard_map/ppermute | solution.py:44
  80.4 3.4 %collective-permute-done.6 = f32[2,1536]{1,0:T(2,128)S(1)} collective-permute-done((f32[2,1536]{1,0:T(2,128)S(1)}, f32[2,1536]{1,0:T(2,128)S(1)}, u32[]{:S(2)}, u32[]{:S(2)}) %collective-permute-start.6) | collective-permute-done | bytes 12320 | tf_op jit(solution)/shard_map/ppermute | solution.py:44
  84.5 2.7 %broadcast_select_fusion.1 = (bf16[4,192,1536]{2,1,0:T(8,128)(2,1)S(1)}, bf16[4,192,1536]{2,1,0:T(8,128)(2,1)S(1)}) fusion(bf16[4,192,1536]{2,1,0:T(8,128)(2,1)} %bitcast.21, bf16[4,192,1536]{2,1,0:T(8,128)(2,1)} %collective-permute-done.7, pred[]{:T(512)S(6)} %eq.11), kind=kLoop, calls=%fused_computation.38 | loop fusion | flops 2359296 | bytes 9437185 | tf_op jit(solution)/shard_map/jit(_where)/select_n | solution.py:83
  88.5 2.6 %fusion.141 = (f32[1536]{0:T(1024)S(1)}, f32[1536]{0:T(1024)S(1)}, bf16[2,64,1536]{2,1,0:T(8,128)(2,1)S(1)}, f32[2,64,1536]{2,1,0:T(8,128)}) fusion(f32[1536]{0:T(1024)S(1)} %get-tuple-element.90, f32[2,64,1536]{2,1,0:T(8,128)S(1)} %get-tuple-element.92, f32[1536]{0:T(1024)S(1)} %get-tuple-element.100, f32[1536]{0:T(1024)S(1)} %copy-done.77, ...), kind=kOutput, calls=%fused_computation.379 | convolution fusion | flops 607122432 | bytes 7114752 | tf_op jit(solution)/shard_map/btd,cd->btc/dot_general | solution.py:130
  94.0 2.2 collective-permute-done.9
  96.2 1.6 collective-permute-start.10
  97.8 2.2 collective-permute-done.10
  100.1 4.4 %collective-permute-done.11 = f32[2,1536]{1,0:T(2,128)S(1)} collective-permute-done((f32[2,1536]{1,0:T(2,128)S(1)}, f32[2,1536]{1,0:T(2,128)S(1)}, u32[]{:S(2)}, u32[]{:S(2)}) %collective-permute-start.11) | collective-permute-done | bytes 12320 | tf_op jit(solution)/shard_map/ppermute | solution.py:34
  106.0 4.3 %all-to-all-start = ((bf16[128,4,384]{2,0,1:T(8,128)(2,1)}), bf16[128,4,384]{2,0,1:T(8,128)(2,1)}, u32[]{:S(2)}, u32[]{:S(2)}) async-start(bf16[128,4,384]{2,0,1:T(8,128)(2,1)} %copy.12), calls=%async_computation | async-start | bytes 786432 | tf_op jit(solution)/shard_map/all_to_all | solution.py:125
  111.0 2.5 %fusion.81 = (f32[1536]{0:T(1024)S(1)}, f32[1536]{0:T(1024)S(1)}, f32[1536]{0:T(1024)S(1)}, f32[1536]{0:T(1024)S(1)}, f32[1536]{0:T(1024)S(1)}, /*index=5*/f32[1...) fusion(bf16[2,15,1536]{2,1,0:T(8,128)(2,1)S(1)} %collective-permute-done, ...), kind=kLoop, calls=%fused_computation.210 | loop fusion | flops 12372480 | bytes 2537472 | tf_op jit(solution)/shard_map/reduce_sum | solution.py:148
  116.8 2.8 %stack.172 = f32[31,1536]{1,0:T(8,128)} concatenate(f32[1,1536]{1,0:T(1,128)S(1)} %stack.141, f32[1,1536]{1,0:T(1,128)S(1)} %stack.142, f32[1,1536]{1,0:T(1,128)S(1)} %stack.143, f32[1,1536]{1,0:T(1,128)S(1)} %stack.144, f32[1,1536]{1,0:T(1,128)S(1)} %stack.145, f32[1,1536]{1,0:T(1,128)S(1)} %stack.146, f32[1,1536]{1,0:T(1,128)S(1)} %stack.147, f32[1,1536]{1,0:T(1,128)S(1)} %stack.148, ...), dimensions={0} | concatenate | bytes 380928 | tf_op jit(solution)/shard_map/stack | solution.py:146
  119.6 18.5 %all-gather.4.cloned.1.call-done = bf16[512,1536]{1,0:T(8,128)(2,1)} async-done(((bf16[128,1536]{1,0:T(8,128)(2,1)}), bf16[512,1536]{1,0:T(8,128)(2,1)}) %all-gather.4.cloned.1.call-update) | async-done | bytes 1572880 | tf_op jit(solution)/shard_map/all_gather | solution.py:100
  138.1 2.3 %fusion.148 = f32[384,1536]{1,0:T(8,128)S(1)} fusion(bf16[512,384]{1,0:T(8,128)(2,1)} %bitcast.6, bf16[512,1536]{1,0:T(8,128)(2,1)} %all-gather.4.cloned.1.call-done), kind=kOutput, calls=%fused_computation.384 | convolution fusion | flops 603979776 | bytes 4325376 | tf_op jit(solution)/shard_map/fc,fd->cd/dot_general | solution.py:126
  141.5 3.2 %collective-permute-done.15 = f32[192,1536]{1,0:T(8,128)} collective-permute-done((f32[192,1536]{1,0:T(8,128)}, f32[192,1536]{1,0:T(8,128)}, u32[]{:S(2)}, u32[]{:S(2)}) %collective-permute-start.15) | collective-permute-done | bytes 1179680 | tf_op jit(solution)/shard_map/ppermute | solution.py:65
  144.7 2.4 %dynamic-slice_add_fusion = f32[192,1536]{1,0:T(8,128)} fusion(f32[192,1536]{1,0:T(8,128)} %collective-permute-done.15, f32[384,1536]{1,0:T(8,128)S(1)} %fusion.148, s32[]{:T(128)S(6)} %select_n.65), kind=kLoop, calls=%fused_computation.96 | loop fusion | flops 294912 | bytes 3538948 | tf_op jit(solution)/shard_map/add | solution.py:65
  149.8 13.9 %collective-permute-done.16 = f32[96,1536]{1,0:T(8,128)S(1)} collective-permute-done((f32[96,1536]{1,0:T(8,128)S(1)}, f32[96,1536]{1,0:T(8,128)S(1)}, u32[]{:S(2)}, u32[]{:S(2)}) %collective-permute-start.16) | collective-permute-done | bytes 589856 | tf_op jit(solution)/shard_map/ppermute | solution.py:65
  166.5 6.7 %collective-permute-done.17 = f32[48,1536]{1,0:T(8,128)S(1)} collective-permute-done((f32[48,1536]{1,0:T(8,128)S(1)}, f32[48,1536]{1,0:T(8,128)S(1)}, u32[]{:S(2)}, u32[]{:S(2)}) %collective-permute-start.17) | collective-permute-done | bytes 294944 | tf_op jit(solution)/shard_map/ppermute | solution.py:65
  174.8 5.8 %collective-permute-done.18 = f32[48,1536]{1,0:T(8,128)S(1)} collective-permute-done((f32[48,1536]{1,0:T(8,128)S(1)}, f32[48,1536]{1,0:T(8,128)S(1)}, u32[]{:S(2)}, u32[]{:S(2)}) %collective-permute-start.18) | collective-permute-done | bytes 294944 | tf_op jit(solution)/shard_map/ppermute | solution.py:69
  182.2 3.9 %convolution_convert_fusion = bf16[2,64,1536]{2,1,0:T(8,128)(2,1)} fusion(bf16[2,64,1536]{2,1,0:T(8,128)(2,1)S(1)} %copy-done.6, bf16[1536,1536,1]{1,0,2:T(8,128)(2,1)} %bitcast.19), kind=kOutput, calls=%fused_computation.35 | convolution fusion | flops 604176384 | bytes 5505024 | tf_op jit(solution)/shard_map/btc,cd->btd/dot_general | solution.py:127
  188.3 4.6 %collective-permute-start.14 = (bf16[2,15,1536]{2,1,0:T(8,128)(2,1)S(1)}, bf16[2,15,1536]{2,1,0:T(8,128)(2,1)S(1)}, u32[]{:S(2)}, u32[]{:S(2)}) collective-permute-start(bf16[2,15,1536]{2,1,0:T(8,128)(2,1)S(1)} %get-tuple-element.97), channel_id=1, source_target_pairs={{0,1},{1,2},{2,3},{4,5},{5,6},{6,7},{8,9},{9,10},{10,11},{12,13},{... | collective-permute-start | bytes 276488 | tf_op jit(solution)/shard_map/ppermute | solution.py:16
  192.9 4.7 %collective-permute-done.22 = f32[31,1536]{1,0:T(8,128)S(1)} collective-permute-done((f32[31,1536]{1,0:T(8,128)S(1)}, f32[31,1536]{1,0:T(8,128)S(1)}, u32[]{:S(2)}, u32[]{:S(2)}) %collective-permute-start.22) | collective-permute-done | bytes 190496 | tf_op jit(solution)/shard_map/ppermute | solution.py:34
  199.7 4.1 %multiply_convert_fusion = (bf16[2,64,1536]{2,1,0:T(8,128)(2,1)S(1)}, f32[2,64,1536]{2,1,0:T(8,128)S(1)}) fusion(bf16[2,64,3072]{2,1,0:T(8,128)(2,1)S(1)} %copy-done.4, bf16[2,64,1536]{2,1,0:T(8,128)(2,1)S(1)} %copy-done.3, bf16[2,15,1536]{2,1,0:T(8,128)(2,1)S(1)} %collective-permute-done.14, f32[1536]{0:T(1024)S(1)} %copy-done.65, f32[1536]{0:T(1024)S(1)} %copy-done.67, ...), kind=kLoop, calls=%fused_computation.212 | loop fusion | flops 36962304 | bytes 2340864 | tf_op jit(solution)/shard_map/convert
  204.2 7.0 %collective-permute-done.24 = f32[31,1536]{1,0:T(8,128)S(1)} collective-permute-done((f32[31,1536]{1,0:T(8,128)S(1)}, f32[31,1536]{1,0:T(8,128)S(1)}, u32[]{:S(2)}, u32[]{:S(2)}) %collective-permute-start.24) | collective-permute-done | bytes 190496 | tf_op jit(solution)/shard_map/ppermute | solution.py:34
  212.3 10.5 %collective-permute-done.25 = f32[31,1536]{1,0:T(8,128)S(1)} collective-permute-done((f32[31,1536]{1,0:T(8,128)S(1)}, f32[31,1536]{1,0:T(8,128)S(1)}, u32[]{:S(2)}, u32[]{:S(2)}) %collective-permute-start.25) | collective-permute-done | bytes 190496 | tf_op jit(solution)/shard_map/ppermute | solution.py:34
  223.5 1.6 maximum_select_fusion
  (276 shorter events, 36.3 us)
Async XLA Ops:
  7.2 56.2 %all-gather.6.cloned.1.call-start = ((), (), s32[]{:S(2)}) async-start(), calls=%async_computation.2 | async-start | bytes 2949120 | tf_op jit(solution)/shard_map/all_gather | solution.py:81
  9.3 74.5 %copy-start.75 = (f32[1536]{0:T(1024)S(1)}, f32[1536]{0:T(1024)}, u32[]{:S(2)}) copy-start(f32[1536]{0:T(1024)} %param.8) | copy-start | bytes 18436
  9.3 128.8 %all-gather.4.cloned.1.call-start = ((), (), s32[]{:S(2)}) async-start(), calls=%async_computation.1 | async-start | bytes 1966080 | tf_op jit(solution)/shard_map/all_gather | solution.py:100
  10.8 7.1 %collective-permute-start = (bf16[2,15,1536]{2,1,0:T(8,128)(2,1)S(1)}, bf16[2,15,1536]{2,1,0:T(8,128)(2,1)S(1)}, u32[]{:S(2)}, u32[]{:S(2)}) collective-permute-start(bf16[2,15,1536]{2,1,0:T(8,128)(2,1)S(1)} %get-tuple-element.98), channel_id=1, source_target_pairs={{0,1},{1,2},{2,3},{4,5},{5,6},{6,7},{8,9},{9,10},{10,11},{12,13},{... | collective-permute-start | bytes 276488 | tf_op jit(solution)/shard_map/ppermute | solution.py:16
  15.7 6.5 %collective-permute-start.1 = (bf16[2,15,1536]{2,1,0:T(8,128)(2,1)S(1)}, bf16[2,15,1536]{2,1,0:T(8,128)(2,1)S(1)}, u32[]{:S(2)}, u32[]{:S(2)}) collective-permute-start(bf16[2,15,1536]{2,1,0:T(8,128)(2,1)S(1)} %get-tuple-element.99), channel_id=1, source_target_pairs={{1,0},{2,1},{3,2},{5,4},{6,5},{7,6},{9,8},{10,9},{11,10},{13,12},{... | collective-permute-start | bytes 276488 | tf_op jit(solution)/shard_map/ppermute | solution.py:17
  17.3 69.9 %copy-start.10 = (f32[1536]{0:T(1024)}, f32[1536]{0:T(1024)S(1)}, u32[]{:S(2)}) copy-start(f32[1536]{0:T(1024)S(1)} %get-tuple-element.45) | copy-start | bytes 18436
  17.3 69.9 %copy-start.12 = (f32[1536]{0:T(1024)}, f32[1536]{0:T(1024)S(1)}, u32[]{:S(2)}) copy-start(f32[1536]{0:T(1024)S(1)} %get-tuple-element.46) | copy-start | bytes 18436
  63.4 21.1 %collective-permute-start.7 = (bf16[4,192,1536]{2,1,0:T(8,128)(2,1)}, bf16[4,192,1536]{2,1,0:T(8,128)(2,1)}, u32[]{:S(2)}, u32[]{:S(2)}) collective-permute-start(bf16[4,192,1536]{2,1,0:T(8,128)(2,1)} %bitcast.20), channel_id=1, source_target_pairs={{0,4},{4,0},{8,12},{12,8},{16,20},{20,16},{24,28},{28,24},{1,5},{5... | collective-permute-start | bytes 7077896 | tf_op jit(solution)/shard_map/ppermute | solution.py:82
  63.4 4.2 %collective-permute-start.2 = (f32[2,1536]{1,0:T(2,128)S(1)}, f32[2,1536]{1,0:T(2,128)S(1)}, u32[]{:S(2)}, u32[]{:S(2)}) collective-permute-start(f32[2,1536]{1,0:T(2,128)S(1)} %pad_maximum_fusion.6), channel_id=1, source_target_pairs={{0,4},{4,0},{8,12},{12,8},{16,20},{20,16},{24,28},{28,24},{1,5},{5... | collective-permute-start | bytes 36872 | tf_op jit(solution)/shard_map/ppermute | solution.py:44
  67.6 3.8 %collective-permute-start.3 = (f32[2,1536]{1,0:T(2,128)S(1)}, f32[2,1536]{1,0:T(2,128)S(1)}, u32[]{:S(2)}, u32[]{:S(2)}) collective-permute-start(f32[2,1536]{1,0:T(2,128)S(1)} %pad_maximum_fusion.7), channel_id=1, source_target_pairs={{0,8},{4,12},{8,0},{12,4},{16,24},{20,28},{24,16},{28,20},{1,9},{5... | collective-permute-start | bytes 36872 | tf_op jit(solution)/shard_map/ppermute | solution.py:44
  71.5 3.8 %collective-permute-start.4 = (f32[2,1536]{1,0:T(2,128)S(1)}, f32[2,1536]{1,0:T(2,128)S(1)}, u32[]{:S(2)}, u32[]{:S(2)}) collective-permute-start(f32[2,1536]{1,0:T(2,128)S(1)} %pad_maximum_fusion.8), channel_id=1, source_target_pairs={{0,16},{4,20},{8,24},{12,28},{16,0},{20,4},{24,8},{28,12},{1,17},{... | collective-permute-start | bytes 36872 | tf_op jit(solution)/shard_map/ppermute | solution.py:44
  75.3 3.8 %collective-permute-start.5 = (f32[2,1536]{1,0:T(2,128)S(1)}, f32[2,1536]{1,0:T(2,128)S(1)}, u32[]{:S(2)}, u32[]{:S(2)}) collective-permute-start(f32[2,1536]{1,0:T(2,128)S(1)} %pad_maximum_fusion.9), channel_id=1, source_target_pairs={{0,1},{1,0},{2,3},{3,2},{4,5},{5,4},{6,7},{7,6},{8,9},{9,8},{10,11... | collective-permute-start | bytes 36872 | tf_op jit(solution)/shard_map/ppermute | solution.py:44
  79.1 4.7 %collective-permute-start.6 = (f32[2,1536]{1,0:T(2,128)S(1)}, f32[2,1536]{1,0:T(2,128)S(1)}, u32[]{:S(2)}, u32[]{:S(2)}) collective-permute-start(f32[2,1536]{1,0:T(2,128)S(1)} %pad_maximum_fusion.10), channel_id=1, source_target_pairs={{0,2},{1,3},{2,0},{3,1},{4,6},{5,7},{6,4},{7,5},{8,10},{9,11},{10,... | collective-permute-start | bytes 36872 | tf_op jit(solution)/shard_map/ppermute | solution.py:44
  91.2 1.2 collective-permute-start.8
  92.4 3.8 %collective-permute-start.9 = (f32[2,1536]{1,0:T(2,128)S(1)}, f32[2,1536]{1,0:T(2,128)S(1)}, u32[]{:S(2)}, u32[]{:S(2)}) collective-permute-start(f32[2,1536]{1,0:T(2,128)S(1)} %fusion.140), channel_id=1, source_target_pairs={{0,8},{4,12},{8,0},{12,4},{16,24},{20,28},{24,16},{28,20},{1,9},{5... | collective-permute-start | bytes 36872 | tf_op jit(solution)/shard_map/ppermute | solution.py:34
  96.2 3.8 %collective-permute-start.10 = (f32[2,1536]{1,0:T(2,128)S(1)}, f32[2,1536]{1,0:T(2,128)S(1)}, u32[]{:S(2)}, u32[]{:S(2)}) collective-permute-start(f32[2,1536]{1,0:T(2,128)S(1)} %fusion.155), channel_id=1, source_target_pairs={{0,16},{4,20},{8,24},{12,28},{16,0},{20,4},{24,8},{28,12},{1,17},{... | collective-permute-start | bytes 36872 | tf_op jit(solution)/shard_map/ppermute | solution.py:34
  100.0 4.4 %collective-permute-start.11 = (f32[2,1536]{1,0:T(2,128)S(1)}, f32[2,1536]{1,0:T(2,128)S(1)}, u32[]{:S(2)}, u32[]{:S(2)}) collective-permute-start(f32[2,1536]{1,0:T(2,128)S(1)} %add.512), channel_id=1, source_target_pairs={{0,1},{1,0},{2,3},{3,2},{4,5},{5,4},{6,7},{7,6},{8,9},{9,8},{10,11... | collective-permute-start | bytes 36872 | tf_op jit(solution)/shard_map/ppermute | solution.py:34
  104.4 5.9 %collective-permute-start.12 = (f32[2,1536]{1,0:T(2,128)S(1)}, f32[2,1536]{1,0:T(2,128)S(1)}, u32[]{:S(2)}, u32[]{:S(2)}) collective-permute-start(f32[2,1536]{1,0:T(2,128)S(1)} %add.513), channel_id=1, source_target_pairs={{0,2},{1,3},{2,0},{3,1},{4,6},{5,7},{6,4},{7,5},{8,10},{9,11},{10,... | collective-permute-start | bytes 36872 | tf_op jit(solution)/shard_map/ppermute | solution.py:34
  106.0 32.1 %all-to-all-start = ((bf16[128,4,384]{2,0,1:T(8,128)(2,1)}), bf16[128,4,384]{2,0,1:T(8,128)(2,1)}, u32[]{:S(2)}, u32[]{:S(2)}) async-start(bf16[128,4,384]{2,0,1:T(8,128)(2,1)} %copy.12), calls=%async_computation | async-start | bytes 786432 | tf_op jit(solution)/shard_map/all_to_all | solution.py:125
  141.5 3.2 %collective-permute-start.15 = (f32[192,1536]{1,0:T(8,128)}, f32[192,1536]{1,0:T(8,128)}, u32[]{:S(2)}, u32[]{:S(2)}) collective-permute-start(f32[192,1536]{1,0:T(8,128)} %constant_dynamic-slice_fusion.2), channel_id=1, source_target_pairs={{0,4},{4,0},{8,12},{12,8},{16,20},{20,16},{24,28},{28,24},{1,5},{5... | collective-permute-start | bytes 3538952 | tf_op jit(solution)/shard_map/ppermute | solution.py:65
  148.3 15.4 %collective-permute-start.16 = (f32[96,1536]{1,0:T(8,128)S(1)}, f32[96,1536]{1,0:T(8,128)S(1)}, u32[]{:S(2)}, u32[]{:S(2)}) collective-permute-start(f32[96,1536]{1,0:T(8,128)S(1)} %constant_dynamic-slice_fusion.1), channel_id=1, source_target_pairs={{0,8},{4,12},{8,0},{12,4},{16,24},{20,28},{24,16},{28,20},{1,9},{5... | collective-permute-start | bytes 1769480 | tf_op jit(solution)/shard_map/ppermute | solution.py:65
  164.9 8.3 %collective-permute-start.17 = (f32[48,1536]{1,0:T(8,128)S(1)}, f32[48,1536]{1,0:T(8,128)S(1)}, u32[]{:S(2)}, u32[]{:S(2)}) collective-permute-start(f32[48,1536]{1,0:T(8,128)S(1)} %constant_dynamic-slice_fusion), channel_id=1, source_target_pairs={{0,16},{4,20},{8,24},{12,28},{16,0},{20,4},{24,8},{28,12},{1,17},{... | collective-permute-start | bytes 884744 | tf_op jit(solution)/shard_map/ppermute | solution.py:65
  173.2 7.4 %collective-permute-start.18 = (f32[48,1536]{1,0:T(8,128)S(1)}, f32[48,1536]{1,0:T(8,128)S(1)}, u32[]{:S(2)}, u32[]{:S(2)}) collective-permute-start(f32[48,1536]{1,0:T(8,128)S(1)} %dynamic-slice_add_fusion.2), channel_id=1, source_target_pairs={{0,16},{4,20},{8,24},{12,28},{16,0},{20,4},{24,8},{28,12},{1,17},{... | collective-permute-start | bytes 884744 | tf_op jit(solution)/shard_map/ppermute | solution.py:69
  174.8 11.6 %collective-permute-start.21 = (f32[31,1536]{1,0:T(8,128)S(1)}, f32[31,1536]{1,0:T(8,128)S(1)}, u32[]{:S(2)}, u32[]{:S(2)}) collective-permute-start(f32[31,1536]{1,0:T(8,128)S(1)} %copy-done.7), channel_id=1, source_target_pairs={{0,4},{4,0},{8,12},{12,8},{16,20},{20,16},{24,28},{28,24},{1,5},{5... | collective-permute-start | bytes 571400 | tf_op jit(solution)/shard_map/ppermute | solution.py:34
  180.7 18.5 %collective-permute-start.19 = (f32[96,1536]{1,0:T(8,128)S(1)}, f32[96,1536]{1,0:T(8,128)S(1)}, u32[]{:S(2)}, u32[]{:S(2)}) collective-permute-start(f32[96,1536]{1,0:T(8,128)S(1)} %maximum_select_fusion.2), channel_id=1, source_target_pairs={{0,8},{4,12},{8,0},{12,4},{16,24},{20,28},{24,16},{28,20},{1,9},{5... | collective-permute-start | bytes 1769480 | tf_op jit(solution)/shard_map/ppermute | solution.py:69
  186.4 11.3 %collective-permute-start.22 = (f32[31,1536]{1,0:T(8,128)S(1)}, f32[31,1536]{1,0:T(8,128)S(1)}, u32[]{:S(2)}, u32[]{:S(2)}) collective-permute-start(f32[31,1536]{1,0:T(8,128)S(1)} %add.553), channel_id=1, source_target_pairs={{0,8},{4,12},{8,0},{12,4},{16,24},{20,28},{24,16},{28,20},{1,9},{5... | collective-permute-start | bytes 571400 | tf_op jit(solution)/shard_map/ppermute | solution.py:34
  187.0 12.3 %collective-permute-start.13 = (bf16[2,15,1536]{2,1,0:T(8,128)(2,1)S(1)}, bf16[2,15,1536]{2,1,0:T(8,128)(2,1)S(1)}, u32[]{:S(2)}, u32[]{:S(2)}) collective-permute-start(bf16[2,15,1536]{2,1,0:T(8,128)(2,1)S(1)} %get-tuple-element.96), channel_id=1, source_target_pairs={{1,0},{2,1},{3,2},{5,4},{6,5},{7,6},{9,8},{10,9},{11,10},{13,12},{... | collective-permute-start | bytes 276488 | tf_op jit(solution)/shard_map/ppermute | solution.py:17
  188.3 11.1 %collective-permute-start.14 = (bf16[2,15,1536]{2,1,0:T(8,128)(2,1)S(1)}, bf16[2,15,1536]{2,1,0:T(8,128)(2,1)S(1)}, u32[]{:S(2)}, u32[]{:S(2)}) collective-permute-start(bf16[2,15,1536]{2,1,0:T(8,128)(2,1)S(1)} %get-tuple-element.97), channel_id=1, source_target_pairs={{0,1},{1,2},{2,3},{4,5},{5,6},{6,7},{8,9},{9,10},{10,11},{12,13},{... | collective-permute-start | bytes 276488 | tf_op jit(solution)/shard_map/ppermute | solution.py:16
  197.7 6.1 %collective-permute-start.23 = (f32[31,1536]{1,0:T(8,128)S(1)}, f32[31,1536]{1,0:T(8,128)S(1)}, u32[]{:S(2)}, u32[]{:S(2)}) collective-permute-start(f32[31,1536]{1,0:T(8,128)S(1)} %add.554), channel_id=1, source_target_pairs={{0,16},{4,20},{8,24},{12,28},{16,0},{20,4},{24,8},{28,12},{1,17},{... | collective-permute-start | bytes 571400 | tf_op jit(solution)/shard_map/ppermute | solution.py:34
  199.3 24.2 %collective-permute-start.20 = (f32[192,1536]{1,0:T(8,128)S(1)}, f32[192,1536]{1,0:T(8,128)S(1)}, u32[]{:S(2)}, u32[]{:S(2)}) collective-permute-start(f32[192,1536]{1,0:T(8,128)S(1)} %maximum_select_fusion.1), channel_id=1, source_target_pairs={{0,4},{4,0},{8,12},{12,8},{16,20},{20,16},{24,28},{28,24},{1,5},{5... | collective-permute-start | bytes 3538952 | tf_op jit(solution)/shard_map/ppermute | solution.py:69
  203.8 7.3 %collective-permute-start.24 = (f32[31,1536]{1,0:T(8,128)S(1)}, f32[31,1536]{1,0:T(8,128)S(1)}, u32[]{:S(2)}, u32[]{:S(2)}) collective-permute-start(f32[31,1536]{1,0:T(8,128)S(1)} %add.555), channel_id=1, source_target_pairs={{0,1},{1,0},{2,3},{3,2},{4,5},{5,4},{6,7},{7,6},{8,9},{9,8},{10,11... | collective-permute-start | bytes 571400 | tf_op jit(solution)/shard_map/ppermute | solution.py:34
  211.2 11.6 %collective-permute-start.25 = (f32[31,1536]{1,0:T(8,128)S(1)}, f32[31,1536]{1,0:T(8,128)S(1)}, u32[]{:S(2)}, u32[]{:S(2)}) collective-permute-start(f32[31,1536]{1,0:T(8,128)S(1)} %add.556), channel_id=1, source_target_pairs={{0,2},{1,3},{2,0},{3,1},{4,6},{5,7},{6,4},{7,5},{8,10},{9,11},{10,... | collective-permute-start | bytes 571400 | tf_op jit(solution)/shard_map/ppermute | solution.py:34
  (75 other events, 2344.9 us)
Sparse Core Ops, SparseCore 0:
  10.2 53.1 all-gather.5
  94.1 43.9 all-gather.3

commit v5 on v4

--- a/solution.py
+++ b/solution.py
@@ -95,9 +95,11 @@
     me = lax.axis_index("tensor")
     local = glu_input.shape[0] * frames
     everyone = local * lax.axis_size("dp") * peers
-    full_weight = gather_weight(proj_weight)
     flat_grad = out_grad.reshape(-1, width)
     group_grad = lax.all_gather(flat_grad, "tensor", axis=0, tiled=True)
+    own_columns = jnp.einsum("fd,cd->fc", group_grad, proj_weight, preferred_element_type=jnp.float32)
+    grad_act = lax.all_to_all(own_columns, "tensor", split_axis=0, concat_axis=1, tiled=True)
+    grad_act = grad_act.reshape(out_grad.shape)
     values = glu_input[..., :width].astype(jnp.float32)
     gates = jax.nn.sigmoid(glu_input[..., width:].astype(jnp.float32))
     gated = (values * gates).astype(jnp.bfloat16)
@@ -124,10 +126,6 @@
     flat_act = activated.reshape(-1, width)
     group_act = lax.all_to_all(flat_act, "tensor", split_axis=1, concat_axis=0, tiled=True)
     local_grad = jnp.einsum("fc,fd->cd", group_act, group_grad, preferred_element_type=jnp.float32)
-    conv_output = jnp.einsum(
-        "btc,cd->btd", activated, full_weight, preferred_element_type=jnp.float32
-    ).astype(jnp.bfloat16)
-    grad_act = jnp.einsum("btd,cd->btc", out_grad, full_weight, preferred_element_type=jnp.float32)
     grad_affine = grad_act * (sig_affine + affine * sig_affine * (1.0 - sig_affine))
     sums = jnp.stack([jnp.sum(grad_affine, axis=(0, 1)), jnp.sum(grad_affine * normed, axis=(0, 1))])
     sums = all_sum(sums, ("dp", "tensor"))
@@ -157,6 +155,10 @@
     input_grad = jnp.concatenate(
         [grad_gated * gates, grad_gated * values * gates * (1.0 - gates)], axis=-1
     ).astype(jnp.bfloat16)
+    full_weight = gather_weight(proj_weight)
+    conv_output = jnp.einsum(
+        "btc,cd->btd", activated, full_weight, preferred_element_type=jnp.float32
+    ).astype(jnp.bfloat16)
     return (conv_output, input_grad, weight_grad, kernel_grad, scale_grad, shift_grad)
 
 

time: 233 us -> 203 us (0.87)
  waiting for transfers between devices: 137 us -> 92.3 us
  starting transfers between devices: 33.9 us -> 44.1 us
  local copies, waits for them, and re-layouts: 10.3 us -> 14.4 us
    all_gather x1, waiting for transfers between devices: 37.2 us -> 16.2 us  [gather_weight(): held = lax.all_gather(mine, 'tensor', axis=0, tiled=False)]
    ppermute x3, waiting for transfers between devices: 23.8 us -> 4.24 us  [rows_sum(): x = keep + lax.ppermute(give, axis, [(i, i ^ step) for i in range(peers)])]
    ppermute x10, waiting for transfers between devices: 32.2 us -> 18.1 us  [all_sum(): x = x + lax.ppermute(x, axis, [(i, i ^ step) for i in range(peers)])]
    all_to_all x1, waiting for transfers between devices: 0.01 us -> 8.66 us  [on_device(): lax.all_to_all(flat_act, 'tensor', split_axis=1, concat_axis=0, tiled=True)]
    ppermute x5, starting transfers between devices: 5.02 us -> 9.87 us  [all_moments(): lax.ppermute(jnp.stack([mean, spread]), axis, [(i, i ^ step) for i in ran...]
    all_to_all x0 -> x1, starting transfers between devices: none -> 3.51 us  [on_device(): lax.all_to_all(own_columns, 'tensor', split_axis=0, concat_axis=1, tiled=...]
    select_n x1, other arithmetic: 2.69 us -> 0.31 us  [gather_weight(): first = jnp.where(core == 0, held, other)]
    dot_general x1, matrix products: 3.87 us -> 1.53 us  [on_device(): jnp.einsum('btc,cd->btd', activated, full_weight, preferred_element_type=...]
  transfers between devices with their start and end apart: 29 -> 30, of which waited for: 20 -> 19; matrix products, arithmetic and copies ran while one was open for 11% -> 20% of each run, Pallas kernels for 0% -> 0%
where the time goes in v5:
time: 203 us; the launch traced here: 202 us
  waiting for transfers between devices  92.3 us (45%)
  starting transfers between devices  44.1 us (22%)
  other arithmetic  28.4 us (14%)
  between operations  15.8 us (8%)
  local copies, waits for them, and re-layouts  14.4 us (7%)
  matrix products  7.14 us (4%)
    ppermute x10, waiting for transfers between devices, all_sum(): x = x + lax.ppermute(x, axis, [(i, i ^ step) for i in range(peers)])  18.1 us
    ppermute x5, waiting for transfers between devices, all_moments(): lax.ppermute(jnp.stack([mean, spread]), axis, [(i, i ^ step) for i in ran...  17.3 us
    all_gather x1, waiting for transfers between devices, on_device(): group_grad = lax.all_gather(flat_grad, 'tensor', axis=0, tiled=True)  17.3 us
    all_gather x1, waiting for transfers between devices, gather_weight(): held = lax.all_gather(mine, 'tensor', axis=0, tiled=False)  16.2 us
    ppermute x5, starting transfers between devices, all_moments(): lax.ppermute(jnp.stack([mean, spread]), axis, [(i, i ^ step) for i in ran...  9.87 us
    ppermute x2, starting transfers between devices, extended(): before = lax.ppermute(last, axis, up)  9.48 us
    all_to_all x1, waiting for transfers between devices, on_device(): lax.all_to_all(flat_act, 'tensor', split_axis=1, concat_axis=0, tiled=True)  8.66 us
    ppermute x10, starting transfers between devices, all_sum(): x = x + lax.ppermute(x, axis, [(i, i ^ step) for i in range(peers)])  8.36 us
  transfers between devices with their start and end apart: 30, of which 19 were waited for; matrix products, arithmetic and copies ran while one was open for 20% of the time, Pallas kernels for 0%

profile of v5, /device:TPU:0, one launch (start us, length us, event | category | flops | bytes accessed | tf_op | source)
XLA Modules:
  0.0 202.0 jit_solution(15892937583322109170)
XLA Ops:
  9.3 4.9 %collective-permute-start = (bf16[2,15,1536]{2,1,0:T(8,128)(2,1)S(1)}, bf16[2,15,1536]{2,1,0:T(8,128)(2,1)S(1)}, u32[]{:S(2)}, u32[]{:S(2)}) collective-permute-start(bf16[2,15,1536]{2,1,0:T(8,128)(2,1)S(1)} %get-tuple-element.99), channel_id=1, source_target_pairs={{0,1},{1,2},{2,3},{4,5},{5,6},{6,7},{8,9},{9,10},{10,11},{12,13},{... | collective-permute-start | bytes 276488 | tf_op jit(solution)/shard_map/ppermute | solution.py:16
  16.4 4.3 %collective-permute-done.1 = bf16[2,15,1536]{2,1,0:T(8,128)(2,1)S(1)} collective-permute-done((bf16[2,15,1536]{2,1,0:T(8,128)(2,1)S(1)}, bf16[2,15,1536]{2,1,0:T(8,128)(2,1)S(1)}, u32[]{:S(2)}, u32[]{:S(2)}) %collective-permute-start.1) | collective-permute-done | bytes 92192 | tf_op jit(solution)/shard_map/ppermute | solution.py:17
  21.4 3.8 %fusion.143 = (f32[1536]{0:T(1024)S(1)}, f32[2,64,1536]{2,1,0:T(8,128)S(1)}) fusion(bf16[2,15,1536]{2,1,0:T(8,128)(2,1)S(1)} %collective-permute-done.1, bf16[2,64,1536]{2,1,0:T(8,128)(2,1)S(1)} %fusion, f32[1536]{0:T(1024)S(1)} %get-tuple-element.72, f32[1536]{0:T(1024)S(1)} %get-tuple-element.73, f32[1536]{0:T(1024)S(1)} %get-tuple-element.44, ...), kind=kLoop, calls=%fused_computation.380 | loop fusion | flops 35977728 | bytes 1560576 | tf_op jit(solution)/shard_map/reduce_sum | solution.py:110
  28.3 2.2 %collective-permute-done.3 = f32[2,1536]{1,0:T(2,128)S(1)} collective-permute-done((f32[2,1536]{1,0:T(2,128)S(1)}, f32[2,1536]{1,0:T(2,128)S(1)}, u32[]{:S(2)}, u32[]{:S(2)}) %collective-permute-start.3) | collective-permute-done | bytes 12320 | tf_op jit(solution)/shard_map/ppermute | solution.py:44
  32.2 17.3 %all-gather.4.cloned.1.call-done = bf16[512,1536]{1,0:T(8,128)(2,1)} async-done(((bf16[128,1536]{1,0:T(8,128)(2,1)}), bf16[512,1536]{1,0:T(8,128)(2,1)}) %all-gather.4.cloned.1.call-update) | async-done | bytes 1572880 | tf_op jit(solution)/shard_map/all_gather | solution.py:99
  49.4 3.3 %fusion.147 = f32[512,384]{1,0:T(8,128)} fusion(bf16[512,1536]{1,0:T(8,128)(2,1)} %all-gather.4.cloned.1.call-done, bf16[384,1536]{1,0:T(8,128)(2,1)S(1)} %copy-done), kind=kOutput, calls=%fused_computation.383 | convolution fusion | flops 603979776 | bytes 3538944 | tf_op jit(solution)/shard_map/fd,cd->fc/dot_general | solution.py:100
  53.0 3.5 %all-to-all-start = ((f32[4,128,384]{2,1,0:T(8,128)}), f32[4,128,384]{2,1,0:T(8,128)S(1)}, u32[]{:S(2)}, u32[]{:S(2)}) async-start(f32[4,128,384]{2,1,0:T(8,128)} %bitcast.20), calls=%async_computation | async-start | bytes 1572864 | tf_op jit(solution)/shard_map/all_to_all | solution.py:101
  56.6 2.0 collective-permute-start.5
  58.6 11.1 %collective-permute-done.5 = f32[2,1536]{1,0:T(2,128)S(1)} collective-permute-done((f32[2,1536]{1,0:T(2,128)S(1)}, f32[2,1536]{1,0:T(2,128)S(1)}, u32[]{:S(2)}, u32[]{:S(2)}) %collective-permute-start.5) | collective-permute-done | bytes 12320 | tf_op jit(solution)/shard_map/ppermute | solution.py:44
  69.8 4.7 %collective-permute-start.6 = (f32[2,1536]{1,0:T(2,128)S(1)}, f32[2,1536]{1,0:T(2,128)S(1)}, u32[]{:S(2)}, u32[]{:S(2)}) collective-permute-start(f32[2,1536]{1,0:T(2,128)S(1)} %pad_maximum_fusion.10), channel_id=1, source_target_pairs={{0,2},{1,3},{2,0},{3,1},{4,6},{5,7},{6,4},{7,5},{8,10},{9,11},{10,... | collective-permute-start | bytes 36872 | tf_op jit(solution)/shard_map/ppermute | solution.py:44
  74.5 2.8 %collective-permute-done.6 = f32[2,1536]{1,0:T(2,128)S(1)} collective-permute-done((f32[2,1536]{1,0:T(2,128)S(1)}, f32[2,1536]{1,0:T(2,128)S(1)}, u32[]{:S(2)}, u32[]{:S(2)}) %collective-permute-start.6) | collective-permute-done | bytes 12320 | tf_op jit(solution)/shard_map/ppermute | solution.py:44
  80.8 2.1 %fusion.140 = (f32[1536]{0:T(1024)S(1)}, f32[1536]{0:T(1024)S(1)}, f32[2,64,1536]{2,1,0:T(8,128)}, bf16[2,64,1536]{2,1,0:T(8,128)(2,1)S(1)}) fusion(f32[1536]{0:T(1024)} %get-tuple-element.90, f32[2,64,1536]{2,1,0:T(8,128)S(1)} %get-tuple-element.93, f32[1536]{0:T(1024)} %get-tuple-element.101, f32[2,64,1536]{2,1,0:T(8,128)S(1)} %reshape.208, ...), kind=kLoop, calls=%fused_computation.378 | loop fusion | flops 3142656 | bytes 2789376 | tf_op jit(solution)/shard_map/reduce_sum | solution.py:130
  85.7 2.2 %collective-permute-done.9 = f32[2,1536]{1,0:T(2,128)S(1)} collective-permute-done((f32[2,1536]{1,0:T(2,128)S(1)}, f32[2,1536]{1,0:T(2,128)S(1)}, u32[]{:S(2)}, u32[]{:S(2)}) %collective-permute-start.9) | collective-permute-done | bytes 12320 | tf_op jit(solution)/shard_map/ppermute | solution.py:34
  89.5 2.2 %collective-permute-done.10 = f32[2,1536]{1,0:T(2,128)S(1)} collective-permute-done((f32[2,1536]{1,0:T(2,128)S(1)}, f32[2,1536]{1,0:T(2,128)S(1)}, u32[]{:S(2)}, u32[]{:S(2)}) %collective-permute-start.10) | collective-permute-done | bytes 12320 | tf_op jit(solution)/shard_map/ppermute | solution.py:34
  91.8 3.7 %collective-permute-done.11 = f32[2,1536]{1,0:T(2,128)S(1)} collective-permute-done((f32[2,1536]{1,0:T(2,128)S(1)}, f32[2,1536]{1,0:T(2,128)S(1)}, u32[]{:S(2)}, u32[]{:S(2)}) %collective-permute-start.11) | collective-permute-done | bytes 12320 | tf_op jit(solution)/shard_map/ppermute | solution.py:34
  96.1 1.8 collective-permute-start.12
  99.6 1.8 copy.17
  101.4 4.3 %all-to-all-start.1 = ((bf16[128,4,384]{2,0,1:T(8,128)(2,1)}), bf16[128,4,384]{2,0,1:T(8,128)(2,1)}, u32[]{:S(2)}, u32[]{:S(2)}) async-start(bf16[128,4,384]{2,0,1:T(8,128)(2,1)} %copy.17), calls=%async_computation.1 | async-start | bytes 786432 | tf_op jit(solution)/shard_map/all_to_all | solution.py:127
  107.2 2.9 %fusion.80 = (f32[1536]{0:T(1024)S(1)}, f32[1536]{0:T(1024)S(1)}, f32[1536]{0:T(1024)S(1)}, f32[1536]{0:T(1024)S(1)}, f32[1536]{0:T(1024)S(1)}, /*index=5*/f32[1...) fusion(bf16[2,15,1536]{2,1,0:T(8,128)(2,1)} %copy-done.8, ...), kind=kLoop, calls=%fused_computation.208 | loop fusion | flops 12372480 | bytes 2537472 | tf_op jit(solution)/shard_map/reduce_sum | solution.py:146
  113.4 2.8 %stack.172 = f32[31,1536]{1,0:T(8,128)} concatenate(f32[1,1536]{1,0:T(1,128)S(1)} %stack.141, f32[1,1536]{1,0:T(1,128)S(1)} %stack.142, f32[1,1536]{1,0:T(1,128)S(1)} %stack.143, f32[1,1536]{1,0:T(1,128)S(1)} %stack.144, f32[1,1536]{1,0:T(1,128)S(1)} %stack.145, f32[1,1536]{1,0:T(1,128)S(1)} %stack.146, f32[1,1536]{1,0:T(1,128)S(1)} %stack.147, f32[1,1536]{1,0:T(1,128)S(1)} %stack.148, ...), dimensions={0} | concatenate | bytes 380928 | tf_op jit(solution)/shard_map/stack | solution.py:144
  116.2 8.7 %all-to-all-done.1 = bf16[128,4,384]{2,0,1:T(8,128)(2,1)} async-done(((bf16[128,4,384]{2,0,1:T(8,128)(2,1)}), bf16[128,4,384]{2,0,1:T(8,128)(2,1)}, u32[]{:S(2)}, u32[]{:S(2)}) %all-to-all-start.1) | async-done | bytes 393248 | tf_op jit(solution)/shard_map/all_to_all | solution.py:127
  124.8 2.3 %fusion.148 = f32[384,1536]{1,0:T(8,128)S(1)} fusion(bf16[512,384]{1,0:T(8,128)(2,1)} %bitcast.7, bf16[512,1536]{1,0:T(8,128)(2,1)} %all-gather.4.cloned.1.call-done), kind=kOutput, calls=%fused_computation.384 | convolution fusion | flops 603979776 | bytes 4325376 | tf_op jit(solution)/shard_map/fc,fd->cd/dot_general | solution.py:128
  128.3 3.2 %collective-permute-done.15 = f32[192,1536]{1,0:T(8,128)} collective-permute-done((f32[192,1536]{1,0:T(8,128)}, f32[192,1536]{1,0:T(8,128)}, u32[]{:S(2)}, u32[]{:S(2)}) %collective-permute-start.15) | collective-permute-done | bytes 1179680 | tf_op jit(solution)/shard_map/ppermute | solution.py:65
  131.5 2.4 %dynamic-slice_add_fusion = f32[192,1536]{1,0:T(8,128)} fusion(f32[192,1536]{1,0:T(8,128)} %collective-permute-done.15, f32[384,1536]{1,0:T(8,128)S(1)} %fusion.148, s32[]{:T(128)S(6)} %select_n.65), kind=kLoop, calls=%fused_computation.94 | loop fusion | flops 294912 | bytes 3538948 | tf_op jit(solution)/shard_map/add | solution.py:65
  136.5 16.2 %all-gather.6.cloned.1.call-done = bf16[768,1536]{1,0:T(8,128)(2,1)} async-done(((bf16[192,1536]{1,0:T(8,128)(2,1)}), bf16[768,1536]{1,0:T(8,128)(2,1)}) %all-gather.6.cloned.1.call-update) | async-done | bytes 2359312 | tf_op jit(solution)/shard_map/all_gather | solution.py:81
  159.6 4.6 %collective-permute-start.14 = (bf16[2,15,1536]{2,1,0:T(8,128)(2,1)S(1)}, bf16[2,15,1536]{2,1,0:T(8,128)(2,1)S(1)}, u32[]{:S(2)}, u32[]{:S(2)}) collective-permute-start(bf16[2,15,1536]{2,1,0:T(8,128)(2,1)S(1)} %get-tuple-element.98), channel_id=1, source_target_pairs={{0,1},{1,2},{2,3},{4,5},{5,6},{6,7},{8,9},{9,10},{10,11},{12,13},{... | collective-permute-start | bytes 276488 | tf_op jit(solution)/shard_map/ppermute | solution.py:16
  165.9 2.1 %collective-permute-start.18 = (f32[48,1536]{1,0:T(8,128)S(1)}, f32[48,1536]{1,0:T(8,128)S(1)}, u32[]{:S(2)}, u32[]{:S(2)}) collective-permute-start(f32[48,1536]{1,0:T(8,128)S(1)} %dynamic-slice_add_fusion.2), channel_id=1, source_target_pairs={{0,16},{4,20},{8,24},{12,28},{16,0},{20,4},{24,8},{28,12},{1,17},{... | collective-permute-start | bytes 884744 | tf_op jit(solution)/shard_map/ppermute | solution.py:69
  168.3 4.1 %multiply_convert_fusion = (bf16[2,64,1536]{2,1,0:T(8,128)(2,1)S(1)}, f32[2,64,1536]{2,1,0:T(8,128)S(1)}) fusion(bf16[2,64,3072]{2,1,0:T(8,128)(2,1)S(1)} %copy-done.3, bf16[2,64,1536]{2,1,0:T(8,128)(2,1)S(1)} %copy-done.2, bf16[2,15,1536]{2,1,0:T(8,128)(2,1)S(1)} %collective-permute-done.14, f32[1536]{0:T(1024)S(1)} %copy-done.68, f32[1536]{0:T(1024)S(1)} %copy-done.70, ...), kind=kLoop, calls=%fused_computation.210 | loop fusion | flops 36962304 | bytes 2340864 | tf_op jit(solution)/shard_map/convert
  173.2 3.5 %collective-permute-done.18 = f32[48,1536]{1,0:T(8,128)S(1)} collective-permute-done((f32[48,1536]{1,0:T(8,128)S(1)}, f32[48,1536]{1,0:T(8,128)S(1)}, u32[]{:S(2)}, u32[]{:S(2)}) %collective-permute-start.18) | collective-permute-done | bytes 294944 | tf_op jit(solution)/shard_map/ppermute | solution.py:69
  179.5 8.3 %collective-permute-done.25 = f32[31,1536]{1,0:T(8,128)S(1)} collective-permute-done((f32[31,1536]{1,0:T(8,128)S(1)}, f32[31,1536]{1,0:T(8,128)S(1)}, u32[]{:S(2)}, u32[]{:S(2)}) %collective-permute-start.25) | collective-permute-done | bytes 190496 | tf_op jit(solution)/shard_map/ppermute | solution.py:34
  188.5 2.0 collective-permute-done.19
  193.5 1.6 maximum_select_fusion
  (273 shorter events, 43.7 us)
Async XLA Ops:
  7.2 42.3 %copy-start = (bf16[384,1536]{1,0:T(8,128)(2,1)S(1)}, bf16[384,1536]{1,0:T(8,128)(2,1)}, u32[]{:S(2)}) copy-start(bf16[384,1536]{1,0:T(8,128)(2,1)} %param.10) | copy-start | bytes 3538948
  7.2 42.2 %all-gather.4.cloned.1.call-start = ((), (), s32[]{:S(2)}) async-start(), calls=%async_computation.2 | async-start | bytes 1966080 | tf_op jit(solution)/shard_map/all_gather | solution.py:99
  9.3 7.1 %collective-permute-start = (bf16[2,15,1536]{2,1,0:T(8,128)(2,1)S(1)}, bf16[2,15,1536]{2,1,0:T(8,128)(2,1)S(1)}, u32[]{:S(2)}, u32[]{:S(2)}) collective-permute-start(bf16[2,15,1536]{2,1,0:T(8,128)(2,1)S(1)} %get-tuple-element.99), channel_id=1, source_target_pairs={{0,1},{1,2},{2,3},{4,5},{5,6},{6,7},{8,9},{9,10},{10,11},{12,13},{... | collective-permute-start | bytes 276488 | tf_op jit(solution)/shard_map/ppermute | solution.py:16
  14.2 6.5 %collective-permute-start.1 = (bf16[2,15,1536]{2,1,0:T(8,128)(2,1)S(1)}, bf16[2,15,1536]{2,1,0:T(8,128)(2,1)S(1)}, u32[]{:S(2)}, u32[]{:S(2)}) collective-permute-start(bf16[2,15,1536]{2,1,0:T(8,128)(2,1)S(1)} %get-tuple-element.100), channel_id=1, source_target_pairs={{1,0},{2,1},{3,2},{5,4},{6,5},{7,6},{9,8},{10,9},{11,10},{13,12},{... | collective-permute-start | bytes 276488 | tf_op jit(solution)/shard_map/ppermute | solution.py:17
  15.9 36.8 %copy-start.15 = (f32[1536]{0:T(1024)}, f32[1536]{0:T(1024)S(1)}, u32[]{:S(2)}) copy-start(f32[1536]{0:T(1024)S(1)} %get-tuple-element.46) | copy-start | bytes 18436
  25.4 1.2 collective-permute-start.2
  26.7 3.8 %collective-permute-start.3 = (f32[2,1536]{1,0:T(2,128)S(1)}, f32[2,1536]{1,0:T(2,128)S(1)}, u32[]{:S(2)}, u32[]{:S(2)}) collective-permute-start(f32[2,1536]{1,0:T(2,128)S(1)} %pad_maximum_fusion.7), channel_id=1, source_target_pairs={{0,8},{4,12},{8,0},{12,4},{16,24},{20,28},{24,16},{28,20},{1,9},{5... | collective-permute-start | bytes 36872 | tf_op jit(solution)/shard_map/ppermute | solution.py:44
  30.6 26.0 %collective-permute-start.4 = (f32[2,1536]{1,0:T(2,128)S(1)}, f32[2,1536]{1,0:T(2,128)S(1)}, u32[]{:S(2)}, u32[]{:S(2)}) collective-permute-start(f32[2,1536]{1,0:T(2,128)S(1)} %pad_maximum_fusion.8), channel_id=1, source_target_pairs={{0,16},{4,20},{8,24},{12,28},{16,0},{20,4},{24,8},{28,12},{1,17},{... | collective-permute-start | bytes 36872 | tf_op jit(solution)/shard_map/ppermute | solution.py:44
  53.0 25.0 %all-to-all-start = ((f32[4,128,384]{2,1,0:T(8,128)}), f32[4,128,384]{2,1,0:T(8,128)S(1)}, u32[]{:S(2)}, u32[]{:S(2)}) async-start(f32[4,128,384]{2,1,0:T(8,128)} %bitcast.20), calls=%async_computation | async-start | bytes 1572864 | tf_op jit(solution)/shard_map/all_to_all | solution.py:101
  56.5 96.2 %all-gather.6.cloned.1.call-start = ((), (), s32[]{:S(2)}) async-start(), calls=%async_computation.3 | async-start | bytes 2949120 | tf_op jit(solution)/shard_map/all_gather | solution.py:81
  56.6 13.1 %collective-permute-start.5 = (f32[2,1536]{1,0:T(2,128)S(1)}, f32[2,1536]{1,0:T(2,128)S(1)}, u32[]{:S(2)}, u32[]{:S(2)}) collective-permute-start(f32[2,1536]{1,0:T(2,128)S(1)} %pad_maximum_fusion.9), channel_id=1, source_target_pairs={{0,1},{1,0},{2,3},{3,2},{4,5},{5,4},{6,7},{7,6},{8,9},{9,8},{10,11... | collective-permute-start | bytes 36872 | tf_op jit(solution)/shard_map/ppermute | solution.py:44
  69.8 7.4 %collective-permute-start.6 = (f32[2,1536]{1,0:T(2,128)S(1)}, f32[2,1536]{1,0:T(2,128)S(1)}, u32[]{:S(2)}, u32[]{:S(2)}) collective-permute-start(f32[2,1536]{1,0:T(2,128)S(1)} %pad_maximum_fusion.10), channel_id=1, source_target_pairs={{0,2},{1,3},{2,0},{3,1},{4,6},{5,7},{6,4},{7,5},{8,10},{9,11},{10,... | collective-permute-start | bytes 36872 | tf_op jit(solution)/shard_map/ppermute | solution.py:44
  82.9 1.2 collective-permute-start.8
  84.2 3.8 %collective-permute-start.9 = (f32[2,1536]{1,0:T(2,128)S(1)}, f32[2,1536]{1,0:T(2,128)S(1)}, u32[]{:S(2)}, u32[]{:S(2)}) collective-permute-start(f32[2,1536]{1,0:T(2,128)S(1)} %fusion.139), channel_id=1, source_target_pairs={{0,8},{4,12},{8,0},{12,4},{16,24},{20,28},{24,16},{28,20},{1,9},{5... | collective-permute-start | bytes 36872 | tf_op jit(solution)/shard_map/ppermute | solution.py:34
  87.9 3.8 %collective-permute-start.10 = (f32[2,1536]{1,0:T(2,128)S(1)}, f32[2,1536]{1,0:T(2,128)S(1)}, u32[]{:S(2)}, u32[]{:S(2)}) collective-permute-start(f32[2,1536]{1,0:T(2,128)S(1)} %fusion.155), channel_id=1, source_target_pairs={{0,16},{4,20},{8,24},{12,28},{16,0},{20,4},{24,8},{28,12},{1,17},{... | collective-permute-start | bytes 36872 | tf_op jit(solution)/shard_map/ppermute | solution.py:34
  91.7 3.8 %collective-permute-start.11 = (f32[2,1536]{1,0:T(2,128)S(1)}, f32[2,1536]{1,0:T(2,128)S(1)}, u32[]{:S(2)}, u32[]{:S(2)}) collective-permute-start(f32[2,1536]{1,0:T(2,128)S(1)} %add.512), channel_id=1, source_target_pairs={{0,1},{1,0},{2,3},{3,2},{4,5},{5,4},{6,7},{7,6},{8,9},{9,8},{10,11... | collective-permute-start | bytes 36872 | tf_op jit(solution)/shard_map/ppermute | solution.py:34
  96.1 9.7 %collective-permute-start.12 = (f32[2,1536]{1,0:T(2,128)}, f32[2,1536]{1,0:T(2,128)}, u32[]{:S(2)}, u32[]{:S(2)}) collective-permute-start(f32[2,1536]{1,0:T(2,128)} %add.513), channel_id=1, source_target_pairs={{0,2},{1,3},{2,0},{3,1},{4,6},{5,7},{6,4},{7,5},{8,10},{9,11},{10,... | collective-permute-start | bytes 36872 | tf_op jit(solution)/shard_map/ppermute | solution.py:34
  101.4 23.4 %all-to-all-start.1 = ((bf16[128,4,384]{2,0,1:T(8,128)(2,1)}), bf16[128,4,384]{2,0,1:T(8,128)(2,1)}, u32[]{:S(2)}, u32[]{:S(2)}) async-start(bf16[128,4,384]{2,0,1:T(8,128)(2,1)} %copy.17), calls=%async_computation.1 | async-start | bytes 786432 | tf_op jit(solution)/shard_map/all_to_all | solution.py:127
  128.3 3.2 %collective-permute-start.15 = (f32[192,1536]{1,0:T(8,128)}, f32[192,1536]{1,0:T(8,128)}, u32[]{:S(2)}, u32[]{:S(2)}) collective-permute-start(f32[192,1536]{1,0:T(8,128)} %constant_dynamic-slice_fusion.2), channel_id=1, source_target_pairs={{0,4},{4,0},{8,12},{12,8},{16,20},{20,16},{24,28},{28,24},{1,5},{5... | collective-permute-start | bytes 3538952 | tf_op jit(solution)/shard_map/ppermute | solution.py:65
  135.0 20.3 %collective-permute-start.16 = (f32[96,1536]{1,0:T(8,128)S(1)}, f32[96,1536]{1,0:T(8,128)S(1)}, u32[]{:S(2)}, u32[]{:S(2)}) collective-permute-start(f32[96,1536]{1,0:T(8,128)S(1)} %constant_dynamic-slice_fusion.1), channel_id=1, source_target_pairs={{0,8},{4,12},{8,0},{12,4},{16,24},{20,28},{24,16},{28,20},{1,9},{5... | collective-permute-start | bytes 1769480 | tf_op jit(solution)/shard_map/ppermute | solution.py:65
  136.5 16.2 %collective-permute-start.21 = (f32[31,1536]{1,0:T(8,128)}, f32[31,1536]{1,0:T(8,128)S(1)}, u32[]{:S(2)}, u32[]{:S(2)}) collective-permute-start(f32[31,1536]{1,0:T(8,128)} %stack.172), channel_id=1, source_target_pairs={{0,4},{4,0},{8,12},{12,8},{16,20},{20,16},{24,28},{28,24},{1,5},{5... | collective-permute-start | bytes 571400 | tf_op jit(solution)/shard_map/ppermute | solution.py:34
  152.7 38.0 %collective-permute-start.7 = (bf16[4,192,1536]{2,1,0:T(8,128)(2,1)}, bf16[4,192,1536]{2,1,0:T(8,128)(2,1)S(1)}, u32[]{:S(2)}, u32[]{:S(2)}) collective-permute-start(bf16[4,192,1536]{2,1,0:T(8,128)(2,1)} %bitcast.18), channel_id=1, source_target_pairs={{0,4},{4,0},{8,12},{12,8},{16,20},{20,16},{24,28},{28,24},{1,5},{5... | collective-permute-start | bytes 7077896 | tf_op jit(solution)/shard_map/ppermute | solution.py:82
  153.7 10.5 %collective-permute-start.22 = (f32[31,1536]{1,0:T(8,128)S(1)}, f32[31,1536]{1,0:T(8,128)S(1)}, u32[]{:S(2)}, u32[]{:S(2)}) collective-permute-start(f32[31,1536]{1,0:T(8,128)S(1)} %add.553), channel_id=1, source_target_pairs={{0,8},{4,12},{8,0},{12,4},{16,24},{20,28},{24,16},{28,20},{1,9},{5... | collective-permute-start | bytes 571400 | tf_op jit(solution)/shard_map/ppermute | solution.py:34
  156.7 9.1 %collective-permute-start.17 = (f32[48,1536]{1,0:T(8,128)S(1)}, f32[48,1536]{1,0:T(8,128)S(1)}, u32[]{:S(2)}, u32[]{:S(2)}) collective-permute-start(f32[48,1536]{1,0:T(8,128)S(1)} %constant_dynamic-slice_fusion), channel_id=1, source_target_pairs={{0,16},{4,20},{8,24},{12,28},{16,0},{20,4},{24,8},{28,12},{1,17},{... | collective-permute-start | bytes 884744 | tf_op jit(solution)/shard_map/ppermute | solution.py:65
  158.3 9.7 %collective-permute-start.13 = (bf16[2,15,1536]{2,1,0:T(8,128)(2,1)S(1)}, bf16[2,15,1536]{2,1,0:T(8,128)(2,1)S(1)}, u32[]{:S(2)}, u32[]{:S(2)}) collective-permute-start(bf16[2,15,1536]{2,1,0:T(8,128)(2,1)S(1)} %get-tuple-element.97), channel_id=1, source_target_pairs={{1,0},{2,1},{3,2},{5,4},{6,5},{7,6},{9,8},{10,9},{11,10},{13,12},{... | collective-permute-start | bytes 276488 | tf_op jit(solution)/shard_map/ppermute | solution.py:17
  159.6 8.4 %collective-permute-start.14 = (bf16[2,15,1536]{2,1,0:T(8,128)(2,1)S(1)}, bf16[2,15,1536]{2,1,0:T(8,128)(2,1)S(1)}, u32[]{:S(2)}, u32[]{:S(2)}) collective-permute-start(bf16[2,15,1536]{2,1,0:T(8,128)(2,1)S(1)} %get-tuple-element.98), channel_id=1, source_target_pairs={{0,1},{1,2},{2,3},{4,5},{5,6},{6,7},{8,9},{9,10},{10,11},{12,13},{... | collective-permute-start | bytes 276488 | tf_op jit(solution)/shard_map/ppermute | solution.py:16
  164.2 8.2 %collective-permute-start.23 = (f32[31,1536]{1,0:T(8,128)S(1)}, f32[31,1536]{1,0:T(8,128)S(1)}, u32[]{:S(2)}, u32[]{:S(2)}) collective-permute-start(f32[31,1536]{1,0:T(8,128)S(1)} %add.554), channel_id=1, source_target_pairs={{0,16},{4,20},{8,24},{12,28},{16,0},{20,4},{24,8},{28,12},{1,17},{... | collective-permute-start | bytes 571400 | tf_op jit(solution)/shard_map/ppermute | solution.py:34
  165.9 10.8 %collective-permute-start.18 = (f32[48,1536]{1,0:T(8,128)S(1)}, f32[48,1536]{1,0:T(8,128)S(1)}, u32[]{:S(2)}, u32[]{:S(2)}) collective-permute-start(f32[48,1536]{1,0:T(8,128)S(1)} %dynamic-slice_add_fusion.2), channel_id=1, source_target_pairs={{0,16},{4,20},{8,24},{12,28},{16,0},{20,4},{24,8},{28,12},{1,17},{... | collective-permute-start | bytes 884744 | tf_op jit(solution)/shard_map/ppermute | solution.py:69
  172.4 5.7 %collective-permute-start.24 = (f32[31,1536]{1,0:T(8,128)S(1)}, f32[31,1536]{1,0:T(8,128)S(1)}, u32[]{:S(2)}, u32[]{:S(2)}) collective-permute-start(f32[31,1536]{1,0:T(8,128)S(1)} %add.555), channel_id=1, source_target_pairs={{0,1},{1,0},{2,3},{3,2},{4,5},{5,4},{6,7},{7,6},{8,9},{9,8},{10,11... | collective-permute-start | bytes 571400 | tf_op jit(solution)/shard_map/ppermute | solution.py:34
  176.8 13.7 %collective-permute-start.19 = (f32[96,1536]{1,0:T(8,128)S(1)}, f32[96,1536]{1,0:T(8,128)S(1)}, u32[]{:S(2)}, u32[]{:S(2)}) collective-permute-start(f32[96,1536]{1,0:T(8,128)S(1)} %maximum_select_fusion.2), channel_id=1, source_target_pairs={{0,8},{4,12},{8,0},{12,4},{16,24},{20,28},{24,16},{28,20},{1,9},{5... | collective-permute-start | bytes 1769480 | tf_op jit(solution)/shard_map/ppermute | solution.py:69
  178.2 9.6 %collective-permute-start.25 = (f32[31,1536]{1,0:T(8,128)S(1)}, f32[31,1536]{1,0:T(8,128)S(1)}, u32[]{:S(2)}, u32[]{:S(2)}) collective-permute-start(f32[31,1536]{1,0:T(8,128)S(1)} %add.556), channel_id=1, source_target_pairs={{0,2},{1,3},{2,0},{3,1},{4,6},{5,7},{6,4},{7,5},{8,10},{9,11},{10,... | collective-permute-start | bytes 571400 | tf_op jit(solution)/shard_map/ppermute | solution.py:34
  190.6 3.0 %collective-permute-start.20 = (f32[192,1536]{1,0:T(8,128)S(1)}, f32[192,1536]{1,0:T(8,128)S(1)}, u32[]{:S(2)}, u32[]{:S(2)}) collective-permute-start(f32[192,1536]{1,0:T(8,128)S(1)} %maximum_select_fusion.1), channel_id=1, source_target_pairs={{0,4},{4,0},{8,12},{12,8},{16,20},{20,16},{24,28},{28,24},{1,5},{5... | collective-permute-start | bytes 3538952 | tf_op jit(solution)/shard_map/ppermute | solution.py:69
  (72 other events, 1470.9 us)
Sparse Core Ops, SparseCore 0:
  9.6 39.7 all-gather.3
  98.9 53.7 all-gather.5

commit v6 on v5

--- a/solution.py
+++ b/solution.py
@@ -149,13 +149,13 @@
             for offset in range(taps)
         ]
     )
-    local_grad, kernel_terms = lax.optimization_barrier((local_grad, kernel_terms))
+    full_weight = gather_weight(proj_weight)
+    full_weight, local_grad, kernel_terms = lax.optimization_barrier((full_weight, local_grad, kernel_terms))
     weight_grad = rows_sum(local_grad, "dp")
     kernel_grad = all_sum(kernel_terms, ("dp", "tensor"))
     input_grad = jnp.concatenate(
         [grad_gated * gates, grad_gated * values * gates * (1.0 - gates)], axis=-1
     ).astype(jnp.bfloat16)
-    full_weight = gather_weight(proj_weight)
     conv_output = jnp.einsum(
         "btc,cd->btd", activated, full_weight, preferred_element_type=jnp.float32
     ).astype(jnp.bfloat16)

time: 203 us -> 239 us (1.18)
  waiting for transfers between devices: 92.3 us -> 121 us
  other arithmetic: 28.4 us -> 34.7 us
    ppermute x5, waiting for transfers between devices: 17.3 us -> 38.3 us  [all_moments(): lax.ppermute(jnp.stack([mean, spread]), axis, [(i, i ^ step) for i in ran...]
    ppermute x3, waiting for transfers between devices: 4.24 us -> 24 us  [rows_sum(): x = keep + lax.ppermute(give, axis, [(i, i ^ step) for i in range(peers)])]
    all_gather x1, waiting for transfers between devices: 16.2 us -> 7.41 us  [gather_weight(): held = lax.all_gather(mine, 'tensor', axis=0, tiled=False)]
    all_to_all x1, waiting for transfers between devices: 8.66 us -> 0.4 us  [on_device(): lax.all_to_all(flat_act, 'tensor', split_axis=1, concat_axis=0, tiled=True)]
    ppermute x3, waiting for transfers between devices: 5.46 us -> 8.53 us  [rows_sum(): other = lax.ppermute(x, axis, [(i, i ^ step) for i in range(peers)])]
    ppermute x10, waiting for transfers between devices: 18.1 us -> 20.6 us  [all_sum(): x = x + lax.ppermute(x, axis, [(i, i ^ step) for i in range(peers)])]
  transfers between devices with their start and end apart: 30 -> 30, of which waited for: 19 -> 18; matrix products, arithmetic and copies ran while one was open for 20% -> 17% of each run, Pallas kernels for 0% -> 0%
where the time goes in v6:
time: 239 us; the launch traced here: 238 us
  waiting for transfers between devices  121 us (51%)
  starting transfers between devices  45.5 us (19%)
  other arithmetic  34.7 us (15%)
  between operations  15.8 us (7%)
  local copies, waits for them, and re-layouts  13.8 us (6%)
  matrix products  7.3 us (3%)
    ppermute x5, waiting for transfers between devices, all_moments(): lax.ppermute(jnp.stack([mean, spread]), axis, [(i, i ^ step) for i in ran...  38.3 us
    ppermute x3, waiting for transfers between devices, rows_sum(): x = keep + lax.ppermute(give, axis, [(i, i ^ step) for i in range(peers)])  24 us
    ppermute x10, waiting for transfers between devices, all_sum(): x = x + lax.ppermute(x, axis, [(i, i ^ step) for i in range(peers)])  20.6 us
    all_gather x1, waiting for transfers between devices, on_device(): group_grad = lax.all_gather(flat_grad, 'tensor', axis=0, tiled=True)  17.6 us
    ppermute x5, starting transfers between devices, all_moments(): lax.ppermute(jnp.stack([mean, spread]), axis, [(i, i ^ step) for i in ran...  10.4 us
    ppermute x10, starting transfers between devices, all_sum(): x = x + lax.ppermute(x, axis, [(i, i ^ step) for i in range(peers)])  9.66 us
    ppermute x2, starting transfers between devices, extended(): before = lax.ppermute(last, axis, up)  9.48 us
    ppermute x3, waiting for transfers between devices, rows_sum(): other = lax.ppermute(x, axis, [(i, i ^ step) for i in range(peers)])  8.53 us
  transfers between devices with their start and end apart: 30, of which 18 were waited for; matrix products, arithmetic and copies ran while one was open for 17% of the time, Pallas kernels for 0%

profile of v6, /device:TPU:0, one launch (start us, length us, event | category | flops | bytes accessed | tf_op | source)
XLA Modules:
  0.0 238.1 jit_solution(8112021862599145379)
XLA Ops:
  9.4 4.9 %collective-permute-start = (bf16[2,15,1536]{2,1,0:T(8,128)(2,1)S(1)}, bf16[2,15,1536]{2,1,0:T(8,128)(2,1)S(1)}, u32[]{:S(2)}, u32[]{:S(2)}) collective-permute-start(bf16[2,15,1536]{2,1,0:T(8,128)(2,1)S(1)} %get-tuple-element.101), channel_id=1, source_target_pairs={{0,1},{1,2},{2,3},{4,5},{5,6},{6,7},{8,9},{9,10},{10,11},{12,13},{... | collective-permute-start | bytes 276488 | tf_op jit(solution)/shard_map/ppermute | solution.py:16
  17.4 3.4 %collective-permute-done.1 = bf16[2,15,1536]{2,1,0:T(8,128)(2,1)S(1)} collective-permute-done((bf16[2,15,1536]{2,1,0:T(8,128)(2,1)S(1)}, bf16[2,15,1536]{2,1,0:T(8,128)(2,1)S(1)}, u32[]{:S(2)}, u32[]{:S(2)}) %collective-permute-start.1) | collective-permute-done | bytes 92192 | tf_op jit(solution)/shard_map/ppermute | solution.py:17
  20.8 3.8 %fusion.148 = (f32[1536]{0:T(1024)S(1)}, f32[2,64,1536]{2,1,0:T(8,128)S(1)}) fusion(bf16[2,15,1536]{2,1,0:T(8,128)(2,1)S(1)} %collective-permute-done.1, bf16[2,64,1536]{2,1,0:T(8,128)(2,1)S(1)} %fusion.5, f32[1536]{0:T(1024)S(1)} %get-tuple-element.74, f32[1536]{0:T(1024)S(1)} %get-tuple-element.75, f32[1536]{0:T(1024)S(1)} %get-tuple-element.46, ...), kind=kLoop, calls=%fused_computation.382 | loop fusion | flops 35977728 | bytes 1560576 | tf_op jit(solution)/shard_map/reduce_sum | solution.py:110
  27.8 2.2 collective-permute-done.3
  31.9 17.6 %all-gather.4.cloned.1.call-done = bf16[512,1536]{1,0:T(8,128)(2,1)} async-done(((bf16[128,1536]{1,0:T(8,128)(2,1)}), bf16[512,1536]{1,0:T(8,128)(2,1)}) %all-gather.4.cloned.1.call-update) | async-done | bytes 1572880 | tf_op jit(solution)/shard_map/all_gather | solution.py:99
  49.4 3.3 %fusion.153 = f32[512,384]{1,0:T(8,128)} fusion(bf16[512,1536]{1,0:T(8,128)(2,1)} %all-gather.4.cloned.1.call-done, bf16[384,1536]{1,0:T(8,128)(2,1)S(1)} %copy-done), kind=kOutput, calls=%fused_computation.386 | convolution fusion | flops 603979776 | bytes 3538944 | tf_op jit(solution)/shard_map/fd,cd->fc/dot_general | solution.py:100
  52.7 3.6 %all-to-all-start.1 = ((f32[4,128,384]{2,1,0:T(8,128)}), f32[4,128,384]{2,1,0:T(8,128)S(1)}, u32[]{:S(2)}, u32[]{:S(2)}) async-start(f32[4,128,384]{2,1,0:T(8,128)} %bitcast.24), calls=%async_computation.1 | async-start | bytes 1572864 | tf_op jit(solution)/shard_map/all_to_all | solution.py:101
  56.4 2.0 collective-permute-start.5
  58.5 22.8 %collective-permute-done.5 = f32[2,1536]{1,0:T(2,128)S(1)} collective-permute-done((f32[2,1536]{1,0:T(2,128)S(1)}, f32[2,1536]{1,0:T(2,128)S(1)}, u32[]{:S(2)}, u32[]{:S(2)}) %collective-permute-start.5) | collective-permute-done | bytes 12320 | tf_op jit(solution)/shard_map/ppermute | solution.py:44
  81.3 5.1 %collective-permute-start.6 = (f32[2,1536]{1,0:T(2,128)S(1)}, f32[2,1536]{1,0:T(2,128)S(1)}, u32[]{:S(2)}, u32[]{:S(2)}) collective-permute-start(f32[2,1536]{1,0:T(2,128)S(1)} %pad_maximum_fusion.10), channel_id=1, source_target_pairs={{0,2},{1,3},{2,0},{3,1},{4,6},{5,7},{6,4},{7,5},{8,10},{9,11},{10,... | collective-permute-start | bytes 36872 | tf_op jit(solution)/shard_map/ppermute | solution.py:44
  86.5 12.1 %collective-permute-done.6 = f32[2,1536]{1,0:T(2,128)S(1)} collective-permute-done((f32[2,1536]{1,0:T(2,128)S(1)}, f32[2,1536]{1,0:T(2,128)S(1)}, u32[]{:S(2)}, u32[]{:S(2)}) %collective-permute-start.6) | collective-permute-done | bytes 12320 | tf_op jit(solution)/shard_map/ppermute | solution.py:44
  102.1 2.0 fusion.145
  108.2 7.4 %all-gather.6.cloned.1.call-done = bf16[768,1536]{1,0:T(8,128)(2,1)} async-done(((bf16[192,1536]{1,0:T(8,128)(2,1)}), bf16[768,1536]{1,0:T(8,128)(2,1)}) %all-gather.6.cloned.1.call-update) | async-done | bytes 2359312 | tf_op jit(solution)/shard_map/all_gather | solution.py:81
  117.9 2.2 collective-permute-done.10
  120.2 3.7 %collective-permute-done.11 = f32[2,1536]{1,0:T(2,128)S(1)} collective-permute-done((f32[2,1536]{1,0:T(2,128)S(1)}, f32[2,1536]{1,0:T(2,128)S(1)}, u32[]{:S(2)}, u32[]{:S(2)}) %collective-permute-start.11) | collective-permute-done | bytes 12320 | tf_op jit(solution)/shard_map/ppermute | solution.py:34
  125.4 1.8 copy.16
  127.2 4.3 %all-to-all-start = ((bf16[128,4,384]{2,0,1:T(8,128)(2,1)}), bf16[128,4,384]{2,0,1:T(8,128)(2,1)}, u32[]{:S(2)}, u32[]{:S(2)}) async-start(bf16[128,4,384]{2,0,1:T(8,128)(2,1)} %copy.16), calls=%async_computation | async-start | bytes 786432 | tf_op jit(solution)/shard_map/all_to_all | solution.py:127
  132.4 2.9 %fusion.69 = (f32[1536]{0:T(1024)S(1)}, f32[1536]{0:T(1024)S(1)}, f32[1536]{0:T(1024)S(1)}, f32[1536]{0:T(1024)S(1)}, f32[1536]{0:T(1024)S(1)}, /*index=5*/f32[1...) fusion(bf16[2,15,1536]{2,1,0:T(8,128)(2,1)} %copy-done.8, ...), kind=kLoop, calls=%fused_computation.194 | loop fusion | flops 12372480 | bytes 2537472 | tf_op jit(solution)/shard_map/reduce_sum | solution.py:146
  138.7 2.8 %stack.172 = f32[31,1536]{1,0:T(8,128)} concatenate(f32[1,1536]{1,0:T(1,128)S(1)} %stack.141, f32[1,1536]{1,0:T(1,128)S(1)} %stack.142, f32[1,1536]{1,0:T(1,128)S(1)} %stack.143, f32[1,1536]{1,0:T(1,128)S(1)} %stack.144, f32[1,1536]{1,0:T(1,128)S(1)} %stack.145, f32[1,1536]{1,0:T(1,128)S(1)} %stack.146, f32[1,1536]{1,0:T(1,128)S(1)} %stack.147, f32[1,1536]{1,0:T(1,128)S(1)} %stack.148, ...), dimensions={0} | concatenate | bytes 380928 | tf_op jit(solution)/shard_map/stack | solution.py:144
  141.8 2.5 %fusion.152 = f32[384,1536]{1,0:T(8,128)S(1)} fusion(bf16[512,384]{1,0:T(8,128)(2,1)} %bitcast.3, bf16[512,1536]{1,0:T(8,128)(2,1)} %all-gather.4.cloned.1.call-done), kind=kOutput, calls=%fused_computation.385 | convolution fusion | flops 603979776 | bytes 4325376 | tf_op jit(solution)/shard_map/fc,fd->cd/dot_general | solution.py:128
  144.3 2.0 broadcast_select_fusion.1
  146.3 2.4 %pad_maximum_fusion = bf16[4,384,1536]{2,1,0:T(8,128)(2,1)} fusion(bf16[4,192,1536]{2,1,0:T(8,128)(2,1)S(1)} %get-tuple-element.97, bf16[4,192,1536]{2,1,0:T(8,128)(2,1)S(1)} %get-tuple-element.96), kind=kLoop, calls=%fused_computation.32 | loop fusion | flops 9437184 | bytes 9437184 | tf_op jit(solution)/shard_map/concatenate | solution.py:85
  149.8 3.2 %collective-permute-done.15 = f32[192,1536]{1,0:T(8,128)} collective-permute-done((f32[192,1536]{1,0:T(8,128)}, f32[192,1536]{1,0:T(8,128)}, u32[]{:S(2)}, u32[]{:S(2)}) %collective-permute-start.15) | collective-permute-done | bytes 1179680 | tf_op jit(solution)/shard_map/ppermute | solution.py:65
  153.0 2.4 %dynamic-slice_add_fusion = f32[192,1536]{1,0:T(8,128)} fusion(f32[192,1536]{1,0:T(8,128)} %collective-permute-done.15, f32[384,1536]{1,0:T(8,128)S(1)} %fusion.152, s32[]{:T(128)S(6)} %select_n.65), kind=kLoop, calls=%fused_computation.96 | loop fusion | flops 294912 | bytes 3538948 | tf_op jit(solution)/shard_map/add | solution.py:65
  158.1 14.0 %collective-permute-done.16 = f32[96,1536]{1,0:T(8,128)} collective-permute-done((f32[96,1536]{1,0:T(8,128)S(1)}, f32[96,1536]{1,0:T(8,128)}, u32[]{:S(2)}, u32[]{:S(2)}) %collective-permute-start.16) | collective-permute-done | bytes 589856 | tf_op jit(solution)/shard_map/ppermute | solution.py:65
  176.1 6.8 %collective-permute-done.17 = f32[48,1536]{1,0:T(8,128)} collective-permute-done((f32[48,1536]{1,0:T(8,128)}, f32[48,1536]{1,0:T(8,128)}, u32[]{:S(2)}, u32[]{:S(2)}) %collective-permute-start.17) | collective-permute-done | bytes 294944 | tf_op jit(solution)/shard_map/ppermute | solution.py:65
  186.8 4.6 %collective-permute-start.14 = (bf16[2,15,1536]{2,1,0:T(8,128)(2,1)S(1)}, bf16[2,15,1536]{2,1,0:T(8,128)(2,1)S(1)}, u32[]{:S(2)}, u32[]{:S(2)}) collective-permute-start(bf16[2,15,1536]{2,1,0:T(8,128)(2,1)S(1)} %get-tuple-element.100), channel_id=1, source_target_pairs={{0,1},{1,2},{2,3},{4,5},{5,6},{6,7},{8,9},{9,10},{10,11},{12,13},{... | collective-permute-start | bytes 276488 | tf_op jit(solution)/shard_map/ppermute | solution.py:16
  194.8 4.1 %multiply_convert_fusion = (bf16[2,64,1536]{2,1,0:T(8,128)(2,1)S(1)}, f32[2,64,1536]{2,1,0:T(8,128)S(1)}) fusion(bf16[2,64,3072]{2,1,0:T(8,128)(2,1)S(1)} %copy-done.3, bf16[2,64,1536]{2,1,0:T(8,128)(2,1)S(1)} %copy-done.2, bf16[2,15,1536]{2,1,0:T(8,128)(2,1)S(1)} %collective-permute-done.14, f32[1536]{0:T(1024)S(1)} %copy-done.76, f32[1536]{0:T(1024)S(1)} %copy-done.78, ...), kind=kLoop, calls=%fused_computation.212 | loop fusion | flops 36962304 | bytes 2340864 | tf_op jit(solution)/shard_map/convert
  200.8 8.5 %collective-permute-done.19 = f32[96,1536]{1,0:T(8,128)S(1)} collective-permute-done((f32[96,1536]{1,0:T(8,128)S(1)}, f32[96,1536]{1,0:T(8,128)S(1)}, u32[]{:S(2)}, u32[]{:S(2)}) %collective-permute-start.19) | collective-permute-done | bytes 589856 | tf_op jit(solution)/shard_map/ppermute | solution.py:69
  212.5 4.7 %collective-permute-done.24 = f32[31,1536]{1,0:T(8,128)S(1)} collective-permute-done((f32[31,1536]{1,0:T(8,128)S(1)}, f32[31,1536]{1,0:T(8,128)S(1)}, u32[]{:S(2)}, u32[]{:S(2)}) %collective-permute-start.24) | collective-permute-done | bytes 190496 | tf_op jit(solution)/shard_map/ppermute | solution.py:34
  217.3 2.6 %collective-permute-start.25 = (f32[31,1536]{1,0:T(8,128)S(1)}, f32[31,1536]{1,0:T(8,128)S(1)}, u32[]{:S(2)}, u32[]{:S(2)}) collective-permute-start(f32[31,1536]{1,0:T(8,128)S(1)} %add.556), channel_id=1, source_target_pairs={{0,2},{1,3},{2,0},{3,1},{4,6},{5,7},{6,4},{7,5},{8,10},{9,11},{10,... | collective-permute-start | bytes 571400 | tf_op jit(solution)/shard_map/ppermute | solution.py:34
  221.4 7.6 %collective-permute-done.25 = f32[31,1536]{1,0:T(8,128)S(1)} collective-permute-done((f32[31,1536]{1,0:T(8,128)S(1)}, f32[31,1536]{1,0:T(8,128)S(1)}, u32[]{:S(2)}, u32[]{:S(2)}) %collective-permute-start.25) | collective-permute-done | bytes 190496 | tf_op jit(solution)/shard_map/ppermute | solution.py:34
  (296 shorter events, 48.9 us)
Async XLA Ops:
  7.2 42.2 %all-gather.4.cloned.1.call-start = ((), (), s32[]{:S(2)}) async-start(), calls=%async_computation.2 | async-start | bytes 1966080 | tf_op jit(solution)/shard_map/all_gather | solution.py:99
  7.9 107.6 %all-gather.6.cloned.1.call-start = ((), (), s32[]{:S(2)}) async-start(), calls=%async_computation.3 | async-start | bytes 2949120 | tf_op jit(solution)/shard_map/all_gather | solution.py:81
  9.4 8.0 %collective-permute-start = (bf16[2,15,1536]{2,1,0:T(8,128)(2,1)S(1)}, bf16[2,15,1536]{2,1,0:T(8,128)(2,1)S(1)}, u32[]{:S(2)}, u32[]{:S(2)}) collective-permute-start(bf16[2,15,1536]{2,1,0:T(8,128)(2,1)S(1)} %get-tuple-element.101), channel_id=1, source_target_pairs={{0,1},{1,2},{2,3},{4,5},{5,6},{6,7},{8,9},{9,10},{10,11},{12,13},{... | collective-permute-start | bytes 276488 | tf_op jit(solution)/shard_map/ppermute | solution.py:16
  14.3 6.5 %collective-permute-start.1 = (bf16[2,15,1536]{2,1,0:T(8,128)(2,1)S(1)}, bf16[2,15,1536]{2,1,0:T(8,128)(2,1)S(1)}, u32[]{:S(2)}, u32[]{:S(2)}) collective-permute-start(bf16[2,15,1536]{2,1,0:T(8,128)(2,1)S(1)} %get-tuple-element.102), channel_id=1, source_target_pairs={{1,0},{2,1},{3,2},{5,4},{6,5},{7,6},{9,8},{10,9},{11,10},{13,12},{... | collective-permute-start | bytes 276488 | tf_op jit(solution)/shard_map/ppermute | solution.py:17
  24.8 1.2 collective-permute-start.2
  26.2 3.8 %collective-permute-start.3 = (f32[2,1536]{1,0:T(2,128)S(1)}, f32[2,1536]{1,0:T(2,128)S(1)}, u32[]{:S(2)}, u32[]{:S(2)}) collective-permute-start(f32[2,1536]{1,0:T(2,128)S(1)} %pad_maximum_fusion.7), channel_id=1, source_target_pairs={{0,8},{4,12},{8,0},{12,4},{16,24},{20,28},{24,16},{28,20},{1,9},{5... | collective-permute-start | bytes 36872 | tf_op jit(solution)/shard_map/ppermute | solution.py:44
  30.3 26.1 %collective-permute-start.4 = (f32[2,1536]{1,0:T(2,128)S(1)}, f32[2,1536]{1,0:T(2,128)S(1)}, u32[]{:S(2)}, u32[]{:S(2)}) collective-permute-start(f32[2,1536]{1,0:T(2,128)S(1)} %pad_maximum_fusion.8), channel_id=1, source_target_pairs={{0,16},{4,20},{8,24},{12,28},{16,0},{20,4},{24,8},{28,12},{1,17},{... | collective-permute-start | bytes 36872 | tf_op jit(solution)/shard_map/ppermute | solution.py:44
  52.7 45.9 %copy-start.80 = (f32[1536]{0:T(1024)S(1)}, f32[1536]{0:T(1024)}, u32[]{:S(2)}) copy-start(f32[1536]{0:T(1024)} %param.8) | copy-start | bytes 18436
  52.7 46.6 %all-to-all-start.1 = ((f32[4,128,384]{2,1,0:T(8,128)}), f32[4,128,384]{2,1,0:T(8,128)S(1)}, u32[]{:S(2)}, u32[]{:S(2)}) async-start(f32[4,128,384]{2,1,0:T(8,128)} %bitcast.24), calls=%async_computation.1 | async-start | bytes 1572864 | tf_op jit(solution)/shard_map/all_to_all | solution.py:101
  56.4 24.8 %collective-permute-start.5 = (f32[2,1536]{1,0:T(2,128)S(1)}, f32[2,1536]{1,0:T(2,128)S(1)}, u32[]{:S(2)}, u32[]{:S(2)}) collective-permute-start(f32[2,1536]{1,0:T(2,128)S(1)} %pad_maximum_fusion.9), channel_id=1, source_target_pairs={{0,1},{1,0},{2,3},{3,2},{4,5},{5,4},{6,7},{7,6},{8,9},{9,8},{10,11... | collective-permute-start | bytes 36872 | tf_op jit(solution)/shard_map/ppermute | solution.py:44
  81.3 17.3 %collective-permute-start.6 = (f32[2,1536]{1,0:T(2,128)S(1)}, f32[2,1536]{1,0:T(2,128)S(1)}, u32[]{:S(2)}, u32[]{:S(2)}) collective-permute-start(f32[2,1536]{1,0:T(2,128)S(1)} %pad_maximum_fusion.10), channel_id=1, source_target_pairs={{0,2},{1,3},{2,0},{3,1},{4,6},{5,7},{6,4},{7,5},{8,10},{9,11},{10,... | collective-permute-start | bytes 36872 | tf_op jit(solution)/shard_map/ppermute | solution.py:44
  104.2 1.2 collective-permute-start.8
  106.7 8.9 %collective-permute-start.9 = (f32[2,1536]{1,0:T(2,128)}, f32[2,1536]{1,0:T(2,128)}, u32[]{:S(2)}, u32[]{:S(2)}) collective-permute-start(f32[2,1536]{1,0:T(2,128)} %fusion.144), channel_id=1, source_target_pairs={{0,8},{4,12},{8,0},{12,4},{16,24},{20,28},{24,16},{28,20},{1,9},{5... | collective-permute-start | bytes 36872 | tf_op jit(solution)/shard_map/ppermute | solution.py:34
  115.6 28.7 %collective-permute-start.7 = (bf16[4,192,1536]{2,1,0:T(8,128)(2,1)}, bf16[4,192,1536]{2,1,0:T(8,128)(2,1)}, u32[]{:S(2)}, u32[]{:S(2)}) collective-permute-start(bf16[4,192,1536]{2,1,0:T(8,128)(2,1)} %bitcast.22), channel_id=1, source_target_pairs={{0,4},{4,0},{8,12},{12,8},{16,20},{20,16},{24,28},{28,24},{1,5},{5... | collective-permute-start | bytes 7077896 | tf_op jit(solution)/shard_map/ppermute | solution.py:82
  116.4 3.8 %collective-permute-start.10 = (f32[2,1536]{1,0:T(2,128)S(1)}, f32[2,1536]{1,0:T(2,128)S(1)}, u32[]{:S(2)}, u32[]{:S(2)}) collective-permute-start(f32[2,1536]{1,0:T(2,128)S(1)} %fusion.159), channel_id=1, source_target_pairs={{0,16},{4,20},{8,24},{12,28},{16,0},{20,4},{24,8},{28,12},{1,17},{... | collective-permute-start | bytes 36872 | tf_op jit(solution)/shard_map/ppermute | solution.py:34
  120.1 3.8 %collective-permute-start.11 = (f32[2,1536]{1,0:T(2,128)S(1)}, f32[2,1536]{1,0:T(2,128)S(1)}, u32[]{:S(2)}, u32[]{:S(2)}) collective-permute-start(f32[2,1536]{1,0:T(2,128)S(1)} %add.512), channel_id=1, source_target_pairs={{0,1},{1,0},{2,3},{3,2},{4,5},{5,4},{6,7},{7,6},{8,9},{9,8},{10,11... | collective-permute-start | bytes 36872 | tf_op jit(solution)/shard_map/ppermute | solution.py:34
  124.5 7.0 %collective-permute-start.12 = (f32[2,1536]{1,0:T(2,128)}, f32[2,1536]{1,0:T(2,128)}, u32[]{:S(2)}, u32[]{:S(2)}) collective-permute-start(f32[2,1536]{1,0:T(2,128)} %add.513), channel_id=1, source_target_pairs={{0,2},{1,3},{2,0},{3,1},{4,6},{5,7},{6,4},{7,5},{8,10},{9,11},{10,... | collective-permute-start | bytes 36872 | tf_op jit(solution)/shard_map/ppermute | solution.py:34
  127.2 14.6 %all-to-all-start = ((bf16[128,4,384]{2,0,1:T(8,128)(2,1)}), bf16[128,4,384]{2,0,1:T(8,128)(2,1)}, u32[]{:S(2)}, u32[]{:S(2)}) async-start(bf16[128,4,384]{2,0,1:T(8,128)(2,1)} %copy.16), calls=%async_computation | async-start | bytes 786432 | tf_op jit(solution)/shard_map/all_to_all | solution.py:127
  149.8 3.2 %collective-permute-start.15 = (f32[192,1536]{1,0:T(8,128)}, f32[192,1536]{1,0:T(8,128)}, u32[]{:S(2)}, u32[]{:S(2)}) collective-permute-start(f32[192,1536]{1,0:T(8,128)} %constant_dynamic-slice_fusion.2), channel_id=1, source_target_pairs={{0,4},{4,0},{8,12},{12,8},{16,20},{20,16},{24,28},{28,24},{1,5},{5... | collective-permute-start | bytes 3538952 | tf_op jit(solution)/shard_map/ppermute | solution.py:65
  156.5 15.5 %collective-permute-start.16 = (f32[96,1536]{1,0:T(8,128)S(1)}, f32[96,1536]{1,0:T(8,128)}, u32[]{:S(2)}, u32[]{:S(2)}) collective-permute-start(f32[96,1536]{1,0:T(8,128)S(1)} %constant_dynamic-slice_fusion.1), channel_id=1, source_target_pairs={{0,8},{4,12},{8,0},{12,4},{16,24},{20,28},{24,16},{28,20},{1,9},{5... | collective-permute-start | bytes 1769480 | tf_op jit(solution)/shard_map/ppermute | solution.py:65
  172.1 47.7 %slice-start = ((s8[4718592]{0:T(1024)(128)(4,1)}), s8[524288]{0:T(1024)(128)(4,1)S(1)}, s32[]{:S(2)}) async-start(s8[4718592]{0:T(1024)(128)(4,1)} %bitcast.18), calls=%async_computation.4 | async-start | bytes 1048576
  174.3 8.6 %collective-permute-start.17 = (f32[48,1536]{1,0:T(8,128)}, f32[48,1536]{1,0:T(8,128)}, u32[]{:S(2)}, u32[]{:S(2)}) collective-permute-start(f32[48,1536]{1,0:T(8,128)} %constant_dynamic-slice_fusion), channel_id=1, source_target_pairs={{0,16},{4,20},{8,24},{12,28},{16,0},{20,4},{24,8},{28,12},{1,17},{... | collective-permute-start | bytes 884744 | tf_op jit(solution)/shard_map/ppermute | solution.py:65
  176.0 15.3 %collective-permute-start.21 = (f32[31,1536]{1,0:T(8,128)}, f32[31,1536]{1,0:T(8,128)S(1)}, u32[]{:S(2)}, u32[]{:S(2)}) collective-permute-start(f32[31,1536]{1,0:T(8,128)} %stack.172), channel_id=1, source_target_pairs={{0,4},{4,0},{8,12},{12,8},{16,20},{20,16},{24,28},{28,24},{1,5},{5... | collective-permute-start | bytes 571400 | tf_op jit(solution)/shard_map/ppermute | solution.py:34
  183.9 9.9 %collective-permute-start.18 = (f32[48,1536]{1,0:T(8,128)S(1)}, f32[48,1536]{1,0:T(8,128)S(1)}, u32[]{:S(2)}, u32[]{:S(2)}) collective-permute-start(f32[48,1536]{1,0:T(8,128)S(1)} %dynamic-slice_add_fusion.2), channel_id=1, source_target_pairs={{0,16},{4,20},{8,24},{12,28},{16,0},{20,4},{24,8},{28,12},{1,17},{... | collective-permute-start | bytes 884744 | tf_op jit(solution)/shard_map/ppermute | solution.py:69
  185.5 9.1 %collective-permute-start.13 = (bf16[2,15,1536]{2,1,0:T(8,128)(2,1)S(1)}, bf16[2,15,1536]{2,1,0:T(8,128)(2,1)S(1)}, u32[]{:S(2)}, u32[]{:S(2)}) collective-permute-start(bf16[2,15,1536]{2,1,0:T(8,128)(2,1)S(1)} %get-tuple-element.99), channel_id=1, source_target_pairs={{1,0},{2,1},{3,2},{5,4},{6,5},{7,6},{9,8},{10,9},{11,10},{13,12},{... | collective-permute-start | bytes 276488 | tf_op jit(solution)/shard_map/ppermute | solution.py:17
  186.8 7.8 %collective-permute-start.14 = (bf16[2,15,1536]{2,1,0:T(8,128)(2,1)S(1)}, bf16[2,15,1536]{2,1,0:T(8,128)(2,1)S(1)}, u32[]{:S(2)}, u32[]{:S(2)}) collective-permute-start(bf16[2,15,1536]{2,1,0:T(8,128)(2,1)S(1)} %get-tuple-element.100), channel_id=1, source_target_pairs={{0,1},{1,2},{2,3},{4,5},{5,6},{6,7},{8,9},{9,10},{10,11},{12,13},{... | collective-permute-start | bytes 276488 | tf_op jit(solution)/shard_map/ppermute | solution.py:16
  192.3 7.9 %collective-permute-start.22 = (f32[31,1536]{1,0:T(8,128)S(1)}, f32[31,1536]{1,0:T(8,128)S(1)}, u32[]{:S(2)}, u32[]{:S(2)}) collective-permute-start(f32[31,1536]{1,0:T(8,128)S(1)} %add.553), channel_id=1, source_target_pairs={{0,8},{4,12},{8,0},{12,4},{16,24},{20,28},{24,16},{28,20},{1,9},{5... | collective-permute-start | bytes 571400 | tf_op jit(solution)/shard_map/ppermute | solution.py:34
  193.9 15.5 %collective-permute-start.19 = (f32[96,1536]{1,0:T(8,128)S(1)}, f32[96,1536]{1,0:T(8,128)S(1)}, u32[]{:S(2)}, u32[]{:S(2)}) collective-permute-start(f32[96,1536]{1,0:T(8,128)S(1)} %maximum_select_fusion.2), channel_id=1, source_target_pairs={{0,8},{4,12},{8,0},{12,4},{16,24},{20,28},{24,16},{28,20},{1,9},{5... | collective-permute-start | bytes 1769480 | tf_op jit(solution)/shard_map/ppermute | solution.py:69
  200.2 9.6 %collective-permute-start.23 = (f32[31,1536]{1,0:T(8,128)S(1)}, f32[31,1536]{1,0:T(8,128)S(1)}, u32[]{:S(2)}, u32[]{:S(2)}) collective-permute-start(f32[31,1536]{1,0:T(8,128)S(1)} %add.554), channel_id=1, source_target_pairs={{0,16},{4,20},{8,24},{12,28},{16,0},{20,4},{24,8},{28,12},{1,17},{... | collective-permute-start | bytes 571400 | tf_op jit(solution)/shard_map/ppermute | solution.py:34
  209.4 20.2 %collective-permute-start.20 = (f32[192,1536]{1,0:T(8,128)S(1)}, f32[192,1536]{1,0:T(8,128)S(1)}, u32[]{:S(2)}, u32[]{:S(2)}) collective-permute-start(f32[192,1536]{1,0:T(8,128)S(1)} %maximum_select_fusion.1), channel_id=1, source_target_pairs={{0,4},{4,0},{8,12},{12,8},{16,20},{20,16},{24,28},{28,24},{1,5},{5... | collective-permute-start | bytes 3538952 | tf_op jit(solution)/shard_map/ppermute | solution.py:69
  209.9 7.4 %collective-permute-start.24 = (f32[31,1536]{1,0:T(8,128)S(1)}, f32[31,1536]{1,0:T(8,128)S(1)}, u32[]{:S(2)}, u32[]{:S(2)}) collective-permute-start(f32[31,1536]{1,0:T(8,128)S(1)} %add.555), channel_id=1, source_target_pairs={{0,1},{1,0},{2,3},{3,2},{4,5},{5,4},{6,7},{7,6},{8,9},{9,8},{10,11... | collective-permute-start | bytes 571400 | tf_op jit(solution)/shard_map/ppermute | solution.py:34
  217.3 11.7 %collective-permute-start.25 = (f32[31,1536]{1,0:T(8,128)S(1)}, f32[31,1536]{1,0:T(8,128)S(1)}, u32[]{:S(2)}, u32[]{:S(2)}) collective-permute-start(f32[31,1536]{1,0:T(8,128)S(1)} %add.556), channel_id=1, source_target_pairs={{0,2},{1,3},{2,0},{3,1},{4,6},{5,7},{6,4},{7,5},{8,10},{9,11},{10,... | collective-permute-start | bytes 571400 | tf_op jit(solution)/shard_map/ppermute | solution.py:34
  (83 other events, 1270.9 us)
Sparse Core Ops, SparseCore 0:
  9.6 39.7 all-gather.3
  51.5 63.9 all-gather.5

commit v7 on v5

--- a/solution.py
+++ b/solution.py
@@ -72,17 +72,12 @@
 
 
 def gather_weight(block):
-    if lax.axis_size("dp") % 2:
+    group = lax.axis_size("dp")
+    if block.shape[0] % group:
         return lax.all_gather(block, "tensor", axis=0, tiled=True)
-    peers = lax.axis_size("tensor")
-    half = block.shape[0] // 2
-    core = lax.rem(lax.axis_index("dp"), 2)
-    mine = lax.dynamic_slice_in_dim(block, core * half, half, axis=0)
-    held = lax.all_gather(mine, "tensor", axis=0, tiled=False)
-    other = lax.ppermute(held, "dp", [(i, i ^ 1) for i in range(lax.axis_size("dp"))])
-    first = jnp.where(core == 0, held, other)
-    second = jnp.where(core == 0, other, held)
-    return jnp.concatenate([first, second], axis=1).reshape(peers * block.shape[0], block.shape[1])
+    piece = block.shape[0] // group
+    mine = lax.dynamic_slice_in_dim(block, lax.axis_index("dp") * piece, piece, axis=0)
+    return lax.all_gather(mine, ("tensor", "dp"), axis=0, tiled=True)
 
 
 def on_device(glu_input, depth_kernel, norm_scale, norm_shift, proj_weight, out_grad):

time: 203 us -> 233 us (1.15)
  waiting for transfers between devices: 92.3 us -> 117 us
  starting transfers between devices: 44.1 us -> 47.4 us
  matrix products: 7.14 us -> 9.48 us
    ppermute x3, waiting for transfers between devices: 4.24 us -> 30.9 us  [rows_sum(): x = keep + lax.ppermute(give, axis, [(i, i ^ step) for i in range(peers)])]
    all_gather x1, waiting for transfers between devices: 16.2 us -> 0.01 us  [gather_weight(): return lax.all_gather(mine, ('tensor', 'dp'), axis=0, tiled=True)]
    ppermute x10, waiting for transfers between devices: 18.1 us -> 32.3 us  [all_sum(): x = x + lax.ppermute(x, axis, [(i, i ^ step) for i in range(peers)])]
    all_to_all x1, waiting for transfers between devices: 8.66 us -> 1.02 us  [on_device(): lax.all_to_all(flat_act, 'tensor', split_axis=1, concat_axis=0, tiled=True)]
    all_gather x1, waiting for transfers between devices: 17.3 us -> 23.6 us  [on_device(): group_grad = lax.all_gather(flat_grad, 'tensor', axis=0, tiled=True)]
    ppermute x10, starting transfers between devices: 8.36 us -> 12.5 us  [all_sum(): x = x + lax.ppermute(x, axis, [(i, i ^ step) for i in range(peers)])]
    dot_general x1, matrix products: 1.53 us -> 3.87 us  [on_device(): jnp.einsum('btc,cd->btd', activated, full_weight, preferred_element_type=...]
  transfers between devices with their start and end apart: 30 -> 29, of which waited for: 19 -> 18; matrix products, arithmetic and copies ran while one was open for 20% -> 16% of each run, Pallas kernels for 0% -> 0%
where the time goes in v7:
time: 233 us; the launch traced here: 232 us
  waiting for transfers between devices  117 us (50%)
  starting transfers between devices  47.4 us (20%)
  other arithmetic  28.3 us (12%)
  between operations  17.2 us (7%)
  local copies, waits for them, and re-layouts  12.3 us (5%)
  matrix products  9.48 us (4%)
    ppermute x10, waiting for transfers between devices, all_sum(): x = x + lax.ppermute(x, axis, [(i, i ^ step) for i in range(peers)])  32.3 us
    ppermute x3, waiting for transfers between devices, rows_sum(): x = keep + lax.ppermute(give, axis, [(i, i ^ step) for i in range(peers)])  30.9 us
    all_gather x1, waiting for transfers between devices, on_device(): group_grad = lax.all_gather(flat_grad, 'tensor', axis=0, tiled=True)  23.6 us
    ppermute x5, waiting for transfers between devices, all_moments(): lax.ppermute(jnp.stack([mean, spread]), axis, [(i, i ^ step) for i in ran...  17.3 us
    ppermute x10, starting transfers between devices, all_sum(): x = x + lax.ppermute(x, axis, [(i, i ^ step) for i in range(peers)])  12.5 us
    ppermute x5, starting transfers between devices, all_moments(): lax.ppermute(jnp.stack([mean, spread]), axis, [(i, i ^ step) for i in ran...  9.86 us
    ppermute x2, starting transfers between devices, extended(): before = lax.ppermute(last, axis, up)  9.63 us
    ppermute x3, waiting for transfers between devices, rows_sum(): other = lax.ppermute(x, axis, [(i, i ^ step) for i in range(peers)])  7.48 us
  transfers between devices with their start and end apart: 29, of which 18 were waited for; matrix products, arithmetic and copies ran while one was open for 16% of the time, Pallas kernels for 0%

profile of v7, /device:TPU:0, one launch (start us, length us, event | category | flops | bytes accessed | tf_op | source)
XLA Modules:
  0.0 231.7 jit_solution(14496970878105586228)
XLA Ops:
  9.6 4.9 %collective-permute-start = (bf16[2,15,1536]{2,1,0:T(8,128)(2,1)S(1)}, bf16[2,15,1536]{2,1,0:T(8,128)(2,1)S(1)}, u32[]{:S(2)}, u32[]{:S(2)}) collective-permute-start(bf16[2,15,1536]{2,1,0:T(8,128)(2,1)S(1)} %get-tuple-element.97), channel_id=1, source_target_pairs={{0,1},{1,2},{2,3},{4,5},{5,6},{6,7},{8,9},{9,10},{10,11},{12,13},{... | collective-permute-start | bytes 276488 | tf_op jit(solution)/shard_map/ppermute | solution.py:16
  16.7 4.3 %collective-permute-done.1 = bf16[2,15,1536]{2,1,0:T(8,128)(2,1)S(1)} collective-permute-done((bf16[2,15,1536]{2,1,0:T(8,128)(2,1)S(1)}, bf16[2,15,1536]{2,1,0:T(8,128)(2,1)S(1)}, u32[]{:S(2)}, u32[]{:S(2)}) %collective-permute-start.1) | collective-permute-done | bytes 92192 | tf_op jit(solution)/shard_map/ppermute | solution.py:17
  21.0 3.8 %fusion.148 = (f32[1536]{0:T(1024)S(1)}, f32[2,64,1536]{2,1,0:T(8,128)S(1)}) fusion(bf16[2,15,1536]{2,1,0:T(8,128)(2,1)S(1)} %collective-permute-done.1, bf16[2,64,1536]{2,1,0:T(8,128)(2,1)S(1)} %fusion.5, f32[1536]{0:T(1024)S(1)} %get-tuple-element.72, f32[1536]{0:T(1024)S(1)} %get-tuple-element.73, f32[1536]{0:T(1024)S(1)} %get-tuple-element.44, ...), kind=kLoop, calls=%fused_computation.379 | loop fusion | flops 35977728 | bytes 1560576 | tf_op jit(solution)/shard_map/reduce_sum | solution.py:105
  27.9 2.2 collective-permute-done.3
  31.8 23.6 %all-gather.5.cloned.1.call-done = bf16[512,1536]{1,0:T(8,128)(2,1)} async-done(((bf16[128,1536]{1,0:T(8,128)(2,1)}), bf16[512,1536]{1,0:T(8,128)(2,1)}) %all-gather.5.cloned.1.call-update) | async-done | bytes 1572880 | tf_op jit(solution)/shard_map/all_gather | solution.py:94
  55.4 3.3 %fusion.152 = f32[512,384]{1,0:T(8,128)} fusion(bf16[512,1536]{1,0:T(8,128)(2,1)} %all-gather.5.cloned.1.call-done, bf16[384,1536]{1,0:T(8,128)(2,1)S(1)} %copy-done), kind=kOutput, calls=%fused_computation.382 | convolution fusion | flops 603979776 | bytes 3538944 | tf_op jit(solution)/shard_map/fd,cd->fc/dot_general | solution.py:95
  59.0 3.5 %all-to-all-start = ((f32[4,128,384]{2,1,0:T(8,128)}), f32[4,128,384]{2,1,0:T(8,128)S(1)}, u32[]{:S(2)}, u32[]{:S(2)}) async-start(f32[4,128,384]{2,1,0:T(8,128)} %bitcast.17), calls=%async_computation | async-start | bytes 1572864 | tf_op jit(solution)/shard_map/all_to_all | solution.py:96
  62.6 2.0 collective-permute-start.5
  64.6 11.1 %collective-permute-done.5 = f32[2,1536]{1,0:T(2,128)S(1)} collective-permute-done((f32[2,1536]{1,0:T(2,128)S(1)}, f32[2,1536]{1,0:T(2,128)S(1)}, u32[]{:S(2)}, u32[]{:S(2)}) %collective-permute-start.5) | collective-permute-done | bytes 12320 | tf_op jit(solution)/shard_map/ppermute | solution.py:44
  75.8 4.7 %collective-permute-start.6 = (f32[2,1536]{1,0:T(2,128)S(1)}, f32[2,1536]{1,0:T(2,128)S(1)}, u32[]{:S(2)}, u32[]{:S(2)}) collective-permute-start(f32[2,1536]{1,0:T(2,128)S(1)} %pad_maximum_fusion.9), channel_id=1, source_target_pairs={{0,2},{1,3},{2,0},{3,1},{4,6},{5,7},{6,4},{7,5},{8,10},{9,11},{10,... | collective-permute-start | bytes 36872 | tf_op jit(solution)/shard_map/ppermute | solution.py:44
  80.5 2.8 %collective-permute-done.6 = f32[2,1536]{1,0:T(2,128)S(1)} collective-permute-done((f32[2,1536]{1,0:T(2,128)S(1)}, f32[2,1536]{1,0:T(2,128)S(1)}, u32[]{:S(2)}, u32[]{:S(2)}) %collective-permute-start.6) | collective-permute-done | bytes 12320 | tf_op jit(solution)/shard_map/ppermute | solution.py:44
  86.8 2.1 fusion.145
  91.7 2.2 collective-permute-done.8
  95.5 2.2 collective-permute-done.9
  98.3 4.0 %collective-permute-done.10 = f32[2,1536]{1,0:T(2,128)} collective-permute-done((f32[2,1536]{1,0:T(2,128)}, f32[2,1536]{1,0:T(2,128)}, u32[]{:S(2)}, u32[]{:S(2)}) %collective-permute-start.10) | collective-permute-done | bytes 12320 | tf_op jit(solution)/shard_map/ppermute | solution.py:34
  108.8 4.3 %all-to-all-start.1 = ((bf16[128,4,384]{2,0,1:T(8,128)(2,1)}), bf16[128,4,384]{2,0,1:T(8,128)(2,1)}, u32[]{:S(2)}, u32[]{:S(2)}) async-start(bf16[128,4,384]{2,0,1:T(8,128)(2,1)} %copy.17), calls=%async_computation.1 | async-start | bytes 786432 | tf_op jit(solution)/shard_map/all_to_all | solution.py:122
  114.0 2.9 %fusion.85 = (f32[1536]{0:T(1024)S(1)}, f32[1536]{0:T(1024)S(1)}, f32[1536]{0:T(1024)S(1)}, f32[1536]{0:T(1024)S(1)}, f32[1536]{0:T(1024)S(1)}, /*index=5*/f32[1...) fusion(bf16[2,15,1536]{2,1,0:T(8,128)(2,1)} %copy-done.7, ...), kind=kLoop, calls=%fused_computation.207 | loop fusion | flops 12372480 | bytes 2537472 | tf_op jit(solution)/shard_map/reduce_sum | solution.py:141
  120.3 2.8 %stack.172 = f32[31,1536]{1,0:T(8,128)} concatenate(f32[1,1536]{1,0:T(1,128)S(1)} %stack.141, f32[1,1536]{1,0:T(1,128)S(1)} %stack.142, f32[1,1536]{1,0:T(1,128)S(1)} %stack.143, f32[1,1536]{1,0:T(1,128)S(1)} %stack.144, f32[1,1536]{1,0:T(1,128)S(1)} %stack.145, f32[1,1536]{1,0:T(1,128)S(1)} %stack.146, f32[1,1536]{1,0:T(1,128)S(1)} %stack.147, f32[1,1536]{1,0:T(1,128)S(1)} %stack.148, ...), dimensions={0} | concatenate | bytes 380928 | tf_op jit(solution)/shard_map/stack | solution.py:139
  124.1 2.3 %fusion.153 = f32[384,1536]{1,0:T(8,128)S(1)} fusion(bf16[512,384]{1,0:T(8,128)(2,1)} %bitcast.5, bf16[512,1536]{1,0:T(8,128)(2,1)} %all-gather.5.cloned.1.call-done), kind=kOutput, calls=%fused_computation.383 | convolution fusion | flops 603979776 | bytes 4325376 | tf_op jit(solution)/shard_map/fc,fd->cd/dot_general | solution.py:123
  127.5 3.2 %collective-permute-done.14 = f32[192,1536]{1,0:T(8,128)} collective-permute-done((f32[192,1536]{1,0:T(8,128)}, f32[192,1536]{1,0:T(8,128)}, u32[]{:S(2)}, u32[]{:S(2)}) %collective-permute-start.14) | collective-permute-done | bytes 1179680 | tf_op jit(solution)/shard_map/ppermute | solution.py:65
  130.7 2.4 %dynamic-slice_add_fusion = f32[192,1536]{1,0:T(8,128)} fusion(f32[192,1536]{1,0:T(8,128)} %collective-permute-done.14, f32[384,1536]{1,0:T(8,128)S(1)} %fusion.153, s32[]{:T(128)S(6)} %select_n.60), kind=kLoop, calls=%fused_computation.93 | loop fusion | flops 294912 | bytes 3538948 | tf_op jit(solution)/shard_map/add | solution.py:65
  135.8 13.9 %collective-permute-done.15 = f32[96,1536]{1,0:T(8,128)S(1)} collective-permute-done((f32[96,1536]{1,0:T(8,128)S(1)}, f32[96,1536]{1,0:T(8,128)S(1)}, u32[]{:S(2)}, u32[]{:S(2)}) %collective-permute-start.15) | collective-permute-done | bytes 589856 | tf_op jit(solution)/shard_map/ppermute | solution.py:65
  152.5 13.8 %collective-permute-done.16 = f32[48,1536]{1,0:T(8,128)S(1)} collective-permute-done((f32[48,1536]{1,0:T(8,128)S(1)}, f32[48,1536]{1,0:T(8,128)S(1)}, u32[]{:S(2)}, u32[]{:S(2)}) %collective-permute-start.16) | collective-permute-done | bytes 294944 | tf_op jit(solution)/shard_map/ppermute | solution.py:65
  166.8 7.5 %collective-permute-done.17 = f32[48,1536]{1,0:T(8,128)S(1)} collective-permute-done((f32[48,1536]{1,0:T(8,128)S(1)}, f32[48,1536]{1,0:T(8,128)S(1)}, u32[]{:S(2)}, u32[]{:S(2)}) %collective-permute-start.17) | collective-permute-done | bytes 294944 | tf_op jit(solution)/shard_map/ppermute | solution.py:69
  178.3 4.7 %collective-permute-start.13 = (bf16[2,15,1536]{2,1,0:T(8,128)(2,1)S(1)}, bf16[2,15,1536]{2,1,0:T(8,128)(2,1)S(1)}, u32[]{:S(2)}, u32[]{:S(2)}) collective-permute-start(bf16[2,15,1536]{2,1,0:T(8,128)(2,1)S(1)} %get-tuple-element.96), channel_id=1, source_target_pairs={{0,1},{1,2},{2,3},{4,5},{5,6},{6,7},{8,9},{9,10},{10,11},{12,13},{... | collective-permute-start | bytes 276488 | tf_op jit(solution)/shard_map/ppermute | solution.py:16
  183.0 9.0 %collective-permute-done.21 = f32[31,1536]{1,0:T(8,128)S(1)} collective-permute-done((f32[31,1536]{1,0:T(8,128)S(1)}, f32[31,1536]{1,0:T(8,128)S(1)}, u32[]{:S(2)}, u32[]{:S(2)}) %collective-permute-start.21) | collective-permute-done | bytes 190496 | tf_op jit(solution)/shard_map/ppermute | solution.py:34
  194.2 4.1 %multiply_convert_fusion = (bf16[2,64,1536]{2,1,0:T(8,128)(2,1)S(1)}, f32[2,64,1536]{2,1,0:T(8,128)S(1)}) fusion(bf16[2,64,3072]{2,1,0:T(8,128)(2,1)S(1)} %copy-done.3, bf16[2,64,1536]{2,1,0:T(8,128)(2,1)S(1)} %copy-done.2, bf16[2,15,1536]{2,1,0:T(8,128)(2,1)S(1)} %collective-permute-done.13, f32[1536]{0:T(1024)S(1)} %copy-done.68, f32[1536]{0:T(1024)S(1)} %copy-done.70, ...), kind=kLoop, calls=%fused_computation.209 | loop fusion | flops 36962304 | bytes 2340864 | tf_op jit(solution)/shard_map/convert
  198.3 2.3 collective-permute-start.23
  200.9 5.3 %collective-permute-done.23 = f32[31,1536]{1,0:T(8,128)S(1)} collective-permute-done((f32[31,1536]{1,0:T(8,128)S(1)}, f32[31,1536]{1,0:T(8,128)S(1)}, u32[]{:S(2)}, u32[]{:S(2)}) %collective-permute-start.23) | collective-permute-done | bytes 190496 | tf_op jit(solution)/shard_map/ppermute | solution.py:34
  206.2 2.5 %collective-permute-start.24 = (f32[31,1536]{1,0:T(8,128)S(1)}, f32[31,1536]{1,0:T(8,128)S(1)}, u32[]{:S(2)}, u32[]{:S(2)}) collective-permute-start(f32[31,1536]{1,0:T(8,128)S(1)} %add.559), channel_id=1, source_target_pairs={{0,2},{1,3},{2,0},{3,1},{4,6},{5,7},{6,4},{7,5},{8,10},{9,11},{10,... | collective-permute-start | bytes 571400 | tf_op jit(solution)/shard_map/ppermute | solution.py:34
  209.6 8.4 %collective-permute-done.24 = f32[31,1536]{1,0:T(8,128)S(1)} collective-permute-done((f32[31,1536]{1,0:T(8,128)S(1)}, f32[31,1536]{1,0:T(8,128)S(1)}, u32[]{:S(2)}, u32[]{:S(2)}) %collective-permute-start.24) | collective-permute-done | bytes 190496 | tf_op jit(solution)/shard_map/ppermute | solution.py:34
  220.4 3.9 %fusion.2 = bf16[2,64,1536]{2,1,0:T(8,128)(2,1)} fusion(bf16[2,64,1536]{2,1,0:T(8,128)(2,1)S(1)} %copy-done.5, bf16[1536,1536]{1,0:T(8,128)(2,1)} %all-gather.3.cloned.1.call-done), kind=kOutput, calls=%fused_computation.34 | convolution fusion | flops 604176384 | bytes 5505024 | tf_op jit(solution)/shard_map/btc,cd->btd/dot_general | solution.py:154
  (269 shorter events, 44.6 us)
Async XLA Ops:
  8.0 47.4 %copy-start = (bf16[384,1536]{1,0:T(8,128)(2,1)S(1)}, bf16[384,1536]{1,0:T(8,128)(2,1)}, u32[]{:S(2)}) copy-start(bf16[384,1536]{1,0:T(8,128)(2,1)} %param.10) | copy-start | bytes 3538948
  8.0 47.4 %all-gather.5.cloned.1.call-start = ((), (), s32[]{:S(2)}) async-start(), calls=%async_computation.3 | async-start | bytes 1966080 | tf_op jit(solution)/shard_map/all_gather | solution.py:94
  9.6 7.1 %collective-permute-start = (bf16[2,15,1536]{2,1,0:T(8,128)(2,1)S(1)}, bf16[2,15,1536]{2,1,0:T(8,128)(2,1)S(1)}, u32[]{:S(2)}, u32[]{:S(2)}) collective-permute-start(bf16[2,15,1536]{2,1,0:T(8,128)(2,1)S(1)} %get-tuple-element.97), channel_id=1, source_target_pairs={{0,1},{1,2},{2,3},{4,5},{5,6},{6,7},{8,9},{9,10},{10,11},{12,13},{... | collective-permute-start | bytes 276488 | tf_op jit(solution)/shard_map/ppermute | solution.py:16
  14.5 6.5 %collective-permute-start.1 = (bf16[2,15,1536]{2,1,0:T(8,128)(2,1)S(1)}, bf16[2,15,1536]{2,1,0:T(8,128)(2,1)S(1)}, u32[]{:S(2)}, u32[]{:S(2)}) collective-permute-start(bf16[2,15,1536]{2,1,0:T(8,128)(2,1)S(1)} %get-tuple-element.98), channel_id=1, source_target_pairs={{1,0},{2,1},{3,2},{5,4},{6,5},{7,6},{9,8},{10,9},{11,10},{13,12},{... | collective-permute-start | bytes 276488 | tf_op jit(solution)/shard_map/ppermute | solution.py:17
  16.2 42.5 %copy-start.15 = (f32[1536]{0:T(1024)}, f32[1536]{0:T(1024)S(1)}, u32[]{:S(2)}) copy-start(f32[1536]{0:T(1024)S(1)} %get-tuple-element.46) | copy-start | bytes 18436
  16.2 42.5 %copy-start.17 = (f32[1536]{0:T(1024)}, f32[1536]{0:T(1024)S(1)}, u32[]{:S(2)}) copy-start(f32[1536]{0:T(1024)S(1)} %get-tuple-element.47) | copy-start | bytes 18436
  25.1 1.2 collective-permute-start.2
  26.4 3.8 %collective-permute-start.3 = (f32[2,1536]{1,0:T(2,128)S(1)}, f32[2,1536]{1,0:T(2,128)S(1)}, u32[]{:S(2)}, u32[]{:S(2)}) collective-permute-start(f32[2,1536]{1,0:T(2,128)S(1)} %pad_maximum_fusion.6), channel_id=1, source_target_pairs={{0,8},{4,12},{8,0},{12,4},{16,24},{20,28},{24,16},{28,20},{1,9},{5... | collective-permute-start | bytes 36872 | tf_op jit(solution)/shard_map/ppermute | solution.py:44
  30.2 32.3 %collective-permute-start.4 = (f32[2,1536]{1,0:T(2,128)S(1)}, f32[2,1536]{1,0:T(2,128)S(1)}, u32[]{:S(2)}, u32[]{:S(2)}) collective-permute-start(f32[2,1536]{1,0:T(2,128)S(1)} %pad_maximum_fusion.7), channel_id=1, source_target_pairs={{0,16},{4,20},{8,24},{12,28},{16,0},{20,4},{24,8},{28,12},{1,17},{... | collective-permute-start | bytes 36872 | tf_op jit(solution)/shard_map/ppermute | solution.py:44
  59.0 25.0 %all-to-all-start = ((f32[4,128,384]{2,1,0:T(8,128)}), f32[4,128,384]{2,1,0:T(8,128)S(1)}, u32[]{:S(2)}, u32[]{:S(2)}) async-start(f32[4,128,384]{2,1,0:T(8,128)} %bitcast.17), calls=%async_computation | async-start | bytes 1572864 | tf_op jit(solution)/shard_map/all_to_all | solution.py:96
  62.5 157.9 %all-gather.3.cloned.1.call-start = ((), (), s32[]{:S(2)}) async-start(), calls=%async_computation.2 | async-start | bytes 4866048 | tf_op jit(solution)/shard_map/all_gather | solution.py:80
  62.6 13.1 %collective-permute-start.5 = (f32[2,1536]{1,0:T(2,128)S(1)}, f32[2,1536]{1,0:T(2,128)S(1)}, u32[]{:S(2)}, u32[]{:S(2)}) collective-permute-start(f32[2,1536]{1,0:T(2,128)S(1)} %pad_maximum_fusion.8), channel_id=1, source_target_pairs={{0,1},{1,0},{2,3},{3,2},{4,5},{5,4},{6,7},{7,6},{8,9},{9,8},{10,11... | collective-permute-start | bytes 36872 | tf_op jit(solution)/shard_map/ppermute | solution.py:44
  75.8 7.4 %collective-permute-start.6 = (f32[2,1536]{1,0:T(2,128)S(1)}, f32[2,1536]{1,0:T(2,128)S(1)}, u32[]{:S(2)}, u32[]{:S(2)}) collective-permute-start(f32[2,1536]{1,0:T(2,128)S(1)} %pad_maximum_fusion.9), channel_id=1, source_target_pairs={{0,2},{1,3},{2,0},{3,1},{4,6},{5,7},{6,4},{7,5},{8,10},{9,11},{10,... | collective-permute-start | bytes 36872 | tf_op jit(solution)/shard_map/ppermute | solution.py:44
  88.9 1.2 collective-permute-start.7
  90.2 3.8 %collective-permute-start.8 = (f32[2,1536]{1,0:T(2,128)S(1)}, f32[2,1536]{1,0:T(2,128)S(1)}, u32[]{:S(2)}, u32[]{:S(2)}) collective-permute-start(f32[2,1536]{1,0:T(2,128)S(1)} %fusion.144), channel_id=1, source_target_pairs={{0,8},{4,12},{8,0},{12,4},{16,24},{20,28},{24,16},{28,20},{1,9},{5... | collective-permute-start | bytes 36872 | tf_op jit(solution)/shard_map/ppermute | solution.py:34
  93.9 3.8 %collective-permute-start.9 = (f32[2,1536]{1,0:T(2,128)S(1)}, f32[2,1536]{1,0:T(2,128)S(1)}, u32[]{:S(2)}, u32[]{:S(2)}) collective-permute-start(f32[2,1536]{1,0:T(2,128)S(1)} %fusion.159), channel_id=1, source_target_pairs={{0,16},{4,20},{8,24},{12,28},{16,0},{20,4},{24,8},{28,12},{1,17},{... | collective-permute-start | bytes 36872 | tf_op jit(solution)/shard_map/ppermute | solution.py:34
  98.3 4.0 %collective-permute-start.10 = (f32[2,1536]{1,0:T(2,128)}, f32[2,1536]{1,0:T(2,128)}, u32[]{:S(2)}, u32[]{:S(2)}) collective-permute-start(f32[2,1536]{1,0:T(2,128)} %add.514), channel_id=1, source_target_pairs={{0,1},{1,0},{2,3},{3,2},{4,5},{5,4},{6,7},{7,6},{8,9},{9,8},{10,11... | collective-permute-start | bytes 36872 | tf_op jit(solution)/shard_map/ppermute | solution.py:34
  103.7 9.4 %collective-permute-start.11 = (f32[2,1536]{1,0:T(2,128)}, f32[2,1536]{1,0:T(2,128)}, u32[]{:S(2)}, u32[]{:S(2)}) collective-permute-start(f32[2,1536]{1,0:T(2,128)} %add.515), channel_id=1, source_target_pairs={{0,2},{1,3},{2,0},{3,1},{4,6},{5,7},{6,4},{7,5},{8,10},{9,11},{10,... | collective-permute-start | bytes 36872 | tf_op jit(solution)/shard_map/ppermute | solution.py:34
  108.8 15.2 %all-to-all-start.1 = ((bf16[128,4,384]{2,0,1:T(8,128)(2,1)}), bf16[128,4,384]{2,0,1:T(8,128)(2,1)}, u32[]{:S(2)}, u32[]{:S(2)}) async-start(bf16[128,4,384]{2,0,1:T(8,128)(2,1)} %copy.17), calls=%async_computation.1 | async-start | bytes 786432 | tf_op jit(solution)/shard_map/all_to_all | solution.py:122
  127.5 3.2 %collective-permute-start.14 = (f32[192,1536]{1,0:T(8,128)}, f32[192,1536]{1,0:T(8,128)}, u32[]{:S(2)}, u32[]{:S(2)}) collective-permute-start(f32[192,1536]{1,0:T(8,128)} %constant_dynamic-slice_fusion.2), channel_id=1, source_target_pairs={{0,4},{4,0},{8,12},{12,8},{16,20},{20,16},{24,28},{28,24},{1,5},{5... | collective-permute-start | bytes 3538952 | tf_op jit(solution)/shard_map/ppermute | solution.py:65
  134.2 15.5 %collective-permute-start.15 = (f32[96,1536]{1,0:T(8,128)S(1)}, f32[96,1536]{1,0:T(8,128)S(1)}, u32[]{:S(2)}, u32[]{:S(2)}) collective-permute-start(f32[96,1536]{1,0:T(8,128)S(1)} %constant_dynamic-slice_fusion.1), channel_id=1, source_target_pairs={{0,8},{4,12},{8,0},{12,4},{16,24},{20,28},{24,16},{28,20},{1,9},{5... | collective-permute-start | bytes 1769480 | tf_op jit(solution)/shard_map/ppermute | solution.py:65
  150.9 15.4 %collective-permute-start.16 = (f32[48,1536]{1,0:T(8,128)S(1)}, f32[48,1536]{1,0:T(8,128)S(1)}, u32[]{:S(2)}, u32[]{:S(2)}) collective-permute-start(f32[48,1536]{1,0:T(8,128)S(1)} %constant_dynamic-slice_fusion), channel_id=1, source_target_pairs={{0,16},{4,20},{8,24},{12,28},{16,0},{20,4},{24,8},{28,12},{1,17},{... | collective-permute-start | bytes 884744 | tf_op jit(solution)/shard_map/ppermute | solution.py:65
  166.4 7.9 %collective-permute-start.17 = (f32[48,1536]{1,0:T(8,128)S(1)}, f32[48,1536]{1,0:T(8,128)S(1)}, u32[]{:S(2)}, u32[]{:S(2)}) collective-permute-start(f32[48,1536]{1,0:T(8,128)S(1)} %dynamic-slice_add_fusion.2), channel_id=1, source_target_pairs={{0,16},{4,20},{8,24},{12,28},{16,0},{20,4},{24,8},{28,12},{1,17},{... | collective-permute-start | bytes 884744 | tf_op jit(solution)/shard_map/ppermute | solution.py:69
  166.8 8.6 %collective-permute-start.20 = (f32[31,1536]{1,0:T(8,128)S(1)}, f32[31,1536]{1,0:T(8,128)S(1)}, u32[]{:S(2)}, u32[]{:S(2)}) collective-permute-start(f32[31,1536]{1,0:T(8,128)S(1)} %copy-done.11), channel_id=1, source_target_pairs={{0,4},{4,0},{8,12},{12,8},{16,20},{20,16},{24,28},{28,24},{1,5},{5... | collective-permute-start | bytes 571400 | tf_op jit(solution)/shard_map/ppermute | solution.py:34
  174.3 19.4 %collective-permute-start.18 = (f32[96,1536]{1,0:T(8,128)S(1)}, f32[96,1536]{1,0:T(8,128)S(1)}, u32[]{:S(2)}, u32[]{:S(2)}) collective-permute-start(f32[96,1536]{1,0:T(8,128)S(1)} %maximum_select_fusion.2), channel_id=1, source_target_pairs={{0,8},{4,12},{8,0},{12,4},{16,24},{20,28},{24,16},{28,20},{1,9},{5... | collective-permute-start | bytes 1769480 | tf_op jit(solution)/shard_map/ppermute | solution.py:69
  175.5 16.5 %collective-permute-start.21 = (f32[31,1536]{1,0:T(8,128)S(1)}, f32[31,1536]{1,0:T(8,128)S(1)}, u32[]{:S(2)}, u32[]{:S(2)}) collective-permute-start(f32[31,1536]{1,0:T(8,128)S(1)} %add.556), channel_id=1, source_target_pairs={{0,8},{4,12},{8,0},{12,4},{16,24},{20,28},{24,16},{28,20},{1,9},{5... | collective-permute-start | bytes 571400 | tf_op jit(solution)/shard_map/ppermute | solution.py:34
  176.8 17.1 %collective-permute-start.12 = (bf16[2,15,1536]{2,1,0:T(8,128)(2,1)S(1)}, bf16[2,15,1536]{2,1,0:T(8,128)(2,1)S(1)}, u32[]{:S(2)}, u32[]{:S(2)}) collective-permute-start(bf16[2,15,1536]{2,1,0:T(8,128)(2,1)S(1)} %get-tuple-element.95), channel_id=1, source_target_pairs={{1,0},{2,1},{3,2},{5,4},{6,5},{7,6},{9,8},{10,9},{11,10},{13,12},{... | collective-permute-start | bytes 276488 | tf_op jit(solution)/shard_map/ppermute | solution.py:17
  178.3 15.7 %collective-permute-start.13 = (bf16[2,15,1536]{2,1,0:T(8,128)(2,1)S(1)}, bf16[2,15,1536]{2,1,0:T(8,128)(2,1)S(1)}, u32[]{:S(2)}, u32[]{:S(2)}) collective-permute-start(bf16[2,15,1536]{2,1,0:T(8,128)(2,1)S(1)} %get-tuple-element.96), channel_id=1, source_target_pairs={{0,1},{1,2},{2,3},{4,5},{5,6},{6,7},{8,9},{9,10},{10,11},{12,13},{... | collective-permute-start | bytes 276488 | tf_op jit(solution)/shard_map/ppermute | solution.py:16
  192.0 6.3 %collective-permute-start.22 = (f32[31,1536]{1,0:T(8,128)S(1)}, f32[31,1536]{1,0:T(8,128)S(1)}, u32[]{:S(2)}, u32[]{:S(2)}) collective-permute-start(f32[31,1536]{1,0:T(8,128)S(1)} %add.557), channel_id=1, source_target_pairs={{0,16},{4,20},{8,24},{12,28},{16,0},{20,4},{24,8},{28,12},{1,17},{... | collective-permute-start | bytes 571400 | tf_op jit(solution)/shard_map/ppermute | solution.py:34
  193.8 24.9 %collective-permute-start.19 = (f32[192,1536]{1,0:T(8,128)S(1)}, f32[192,1536]{1,0:T(8,128)S(1)}, u32[]{:S(2)}, u32[]{:S(2)}) collective-permute-start(f32[192,1536]{1,0:T(8,128)S(1)} %maximum_select_fusion.1), channel_id=1, source_target_pairs={{0,4},{4,0},{8,12},{12,8},{16,20},{20,16},{24,28},{28,24},{1,5},{5... | collective-permute-start | bytes 3538952 | tf_op jit(solution)/shard_map/ppermute | solution.py:69
  198.3 7.8 %collective-permute-start.23 = (f32[31,1536]{1,0:T(8,128)S(1)}, f32[31,1536]{1,0:T(8,128)S(1)}, u32[]{:S(2)}, u32[]{:S(2)}) collective-permute-start(f32[31,1536]{1,0:T(8,128)S(1)} %add.558), channel_id=1, source_target_pairs={{0,1},{1,0},{2,3},{3,2},{4,5},{5,4},{6,7},{7,6},{8,9},{9,8},{10,11... | collective-permute-start | bytes 571400 | tf_op jit(solution)/shard_map/ppermute | solution.py:34
  206.2 11.9 %collective-permute-start.24 = (f32[31,1536]{1,0:T(8,128)S(1)}, f32[31,1536]{1,0:T(8,128)S(1)}, u32[]{:S(2)}, u32[]{:S(2)}) collective-permute-start(f32[31,1536]{1,0:T(8,128)S(1)} %add.559), channel_id=1, source_target_pairs={{0,2},{1,3},{2,0},{3,1},{4,6},{5,7},{6,4},{7,5},{8,10},{9,11},{10,... | collective-permute-start | bytes 571400 | tf_op jit(solution)/shard_map/ppermute | solution.py:34
  (71 other events, 1873.6 us)
Sparse Core Ops, SparseCore 0:
  16.0 39.3 all-gather.4
Sparse Core Ops, SparseCore 1:
  106.2 68.5 all-gather.2

commit v8 on v5

--- a/solution.py
+++ b/solution.py
@@ -156,8 +156,9 @@
         [grad_gated * gates, grad_gated * values * gates * (1.0 - gates)], axis=-1
     ).astype(jnp.bfloat16)
     full_weight = gather_weight(proj_weight)
+    late_act, kernel_grad = lax.optimization_barrier((activated, kernel_grad))
     conv_output = jnp.einsum(
-        "btc,cd->btd", activated, full_weight, preferred_element_type=jnp.float32
+        "btc,cd->btd", late_act, full_weight, preferred_element_type=jnp.float32
     ).astype(jnp.bfloat16)
     return (conv_output, input_grad, weight_grad, kernel_grad, scale_grad, shift_grad)
 

time: 203 us -> 208 us (1.025)
  waiting for transfers between devices: 92.3 us -> 99.3 us
    all_gather x1, waiting for transfers between devices: 17.3 us -> 24.6 us  [on_device(): group_grad = lax.all_gather(flat_grad, 'tensor', axis=0, tiled=True)]
    ppermute x2, waiting for transfers between devices: 4.32 us -> 0.01 us  [extended(): after = lax.ppermute(leading, axis, down)]
    ppermute x3, waiting for transfers between devices: 4.24 us -> 7.24 us  [rows_sum(): x = keep + lax.ppermute(give, axis, [(i, i ^ step) for i in range(peers)])]
    ppermute x2, starting transfers between devices: 9.48 us -> 6.86 us  [extended(): before = lax.ppermute(last, axis, up)]
  transfers between devices with their start and end apart: 30 -> 30, of which waited for: 19 -> 19; matrix products, arithmetic and copies ran while one was open for 20% -> 19% of each run, Pallas kernels for 0% -> 0%
where the time goes in v8:
time: 208 us; the launch traced here: 207 us
  waiting for transfers between devices  99.3 us (48%)
  starting transfers between devices  42.2 us (20%)
  other arithmetic  28.5 us (14%)
  between operations  15.8 us (8%)
  local copies, waits for them, and re-layouts  13.7 us (7%)
  matrix products  7.14 us (3%)
    all_gather x1, waiting for transfers between devices, on_device(): group_grad = lax.all_gather(flat_grad, 'tensor', axis=0, tiled=True)  24.6 us
    ppermute x10, waiting for transfers between devices, all_sum(): x = x + lax.ppermute(x, axis, [(i, i ^ step) for i in range(peers)])  18 us
    ppermute x5, waiting for transfers between devices, all_moments(): lax.ppermute(jnp.stack([mean, spread]), axis, [(i, i ^ step) for i in ran...  16.8 us
    all_gather x1, waiting for transfers between devices, gather_weight(): held = lax.all_gather(mine, 'tensor', axis=0, tiled=False)  16.1 us
    ppermute x5, starting transfers between devices, all_moments(): lax.ppermute(jnp.stack([mean, spread]), axis, [(i, i ^ step) for i in ran...  10.7 us
    ppermute x10, starting transfers between devices, all_sum(): x = x + lax.ppermute(x, axis, [(i, i ^ step) for i in range(peers)])  8.87 us
    all_to_all x1, waiting for transfers between devices, on_device(): lax.all_to_all(flat_act, 'tensor', split_axis=1, concat_axis=0, tiled=True)  8.66 us
    ppermute x3, waiting for transfers between devices, rows_sum(): x = keep + lax.ppermute(give, axis, [(i, i ^ step) for i in range(peers)])  7.24 us
  transfers between devices with their start and end apart: 30, of which 19 were waited for; matrix products, arithmetic and copies ran while one was open for 19% of the time, Pallas kernels for 0%

profile of v8, /device:TPU:0, one launch (start us, length us, event | category | flops | bytes accessed | tf_op | source)
XLA Modules:
  0.0 206.8 jit_solution(7546287578738781755)
XLA Ops:
  10.0 5.6 %collective-permute-start = (bf16[2,15,1536]{2,1,0:T(8,128)(2,1)S(1)}, bf16[2,15,1536]{2,1,0:T(8,128)(2,1)S(1)}, u32[]{:S(2)}, u32[]{:S(2)}) collective-permute-start(bf16[2,15,1536]{2,1,0:T(8,128)(2,1)S(1)} %get-tuple-element.103), channel_id=1, source_target_pairs={{0,1},{1,2},{2,3},{4,5},{5,6},{6,7},{8,9},{9,10},{10,11},{12,13},{... | collective-permute-start | bytes 276488 | tf_op jit(solution)/shard_map/ppermute | solution.py:16
  17.8 3.8 %fusion.143 = (f32[1536]{0:T(1024)S(1)}, f32[2,64,1536]{2,1,0:T(8,128)S(1)}) fusion(bf16[2,15,1536]{2,1,0:T(8,128)(2,1)S(1)} %collective-permute-done.1, bf16[2,64,1536]{2,1,0:T(8,128)(2,1)S(1)} %fusion, f32[1536]{0:T(1024)S(1)} %get-tuple-element.76, f32[1536]{0:T(1024)S(1)} %get-tuple-element.77, f32[1536]{0:T(1024)S(1)} %get-tuple-element.48, ...), kind=kLoop, calls=%fused_computation.380 | loop fusion | flops 35977728 | bytes 1560576 | tf_op jit(solution)/shard_map/reduce_sum | solution.py:110
  23.1 2.0 collective-permute-start.3
  25.1 1.8 collective-permute-done.3
  27.0 2.0 collective-permute-start.4
  29.0 24.6 %all-gather.4.cloned.1.call-done = bf16[512,1536]{1,0:T(8,128)(2,1)} async-done(((bf16[128,1536]{1,0:T(8,128)(2,1)}), bf16[512,1536]{1,0:T(8,128)(2,1)}) %all-gather.4.cloned.1.call-update) | async-done | bytes 1572880 | tf_op jit(solution)/shard_map/all_gather | solution.py:99
  53.6 3.3 %fusion.148 = f32[512,384]{1,0:T(8,128)} fusion(bf16[512,1536]{1,0:T(8,128)(2,1)} %all-gather.4.cloned.1.call-done, bf16[384,1536]{1,0:T(8,128)(2,1)S(1)} %copy-done), kind=kOutput, calls=%fused_computation.384 | convolution fusion | flops 603979776 | bytes 3538944 | tf_op jit(solution)/shard_map/fd,cd->fc/dot_general | solution.py:100
  57.1 3.5 %all-to-all-start.1 = ((f32[4,128,384]{2,1,0:T(8,128)}), f32[4,128,384]{2,1,0:T(8,128)S(1)}, u32[]{:S(2)}, u32[]{:S(2)}) async-start(f32[4,128,384]{2,1,0:T(8,128)} %bitcast.20), calls=%async_computation.1 | async-start | bytes 1572864 | tf_op jit(solution)/shard_map/all_to_all | solution.py:101
  60.8 2.0 collective-permute-start.5
  62.8 11.1 %collective-permute-done.5 = f32[2,1536]{1,0:T(2,128)S(1)} collective-permute-done((f32[2,1536]{1,0:T(2,128)S(1)}, f32[2,1536]{1,0:T(2,128)S(1)}, u32[]{:S(2)}, u32[]{:S(2)}) %collective-permute-start.5) | collective-permute-done | bytes 12320 | tf_op jit(solution)/shard_map/ppermute | solution.py:44
  74.0 4.7 %collective-permute-start.6 = (f32[2,1536]{1,0:T(2,128)S(1)}, f32[2,1536]{1,0:T(2,128)S(1)}, u32[]{:S(2)}, u32[]{:S(2)}) collective-permute-start(f32[2,1536]{1,0:T(2,128)S(1)} %pad_maximum_fusion.10), channel_id=1, source_target_pairs={{0,2},{1,3},{2,0},{3,1},{4,6},{5,7},{6,4},{7,5},{8,10},{9,11},{10,... | collective-permute-start | bytes 36872 | tf_op jit(solution)/shard_map/ppermute | solution.py:44
  78.6 2.8 %collective-permute-done.6 = f32[2,1536]{1,0:T(2,128)S(1)} collective-permute-done((f32[2,1536]{1,0:T(2,128)S(1)}, f32[2,1536]{1,0:T(2,128)S(1)}, u32[]{:S(2)}, u32[]{:S(2)}) %collective-permute-start.6) | collective-permute-done | bytes 12320 | tf_op jit(solution)/shard_map/ppermute | solution.py:44
  84.9 2.1 fusion.140
  89.8 2.2 %collective-permute-done.8 = f32[2,1536]{1,0:T(2,128)S(1)} collective-permute-done((f32[2,1536]{1,0:T(2,128)S(1)}, f32[2,1536]{1,0:T(2,128)S(1)}, u32[]{:S(2)}, u32[]{:S(2)}) %collective-permute-start.8) | collective-permute-done | bytes 12320 | tf_op jit(solution)/shard_map/ppermute | solution.py:34
  93.6 2.2 %collective-permute-done.9 = f32[2,1536]{1,0:T(2,128)S(1)} collective-permute-done((f32[2,1536]{1,0:T(2,128)S(1)}, f32[2,1536]{1,0:T(2,128)S(1)}, u32[]{:S(2)}, u32[]{:S(2)}) %collective-permute-start.9) | collective-permute-done | bytes 12320 | tf_op jit(solution)/shard_map/ppermute | solution.py:34
  95.9 3.7 %collective-permute-done.10 = f32[2,1536]{1,0:T(2,128)S(1)} collective-permute-done((f32[2,1536]{1,0:T(2,128)S(1)}, f32[2,1536]{1,0:T(2,128)S(1)}, u32[]{:S(2)}, u32[]{:S(2)}) %collective-permute-start.10) | collective-permute-done | bytes 12320 | tf_op jit(solution)/shard_map/ppermute | solution.py:34
  100.2 1.8 collective-permute-start.11
  103.7 1.8 copy.16
  105.5 4.3 %all-to-all-start = ((bf16[128,4,384]{2,0,1:T(8,128)(2,1)}), bf16[128,4,384]{2,0,1:T(8,128)(2,1)}, u32[]{:S(2)}, u32[]{:S(2)}) async-start(bf16[128,4,384]{2,0,1:T(8,128)(2,1)} %copy.16), calls=%async_computation | async-start | bytes 786432 | tf_op jit(solution)/shard_map/all_to_all | solution.py:127
  111.3 2.9 %fusion.64 = (f32[1536]{0:T(1024)S(1)}, f32[1536]{0:T(1024)S(1)}, f32[1536]{0:T(1024)S(1)}, f32[1536]{0:T(1024)S(1)}, f32[1536]{0:T(1024)S(1)}, /*index=5*/f32[1...) fusion(bf16[2,15,1536]{2,1,0:T(8,128)(2,1)} %copy-done.8, ...), kind=kLoop, calls=%fused_computation.192 | loop fusion | flops 12372480 | bytes 2537472 | tf_op jit(solution)/shard_map/reduce_sum | solution.py:146
  117.5 2.8 %stack.172 = f32[31,1536]{1,0:T(8,128)} concatenate(f32[1,1536]{1,0:T(1,128)S(1)} %stack.141, f32[1,1536]{1,0:T(1,128)S(1)} %stack.142, f32[1,1536]{1,0:T(1,128)S(1)} %stack.143, f32[1,1536]{1,0:T(1,128)S(1)} %stack.144, f32[1,1536]{1,0:T(1,128)S(1)} %stack.145, f32[1,1536]{1,0:T(1,128)S(1)} %stack.146, f32[1,1536]{1,0:T(1,128)S(1)} %stack.147, f32[1,1536]{1,0:T(1,128)S(1)} %stack.148, ...), dimensions={0} | concatenate | bytes 380928 | tf_op jit(solution)/shard_map/stack | solution.py:144
  120.3 8.7 %all-to-all-done = bf16[128,4,384]{2,0,1:T(8,128)(2,1)} async-done(((bf16[128,4,384]{2,0,1:T(8,128)(2,1)}), bf16[128,4,384]{2,0,1:T(8,128)(2,1)}, u32[]{:S(2)}, u32[]{:S(2)}) %all-to-all-start) | async-done | bytes 393248 | tf_op jit(solution)/shard_map/all_to_all | solution.py:127
  129.0 2.3 %fusion.147 = f32[384,1536]{1,0:T(8,128)S(1)} fusion(bf16[512,384]{1,0:T(8,128)(2,1)} %bitcast.1, bf16[512,1536]{1,0:T(8,128)(2,1)} %all-gather.4.cloned.1.call-done), kind=kOutput, calls=%fused_computation.383 | convolution fusion | flops 603979776 | bytes 4325376 | tf_op jit(solution)/shard_map/fc,fd->cd/dot_general | solution.py:128
  132.4 3.2 %collective-permute-done.20 = f32[192,1536]{1,0:T(8,128)} collective-permute-done((f32[192,1536]{1,0:T(8,128)}, f32[192,1536]{1,0:T(8,128)}, u32[]{:S(2)}, u32[]{:S(2)}) %collective-permute-start.20) | collective-permute-done | bytes 1179680 | tf_op jit(solution)/shard_map/ppermute | solution.py:65
  135.6 2.4 %dynamic-slice_add_fusion = f32[192,1536]{1,0:T(8,128)} fusion(f32[192,1536]{1,0:T(8,128)} %collective-permute-done.20, f32[384,1536]{1,0:T(8,128)S(1)} %fusion.147, s32[]{:T(128)S(6)} %select_n.65), kind=kLoop, calls=%fused_computation.94 | loop fusion | flops 294912 | bytes 3538948 | tf_op jit(solution)/shard_map/add | solution.py:65
  140.7 16.1 %all-gather.6.cloned.1.call-done = bf16[768,1536]{1,0:T(8,128)(2,1)} async-done(((bf16[192,1536]{1,0:T(8,128)(2,1)}), bf16[768,1536]{1,0:T(8,128)(2,1)}) %all-gather.6.cloned.1.call-update) | async-done | bytes 2359312 | tf_op jit(solution)/shard_map/all_gather | solution.py:81
  166.7 4.0 %collective-permute-done.22 = f32[48,1536]{1,0:T(8,128)S(1)} collective-permute-done((f32[48,1536]{1,0:T(8,128)S(1)}, f32[48,1536]{1,0:T(8,128)S(1)}, u32[]{:S(2)}, u32[]{:S(2)}) %collective-permute-start.22) | collective-permute-done | bytes 294944 | tf_op jit(solution)/shard_map/ppermute | solution.py:65
  172.7 4.1 %multiply_convert_fusion = (bf16[2,64,1536]{2,1,0:T(8,128)(2,1)S(1)}, f32[2,64,1536]{2,1,0:T(8,128)S(1)}) fusion(bf16[2,64,3072]{2,1,0:T(8,128)(2,1)S(1)} %copy-done.3, bf16[2,64,1536]{2,1,0:T(8,128)(2,1)S(1)} %copy-done.2, bf16[2,15,1536]{2,1,0:T(8,128)(2,1)S(1)} %collective-permute-done.19, f32[1536]{0:T(1024)S(1)} %copy-done.68, f32[1536]{0:T(1024)S(1)} %copy-done.70, ...), kind=kLoop, calls=%fused_computation.210 | loop fusion | flops 36962304 | bytes 2340864 | tf_op jit(solution)/shard_map/convert
  176.9 3.7 %collective-permute-done.23 = f32[48,1536]{1,0:T(8,128)S(1)} collective-permute-done((f32[48,1536]{1,0:T(8,128)S(1)}, f32[48,1536]{1,0:T(8,128)S(1)}, u32[]{:S(2)}, u32[]{:S(2)}) %collective-permute-start.23) | collective-permute-done | bytes 294944 | tf_op jit(solution)/shard_map/ppermute | solution.py:69
  184.1 7.6 %collective-permute-done.16 = f32[31,1536]{1,0:T(8,128)S(1)} collective-permute-done((f32[31,1536]{1,0:T(8,128)S(1)}, f32[31,1536]{1,0:T(8,128)S(1)}, u32[]{:S(2)}, u32[]{:S(2)}) %collective-permute-start.16) | collective-permute-done | bytes 190496 | tf_op jit(solution)/shard_map/ppermute | solution.py:34
  192.4 2.9 %collective-permute-done.24 = f32[96,1536]{1,0:T(8,128)S(1)} collective-permute-done((f32[96,1536]{1,0:T(8,128)S(1)}, f32[96,1536]{1,0:T(8,128)S(1)}, u32[]{:S(2)}, u32[]{:S(2)}) %collective-permute-start.24) | collective-permute-done | bytes 589856 | tf_op jit(solution)/shard_map/ppermute | solution.py:69
  198.3 1.6 maximum_select_fusion
  (273 shorter events, 43.6 us)
Async XLA Ops:
  7.2 46.4 %copy-start = (bf16[384,1536]{1,0:T(8,128)(2,1)S(1)}, bf16[384,1536]{1,0:T(8,128)(2,1)}, u32[]{:S(2)}) copy-start(bf16[384,1536]{1,0:T(8,128)(2,1)} %param.10) | copy-start | bytes 3538948
  7.2 46.4 %all-gather.4.cloned.1.call-start = ((), (), s32[]{:S(2)}) async-start(), calls=%async_computation.2 | async-start | bytes 1966080 | tf_op jit(solution)/shard_map/all_gather | solution.py:99
  8.7 7.7 %collective-permute-start.1 = (bf16[2,15,1536]{2,1,0:T(8,128)(2,1)S(1)}, bf16[2,15,1536]{2,1,0:T(8,128)(2,1)S(1)}, u32[]{:S(2)}, u32[]{:S(2)}) collective-permute-start(bf16[2,15,1536]{2,1,0:T(8,128)(2,1)S(1)} %get-tuple-element.104), channel_id=1, source_target_pairs={{1,0},{2,1},{3,2},{5,4},{6,5},{7,6},{9,8},{10,9},{11,10},{13,12},{... | collective-permute-start | bytes 276488 | tf_op jit(solution)/shard_map/ppermute | solution.py:17
  10.0 7.8 %collective-permute-start = (bf16[2,15,1536]{2,1,0:T(8,128)(2,1)S(1)}, bf16[2,15,1536]{2,1,0:T(8,128)(2,1)S(1)}, u32[]{:S(2)}, u32[]{:S(2)}) collective-permute-start(bf16[2,15,1536]{2,1,0:T(8,128)(2,1)S(1)} %get-tuple-element.103), channel_id=1, source_target_pairs={{0,1},{1,2},{2,3},{4,5},{5,6},{6,7},{8,9},{9,10},{10,11},{12,13},{... | collective-permute-start | bytes 276488 | tf_op jit(solution)/shard_map/ppermute | solution.py:16
  16.0 40.9 %copy-start.15 = (f32[1536]{0:T(1024)}, f32[1536]{0:T(1024)S(1)}, u32[]{:S(2)}) copy-start(f32[1536]{0:T(1024)S(1)} %get-tuple-element.50) | copy-start | bytes 18436
  21.8 1.2 collective-permute-start.2
  23.1 3.8 %collective-permute-start.3 = (f32[2,1536]{1,0:T(2,128)S(1)}, f32[2,1536]{1,0:T(2,128)S(1)}, u32[]{:S(2)}, u32[]{:S(2)}) collective-permute-start(f32[2,1536]{1,0:T(2,128)S(1)} %pad_maximum_fusion.7), channel_id=1, source_target_pairs={{0,8},{4,12},{8,0},{12,4},{16,24},{20,28},{24,16},{28,20},{1,9},{5... | collective-permute-start | bytes 36872 | tf_op jit(solution)/shard_map/ppermute | solution.py:44
  27.0 33.7 %collective-permute-start.4 = (f32[2,1536]{1,0:T(2,128)S(1)}, f32[2,1536]{1,0:T(2,128)S(1)}, u32[]{:S(2)}, u32[]{:S(2)}) collective-permute-start(f32[2,1536]{1,0:T(2,128)S(1)} %pad_maximum_fusion.8), channel_id=1, source_target_pairs={{0,16},{4,20},{8,24},{12,28},{16,0},{20,4},{24,8},{28,12},{1,17},{... | collective-permute-start | bytes 36872 | tf_op jit(solution)/shard_map/ppermute | solution.py:44
  57.1 25.0 %all-to-all-start.1 = ((f32[4,128,384]{2,1,0:T(8,128)}), f32[4,128,384]{2,1,0:T(8,128)S(1)}, u32[]{:S(2)}, u32[]{:S(2)}) async-start(f32[4,128,384]{2,1,0:T(8,128)} %bitcast.20), calls=%async_computation.1 | async-start | bytes 1572864 | tf_op jit(solution)/shard_map/all_to_all | solution.py:101
  60.6 96.2 %all-gather.6.cloned.1.call-start = ((), (), s32[]{:S(2)}) async-start(), calls=%async_computation.3 | async-start | bytes 2949120 | tf_op jit(solution)/shard_map/all_gather | solution.py:81
  60.8 13.1 %collective-permute-start.5 = (f32[2,1536]{1,0:T(2,128)S(1)}, f32[2,1536]{1,0:T(2,128)S(1)}, u32[]{:S(2)}, u32[]{:S(2)}) collective-permute-start(f32[2,1536]{1,0:T(2,128)S(1)} %pad_maximum_fusion.9), channel_id=1, source_target_pairs={{0,1},{1,0},{2,3},{3,2},{4,5},{5,4},{6,7},{7,6},{8,9},{9,8},{10,11... | collective-permute-start | bytes 36872 | tf_op jit(solution)/shard_map/ppermute | solution.py:44
  74.0 7.4 %collective-permute-start.6 = (f32[2,1536]{1,0:T(2,128)S(1)}, f32[2,1536]{1,0:T(2,128)S(1)}, u32[]{:S(2)}, u32[]{:S(2)}) collective-permute-start(f32[2,1536]{1,0:T(2,128)S(1)} %pad_maximum_fusion.10), channel_id=1, source_target_pairs={{0,2},{1,3},{2,0},{3,1},{4,6},{5,7},{6,4},{7,5},{8,10},{9,11},{10,... | collective-permute-start | bytes 36872 | tf_op jit(solution)/shard_map/ppermute | solution.py:44
  87.0 1.2 collective-permute-start.7
  88.3 3.8 %collective-permute-start.8 = (f32[2,1536]{1,0:T(2,128)S(1)}, f32[2,1536]{1,0:T(2,128)S(1)}, u32[]{:S(2)}, u32[]{:S(2)}) collective-permute-start(f32[2,1536]{1,0:T(2,128)S(1)} %fusion.139), channel_id=1, source_target_pairs={{0,8},{4,12},{8,0},{12,4},{16,24},{20,28},{24,16},{28,20},{1,9},{5... | collective-permute-start | bytes 36872 | tf_op jit(solution)/shard_map/ppermute | solution.py:34
  92.1 3.8 %collective-permute-start.9 = (f32[2,1536]{1,0:T(2,128)S(1)}, f32[2,1536]{1,0:T(2,128)S(1)}, u32[]{:S(2)}, u32[]{:S(2)}) collective-permute-start(f32[2,1536]{1,0:T(2,128)S(1)} %fusion.155), channel_id=1, source_target_pairs={{0,16},{4,20},{8,24},{12,28},{16,0},{20,4},{24,8},{28,12},{1,17},{... | collective-permute-start | bytes 36872 | tf_op jit(solution)/shard_map/ppermute | solution.py:34
  95.9 3.8 %collective-permute-start.10 = (f32[2,1536]{1,0:T(2,128)S(1)}, f32[2,1536]{1,0:T(2,128)S(1)}, u32[]{:S(2)}, u32[]{:S(2)}) collective-permute-start(f32[2,1536]{1,0:T(2,128)S(1)} %add.511), channel_id=1, source_target_pairs={{0,1},{1,0},{2,3},{3,2},{4,5},{5,4},{6,7},{7,6},{8,9},{9,8},{10,11... | collective-permute-start | bytes 36872 | tf_op jit(solution)/shard_map/ppermute | solution.py:34
  100.2 9.7 %collective-permute-start.11 = (f32[2,1536]{1,0:T(2,128)}, f32[2,1536]{1,0:T(2,128)}, u32[]{:S(2)}, u32[]{:S(2)}) collective-permute-start(f32[2,1536]{1,0:T(2,128)} %add.512), channel_id=1, source_target_pairs={{0,2},{1,3},{2,0},{3,1},{4,6},{5,7},{6,4},{7,5},{8,10},{9,11},{10,... | collective-permute-start | bytes 36872 | tf_op jit(solution)/shard_map/ppermute | solution.py:34
  105.5 23.4 %all-to-all-start = ((bf16[128,4,384]{2,0,1:T(8,128)(2,1)}), bf16[128,4,384]{2,0,1:T(8,128)(2,1)}, u32[]{:S(2)}, u32[]{:S(2)}) async-start(bf16[128,4,384]{2,0,1:T(8,128)(2,1)} %copy.16), calls=%async_computation | async-start | bytes 786432 | tf_op jit(solution)/shard_map/all_to_all | solution.py:127
  132.4 3.2 %collective-permute-start.20 = (f32[192,1536]{1,0:T(8,128)}, f32[192,1536]{1,0:T(8,128)}, u32[]{:S(2)}, u32[]{:S(2)}) collective-permute-start(f32[192,1536]{1,0:T(8,128)} %constant_dynamic-slice_fusion.2), channel_id=1, source_target_pairs={{0,4},{4,0},{8,12},{12,8},{16,20},{20,16},{24,28},{28,24},{1,5},{5... | collective-permute-start | bytes 3538952 | tf_op jit(solution)/shard_map/ppermute | solution.py:65
  139.1 20.3 %collective-permute-start.21 = (f32[96,1536]{1,0:T(8,128)S(1)}, f32[96,1536]{1,0:T(8,128)S(1)}, u32[]{:S(2)}, u32[]{:S(2)}) collective-permute-start(f32[96,1536]{1,0:T(8,128)S(1)} %constant_dynamic-slice_fusion.1), channel_id=1, source_target_pairs={{0,8},{4,12},{8,0},{12,4},{16,24},{20,28},{24,16},{28,20},{1,9},{5... | collective-permute-start | bytes 1769480 | tf_op jit(solution)/shard_map/ppermute | solution.py:65
  140.7 16.2 %collective-permute-start.12 = (f32[31,1536]{1,0:T(8,128)}, f32[31,1536]{1,0:T(8,128)S(1)}, u32[]{:S(2)}, u32[]{:S(2)}) collective-permute-start(f32[31,1536]{1,0:T(8,128)} %stack.172), channel_id=1, source_target_pairs={{0,4},{4,0},{8,12},{12,8},{16,20},{20,16},{24,28},{28,24},{1,5},{5... | collective-permute-start | bytes 571400 | tf_op jit(solution)/shard_map/ppermute | solution.py:34
  156.8 38.6 %collective-permute-start.17 = (bf16[4,192,1536]{2,1,0:T(8,128)(2,1)}, bf16[4,192,1536]{2,1,0:T(8,128)(2,1)S(1)}, u32[]{:S(2)}, u32[]{:S(2)}) collective-permute-start(bf16[4,192,1536]{2,1,0:T(8,128)(2,1)} %bitcast.18), channel_id=1, source_target_pairs={{0,4},{4,0},{8,12},{12,8},{16,20},{20,16},{24,28},{28,24},{1,5},{5... | collective-permute-start | bytes 7077896 | tf_op jit(solution)/shard_map/ppermute | solution.py:82
  157.8 7.4 %collective-permute-start.13 = (f32[31,1536]{1,0:T(8,128)S(1)}, f32[31,1536]{1,0:T(8,128)S(1)}, u32[]{:S(2)}, u32[]{:S(2)}) collective-permute-start(f32[31,1536]{1,0:T(8,128)S(1)} %add.514), channel_id=1, source_target_pairs={{0,8},{4,12},{8,0},{12,4},{16,24},{20,28},{24,16},{28,20},{1,9},{5... | collective-permute-start | bytes 571400 | tf_op jit(solution)/shard_map/ppermute | solution.py:34
  160.9 9.9 %collective-permute-start.22 = (f32[48,1536]{1,0:T(8,128)S(1)}, f32[48,1536]{1,0:T(8,128)S(1)}, u32[]{:S(2)}, u32[]{:S(2)}) collective-permute-start(f32[48,1536]{1,0:T(8,128)S(1)} %constant_dynamic-slice_fusion), channel_id=1, source_target_pairs={{0,16},{4,20},{8,24},{12,28},{16,0},{20,4},{24,8},{28,12},{1,17},{... | collective-permute-start | bytes 884744 | tf_op jit(solution)/shard_map/ppermute | solution.py:65
  162.4 9.9 %collective-permute-start.19 = (bf16[2,15,1536]{2,1,0:T(8,128)(2,1)S(1)}, bf16[2,15,1536]{2,1,0:T(8,128)(2,1)S(1)}, u32[]{:S(2)}, u32[]{:S(2)}) collective-permute-start(bf16[2,15,1536]{2,1,0:T(8,128)(2,1)S(1)} %get-tuple-element.102), channel_id=1, source_target_pairs={{0,1},{1,2},{2,3},{4,5},{5,6},{6,7},{8,9},{9,10},{10,11},{12,13},{... | collective-permute-start | bytes 276488 | tf_op jit(solution)/shard_map/ppermute | solution.py:16
  163.7 8.6 %collective-permute-start.18 = (bf16[2,15,1536]{2,1,0:T(8,128)(2,1)S(1)}, bf16[2,15,1536]{2,1,0:T(8,128)(2,1)S(1)}, u32[]{:S(2)}, u32[]{:S(2)}) collective-permute-start(bf16[2,15,1536]{2,1,0:T(8,128)(2,1)S(1)} %get-tuple-element.101), channel_id=1, source_target_pairs={{1,0},{2,1},{3,2},{5,4},{6,5},{7,6},{9,8},{10,9},{11,10},{13,12},{... | collective-permute-start | bytes 276488 | tf_op jit(solution)/shard_map/ppermute | solution.py:17
  165.2 11.5 %collective-permute-start.14 = (f32[31,1536]{1,0:T(8,128)S(1)}, f32[31,1536]{1,0:T(8,128)S(1)}, u32[]{:S(2)}, u32[]{:S(2)}) collective-permute-start(f32[31,1536]{1,0:T(8,128)S(1)} %add.515), channel_id=1, source_target_pairs={{0,16},{4,20},{8,24},{12,28},{16,0},{20,4},{24,8},{28,12},{1,17},{... | collective-permute-start | bytes 571400 | tf_op jit(solution)/shard_map/ppermute | solution.py:34
  170.8 9.7 %collective-permute-start.23 = (f32[48,1536]{1,0:T(8,128)S(1)}, f32[48,1536]{1,0:T(8,128)S(1)}, u32[]{:S(2)}, u32[]{:S(2)}) collective-permute-start(f32[48,1536]{1,0:T(8,128)S(1)} %dynamic-slice_add_fusion.2), channel_id=1, source_target_pairs={{0,16},{4,20},{8,24},{12,28},{16,0},{20,4},{24,8},{28,12},{1,17},{... | collective-permute-start | bytes 884744 | tf_op jit(solution)/shard_map/ppermute | solution.py:69
  176.8 5.7 %collective-permute-start.15 = (f32[31,1536]{1,0:T(8,128)S(1)}, f32[31,1536]{1,0:T(8,128)S(1)}, u32[]{:S(2)}, u32[]{:S(2)}) collective-permute-start(f32[31,1536]{1,0:T(8,128)S(1)} %add.516), channel_id=1, source_target_pairs={{0,1},{1,0},{2,3},{3,2},{4,5},{5,4},{6,7},{7,6},{8,9},{9,8},{10,11... | collective-permute-start | bytes 571400 | tf_op jit(solution)/shard_map/ppermute | solution.py:34
  180.6 14.6 %collective-permute-start.24 = (f32[96,1536]{1,0:T(8,128)S(1)}, f32[96,1536]{1,0:T(8,128)S(1)}, u32[]{:S(2)}, u32[]{:S(2)}) collective-permute-start(f32[96,1536]{1,0:T(8,128)S(1)} %maximum_select_fusion.2), channel_id=1, source_target_pairs={{0,8},{4,12},{8,0},{12,4},{16,24},{20,28},{24,16},{28,20},{1,9},{5... | collective-permute-start | bytes 1769480 | tf_op jit(solution)/shard_map/ppermute | solution.py:69
  182.5 9.1 %collective-permute-start.16 = (f32[31,1536]{1,0:T(8,128)S(1)}, f32[31,1536]{1,0:T(8,128)S(1)}, u32[]{:S(2)}, u32[]{:S(2)}) collective-permute-start(f32[31,1536]{1,0:T(8,128)S(1)} %add.517), channel_id=1, source_target_pairs={{0,2},{1,3},{2,0},{3,1},{4,6},{5,7},{6,4},{7,5},{8,10},{9,11},{10,... | collective-permute-start | bytes 571400 | tf_op jit(solution)/shard_map/ppermute | solution.py:34
  195.3 3.0 %collective-permute-start.25 = (f32[192,1536]{1,0:T(8,128)S(1)}, f32[192,1536]{1,0:T(8,128)S(1)}, u32[]{:S(2)}, u32[]{:S(2)}) collective-permute-start(f32[192,1536]{1,0:T(8,128)S(1)} %maximum_select_fusion.1), channel_id=1, source_target_pairs={{0,4},{4,0},{8,12},{12,8},{16,20},{20,16},{24,28},{28,24},{1,5},{5... | collective-permute-start | bytes 3538952 | tf_op jit(solution)/shard_map/ppermute | solution.py:69
  (72 other events, 1651.5 us)
Sparse Core Ops, SparseCore 0:
  15.8 37.7 all-gather.3
  103.0 53.7 all-gather.5

commit v9 on v5

--- a/solution.py
+++ b/solution.py
@@ -97,9 +97,6 @@
     everyone = local * lax.axis_size("dp") * peers
     flat_grad = out_grad.reshape(-1, width)
     group_grad = lax.all_gather(flat_grad, "tensor", axis=0, tiled=True)
-    own_columns = jnp.einsum("fd,cd->fc", group_grad, proj_weight, preferred_element_type=jnp.float32)
-    grad_act = lax.all_to_all(own_columns, "tensor", split_axis=0, concat_axis=1, tiled=True)
-    grad_act = grad_act.reshape(out_grad.shape)
     values = glu_input[..., :width].astype(jnp.float32)
     gates = jax.nn.sigmoid(glu_input[..., width:].astype(jnp.float32))
     gated = (values * gates).astype(jnp.bfloat16)
@@ -117,6 +114,10 @@
         average = lax.psum(jnp.sum(conv_out, axis=(0, 1)), ("dp", "tensor")) / everyone
         centred0 = conv_out - average
         variance = lax.psum(jnp.sum(centred0 * centred0, axis=(0, 1)), ("dp", "tensor")) / everyone
+    group_grad, average = lax.optimization_barrier((group_grad, average))
+    own_columns = jnp.einsum("fd,cd->fc", group_grad, proj_weight, preferred_element_type=jnp.float32)
+    grad_act = lax.all_to_all(own_columns, "tensor", split_axis=0, concat_axis=1, tiled=True)
+    grad_act = grad_act.reshape(out_grad.shape)
     centred = conv_out - average
     inverse = lax.rsqrt(variance + epsilon)
     normed = centred * inverse

time: 203 us -> 199 us (0.980)
  blocking collectives: 0 us -> 22.6 us
  waiting for transfers between devices: 92.3 us -> 75.9 us
  starting transfers between devices: 44.1 us -> 35.7 us
    all_to_all x0 -> x1, blocking collectives: none -> 22.6 us  [on_device(): lax.all_to_all(own_columns, 'tensor', split_axis=0, concat_axis=1, tiled=...]
    all_gather x1, waiting for transfers between devices: 17.3 us -> 3.67 us  [on_device(): group_grad = lax.all_gather(flat_grad, 'tensor', axis=0, tiled=True)]
    all_gather x1, waiting for transfers between devices: 16.2 us -> 21.6 us  [gather_weight(): held = lax.all_gather(mine, 'tensor', axis=0, tiled=False)]
    ppermute x5, waiting for transfers between devices: 17.3 us -> 13.1 us  [all_moments(): lax.ppermute(jnp.stack([mean, spread]), axis, [(i, i ^ step) for i in ran...]
    all_to_all x1, waiting for transfers between devices: 8.66 us -> 4.62 us  [on_device(): lax.all_to_all(flat_act, 'tensor', split_axis=1, concat_axis=0, tiled=True)]
    all_to_all x1 -> x0, starting transfers between devices: 3.51 us -> none  [on_device(): lax.all_to_all(own_columns, 'tensor', split_axis=0, concat_axis=1, tiled=...]
    ppermute x5, starting transfers between devices: 9.87 us -> 6.55 us  [all_moments(): lax.ppermute(jnp.stack([mean, spread]), axis, [(i, i ^ step) for i in ran...]
  transfers between devices with their start and end apart: 30 -> 29, of which waited for: 19 -> 20; matrix products, arithmetic and copies ran while one was open for 20% -> 17% of each run, Pallas kernels for 0% -> 0%
where the time goes in v9:
time: 199 us; the launch traced here: 198 us
  waiting for transfers between devices  75.9 us (38%)
  starting transfers between devices  35.7 us (18%)
  other arithmetic  28.3 us (14%)
  blocking collectives  22.6 us (11%)
  between operations  15.7 us (8%)
  local copies, waits for them, and re-layouts  13.3 us (7%)
  matrix products  6.27 us (3%)
    all_to_all x1, blocking collectives, on_device(): lax.all_to_all(own_columns, 'tensor', split_axis=0, concat_axis=1, tiled=...  22.6 us
    all_gather x1, waiting for transfers between devices, gather_weight(): held = lax.all_gather(mine, 'tensor', axis=0, tiled=False)  21.6 us
    ppermute x10, waiting for transfers between devices, all_sum(): x = x + lax.ppermute(x, axis, [(i, i ^ step) for i in range(peers)])  18 us
    ppermute x5, waiting for transfers between devices, all_moments(): lax.ppermute(jnp.stack([mean, spread]), axis, [(i, i ^ step) for i in ran...  13.1 us
    ppermute x2, starting transfers between devices, extended(): before = lax.ppermute(last, axis, up)  9.48 us
    ppermute x10, starting transfers between devices, all_sum(): x = x + lax.ppermute(x, axis, [(i, i ^ step) for i in range(peers)])  7.11 us
    ppermute x5, starting transfers between devices, all_moments(): lax.ppermute(jnp.stack([mean, spread]), axis, [(i, i ^ step) for i in ran...  6.55 us
    reduce_sum x4, other arithmetic, on_device(): jnp.sum(padded[:, offset:offset + frames, :].astype(jnp.float32) * grad_w...  5.72 us
  transfers between devices with their start and end apart: 29, of which 20 were waited for; matrix products, arithmetic and copies ran while one was open for 17% of the time, Pallas kernels for 0%

profile of v9, /device:TPU:0, one launch (start us, length us, event | category | flops | bytes accessed | tf_op | source)
XLA Modules:
  0.0 197.8 jit_solution(1856512601801711607)
XLA Ops:
  9.3 4.9 %collective-permute-start = (bf16[2,15,1536]{2,1,0:T(8,128)(2,1)S(1)}, bf16[2,15,1536]{2,1,0:T(8,128)(2,1)S(1)}, u32[]{:S(2)}, u32[]{:S(2)}) collective-permute-start(bf16[2,15,1536]{2,1,0:T(8,128)(2,1)S(1)} %get-tuple-element.103), channel_id=1, source_target_pairs={{0,1},{1,2},{2,3},{4,5},{5,6},{6,7},{8,9},{9,10},{10,11},{12,13},{... | collective-permute-start | bytes 276488 | tf_op jit(solution)/shard_map/ppermute | solution.py:16
  16.5 4.3 %collective-permute-done.1 = bf16[2,15,1536]{2,1,0:T(8,128)(2,1)S(1)} collective-permute-done((bf16[2,15,1536]{2,1,0:T(8,128)(2,1)S(1)}, bf16[2,15,1536]{2,1,0:T(8,128)(2,1)S(1)}, u32[]{:S(2)}, u32[]{:S(2)}) %collective-permute-start.1) | collective-permute-done | bytes 92192 | tf_op jit(solution)/shard_map/ppermute | solution.py:17
  21.4 3.8 %fusion.143 = (f32[1536]{0:T(1024)S(1)}, f32[2,64,1536]{2,1,0:T(8,128)S(1)}) fusion(bf16[2,15,1536]{2,1,0:T(8,128)(2,1)S(1)} %collective-permute-done.1, bf16[2,64,1536]{2,1,0:T(8,128)(2,1)S(1)} %fusion, f32[1536]{0:T(1024)S(1)} %get-tuple-element.76, f32[1536]{0:T(1024)S(1)} %get-tuple-element.77, f32[1536]{0:T(1024)S(1)} %get-tuple-element.48, ...), kind=kLoop, calls=%fused_computation.380 | loop fusion | flops 35977728 | bytes 1560576 | tf_op jit(solution)/shard_map/reduce_sum | solution.py:107
  28.3 2.2 %collective-permute-done.3 = f32[2,1536]{1,0:T(2,128)S(1)} collective-permute-done((f32[2,1536]{1,0:T(2,128)S(1)}, f32[2,1536]{1,0:T(2,128)S(1)}, u32[]{:S(2)}, u32[]{:S(2)}) %collective-permute-start.3) | collective-permute-done | bytes 12320 | tf_op jit(solution)/shard_map/ppermute | solution.py:44
  30.6 1.6 collective-permute-start.4
  32.2 2.2 %collective-permute-done.4 = f32[2,1536]{1,0:T(2,128)S(1)} collective-permute-done((f32[2,1536]{1,0:T(2,128)S(1)}, f32[2,1536]{1,0:T(2,128)S(1)}, u32[]{:S(2)}, u32[]{:S(2)}) %collective-permute-start.4) | collective-permute-done | bytes 12320 | tf_op jit(solution)/shard_map/ppermute | solution.py:44
  34.4 1.6 collective-permute-start.5
  36.1 3.3 %collective-permute-done.5 = f32[2,1536]{1,0:T(2,128)S(1)} collective-permute-done((f32[2,1536]{1,0:T(2,128)S(1)}, f32[2,1536]{1,0:T(2,128)S(1)}, u32[]{:S(2)}, u32[]{:S(2)}) %collective-permute-start.5) | collective-permute-done | bytes 12320 | tf_op jit(solution)/shard_map/ppermute | solution.py:44
  39.5 1.7 collective-permute-start.6
  41.2 4.3 %collective-permute-done.6 = f32[2,1536]{1,0:T(2,128)S(1)} collective-permute-done((f32[2,1536]{1,0:T(2,128)S(1)}, f32[2,1536]{1,0:T(2,128)S(1)}, u32[]{:S(2)}, u32[]{:S(2)}) %collective-permute-start.6) | collective-permute-done | bytes 12320 | tf_op jit(solution)/shard_map/ppermute | solution.py:44
  46.3 3.7 %all-gather.4.cloned.1.call-done = bf16[512,1536]{1,0:T(8,128)(2,1)} async-done(((bf16[128,1536]{1,0:T(8,128)(2,1)}), bf16[512,1536]{1,0:T(8,128)(2,1)}) %all-gather.4.cloned.1.call-update) | async-done | bytes 1572880 | tf_op jit(solution)/shard_map/all_gather | solution.py:99
  50.0 2.4 %fusion.147 = f32[512,384]{1,0:T(8,128)S(1)} fusion(bf16[512,1536]{1,0:T(8,128)(2,1)} %all-gather.4.cloned.1.call-done, bf16[384,1536]{1,0:T(8,128)(2,1)S(1)} %copy-done), kind=kOutput, calls=%fused_computation.383 | convolution fusion | flops 603979776 | bytes 3538944 | tf_op jit(solution)/shard_map/fd,cd->fc/dot_general | solution.py:118
  52.4 22.6 %all_to_all.35 = f32[4,128,384]{2,1,0:T(8,128)S(1)} all-to-all(f32[4,128,384]{2,1,0:T(8,128)S(1)} %bitcast.21), channel_id=1, replica_groups=mesh['dp'=8,'tensor'=4] {'tensor'}, dimensions={0} | all-to-all | bytes 1572864 | tf_op jit(solution)/shard_map/all_to_all | solution.py:119
  76.8 1.6 fusion.140
  81.3 2.2 %collective-permute-done.9 = f32[2,1536]{1,0:T(2,128)S(1)} collective-permute-done((f32[2,1536]{1,0:T(2,128)S(1)}, f32[2,1536]{1,0:T(2,128)S(1)}, u32[]{:S(2)}, u32[]{:S(2)}) %collective-permute-start.9) | collective-permute-done | bytes 12320 | tf_op jit(solution)/shard_map/ppermute | solution.py:34
  85.1 2.2 %collective-permute-done.10 = f32[2,1536]{1,0:T(2,128)S(1)} collective-permute-done((f32[2,1536]{1,0:T(2,128)S(1)}, f32[2,1536]{1,0:T(2,128)S(1)}, u32[]{:S(2)}, u32[]{:S(2)}) %collective-permute-start.10) | collective-permute-done | bytes 12320 | tf_op jit(solution)/shard_map/ppermute | solution.py:34
  88.1 3.8 %collective-permute-done.11 = f32[2,1536]{1,0:T(2,128)} collective-permute-done((f32[2,1536]{1,0:T(2,128)}, f32[2,1536]{1,0:T(2,128)}, u32[]{:S(2)}, u32[]{:S(2)}) %collective-permute-start.11) | collective-permute-done | bytes 12320 | tf_op jit(solution)/shard_map/ppermute | solution.py:34
  95.2 1.8 copy.17
  97.0 4.0 %all-to-all-start.1 = ((bf16[128,4,384]{2,0,1:T(8,128)(2,1)}), bf16[128,4,384]{2,0,1:T(8,128)(2,1)S(1)}, u32[]{:S(2)}, u32[]{:S(2)}) async-start(bf16[128,4,384]{2,0,1:T(8,128)(2,1)} %copy.17), calls=%async_computation.1 | async-start | bytes 786432 | tf_op jit(solution)/shard_map/all_to_all | solution.py:128
  101.8 2.9 %fusion.80 = (f32[1536]{0:T(1024)S(1)}, f32[1536]{0:T(1024)S(1)}, f32[1536]{0:T(1024)S(1)}, f32[1536]{0:T(1024)S(1)}, f32[1536]{0:T(1024)S(1)}, /*index=5*/f32[1...) fusion(bf16[2,15,1536]{2,1,0:T(8,128)(2,1)} %copy-done.9, ...), kind=kLoop, calls=%fused_computation.208 | loop fusion | flops 12372480 | bytes 2537472 | tf_op jit(solution)/shard_map/reduce_sum | solution.py:147
  108.1 2.8 %stack.172 = f32[31,1536]{1,0:T(8,128)} concatenate(f32[1,1536]{1,0:T(1,128)S(1)} %stack.141, f32[1,1536]{1,0:T(1,128)S(1)} %stack.142, f32[1,1536]{1,0:T(1,128)S(1)} %stack.143, f32[1,1536]{1,0:T(1,128)S(1)} %stack.144, f32[1,1536]{1,0:T(1,128)S(1)} %stack.145, f32[1,1536]{1,0:T(1,128)S(1)} %stack.146, f32[1,1536]{1,0:T(1,128)S(1)} %stack.147, f32[1,1536]{1,0:T(1,128)S(1)} %stack.148, ...), dimensions={0} | concatenate | bytes 380928 | tf_op jit(solution)/shard_map/stack | solution.py:145
  110.8 4.6 %all-to-all-done.1 = bf16[128,4,384]{2,0,1:T(8,128)(2,1)S(1)} async-done(((bf16[128,4,384]{2,0,1:T(8,128)(2,1)}), bf16[128,4,384]{2,0,1:T(8,128)(2,1)S(1)}, u32[]{:S(2)}, u32[]{:S(2)}) %all-to-all-start.1) | async-done | bytes 393248 | tf_op jit(solution)/shard_map/all_to_all | solution.py:128
  116.2 2.3 %fusion.148 = f32[384,1536]{1,0:T(8,128)S(1)} fusion(bf16[512,384]{1,0:T(8,128)(2,1)} %bitcast.20, bf16[512,1536]{1,0:T(8,128)(2,1)} %all-gather.4.cloned.1.call-done), kind=kOutput, calls=%fused_computation.384 | convolution fusion | flops 603979776 | bytes 4325376 | tf_op jit(solution)/shard_map/fc,fd->cd/dot_general | solution.py:129
  119.7 3.2 %collective-permute-done.15 = f32[192,1536]{1,0:T(8,128)} collective-permute-done((f32[192,1536]{1,0:T(8,128)}, f32[192,1536]{1,0:T(8,128)}, u32[]{:S(2)}, u32[]{:S(2)}) %collective-permute-start.15) | collective-permute-done | bytes 1179680 | tf_op jit(solution)/shard_map/ppermute | solution.py:65
  126.9 21.6 %all-gather.6.cloned.1.call-done = bf16[768,1536]{1,0:T(8,128)(2,1)} async-done(((bf16[192,1536]{1,0:T(8,128)(2,1)}), bf16[768,1536]{1,0:T(8,128)(2,1)}) %all-gather.6.cloned.1.call-update) | async-done | bytes 2359312 | tf_op jit(solution)/shard_map/all_gather | solution.py:81
  155.4 4.6 %collective-permute-start.14 = (bf16[2,15,1536]{2,1,0:T(8,128)(2,1)S(1)}, bf16[2,15,1536]{2,1,0:T(8,128)(2,1)S(1)}, u32[]{:S(2)}, u32[]{:S(2)}) collective-permute-start(bf16[2,15,1536]{2,1,0:T(8,128)(2,1)S(1)} %get-tuple-element.102), channel_id=1, source_target_pairs={{0,1},{1,2},{2,3},{4,5},{5,6},{6,7},{8,9},{9,10},{10,11},{12,13},{... | collective-permute-start | bytes 276488 | tf_op jit(solution)/shard_map/ppermute | solution.py:16
  161.7 2.1 %collective-permute-start.18 = (f32[48,1536]{1,0:T(8,128)S(1)}, f32[48,1536]{1,0:T(8,128)S(1)}, u32[]{:S(2)}, u32[]{:S(2)}) collective-permute-start(f32[48,1536]{1,0:T(8,128)S(1)} %dynamic-slice_add_fusion.2), channel_id=1, source_target_pairs={{0,16},{4,20},{8,24},{12,28},{16,0},{20,4},{24,8},{28,12},{1,17},{... | collective-permute-start | bytes 884744 | tf_op jit(solution)/shard_map/ppermute | solution.py:69
  164.1 4.1 %multiply_convert_fusion = (bf16[2,64,1536]{2,1,0:T(8,128)(2,1)S(1)}, f32[2,64,1536]{2,1,0:T(8,128)S(1)}) fusion(bf16[2,64,3072]{2,1,0:T(8,128)(2,1)S(1)} %copy-done.3, bf16[2,64,1536]{2,1,0:T(8,128)(2,1)S(1)} %copy-done.2, bf16[2,15,1536]{2,1,0:T(8,128)(2,1)S(1)} %collective-permute-done.14, f32[1536]{0:T(1024)S(1)} %copy-done.69, f32[1536]{0:T(1024)S(1)} %copy-done.71, ...), kind=kLoop, calls=%fused_computation.210 | loop fusion | flops 36962304 | bytes 2340864 | tf_op jit(solution)/shard_map/convert
  169.0 3.6 %collective-permute-done.18 = f32[48,1536]{1,0:T(8,128)S(1)} collective-permute-done((f32[48,1536]{1,0:T(8,128)S(1)}, f32[48,1536]{1,0:T(8,128)S(1)}, u32[]{:S(2)}, u32[]{:S(2)}) %collective-permute-start.18) | collective-permute-done | bytes 294944 | tf_op jit(solution)/shard_map/ppermute | solution.py:69
  175.6 8.1 %collective-permute-done.25 = f32[31,1536]{1,0:T(8,128)S(1)} collective-permute-done((f32[31,1536]{1,0:T(8,128)S(1)}, f32[31,1536]{1,0:T(8,128)S(1)}, u32[]{:S(2)}, u32[]{:S(2)}) %collective-permute-start.25) | collective-permute-done | bytes 190496 | tf_op jit(solution)/shard_map/ppermute | solution.py:34
  184.4 1.9 collective-permute-done.19
  189.4 1.6 maximum_select_fusion
  (274 shorter events, 44.4 us)
Async XLA Ops:
  7.2 42.8 %all-gather.4.cloned.1.call-start = ((), (), s32[]{:S(2)}) async-start(), calls=%async_computation.2 | async-start | bytes 1966080 | tf_op jit(solution)/shard_map/all_gather | solution.py:99
  7.9 140.6 %all-gather.6.cloned.1.call-start = ((), (), s32[]{:S(2)}) async-start(), calls=%async_computation.3 | async-start | bytes 2949120 | tf_op jit(solution)/shard_map/all_gather | solution.py:81
  9.3 7.1 %collective-permute-start = (bf16[2,15,1536]{2,1,0:T(8,128)(2,1)S(1)}, bf16[2,15,1536]{2,1,0:T(8,128)(2,1)S(1)}, u32[]{:S(2)}, u32[]{:S(2)}) collective-permute-start(bf16[2,15,1536]{2,1,0:T(8,128)(2,1)S(1)} %get-tuple-element.103), channel_id=1, source_target_pairs={{0,1},{1,2},{2,3},{4,5},{5,6},{6,7},{8,9},{9,10},{10,11},{12,13},{... | collective-permute-start | bytes 276488 | tf_op jit(solution)/shard_map/ppermute | solution.py:16
  14.3 6.5 %collective-permute-start.1 = (bf16[2,15,1536]{2,1,0:T(8,128)(2,1)S(1)}, bf16[2,15,1536]{2,1,0:T(8,128)(2,1)S(1)}, u32[]{:S(2)}, u32[]{:S(2)}) collective-permute-start(bf16[2,15,1536]{2,1,0:T(8,128)(2,1)S(1)} %get-tuple-element.104), channel_id=1, source_target_pairs={{1,0},{2,1},{3,2},{5,4},{6,5},{7,6},{9,8},{10,9},{11,10},{13,12},{... | collective-permute-start | bytes 276488 | tf_op jit(solution)/shard_map/ppermute | solution.py:17
  16.4 58.7 %copy-start.62 = (f32[1536]{0:T(1024)}, f32[1536]{0:T(1024)S(1)}, u32[]{:S(2)}) copy-start(f32[1536]{0:T(1024)S(1)} %get-tuple-element.73) | copy-start | bytes 18436
  16.4 58.7 %copy-start.64 = (f32[1536]{0:T(1024)}, f32[1536]{0:T(1024)S(1)}, u32[]{:S(2)}) copy-start(f32[1536]{0:T(1024)S(1)} %get-tuple-element.74) | copy-start | bytes 18436
  16.4 58.7 %copy-start.66 = (f32[1536]{0:T(1024)}, f32[1536]{0:T(1024)S(1)}, u32[]{:S(2)}) copy-start(f32[1536]{0:T(1024)S(1)} %get-tuple-element.75) | copy-start | bytes 18436
  25.5 1.2 collective-permute-start.2
  26.8 3.8 %collective-permute-start.3 = (f32[2,1536]{1,0:T(2,128)S(1)}, f32[2,1536]{1,0:T(2,128)S(1)}, u32[]{:S(2)}, u32[]{:S(2)}) collective-permute-start(f32[2,1536]{1,0:T(2,128)S(1)} %pad_maximum_fusion.7), channel_id=1, source_target_pairs={{0,8},{4,12},{8,0},{12,4},{16,24},{20,28},{24,16},{28,20},{1,9},{5... | collective-permute-start | bytes 36872 | tf_op jit(solution)/shard_map/ppermute | solution.py:44
  30.6 3.8 %collective-permute-start.4 = (f32[2,1536]{1,0:T(2,128)S(1)}, f32[2,1536]{1,0:T(2,128)S(1)}, u32[]{:S(2)}, u32[]{:S(2)}) collective-permute-start(f32[2,1536]{1,0:T(2,128)S(1)} %pad_maximum_fusion.8), channel_id=1, source_target_pairs={{0,16},{4,20},{8,24},{12,28},{16,0},{20,4},{24,8},{28,12},{1,17},{... | collective-permute-start | bytes 36872 | tf_op jit(solution)/shard_map/ppermute | solution.py:44
  34.4 5.0 %collective-permute-start.5 = (f32[2,1536]{1,0:T(2,128)S(1)}, f32[2,1536]{1,0:T(2,128)S(1)}, u32[]{:S(2)}, u32[]{:S(2)}) collective-permute-start(f32[2,1536]{1,0:T(2,128)S(1)} %pad_maximum_fusion.9), channel_id=1, source_target_pairs={{0,1},{1,0},{2,3},{3,2},{4,5},{5,4},{6,7},{7,6},{8,9},{9,8},{10,11... | collective-permute-start | bytes 36872 | tf_op jit(solution)/shard_map/ppermute | solution.py:44
  39.5 6.0 %collective-permute-start.6 = (f32[2,1536]{1,0:T(2,128)S(1)}, f32[2,1536]{1,0:T(2,128)S(1)}, u32[]{:S(2)}, u32[]{:S(2)}) collective-permute-start(f32[2,1536]{1,0:T(2,128)S(1)} %pad_maximum_fusion.10), channel_id=1, source_target_pairs={{0,2},{1,3},{2,0},{3,1},{4,6},{5,7},{6,4},{7,5},{8,10},{9,11},{10,... | collective-permute-start | bytes 36872 | tf_op jit(solution)/shard_map/ppermute | solution.py:44
  78.5 1.2 collective-permute-start.8
  79.8 3.8 %collective-permute-start.9 = (f32[2,1536]{1,0:T(2,128)S(1)}, f32[2,1536]{1,0:T(2,128)S(1)}, u32[]{:S(2)}, u32[]{:S(2)}) collective-permute-start(f32[2,1536]{1,0:T(2,128)S(1)} %fusion.139), channel_id=1, source_target_pairs={{0,8},{4,12},{8,0},{12,4},{16,24},{20,28},{24,16},{28,20},{1,9},{5... | collective-permute-start | bytes 36872 | tf_op jit(solution)/shard_map/ppermute | solution.py:34
  83.5 3.8 %collective-permute-start.10 = (f32[2,1536]{1,0:T(2,128)S(1)}, f32[2,1536]{1,0:T(2,128)S(1)}, u32[]{:S(2)}, u32[]{:S(2)}) collective-permute-start(f32[2,1536]{1,0:T(2,128)S(1)} %fusion.155), channel_id=1, source_target_pairs={{0,16},{4,20},{8,24},{12,28},{16,0},{20,4},{24,8},{28,12},{1,17},{... | collective-permute-start | bytes 36872 | tf_op jit(solution)/shard_map/ppermute | solution.py:34
  87.9 4.0 %collective-permute-start.11 = (f32[2,1536]{1,0:T(2,128)}, f32[2,1536]{1,0:T(2,128)}, u32[]{:S(2)}, u32[]{:S(2)}) collective-permute-start(f32[2,1536]{1,0:T(2,128)} %add.496), channel_id=1, source_target_pairs={{0,1},{1,0},{2,3},{3,2},{4,5},{5,4},{6,7},{7,6},{8,9},{9,8},{10,11... | collective-permute-start | bytes 36872 | tf_op jit(solution)/shard_map/ppermute | solution.py:34
  93.3 7.7 %collective-permute-start.12 = (f32[2,1536]{1,0:T(2,128)}, f32[2,1536]{1,0:T(2,128)}, u32[]{:S(2)}, u32[]{:S(2)}) collective-permute-start(f32[2,1536]{1,0:T(2,128)} %add.497), channel_id=1, source_target_pairs={{0,2},{1,3},{2,0},{3,1},{4,6},{5,7},{6,4},{7,5},{8,10},{9,11},{10,... | collective-permute-start | bytes 36872 | tf_op jit(solution)/shard_map/ppermute | solution.py:34
  97.0 18.5 %all-to-all-start.1 = ((bf16[128,4,384]{2,0,1:T(8,128)(2,1)}), bf16[128,4,384]{2,0,1:T(8,128)(2,1)S(1)}, u32[]{:S(2)}, u32[]{:S(2)}) async-start(bf16[128,4,384]{2,0,1:T(8,128)(2,1)} %copy.17), calls=%async_computation.1 | async-start | bytes 786432 | tf_op jit(solution)/shard_map/all_to_all | solution.py:128
  119.7 3.2 %collective-permute-start.15 = (f32[192,1536]{1,0:T(8,128)}, f32[192,1536]{1,0:T(8,128)}, u32[]{:S(2)}, u32[]{:S(2)}) collective-permute-start(f32[192,1536]{1,0:T(8,128)} %constant_dynamic-slice_fusion.2), channel_id=1, source_target_pairs={{0,4},{4,0},{8,12},{12,8},{16,20},{20,16},{24,28},{28,24},{1,5},{5... | collective-permute-start | bytes 3538952 | tf_op jit(solution)/shard_map/ppermute | solution.py:65
  125.3 25.7 %collective-permute-start.16 = (f32[96,1536]{1,0:T(8,128)S(1)}, f32[96,1536]{1,0:T(8,128)S(1)}, u32[]{:S(2)}, u32[]{:S(2)}) collective-permute-start(f32[96,1536]{1,0:T(8,128)S(1)} %constant_dynamic-slice_fusion.1), channel_id=1, source_target_pairs={{0,8},{4,12},{8,0},{12,4},{16,24},{20,28},{24,16},{28,20},{1,9},{5... | collective-permute-start | bytes 1769480 | tf_op jit(solution)/shard_map/ppermute | solution.py:65
  126.9 21.6 %collective-permute-start.21 = (f32[31,1536]{1,0:T(8,128)}, f32[31,1536]{1,0:T(8,128)S(1)}, u32[]{:S(2)}, u32[]{:S(2)}) collective-permute-start(f32[31,1536]{1,0:T(8,128)} %stack.172), channel_id=1, source_target_pairs={{0,4},{4,0},{8,12},{12,8},{16,20},{20,16},{24,28},{28,24},{1,5},{5... | collective-permute-start | bytes 571400 | tf_op jit(solution)/shard_map/ppermute | solution.py:34
  148.5 38.0 %collective-permute-start.7 = (bf16[4,192,1536]{2,1,0:T(8,128)(2,1)}, bf16[4,192,1536]{2,1,0:T(8,128)(2,1)S(1)}, u32[]{:S(2)}, u32[]{:S(2)}) collective-permute-start(bf16[4,192,1536]{2,1,0:T(8,128)(2,1)} %bitcast.18), channel_id=1, source_target_pairs={{0,4},{4,0},{8,12},{12,8},{16,20},{20,16},{24,28},{28,24},{1,5},{5... | collective-permute-start | bytes 7077896 | tf_op jit(solution)/shard_map/ppermute | solution.py:82
  149.5 10.4 %collective-permute-start.22 = (f32[31,1536]{1,0:T(8,128)S(1)}, f32[31,1536]{1,0:T(8,128)S(1)}, u32[]{:S(2)}, u32[]{:S(2)}) collective-permute-start(f32[31,1536]{1,0:T(8,128)S(1)} %add.537), channel_id=1, source_target_pairs={{0,8},{4,12},{8,0},{12,4},{16,24},{20,28},{24,16},{28,20},{1,9},{5... | collective-permute-start | bytes 571400 | tf_op jit(solution)/shard_map/ppermute | solution.py:34
  152.5 9.2 %collective-permute-start.17 = (f32[48,1536]{1,0:T(8,128)S(1)}, f32[48,1536]{1,0:T(8,128)S(1)}, u32[]{:S(2)}, u32[]{:S(2)}) collective-permute-start(f32[48,1536]{1,0:T(8,128)S(1)} %constant_dynamic-slice_fusion), channel_id=1, source_target_pairs={{0,16},{4,20},{8,24},{12,28},{16,0},{20,4},{24,8},{28,12},{1,17},{... | collective-permute-start | bytes 884744 | tf_op jit(solution)/shard_map/ppermute | solution.py:65
  154.1 9.7 %collective-permute-start.13 = (bf16[2,15,1536]{2,1,0:T(8,128)(2,1)S(1)}, bf16[2,15,1536]{2,1,0:T(8,128)(2,1)S(1)}, u32[]{:S(2)}, u32[]{:S(2)}) collective-permute-start(bf16[2,15,1536]{2,1,0:T(8,128)(2,1)S(1)} %get-tuple-element.101), channel_id=1, source_target_pairs={{1,0},{2,1},{3,2},{5,4},{6,5},{7,6},{9,8},{10,9},{11,10},{13,12},{... | collective-permute-start | bytes 276488 | tf_op jit(solution)/shard_map/ppermute | solution.py:17
  155.4 8.4 %collective-permute-start.14 = (bf16[2,15,1536]{2,1,0:T(8,128)(2,1)S(1)}, bf16[2,15,1536]{2,1,0:T(8,128)(2,1)S(1)}, u32[]{:S(2)}, u32[]{:S(2)}) collective-permute-start(bf16[2,15,1536]{2,1,0:T(8,128)(2,1)S(1)} %get-tuple-element.102), channel_id=1, source_target_pairs={{0,1},{1,2},{2,3},{4,5},{5,6},{6,7},{8,9},{9,10},{10,11},{12,13},{... | collective-permute-start | bytes 276488 | tf_op jit(solution)/shard_map/ppermute | solution.py:16
  160.0 8.2 %collective-permute-start.23 = (f32[31,1536]{1,0:T(8,128)S(1)}, f32[31,1536]{1,0:T(8,128)S(1)}, u32[]{:S(2)}, u32[]{:S(2)}) collective-permute-start(f32[31,1536]{1,0:T(8,128)S(1)} %add.538), channel_id=1, source_target_pairs={{0,16},{4,20},{8,24},{12,28},{16,0},{20,4},{24,8},{28,12},{1,17},{... | collective-permute-start | bytes 571400 | tf_op jit(solution)/shard_map/ppermute | solution.py:34
  161.7 10.8 %collective-permute-start.18 = (f32[48,1536]{1,0:T(8,128)S(1)}, f32[48,1536]{1,0:T(8,128)S(1)}, u32[]{:S(2)}, u32[]{:S(2)}) collective-permute-start(f32[48,1536]{1,0:T(8,128)S(1)} %dynamic-slice_add_fusion.2), channel_id=1, source_target_pairs={{0,16},{4,20},{8,24},{12,28},{16,0},{20,4},{24,8},{28,12},{1,17},{... | collective-permute-start | bytes 884744 | tf_op jit(solution)/shard_map/ppermute | solution.py:69
  168.2 5.7 %collective-permute-start.24 = (f32[31,1536]{1,0:T(8,128)S(1)}, f32[31,1536]{1,0:T(8,128)S(1)}, u32[]{:S(2)}, u32[]{:S(2)}) collective-permute-start(f32[31,1536]{1,0:T(8,128)S(1)} %add.539), channel_id=1, source_target_pairs={{0,1},{1,0},{2,3},{3,2},{4,5},{5,4},{6,7},{7,6},{8,9},{9,8},{10,11... | collective-permute-start | bytes 571400 | tf_op jit(solution)/shard_map/ppermute | solution.py:34
  172.6 13.8 %collective-permute-start.19 = (f32[96,1536]{1,0:T(8,128)S(1)}, f32[96,1536]{1,0:T(8,128)S(1)}, u32[]{:S(2)}, u32[]{:S(2)}) collective-permute-start(f32[96,1536]{1,0:T(8,128)S(1)} %maximum_select_fusion.2), channel_id=1, source_target_pairs={{0,8},{4,12},{8,0},{12,4},{16,24},{20,28},{24,16},{28,20},{1,9},{5... | collective-permute-start | bytes 1769480 | tf_op jit(solution)/shard_map/ppermute | solution.py:69
  174.0 9.7 %collective-permute-start.25 = (f32[31,1536]{1,0:T(8,128)S(1)}, f32[31,1536]{1,0:T(8,128)S(1)}, u32[]{:S(2)}, u32[]{:S(2)}) collective-permute-start(f32[31,1536]{1,0:T(8,128)S(1)} %add.540), channel_id=1, source_target_pairs={{0,2},{1,3},{2,0},{3,1},{4,6},{5,7},{6,4},{7,5},{8,10},{9,11},{10,... | collective-permute-start | bytes 571400 | tf_op jit(solution)/shard_map/ppermute | solution.py:34
  186.4 3.0 %collective-permute-start.20 = (f32[192,1536]{1,0:T(8,128)S(1)}, f32[192,1536]{1,0:T(8,128)S(1)}, u32[]{:S(2)}, u32[]{:S(2)}) collective-permute-start(f32[192,1536]{1,0:T(8,128)S(1)} %maximum_select_fusion.1), channel_id=1, source_target_pairs={{0,4},{4,0},{8,12},{12,8},{16,20},{20,16},{24,28},{28,24},{1,5},{5... | collective-permute-start | bytes 3538952 | tf_op jit(solution)/shard_map/ppermute | solution.py:69
  (72 other events, 1400.8 us)
Sparse Core Ops, SparseCore 0:
  9.6 40.3 all-gather.3
  94.5 53.9 all-gather.5

commit v10 on v9

--- a/solution.py
+++ b/solution.py
@@ -71,18 +71,19 @@
     return x
 
 
-def gather_weight(block):
+def gather_weight(block, anchor):
     if lax.axis_size("dp") % 2:
-        return lax.all_gather(block, "tensor", axis=0, tiled=True)
+        return lax.all_gather(block, "tensor", axis=0, tiled=True), anchor
     peers = lax.axis_size("tensor")
     half = block.shape[0] // 2
     core = lax.rem(lax.axis_index("dp"), 2)
     mine = lax.dynamic_slice_in_dim(block, core * half, half, axis=0)
     held = lax.all_gather(mine, "tensor", axis=0, tiled=False)
+    held, anchor = lax.optimization_barrier((held, anchor))
     other = lax.ppermute(held, "dp", [(i, i ^ 1) for i in range(lax.axis_size("dp"))])
     first = jnp.where(core == 0, held, other)
     second = jnp.where(core == 0, other, held)
-    return jnp.concatenate([first, second], axis=1).reshape(peers * block.shape[0], block.shape[1])
+    return jnp.concatenate([first, second], axis=1).reshape(peers * block.shape[0], block.shape[1]), anchor
 
 
 def on_device(glu_input, depth_kernel, norm_scale, norm_shift, proj_weight, out_grad):
@@ -153,10 +154,10 @@
     local_grad, kernel_terms = lax.optimization_barrier((local_grad, kernel_terms))
     weight_grad = rows_sum(local_grad, "dp")
     kernel_grad = all_sum(kernel_terms, ("dp", "tensor"))
+    full_weight, kernel_grad = gather_weight(proj_weight, kernel_grad)
     input_grad = jnp.concatenate(
         [grad_gated * gates, grad_gated * values * gates * (1.0 - gates)], axis=-1
     ).astype(jnp.bfloat16)
-    full_weight = gather_weight(proj_weight)
     conv_output = jnp.einsum(
         "btc,cd->btd", activated, full_weight, preferred_element_type=jnp.float32
     ).astype(jnp.bfloat16)

time: 199 us -> 219 us (1.10)
  waiting for transfers between devices: 75.9 us -> 89.6 us
  starting transfers between devices: 35.7 us -> 42.4 us
    ppermute x10, waiting for transfers between devices: 18 us -> 52.4 us  [all_sum(): x = x + lax.ppermute(x, axis, [(i, i ^ step) for i in range(peers)])]
    all_gather x1, waiting for transfers between devices: 21.6 us -> 0.01 us  [gather_weight(): held = lax.all_gather(mine, 'tensor', axis=0, tiled=False)]
    all_gather x1, waiting for transfers between devices: 3.67 us -> 12.2 us  [on_device(): group_grad = lax.all_gather(flat_grad, 'tensor', axis=0, tiled=True)]
    ppermute x3, waiting for transfers between devices: 5.5 us -> 12.1 us  [rows_sum(): other = lax.ppermute(x, axis, [(i, i ^ step) for i in range(peers)])]
    all_to_all x1, waiting for transfers between devices: 4.62 us -> 0.01 us  [on_device(): lax.all_to_all(flat_act, 'tensor', split_axis=1, concat_axis=0, tiled=True)]
    ppermute x5, waiting for transfers between devices: 13.1 us -> 9.19 us  [all_moments(): lax.ppermute(jnp.stack([mean, spread]), axis, [(i, i ^ step) for i in ran...]
    another operation x2, other arithmetic: 4.34 us -> 7.93 us
    ppermute x2, waiting for transfers between devices: 4.32 us -> 0.74 us  [extended(): after = lax.ppermute(leading, axis, down)]
  transfers between devices with their start and end apart: 29 -> 29, of which waited for: 20 -> 18; matrix products, arithmetic and copies ran while one was open for 17% -> 15% of each run, Pallas kernels for 0% -> 0%
where the time goes in v10:
time: 219 us; the launch traced here: 218 us
  waiting for transfers between devices  89.6 us (41%)
  starting transfers between devices  42.4 us (19%)
  other arithmetic  29.8 us (14%)
  blocking collectives  22.7 us (10%)
  between operations  15.3 us (7%)
  local copies, waits for them, and re-layouts  12.1 us (6%)
  matrix products  6.26 us (3%)
    ppermute x10, waiting for transfers between devices, all_sum(): x = x + lax.ppermute(x, axis, [(i, i ^ step) for i in range(peers)])  52.4 us
    all_to_all x1, blocking collectives, on_device(): lax.all_to_all(own_columns, 'tensor', split_axis=0, concat_axis=1, tiled=...  22.7 us
    all_gather x1, waiting for transfers between devices, on_device(): group_grad = lax.all_gather(flat_grad, 'tensor', axis=0, tiled=True)  12.2 us
    ppermute x3, waiting for transfers between devices, rows_sum(): other = lax.ppermute(x, axis, [(i, i ^ step) for i in range(peers)])  12.1 us
    ppermute x2, starting transfers between devices, extended(): before = lax.ppermute(last, axis, up)  10.6 us
    ppermute x5, starting transfers between devices, all_moments(): lax.ppermute(jnp.stack([mean, spread]), axis, [(i, i ^ step) for i in ran...  9.76 us
    ppermute x5, waiting for transfers between devices, all_moments(): lax.ppermute(jnp.stack([mean, spread]), axis, [(i, i ^ step) for i in ran...  9.19 us
    ppermute x10, starting transfers between devices, all_sum(): x = x + lax.ppermute(x, axis, [(i, i ^ step) for i in range(peers)])  8.74 us
  transfers between devices with their start and end apart: 29, of which 18 were waited for; matrix products, arithmetic and copies ran while one was open for 15% of the time, Pallas kernels for 0%

profile of v10, /device:TPU:0, one launch (start us, length us, event | category | flops | bytes accessed | tf_op | source)
XLA Modules:
  0.0 218.2 jit_solution(18191622541688901350)
XLA Ops:
  10.0 5.6 %collective-permute-start = (bf16[2,15,1536]{2,1,0:T(8,128)(2,1)S(1)}, bf16[2,15,1536]{2,1,0:T(8,128)(2,1)S(1)}, u32[]{:S(2)}, u32[]{:S(2)}) collective-permute-start(bf16[2,15,1536]{2,1,0:T(8,128)(2,1)S(1)} %get-tuple-element.107), channel_id=1, source_target_pairs={{0,1},{1,2},{2,3},{4,5},{5,6},{6,7},{8,9},{9,10},{10,11},{12,13},{... | collective-permute-start | bytes 276488 | tf_op jit(solution)/shard_map/ppermute | solution.py:16
  17.8 3.8 %fusion.143 = (f32[1536]{0:T(1024)S(1)}, f32[2,64,1536]{2,1,0:T(8,128)S(1)}) fusion(bf16[2,15,1536]{2,1,0:T(8,128)(2,1)S(1)} %collective-permute-done.1, bf16[2,64,1536]{2,1,0:T(8,128)(2,1)S(1)} %fusion, f32[1536]{0:T(1024)S(1)} %get-tuple-element.80, f32[1536]{0:T(1024)S(1)} %get-tuple-element.81, f32[1536]{0:T(1024)S(1)} %get-tuple-element.52, ...), kind=kLoop, calls=%fused_computation.380 | loop fusion | flops 35977728 | bytes 1560576 | tf_op jit(solution)/shard_map/reduce_sum | solution.py:108
  23.1 2.0 collective-permute-start.3
  25.1 1.8 collective-permute-done.3
  27.0 2.0 collective-permute-start.4
  29.0 1.7 collective-permute-done.4
  30.8 2.5 %collective-permute-start.5 = (f32[2,1536]{1,0:T(2,128)S(1)}, f32[2,1536]{1,0:T(2,128)S(1)}, u32[]{:S(2)}, u32[]{:S(2)}) collective-permute-start(f32[2,1536]{1,0:T(2,128)S(1)} %pad_maximum_fusion.9), channel_id=1, source_target_pairs={{0,1},{1,0},{2,3},{3,2},{4,5},{5,4},{6,7},{7,6},{8,9},{9,8},{10,11... | collective-permute-start | bytes 36872 | tf_op jit(solution)/shard_map/ppermute | solution.py:44
  33.3 2.2 %collective-permute-done.5 = f32[2,1536]{1,0:T(2,128)S(1)} collective-permute-done((f32[2,1536]{1,0:T(2,128)S(1)}, f32[2,1536]{1,0:T(2,128)S(1)}, u32[]{:S(2)}, u32[]{:S(2)}) %collective-permute-start.5) | collective-permute-done | bytes 12320 | tf_op jit(solution)/shard_map/ppermute | solution.py:44
  35.6 3.2 %collective-permute-start.6 = (f32[2,1536]{1,0:T(2,128)S(1)}, f32[2,1536]{1,0:T(2,128)S(1)}, u32[]{:S(2)}, u32[]{:S(2)}) collective-permute-start(f32[2,1536]{1,0:T(2,128)S(1)} %pad_maximum_fusion.10), channel_id=1, source_target_pairs={{0,2},{1,3},{2,0},{3,1},{4,6},{5,7},{6,4},{7,5},{8,10},{9,11},{10,... | collective-permute-start | bytes 36872 | tf_op jit(solution)/shard_map/ppermute | solution.py:44
  38.8 2.3 %collective-permute-done.6 = f32[2,1536]{1,0:T(2,128)S(1)} collective-permute-done((f32[2,1536]{1,0:T(2,128)S(1)}, f32[2,1536]{1,0:T(2,128)S(1)}, u32[]{:S(2)}, u32[]{:S(2)}) %collective-permute-start.6) | collective-permute-done | bytes 12320 | tf_op jit(solution)/shard_map/ppermute | solution.py:44
  41.9 12.2 %all-gather.4.cloned.1.call-done = bf16[512,1536]{1,0:T(8,128)(2,1)} async-done(((bf16[128,1536]{1,0:T(8,128)(2,1)}), bf16[512,1536]{1,0:T(8,128)(2,1)}) %all-gather.4.cloned.1.call-update) | async-done | bytes 1572880 | tf_op jit(solution)/shard_map/all_gather | solution.py:100
  54.1 2.4 %fusion.148 = f32[512,384]{1,0:T(8,128)S(1)} fusion(bf16[512,1536]{1,0:T(8,128)(2,1)} %all-gather.4.cloned.1.call-done, bf16[384,1536]{1,0:T(8,128)(2,1)S(1)} %copy-done), kind=kOutput, calls=%fused_computation.384 | convolution fusion | flops 603979776 | bytes 3538944 | tf_op jit(solution)/shard_map/fd,cd->fc/dot_general | solution.py:119
  56.6 22.7 %all_to_all.35 = f32[4,128,384]{2,1,0:T(8,128)S(1)} all-to-all(f32[4,128,384]{2,1,0:T(8,128)S(1)} %bitcast.20), channel_id=1, replica_groups=mesh['dp'=8,'tensor'=4] {'tensor'}, dimensions={0} | all-to-all | bytes 1572864 | tf_op jit(solution)/shard_map/all_to_all | solution.py:120
  81.0 1.6 fusion.140
  85.5 2.2 %collective-permute-done.8 = f32[2,1536]{1,0:T(2,128)S(1)} collective-permute-done((f32[2,1536]{1,0:T(2,128)S(1)}, f32[2,1536]{1,0:T(2,128)S(1)}, u32[]{:S(2)}, u32[]{:S(2)}) %collective-permute-start.8) | collective-permute-done | bytes 12320 | tf_op jit(solution)/shard_map/ppermute | solution.py:34
  89.3 2.2 %collective-permute-done.9 = f32[2,1536]{1,0:T(2,128)S(1)} collective-permute-done((f32[2,1536]{1,0:T(2,128)S(1)}, f32[2,1536]{1,0:T(2,128)S(1)}, u32[]{:S(2)}, u32[]{:S(2)}) %collective-permute-start.9) | collective-permute-done | bytes 12320 | tf_op jit(solution)/shard_map/ppermute | solution.py:34
  91.8 3.5 %collective-permute-done.10 = f32[2,1536]{1,0:T(2,128)S(1)} collective-permute-done((f32[2,1536]{1,0:T(2,128)S(1)}, f32[2,1536]{1,0:T(2,128)S(1)}, u32[]{:S(2)}, u32[]{:S(2)}) %collective-permute-start.10) | collective-permute-done | bytes 12320 | tf_op jit(solution)/shard_map/ppermute | solution.py:34
  96.9 1.8 copy.16
  98.7 4.1 %all-to-all-start = ((bf16[128,4,384]{2,0,1:T(8,128)(2,1)}), bf16[128,4,384]{2,0,1:T(8,128)(2,1)}, u32[]{:S(2)}, u32[]{:S(2)}) async-start(bf16[128,4,384]{2,0,1:T(8,128)(2,1)} %copy.16), calls=%async_computation | async-start | bytes 786432 | tf_op jit(solution)/shard_map/all_to_all | solution.py:129
  104.5 2.9 %fusion.64 = (f32[1536]{0:T(1024)S(1)}, f32[1536]{0:T(1024)S(1)}, f32[1536]{0:T(1024)S(1)}, f32[1536]{0:T(1024)S(1)}, f32[1536]{0:T(1024)S(1)}, /*index=5*/f32[1...) fusion(bf16[2,15,1536]{2,1,0:T(8,128)(2,1)} %copy-done.8, ...), kind=kLoop, calls=%fused_computation.192 | loop fusion | flops 12372480 | bytes 2537472 | tf_op jit(solution)/shard_map/reduce_sum | solution.py:148
  110.8 2.8 %stack.172 = f32[31,1536]{1,0:T(8,128)} concatenate(f32[1,1536]{1,0:T(1,128)S(1)} %stack.141, f32[1,1536]{1,0:T(1,128)S(1)} %stack.142, f32[1,1536]{1,0:T(1,128)S(1)} %stack.143, f32[1,1536]{1,0:T(1,128)S(1)} %stack.144, f32[1,1536]{1,0:T(1,128)S(1)} %stack.145, f32[1,1536]{1,0:T(1,128)S(1)} %stack.146, f32[1,1536]{1,0:T(1,128)S(1)} %stack.147, f32[1,1536]{1,0:T(1,128)S(1)} %stack.148, ...), dimensions={0} | concatenate | bytes 380928 | tf_op jit(solution)/shard_map/stack | solution.py:146
  113.5 2.3 %fusion.147 = f32[384,1536]{1,0:T(8,128)S(1)} fusion(bf16[512,384]{1,0:T(8,128)(2,1)} %bitcast.3, bf16[512,1536]{1,0:T(8,128)(2,1)} %all-gather.4.cloned.1.call-done), kind=kOutput, calls=%fused_computation.383 | convolution fusion | flops 603979776 | bytes 4325376 | tf_op jit(solution)/shard_map/fc,fd->cd/dot_general | solution.py:130
  118.5 1.7 collective-permute-done.20
  123.8 17.5 %collective-permute-done.13 = f32[31,1536]{1,0:T(8,128)S(1)} collective-permute-done((f32[31,1536]{1,0:T(8,128)S(1)}, f32[31,1536]{1,0:T(8,128)S(1)}, u32[]{:S(2)}, u32[]{:S(2)}) %collective-permute-start.13) | collective-permute-done | bytes 190496 | tf_op jit(solution)/shard_map/ppermute | solution.py:34
  142.9 4.7 %collective-permute-done.14 = f32[31,1536]{1,0:T(8,128)S(1)} collective-permute-done((f32[31,1536]{1,0:T(8,128)S(1)}, f32[31,1536]{1,0:T(8,128)S(1)}, u32[]{:S(2)}, u32[]{:S(2)}) %collective-permute-start.14) | collective-permute-done | bytes 190496 | tf_op jit(solution)/shard_map/ppermute | solution.py:34
  147.7 1.9 collective-permute-start.15
  149.5 18.6 %collective-permute-done.15 = f32[31,1536]{1,0:T(8,128)S(1)} collective-permute-done((f32[31,1536]{1,0:T(8,128)S(1)}, f32[31,1536]{1,0:T(8,128)S(1)}, u32[]{:S(2)}, u32[]{:S(2)}) %collective-permute-start.15) | collective-permute-done | bytes 190496 | tf_op jit(solution)/shard_map/ppermute | solution.py:34
  169.8 1.7 collective-permute-start.22
  172.2 5.0 %collective-permute-start.19 = (bf16[2,15,1536]{2,1,0:T(8,128)(2,1)}, bf16[2,15,1536]{2,1,0:T(8,128)(2,1)}, u32[]{:S(2)}, u32[]{:S(2)}) collective-permute-start(bf16[2,15,1536]{2,1,0:T(8,128)(2,1)} %get-tuple-element.106), channel_id=1, source_target_pairs={{0,1},{1,2},{2,3},{4,5},{5,6},{6,7},{8,9},{9,10},{10,11},{12,13},{... | collective-permute-start | bytes 276488 | tf_op jit(solution)/shard_map/ppermute | solution.py:16
  178.5 2.5 %collective-permute-done.16 = f32[31,1536]{1,0:T(8,128)S(1)} collective-permute-done((f32[31,1536]{1,0:T(8,128)S(1)}, f32[31,1536]{1,0:T(8,128)S(1)}, u32[]{:S(2)}, u32[]{:S(2)}) %collective-permute-start.16) | collective-permute-done | bytes 190496 | tf_op jit(solution)/shard_map/ppermute | solution.py:34
  184.1 7.6 %multiply_convert_fusion = (bf16[2,64,1536]{2,1,0:T(8,128)(2,1)S(1)}, f32[2,64,1536]{2,1,0:T(8,128)S(1)}) fusion(bf16[2,64,3072]{2,1,0:T(8,128)(2,1)S(1)} %copy-done.3, bf16[2,64,1536]{2,1,0:T(8,128)(2,1)S(1)} %copy-done.2, bf16[2,15,1536]{2,1,0:T(8,128)(2,1)} %collective-permute-done.19, f32[1536]{0:T(1024)} %copy-done.41, f32[1536]{0:T(1024)} %copy-done.42, ...), kind=kLoop, calls=%fused_computation.210 | loop fusion | flops 36962304 | bytes 2340864 | tf_op jit(solution)/shard_map/convert
  194.6 12.1 %collective-permute-done.24 = f32[96,1536]{1,0:T(8,128)S(1)} collective-permute-done((f32[96,1536]{1,0:T(8,128)S(1)}, f32[96,1536]{1,0:T(8,128)S(1)}, u32[]{:S(2)}, u32[]{:S(2)}) %collective-permute-start.24) | collective-permute-done | bytes 589856 | tf_op jit(solution)/shard_map/ppermute | solution.py:69
  (216 shorter events, 41.7 us)
Async XLA Ops:
  7.2 46.9 %copy-start = (bf16[384,1536]{1,0:T(8,128)(2,1)S(1)}, bf16[384,1536]{1,0:T(8,128)(2,1)}, u32[]{:S(2)}) copy-start(bf16[384,1536]{1,0:T(8,128)(2,1)} %param.10) | copy-start | bytes 3538948
  7.2 46.9 %all-gather.4.cloned.1.call-start = ((), (), s32[]{:S(2)}) async-start(), calls=%async_computation.2 | async-start | bytes 1966080 | tf_op jit(solution)/shard_map/all_gather | solution.py:100
  8.7 7.7 %collective-permute-start.1 = (bf16[2,15,1536]{2,1,0:T(8,128)(2,1)S(1)}, bf16[2,15,1536]{2,1,0:T(8,128)(2,1)S(1)}, u32[]{:S(2)}, u32[]{:S(2)}) collective-permute-start(bf16[2,15,1536]{2,1,0:T(8,128)(2,1)S(1)} %get-tuple-element.108), channel_id=1, source_target_pairs={{1,0},{2,1},{3,2},{5,4},{6,5},{7,6},{9,8},{10,9},{11,10},{13,12},{... | collective-permute-start | bytes 276488 | tf_op jit(solution)/shard_map/ppermute | solution.py:17
  10.0 7.8 %collective-permute-start = (bf16[2,15,1536]{2,1,0:T(8,128)(2,1)S(1)}, bf16[2,15,1536]{2,1,0:T(8,128)(2,1)S(1)}, u32[]{:S(2)}, u32[]{:S(2)}) collective-permute-start(bf16[2,15,1536]{2,1,0:T(8,128)(2,1)S(1)} %get-tuple-element.107), channel_id=1, source_target_pairs={{0,1},{1,2},{2,3},{4,5},{5,6},{6,7},{8,9},{9,10},{10,11},{12,13},{... | collective-permute-start | bytes 276488 | tf_op jit(solution)/shard_map/ppermute | solution.py:16
  16.3 40.1 %copy-start.31 = (f32[1536]{0:T(1024)}, f32[1536]{0:T(1024)S(1)}, u32[]{:S(2)}) copy-start(f32[1536]{0:T(1024)S(1)} %get-tuple-element.70) | copy-start | bytes 18436
  16.4 40.1 %copy-start.32 = (f32[1536]{0:T(1024)}, f32[1536]{0:T(1024)S(1)}, u32[]{:S(2)}) copy-start(f32[1536]{0:T(1024)S(1)} %get-tuple-element.71) | copy-start | bytes 18436
  21.8 1.2 collective-permute-start.2
  23.1 3.8 %collective-permute-start.3 = (f32[2,1536]{1,0:T(2,128)S(1)}, f32[2,1536]{1,0:T(2,128)S(1)}, u32[]{:S(2)}, u32[]{:S(2)}) collective-permute-start(f32[2,1536]{1,0:T(2,128)S(1)} %pad_maximum_fusion.7), channel_id=1, source_target_pairs={{0,8},{4,12},{8,0},{12,4},{16,24},{20,28},{24,16},{28,20},{1,9},{5... | collective-permute-start | bytes 36872 | tf_op jit(solution)/shard_map/ppermute | solution.py:44
  27.0 3.8 %collective-permute-start.4 = (f32[2,1536]{1,0:T(2,128)S(1)}, f32[2,1536]{1,0:T(2,128)S(1)}, u32[]{:S(2)}, u32[]{:S(2)}) collective-permute-start(f32[2,1536]{1,0:T(2,128)S(1)} %pad_maximum_fusion.8), channel_id=1, source_target_pairs={{0,16},{4,20},{8,24},{12,28},{16,0},{20,4},{24,8},{28,12},{1,17},{... | collective-permute-start | bytes 36872 | tf_op jit(solution)/shard_map/ppermute | solution.py:44
  30.8 4.7 %collective-permute-start.5 = (f32[2,1536]{1,0:T(2,128)S(1)}, f32[2,1536]{1,0:T(2,128)S(1)}, u32[]{:S(2)}, u32[]{:S(2)}) collective-permute-start(f32[2,1536]{1,0:T(2,128)S(1)} %pad_maximum_fusion.9), channel_id=1, source_target_pairs={{0,1},{1,0},{2,3},{3,2},{4,5},{5,4},{6,7},{7,6},{8,9},{9,8},{10,11... | collective-permute-start | bytes 36872 | tf_op jit(solution)/shard_map/ppermute | solution.py:44
  35.6 5.5 %collective-permute-start.6 = (f32[2,1536]{1,0:T(2,128)S(1)}, f32[2,1536]{1,0:T(2,128)S(1)}, u32[]{:S(2)}, u32[]{:S(2)}) collective-permute-start(f32[2,1536]{1,0:T(2,128)S(1)} %pad_maximum_fusion.10), channel_id=1, source_target_pairs={{0,2},{1,3},{2,0},{3,1},{4,6},{5,7},{6,4},{7,5},{8,10},{9,11},{10,... | collective-permute-start | bytes 36872 | tf_op jit(solution)/shard_map/ppermute | solution.py:44
  82.7 1.2 collective-permute-start.7
  84.0 3.8 %collective-permute-start.8 = (f32[2,1536]{1,0:T(2,128)S(1)}, f32[2,1536]{1,0:T(2,128)S(1)}, u32[]{:S(2)}, u32[]{:S(2)}) collective-permute-start(f32[2,1536]{1,0:T(2,128)S(1)} %fusion.139), channel_id=1, source_target_pairs={{0,8},{4,12},{8,0},{12,4},{16,24},{20,28},{24,16},{28,20},{1,9},{5... | collective-permute-start | bytes 36872 | tf_op jit(solution)/shard_map/ppermute | solution.py:34
  87.7 3.8 %collective-permute-start.9 = (f32[2,1536]{1,0:T(2,128)S(1)}, f32[2,1536]{1,0:T(2,128)S(1)}, u32[]{:S(2)}, u32[]{:S(2)}) collective-permute-start(f32[2,1536]{1,0:T(2,128)S(1)} %fusion.155), channel_id=1, source_target_pairs={{0,16},{4,20},{8,24},{12,28},{16,0},{20,4},{24,8},{28,12},{1,17},{... | collective-permute-start | bytes 36872 | tf_op jit(solution)/shard_map/ppermute | solution.py:34
  91.5 3.8 %collective-permute-start.10 = (f32[2,1536]{1,0:T(2,128)S(1)}, f32[2,1536]{1,0:T(2,128)S(1)}, u32[]{:S(2)}, u32[]{:S(2)}) collective-permute-start(f32[2,1536]{1,0:T(2,128)S(1)} %add.496), channel_id=1, source_target_pairs={{0,1},{1,0},{2,3},{3,2},{4,5},{5,4},{6,7},{7,6},{8,9},{9,8},{10,11... | collective-permute-start | bytes 36872 | tf_op jit(solution)/shard_map/ppermute | solution.py:34
  95.9 7.2 %collective-permute-start.11 = (f32[2,1536]{1,0:T(2,128)}, f32[2,1536]{1,0:T(2,128)}, u32[]{:S(2)}, u32[]{:S(2)}) collective-permute-start(f32[2,1536]{1,0:T(2,128)} %add.497), channel_id=1, source_target_pairs={{0,2},{1,3},{2,0},{3,1},{4,6},{5,7},{6,4},{7,5},{8,10},{9,11},{10,... | collective-permute-start | bytes 36872 | tf_op jit(solution)/shard_map/ppermute | solution.py:34
  98.7 14.8 %all-to-all-start = ((bf16[128,4,384]{2,0,1:T(8,128)(2,1)}), bf16[128,4,384]{2,0,1:T(8,128)(2,1)}, u32[]{:S(2)}, u32[]{:S(2)}) async-start(bf16[128,4,384]{2,0,1:T(8,128)(2,1)} %copy.16), calls=%async_computation | async-start | bytes 786432 | tf_op jit(solution)/shard_map/all_to_all | solution.py:129
  102.8 78.9 %all-gather.6.cloned.1.call-start = ((), (), s32[]{:S(2)}) async-start(), calls=%async_computation.3 | async-start | bytes 2949120 | tf_op jit(solution)/shard_map/all_gather | solution.py:81
  117.0 3.2 %collective-permute-start.20 = (f32[192,1536]{1,0:T(8,128)}, f32[192,1536]{1,0:T(8,128)}, u32[]{:S(2)}, u32[]{:S(2)}) collective-permute-start(f32[192,1536]{1,0:T(8,128)} %constant_dynamic-slice_fusion.2), channel_id=1, source_target_pairs={{0,4},{4,0},{8,12},{12,8},{16,20},{20,16},{24,28},{28,24},{1,5},{5... | collective-permute-start | bytes 3538952 | tf_op jit(solution)/shard_map/ppermute | solution.py:65
  117.9 5.3 %collective-permute-start.12 = (f32[31,1536]{1,0:T(8,128)}, f32[31,1536]{1,0:T(8,128)S(1)}, u32[]{:S(2)}, u32[]{:S(2)}) collective-permute-start(f32[31,1536]{1,0:T(8,128)} %stack.172), channel_id=1, source_target_pairs={{0,4},{4,0},{8,12},{12,8},{16,20},{20,16},{24,28},{28,24},{1,5},{5... | collective-permute-start | bytes 571400 | tf_op jit(solution)/shard_map/ppermute | solution.py:34
  121.7 47.0 %collective-permute-start.21 = (f32[96,1536]{1,0:T(8,128)S(1)}, f32[96,1536]{1,0:T(8,128)S(1)}, u32[]{:S(2)}, u32[]{:S(2)}) collective-permute-start(f32[96,1536]{1,0:T(8,128)S(1)} %constant_dynamic-slice_fusion.1), channel_id=1, source_target_pairs={{0,8},{4,12},{8,0},{12,4},{16,24},{20,28},{24,16},{28,20},{1,9},{5... | collective-permute-start | bytes 1769480 | tf_op jit(solution)/shard_map/ppermute | solution.py:65
  123.2 18.1 %collective-permute-start.13 = (f32[31,1536]{1,0:T(8,128)S(1)}, f32[31,1536]{1,0:T(8,128)S(1)}, u32[]{:S(2)}, u32[]{:S(2)}) collective-permute-start(f32[31,1536]{1,0:T(8,128)S(1)} %add.499), channel_id=1, source_target_pairs={{0,8},{4,12},{8,0},{12,4},{16,24},{20,28},{24,16},{28,20},{1,9},{5... | collective-permute-start | bytes 571400 | tf_op jit(solution)/shard_map/ppermute | solution.py:34
  141.3 6.3 %collective-permute-start.14 = (f32[31,1536]{1,0:T(8,128)S(1)}, f32[31,1536]{1,0:T(8,128)S(1)}, u32[]{:S(2)}, u32[]{:S(2)}) collective-permute-start(f32[31,1536]{1,0:T(8,128)S(1)} %add.500), channel_id=1, source_target_pairs={{0,16},{4,20},{8,24},{12,28},{16,0},{20,4},{24,8},{28,12},{1,17},{... | collective-permute-start | bytes 571400 | tf_op jit(solution)/shard_map/ppermute | solution.py:34
  147.7 20.5 %collective-permute-start.15 = (f32[31,1536]{1,0:T(8,128)S(1)}, f32[31,1536]{1,0:T(8,128)S(1)}, u32[]{:S(2)}, u32[]{:S(2)}) collective-permute-start(f32[31,1536]{1,0:T(8,128)S(1)} %add.501), channel_id=1, source_target_pairs={{0,1},{1,0},{2,3},{3,2},{4,5},{5,4},{6,7},{7,6},{8,9},{9,8},{10,11... | collective-permute-start | bytes 571400 | tf_op jit(solution)/shard_map/ppermute | solution.py:34
  168.2 12.8 %collective-permute-start.16 = (f32[31,1536]{1,0:T(8,128)S(1)}, f32[31,1536]{1,0:T(8,128)S(1)}, u32[]{:S(2)}, u32[]{:S(2)}) collective-permute-start(f32[31,1536]{1,0:T(8,128)S(1)} %add.502), channel_id=1, source_target_pairs={{0,2},{1,3},{2,0},{3,1},{4,6},{5,7},{6,4},{7,5},{8,10},{9,11},{10,... | collective-permute-start | bytes 571400 | tf_op jit(solution)/shard_map/ppermute | solution.py:34
  169.8 11.9 %collective-permute-start.22 = (f32[48,1536]{1,0:T(8,128)S(1)}, f32[48,1536]{1,0:T(8,128)S(1)}, u32[]{:S(2)}, u32[]{:S(2)}) collective-permute-start(f32[48,1536]{1,0:T(8,128)S(1)} %constant_dynamic-slice_fusion), channel_id=1, source_target_pairs={{0,16},{4,20},{8,24},{12,28},{16,0},{20,4},{24,8},{28,12},{1,17},{... | collective-permute-start | bytes 884744 | tf_op jit(solution)/shard_map/ppermute | solution.py:65
  172.2 11.1 %collective-permute-start.19 = (bf16[2,15,1536]{2,1,0:T(8,128)(2,1)}, bf16[2,15,1536]{2,1,0:T(8,128)(2,1)}, u32[]{:S(2)}, u32[]{:S(2)}) collective-permute-start(bf16[2,15,1536]{2,1,0:T(8,128)(2,1)} %get-tuple-element.106), channel_id=1, source_target_pairs={{0,1},{1,2},{2,3},{4,5},{5,6},{6,7},{8,9},{9,10},{10,11},{12,13},{... | collective-permute-start | bytes 276488 | tf_op jit(solution)/shard_map/ppermute | solution.py:16
  177.2 6.8 %collective-permute-start.18 = (bf16[2,15,1536]{2,1,0:T(8,128)(2,1)}, bf16[2,15,1536]{2,1,0:T(8,128)(2,1)}, u32[]{:S(2)}, u32[]{:S(2)}) collective-permute-start(bf16[2,15,1536]{2,1,0:T(8,128)(2,1)} %get-tuple-element.105), channel_id=1, source_target_pairs={{1,0},{2,1},{3,2},{5,4},{6,5},{7,6},{9,8},{10,9},{11,10},{13,12},{... | collective-permute-start | bytes 276488 | tf_op jit(solution)/shard_map/ppermute | solution.py:17
  181.7 25.1 %collective-permute-start.17 = (bf16[4,192,1536]{2,1,0:T(8,128)(2,1)}, bf16[4,192,1536]{2,1,0:T(8,128)(2,1)S(1)}, u32[]{:S(2)}, u32[]{:S(2)}) collective-permute-start(bf16[4,192,1536]{2,1,0:T(8,128)(2,1)} %bitcast.18), channel_id=1, source_target_pairs={{0,4},{4,0},{8,12},{12,8},{16,20},{20,16},{24,28},{28,24},{1,5},{5... | collective-permute-start | bytes 7077896 | tf_op jit(solution)/shard_map/ppermute | solution.py:83
  181.8 10.0 %collective-permute-start.23 = (f32[48,1536]{1,0:T(8,128)S(1)}, f32[48,1536]{1,0:T(8,128)S(1)}, u32[]{:S(2)}, u32[]{:S(2)}) collective-permute-start(f32[48,1536]{1,0:T(8,128)S(1)} %dynamic-slice_add_fusion.2), channel_id=1, source_target_pairs={{0,16},{4,20},{8,24},{12,28},{16,0},{20,4},{24,8},{28,12},{1,17},{... | collective-permute-start | bytes 884744 | tf_op jit(solution)/shard_map/ppermute | solution.py:69
  191.8 14.9 %collective-permute-start.24 = (f32[96,1536]{1,0:T(8,128)S(1)}, f32[96,1536]{1,0:T(8,128)S(1)}, u32[]{:S(2)}, u32[]{:S(2)}) collective-permute-start(f32[96,1536]{1,0:T(8,128)S(1)} %maximum_select_fusion.2), channel_id=1, source_target_pairs={{0,8},{4,12},{8,0},{12,4},{16,24},{20,28},{24,16},{28,20},{1,9},{5... | collective-permute-start | bytes 1769480 | tf_op jit(solution)/shard_map/ppermute | solution.py:69
  206.7 3.0 %collective-permute-start.25 = (f32[192,1536]{1,0:T(8,128)S(1)}, f32[192,1536]{1,0:T(8,128)S(1)}, u32[]{:S(2)}, u32[]{:S(2)}) collective-permute-start(f32[192,1536]{1,0:T(8,128)S(1)} %maximum_select_fusion.1), channel_id=1, source_target_pairs={{0,4},{4,0},{8,12},{12,8},{16,20},{20,16},{24,28},{28,24},{1,5},{5... | collective-permute-start | bytes 3538952 | tf_op jit(solution)/shard_map/ppermute | solution.py:69
  (43 other events, 1074.4 us)
Sparse Core Ops, SparseCore 0:
  15.8 38.2 all-gather.3
  118.0 54.2 all-gather.5

commit v11 on v9

--- a/solution.py
+++ b/solution.py
@@ -72,17 +72,20 @@
 
 
 def gather_weight(block):
-    if lax.axis_size("dp") % 2:
+    group = lax.axis_size("dp")
+    if group % 4 or block.shape[0] % 4:
         return lax.all_gather(block, "tensor", axis=0, tiled=True)
     peers = lax.axis_size("tensor")
-    half = block.shape[0] // 2
-    core = lax.rem(lax.axis_index("dp"), 2)
-    mine = lax.dynamic_slice_in_dim(block, core * half, half, axis=0)
+    piece = block.shape[0] // 4
+    where = lax.axis_index("dp")
+    low, high = lax.rem(where, 2), lax.rem(where // 2, 2)
+    mine = lax.dynamic_slice_in_dim(block, (high * 2 + low) * piece, piece, axis=0)
     held = lax.all_gather(mine, "tensor", axis=0, tiled=False)
-    other = lax.ppermute(held, "dp", [(i, i ^ 1) for i in range(lax.axis_size("dp"))])
-    first = jnp.where(core == 0, held, other)
-    second = jnp.where(core == 0, other, held)
-    return jnp.concatenate([first, second], axis=1).reshape(peers * block.shape[0], block.shape[1])
+    other = lax.ppermute(held, "dp", [(i, i ^ 2) for i in range(group)])
+    pair = jnp.stack([jnp.where(high == 0, held, other), jnp.where(high == 0, other, held)], axis=1)
+    other = lax.ppermute(pair, "dp", [(i, i ^ 1) for i in range(group)])
+    whole = jnp.stack([jnp.where(low == 0, pair, other), jnp.where(low == 0, other, pair)], axis=2)
+    return whole.reshape(peers * block.shape[0], block.shape[1])
 
 
 def on_device(glu_input, depth_kernel, norm_scale, norm_shift, proj_weight, out_grad):

time: 199 us -> 215 us (1.080)
  waiting for transfers between devices: 75.9 us -> 92.3 us
    ppermute x1 -> x2, waiting for transfers between devices: 0.01 us -> 25.5 us  [the longest x1 25.5 us: gather_weight(): other = lax.ppermute(held, 'dp', [(i, i ^ 2) for i in range(group)])]
    all_gather x1, waiting for transfers between devices: 21.6 us -> 8.26 us  [gather_weight(): held = lax.all_gather(mine, 'tensor', axis=0, tiled=False)]
    ppermute x3, waiting for transfers between devices: 5.5 us -> 1.52 us  [rows_sum(): other = lax.ppermute(x, axis, [(i, i ^ step) for i in range(peers)])]
    ppermute x3, waiting for transfers between devices: 4.29 us -> 8.02 us  [rows_sum(): x = keep + lax.ppermute(give, axis, [(i, i ^ step) for i in range(peers)])]
    ppermute x10, waiting for transfers between devices: 18 us -> 20.7 us  [all_sum(): x = x + lax.ppermute(x, axis, [(i, i ^ step) for i in range(peers)])]
    another operation x2 -> x6, other arithmetic: 4.34 us -> 6.74 us
  transfers between devices with their start and end apart: 29 -> 30, of which waited for: 20 -> 21; matrix products, arithmetic and copies ran while one was open for 17% -> 16% of each run, Pallas kernels for 0% -> 0%
where the time goes in v11:
time: 215 us; the launch traced here: 214 us
  waiting for transfers between devices  92.3 us (43%)
  starting transfers between devices  37.8 us (18%)
  other arithmetic  28.1 us (13%)
  blocking collectives  22.6 us (11%)
  between operations  15.8 us (7%)
  local copies, waits for them, and re-layouts  11.4 us (5%)
  matrix products  6.26 us (3%)
    ppermute x1, waiting for transfers between devices, gather_weight(): other = lax.ppermute(held, 'dp', [(i, i ^ 2) for i in range(group)])  25.5 us
    all_to_all x1, blocking collectives, on_device(): lax.all_to_all(own_columns, 'tensor', split_axis=0, concat_axis=1, tiled=...  22.6 us
    ppermute x10, waiting for transfers between devices, all_sum(): x = x + lax.ppermute(x, axis, [(i, i ^ step) for i in range(peers)])  20.7 us
    ppermute x5, waiting for transfers between devices, all_moments(): lax.ppermute(jnp.stack([mean, spread]), axis, [(i, i ^ step) for i in ran...  13.2 us
    ppermute x2, starting transfers between devices, extended(): before = lax.ppermute(last, axis, up)  9.48 us
    all_gather x1, waiting for transfers between devices, gather_weight(): held = lax.all_gather(mine, 'tensor', axis=0, tiled=False)  8.26 us
    ppermute x3, waiting for transfers between devices, rows_sum(): x = keep + lax.ppermute(give, axis, [(i, i ^ step) for i in range(peers)])  8.02 us
    ppermute x10, starting transfers between devices, all_sum(): x = x + lax.ppermute(x, axis, [(i, i ^ step) for i in range(peers)])  7.49 us
  transfers between devices with their start and end apart: 30, of which 21 were waited for; matrix products, arithmetic and copies ran while one was open for 16% of the time, Pallas kernels for 0%

profile of v11, /device:TPU:0, one launch (start us, length us, event | category | flops | bytes accessed | tf_op | source)
XLA Modules:
  0.0 214.3 jit_solution(6788732654266996288)
XLA Ops:
  9.3 4.9 %collective-permute-start = (bf16[2,15,1536]{2,1,0:T(8,128)(2,1)S(1)}, bf16[2,15,1536]{2,1,0:T(8,128)(2,1)S(1)}, u32[]{:S(2)}, u32[]{:S(2)}) collective-permute-start(bf16[2,15,1536]{2,1,0:T(8,128)(2,1)S(1)} %get-tuple-element.105), channel_id=1, source_target_pairs={{0,1},{1,2},{2,3},{4,5},{5,6},{6,7},{8,9},{9,10},{10,11},{12,13},{... | collective-permute-start | bytes 276488 | tf_op jit(solution)/shard_map/ppermute | solution.py:16
  16.5 4.3 %collective-permute-done.1 = bf16[2,15,1536]{2,1,0:T(8,128)(2,1)S(1)} collective-permute-done((bf16[2,15,1536]{2,1,0:T(8,128)(2,1)S(1)}, bf16[2,15,1536]{2,1,0:T(8,128)(2,1)S(1)}, u32[]{:S(2)}, u32[]{:S(2)}) %collective-permute-start.1) | collective-permute-done | bytes 92192 | tf_op jit(solution)/shard_map/ppermute | solution.py:17
  21.4 3.8 %fusion.143 = (f32[1536]{0:T(1024)S(1)}, f32[2,64,1536]{2,1,0:T(8,128)S(1)}) fusion(bf16[2,15,1536]{2,1,0:T(8,128)(2,1)S(1)} %collective-permute-done.1, bf16[2,64,1536]{2,1,0:T(8,128)(2,1)S(1)} %fusion, f32[1536]{0:T(1024)S(1)} %get-tuple-element.76, f32[1536]{0:T(1024)S(1)} %get-tuple-element.77, f32[1536]{0:T(1024)S(1)} %get-tuple-element.48, ...), kind=kLoop, calls=%fused_computation.383 | loop fusion | flops 35977728 | bytes 1560576 | tf_op jit(solution)/shard_map/reduce_sum | solution.py:110
  28.3 2.2 %collective-permute-done.3 = f32[2,1536]{1,0:T(2,128)S(1)} collective-permute-done((f32[2,1536]{1,0:T(2,128)S(1)}, f32[2,1536]{1,0:T(2,128)S(1)}, u32[]{:S(2)}, u32[]{:S(2)}) %collective-permute-start.3) | collective-permute-done | bytes 12320 | tf_op jit(solution)/shard_map/ppermute | solution.py:44
  30.6 1.6 collective-permute-start.4
  32.2 2.2 %collective-permute-done.4 = f32[2,1536]{1,0:T(2,128)S(1)} collective-permute-done((f32[2,1536]{1,0:T(2,128)S(1)}, f32[2,1536]{1,0:T(2,128)S(1)}, u32[]{:S(2)}, u32[]{:S(2)}) %collective-permute-start.4) | collective-permute-done | bytes 12320 | tf_op jit(solution)/shard_map/ppermute | solution.py:44
  34.4 1.6 collective-permute-start.5
  36.1 3.3 %collective-permute-done.5 = f32[2,1536]{1,0:T(2,128)S(1)} collective-permute-done((f32[2,1536]{1,0:T(2,128)S(1)}, f32[2,1536]{1,0:T(2,128)S(1)}, u32[]{:S(2)}, u32[]{:S(2)}) %collective-permute-start.5) | collective-permute-done | bytes 12320 | tf_op jit(solution)/shard_map/ppermute | solution.py:44
  39.5 1.7 collective-permute-start.6
  41.2 4.3 %collective-permute-done.6 = f32[2,1536]{1,0:T(2,128)S(1)} collective-permute-done((f32[2,1536]{1,0:T(2,128)S(1)}, f32[2,1536]{1,0:T(2,128)S(1)}, u32[]{:S(2)}, u32[]{:S(2)}) %collective-permute-start.6) | collective-permute-done | bytes 12320 | tf_op jit(solution)/shard_map/ppermute | solution.py:44
  46.3 3.7 %all-gather.4.cloned.1.call-done = bf16[512,1536]{1,0:T(8,128)(2,1)} async-done(((bf16[128,1536]{1,0:T(8,128)(2,1)}), bf16[512,1536]{1,0:T(8,128)(2,1)}) %all-gather.4.cloned.1.call-update) | async-done | bytes 1572880 | tf_op jit(solution)/shard_map/all_gather | solution.py:102
  50.0 2.4 %fusion.147 = f32[512,384]{1,0:T(8,128)S(1)} fusion(bf16[512,1536]{1,0:T(8,128)(2,1)} %all-gather.4.cloned.1.call-done, bf16[384,1536]{1,0:T(8,128)(2,1)S(1)} %copy-done), kind=kOutput, calls=%fused_computation.386 | convolution fusion | flops 603979776 | bytes 3538944 | tf_op jit(solution)/shard_map/fd,cd->fc/dot_general | solution.py:121
  52.4 22.6 %all_to_all.35 = f32[4,128,384]{2,1,0:T(8,128)S(1)} all-to-all(f32[4,128,384]{2,1,0:T(8,128)S(1)} %bitcast.32), channel_id=1, replica_groups=mesh['dp'=8,'tensor'=4] {'tensor'}, dimensions={0} | all-to-all | bytes 1572864 | tf_op jit(solution)/shard_map/all_to_all | solution.py:122
  76.8 1.6 fusion.140
  81.3 2.2 %collective-permute-done.10 = f32[2,1536]{1,0:T(2,128)S(1)} collective-permute-done((f32[2,1536]{1,0:T(2,128)S(1)}, f32[2,1536]{1,0:T(2,128)S(1)}, u32[]{:S(2)}, u32[]{:S(2)}) %collective-permute-start.10) | collective-permute-done | bytes 12320 | tf_op jit(solution)/shard_map/ppermute | solution.py:34
  85.1 2.2 %collective-permute-done.11 = f32[2,1536]{1,0:T(2,128)S(1)} collective-permute-done((f32[2,1536]{1,0:T(2,128)S(1)}, f32[2,1536]{1,0:T(2,128)S(1)}, u32[]{:S(2)}, u32[]{:S(2)}) %collective-permute-start.11) | collective-permute-done | bytes 12320 | tf_op jit(solution)/shard_map/ppermute | solution.py:34
  88.1 3.8 %collective-permute-done.12 = f32[2,1536]{1,0:T(2,128)} collective-permute-done((f32[2,1536]{1,0:T(2,128)}, f32[2,1536]{1,0:T(2,128)}, u32[]{:S(2)}, u32[]{:S(2)}) %collective-permute-start.12) | collective-permute-done | bytes 12320 | tf_op jit(solution)/shard_map/ppermute | solution.py:34
  95.1 1.8 copy.25
  96.8 4.3 %all-to-all-start.1 = ((bf16[128,4,384]{2,0,1:T(8,128)(2,1)}), bf16[128,4,384]{2,0,1:T(8,128)(2,1)}, u32[]{:S(2)}, u32[]{:S(2)}) async-start(bf16[128,4,384]{2,0,1:T(8,128)(2,1)} %copy.25), calls=%async_computation.1 | async-start | bytes 786432 | tf_op jit(solution)/shard_map/all_to_all | solution.py:131
  102.0 2.9 %fusion.80 = (f32[1536]{0:T(1024)S(1)}, f32[1536]{0:T(1024)S(1)}, f32[1536]{0:T(1024)S(1)}, f32[1536]{0:T(1024)S(1)}, f32[1536]{0:T(1024)S(1)}, /*index=5*/f32[1...) fusion(bf16[2,15,1536]{2,1,0:T(8,128)(2,1)} %copy-done.7, ...), kind=kLoop, calls=%fused_computation.211 | loop fusion | flops 12372480 | bytes 2537472 | tf_op jit(solution)/shard_map/reduce_sum | solution.py:150
  108.3 2.8 %stack.196 = f32[31,1536]{1,0:T(8,128)} concatenate(f32[1,1536]{1,0:T(1,128)S(1)} %stack.165, f32[1,1536]{1,0:T(1,128)S(1)} %stack.166, f32[1,1536]{1,0:T(1,128)S(1)} %stack.167, f32[1,1536]{1,0:T(1,128)S(1)} %stack.168, f32[1,1536]{1,0:T(1,128)S(1)} %stack.169, f32[1,1536]{1,0:T(1,128)S(1)} %stack.170, f32[1,1536]{1,0:T(1,128)S(1)} %stack.171, f32[1,1536]{1,0:T(1,128)S(1)} %stack.172, ...), dimensions={0} | concatenate | bytes 380928 | tf_op jit(solution)/shard_map/stack | solution.py:148
  111.0 6.4 %all-to-all-done.1 = bf16[128,4,384]{2,0,1:T(8,128)(2,1)} async-done(((bf16[128,4,384]{2,0,1:T(8,128)(2,1)}), bf16[128,4,384]{2,0,1:T(8,128)(2,1)}, u32[]{:S(2)}, u32[]{:S(2)}) %all-to-all-start.1) | async-done | bytes 393248 | tf_op jit(solution)/shard_map/all_to_all | solution.py:131
  117.4 2.3 %fusion.148 = f32[384,1536]{1,0:T(8,128)S(1)} fusion(bf16[512,384]{1,0:T(8,128)(2,1)} %bitcast.13, bf16[512,1536]{1,0:T(8,128)(2,1)} %all-gather.4.cloned.1.call-done), kind=kOutput, calls=%fused_computation.387 | convolution fusion | flops 603979776 | bytes 4325376 | tf_op jit(solution)/shard_map/fc,fd->cd/dot_general | solution.py:132
  120.9 8.3 %all-gather.6.cloned.1.call-done = bf16[384,1536]{1,0:T(8,128)(2,1)} async-done(((bf16[96,1536]{1,0:T(8,128)(2,1)}), bf16[384,1536]{1,0:T(8,128)(2,1)}) %all-gather.6.cloned.1.call-update) | async-done | bytes 1179664 | tf_op jit(solution)/shard_map/all_gather | solution.py:83
  132.8 25.5 %collective-permute-done.7 = bf16[4,96,1536]{2,1,0:T(8,128)(2,1)} collective-permute-done((bf16[4,96,1536]{2,1,0:T(8,128)(2,1)}, bf16[4,96,1536]{2,1,0:T(8,128)(2,1)}, u32[]{:S(2)}, u32[]{:S(2)}) %collective-permute-start.7) | collective-permute-done | bytes 1179680 | tf_op jit(solution)/shard_map/ppermute | solution.py:84
  162.8 8.0 %collective-permute-done.17 = f32[96,1536]{1,0:T(8,128)S(1)} collective-permute-done((f32[96,1536]{1,0:T(8,128)S(1)}, f32[96,1536]{1,0:T(8,128)S(1)}, u32[]{:S(2)}, u32[]{:S(2)}) %collective-permute-start.17) | collective-permute-done | bytes 589856 | tf_op jit(solution)/shard_map/ppermute | solution.py:65
  174.1 4.6 %collective-permute-start.15 = (bf16[2,15,1536]{2,1,0:T(8,128)(2,1)S(1)}, bf16[2,15,1536]{2,1,0:T(8,128)(2,1)S(1)}, u32[]{:S(2)}, u32[]{:S(2)}) collective-permute-start(bf16[2,15,1536]{2,1,0:T(8,128)(2,1)S(1)} %get-tuple-element.104), channel_id=1, source_target_pairs={{0,1},{1,2},{2,3},{4,5},{5,6},{6,7},{8,9},{9,10},{10,11},{12,13},{... | collective-permute-start | bytes 276488 | tf_op jit(solution)/shard_map/ppermute | solution.py:16
  181.2 4.1 %multiply_convert_fusion = (bf16[2,64,1536]{2,1,0:T(8,128)(2,1)S(1)}, f32[2,64,1536]{2,1,0:T(8,128)S(1)}) fusion(bf16[2,64,3072]{2,1,0:T(8,128)(2,1)S(1)} %copy-done.3, bf16[2,64,1536]{2,1,0:T(8,128)(2,1)S(1)} %copy-done.2, bf16[2,15,1536]{2,1,0:T(8,128)(2,1)S(1)} %collective-permute-done.15, f32[1536]{0:T(1024)S(1)} %copy-done.68, f32[1536]{0:T(1024)S(1)} %copy-done.70, ...), kind=kLoop, calls=%fused_computation.213 | loop fusion | flops 36962304 | bytes 2340864 | tf_op jit(solution)/shard_map/convert
  186.1 1.6 collective-permute-start.25
  191.1 2.2 %collective-permute-done.25 = f32[31,1536]{1,0:T(8,128)S(1)} collective-permute-done((f32[31,1536]{1,0:T(8,128)S(1)}, f32[31,1536]{1,0:T(8,128)S(1)}, u32[]{:S(2)}, u32[]{:S(2)}) %collective-permute-start.25) | collective-permute-done | bytes 190496 | tf_op jit(solution)/shard_map/ppermute | solution.py:34
  194.4 7.7 %collective-permute-done.26 = f32[31,1536]{1,0:T(8,128)S(1)} collective-permute-done((f32[31,1536]{1,0:T(8,128)S(1)}, f32[31,1536]{1,0:T(8,128)S(1)}, u32[]{:S(2)}, u32[]{:S(2)}) %collective-permute-start.26) | collective-permute-done | bytes 190496 | tf_op jit(solution)/shard_map/ppermute | solution.py:34
  205.8 1.6 maximum_select_fusion
  (276 shorter events, 46.0 us)
Async XLA Ops:
  7.2 42.8 %all-gather.4.cloned.1.call-start = ((), (), s32[]{:S(2)}) async-start(), calls=%async_computation.2 | async-start | bytes 1966080 | tf_op jit(solution)/shard_map/all_gather | solution.py:102
  7.9 121.2 %all-gather.6.cloned.1.call-start = ((), (), s32[]{:S(2)}) async-start(), calls=%async_computation.3 | async-start | bytes 1474560 | tf_op jit(solution)/shard_map/all_gather | solution.py:83
  9.3 7.1 %collective-permute-start = (bf16[2,15,1536]{2,1,0:T(8,128)(2,1)S(1)}, bf16[2,15,1536]{2,1,0:T(8,128)(2,1)S(1)}, u32[]{:S(2)}, u32[]{:S(2)}) collective-permute-start(bf16[2,15,1536]{2,1,0:T(8,128)(2,1)S(1)} %get-tuple-element.105), channel_id=1, source_target_pairs={{0,1},{1,2},{2,3},{4,5},{5,6},{6,7},{8,9},{9,10},{10,11},{12,13},{... | collective-permute-start | bytes 276488 | tf_op jit(solution)/shard_map/ppermute | solution.py:16
  14.3 6.5 %collective-permute-start.1 = (bf16[2,15,1536]{2,1,0:T(8,128)(2,1)S(1)}, bf16[2,15,1536]{2,1,0:T(8,128)(2,1)S(1)}, u32[]{:S(2)}, u32[]{:S(2)}) collective-permute-start(bf16[2,15,1536]{2,1,0:T(8,128)(2,1)S(1)} %get-tuple-element.106), channel_id=1, source_target_pairs={{1,0},{2,1},{3,2},{5,4},{6,5},{7,6},{9,8},{10,9},{11,10},{13,12},{... | collective-permute-start | bytes 276488 | tf_op jit(solution)/shard_map/ppermute | solution.py:17
  16.4 58.7 %copy-start.61 = (f32[1536]{0:T(1024)}, f32[1536]{0:T(1024)S(1)}, u32[]{:S(2)}) copy-start(f32[1536]{0:T(1024)S(1)} %get-tuple-element.73) | copy-start | bytes 18436
  16.4 58.7 %copy-start.63 = (f32[1536]{0:T(1024)}, f32[1536]{0:T(1024)S(1)}, u32[]{:S(2)}) copy-start(f32[1536]{0:T(1024)S(1)} %get-tuple-element.74) | copy-start | bytes 18436
  25.5 1.2 collective-permute-start.2
  26.8 3.8 %collective-permute-start.3 = (f32[2,1536]{1,0:T(2,128)S(1)}, f32[2,1536]{1,0:T(2,128)S(1)}, u32[]{:S(2)}, u32[]{:S(2)}) collective-permute-start(f32[2,1536]{1,0:T(2,128)S(1)} %pad_maximum_fusion.8), channel_id=1, source_target_pairs={{0,8},{4,12},{8,0},{12,4},{16,24},{20,28},{24,16},{28,20},{1,9},{5... | collective-permute-start | bytes 36872 | tf_op jit(solution)/shard_map/ppermute | solution.py:44
  30.6 3.8 %collective-permute-start.4 = (f32[2,1536]{1,0:T(2,128)S(1)}, f32[2,1536]{1,0:T(2,128)S(1)}, u32[]{:S(2)}, u32[]{:S(2)}) collective-permute-start(f32[2,1536]{1,0:T(2,128)S(1)} %pad_maximum_fusion.9), channel_id=1, source_target_pairs={{0,16},{4,20},{8,24},{12,28},{16,0},{20,4},{24,8},{28,12},{1,17},{... | collective-permute-start | bytes 36872 | tf_op jit(solution)/shard_map/ppermute | solution.py:44
  34.4 5.0 %collective-permute-start.5 = (f32[2,1536]{1,0:T(2,128)S(1)}, f32[2,1536]{1,0:T(2,128)S(1)}, u32[]{:S(2)}, u32[]{:S(2)}) collective-permute-start(f32[2,1536]{1,0:T(2,128)S(1)} %pad_maximum_fusion.10), channel_id=1, source_target_pairs={{0,1},{1,0},{2,3},{3,2},{4,5},{5,4},{6,7},{7,6},{8,9},{9,8},{10,11... | collective-permute-start | bytes 36872 | tf_op jit(solution)/shard_map/ppermute | solution.py:44
  39.5 6.0 %collective-permute-start.6 = (f32[2,1536]{1,0:T(2,128)S(1)}, f32[2,1536]{1,0:T(2,128)S(1)}, u32[]{:S(2)}, u32[]{:S(2)}) collective-permute-start(f32[2,1536]{1,0:T(2,128)S(1)} %pad_maximum_fusion.11), channel_id=1, source_target_pairs={{0,2},{1,3},{2,0},{3,1},{4,6},{5,7},{6,4},{7,5},{8,10},{9,11},{10,... | collective-permute-start | bytes 36872 | tf_op jit(solution)/shard_map/ppermute | solution.py:44
  78.5 1.2 collective-permute-start.9
  79.8 3.8 %collective-permute-start.10 = (f32[2,1536]{1,0:T(2,128)S(1)}, f32[2,1536]{1,0:T(2,128)S(1)}, u32[]{:S(2)}, u32[]{:S(2)}) collective-permute-start(f32[2,1536]{1,0:T(2,128)S(1)} %fusion.139), channel_id=1, source_target_pairs={{0,8},{4,12},{8,0},{12,4},{16,24},{20,28},{24,16},{28,20},{1,9},{5... | collective-permute-start | bytes 36872 | tf_op jit(solution)/shard_map/ppermute | solution.py:34
  83.5 3.8 %collective-permute-start.11 = (f32[2,1536]{1,0:T(2,128)S(1)}, f32[2,1536]{1,0:T(2,128)S(1)}, u32[]{:S(2)}, u32[]{:S(2)}) collective-permute-start(f32[2,1536]{1,0:T(2,128)S(1)} %fusion.155), channel_id=1, source_target_pairs={{0,16},{4,20},{8,24},{12,28},{16,0},{20,4},{24,8},{28,12},{1,17},{... | collective-permute-start | bytes 36872 | tf_op jit(solution)/shard_map/ppermute | solution.py:34
  87.9 4.0 %collective-permute-start.12 = (f32[2,1536]{1,0:T(2,128)}, f32[2,1536]{1,0:T(2,128)}, u32[]{:S(2)}, u32[]{:S(2)}) collective-permute-start(f32[2,1536]{1,0:T(2,128)} %add.502), channel_id=1, source_target_pairs={{0,1},{1,0},{2,3},{3,2},{4,5},{5,4},{6,7},{7,6},{8,9},{9,8},{10,11... | collective-permute-start | bytes 36872 | tf_op jit(solution)/shard_map/ppermute | solution.py:34
  93.3 7.9 %collective-permute-start.13 = (f32[2,1536]{1,0:T(2,128)}, f32[2,1536]{1,0:T(2,128)}, u32[]{:S(2)}, u32[]{:S(2)}) collective-permute-start(f32[2,1536]{1,0:T(2,128)} %add.503), channel_id=1, source_target_pairs={{0,2},{1,3},{2,0},{3,1},{4,6},{5,7},{6,4},{7,5},{8,10},{9,11},{10,... | collective-permute-start | bytes 36872 | tf_op jit(solution)/shard_map/ppermute | solution.py:34
  96.8 20.6 %all-to-all-start.1 = ((bf16[128,4,384]{2,0,1:T(8,128)(2,1)}), bf16[128,4,384]{2,0,1:T(8,128)(2,1)}, u32[]{:S(2)}, u32[]{:S(2)}) async-start(bf16[128,4,384]{2,0,1:T(8,128)(2,1)} %copy.25), calls=%async_computation.1 | async-start | bytes 786432 | tf_op jit(solution)/shard_map/all_to_all | solution.py:131
  120.9 9.7 %collective-permute-start.16 = (f32[192,1536]{1,0:T(8,128)}, f32[192,1536]{1,0:T(8,128)}, u32[]{:S(2)}, u32[]{:S(2)}) collective-permute-start(f32[192,1536]{1,0:T(8,128)} %constant_dynamic-slice_fusion.2), channel_id=1, source_target_pairs={{0,4},{4,0},{8,12},{12,8},{16,20},{20,16},{24,28},{28,24},{1,5},{5... | collective-permute-start | bytes 3538952 | tf_op jit(solution)/shard_map/ppermute | solution.py:65
  129.1 29.1 %collective-permute-start.7 = (bf16[4,96,1536]{2,1,0:T(8,128)(2,1)}, bf16[4,96,1536]{2,1,0:T(8,128)(2,1)}, u32[]{:S(2)}, u32[]{:S(2)}) collective-permute-start(bf16[4,96,1536]{2,1,0:T(8,128)(2,1)} %bitcast.30), channel_id=1, source_target_pairs={{0,8},{4,12},{8,0},{12,4},{16,24},{20,28},{24,16},{28,20},{1,9},{5... | collective-permute-start | bytes 3538952 | tf_op jit(solution)/shard_map/ppermute | solution.py:84
  132.2 38.6 %collective-permute-start.17 = (f32[96,1536]{1,0:T(8,128)S(1)}, f32[96,1536]{1,0:T(8,128)S(1)}, u32[]{:S(2)}, u32[]{:S(2)}) collective-permute-start(f32[96,1536]{1,0:T(8,128)S(1)} %constant_dynamic-slice_fusion.1), channel_id=1, source_target_pairs={{0,8},{4,12},{8,0},{12,4},{16,24},{20,28},{24,16},{28,20},{1,9},{5... | collective-permute-start | bytes 1769480 | tf_op jit(solution)/shard_map/ppermute | solution.py:65
  159.7 1.5 collective-permute-start.22
  160.1 42.9 %collective-permute-start.8 = (bf16[4,2,96,1536]{3,2,1,0:T(8,128)(2,1)S(1)}, bf16[4,2,96,1536]{3,2,1,0:T(8,128)(2,1)S(1)}, u32[]{:S(2)}, u32[]{:S(2)}) collective-permute-start(bf16[4,2,96,1536]{3,2,1,0:T(8,128)(2,1)S(1)} %pad_maximum_fusion.1), channel_id=1, source_target_pairs={{0,4},{4,0},{8,12},{12,8},{16,20},{20,16},{24,28},{28,24},{1,5},{5... | collective-permute-start | bytes 7077896 | tf_op jit(solution)/shard_map/ppermute | solution.py:86
  161.3 17.4 %collective-permute-start.23 = (f32[31,1536]{1,0:T(8,128)S(1)}, f32[31,1536]{1,0:T(8,128)S(1)}, u32[]{:S(2)}, u32[]{:S(2)}) collective-permute-start(f32[31,1536]{1,0:T(8,128)S(1)} %add.544), channel_id=1, source_target_pairs={{0,8},{4,12},{8,0},{12,4},{16,24},{20,28},{24,16},{28,20},{1,9},{5... | collective-permute-start | bytes 571400 | tf_op jit(solution)/shard_map/ppermute | solution.py:34
  171.2 8.1 %collective-permute-start.18 = (f32[48,1536]{1,0:T(8,128)S(1)}, f32[48,1536]{1,0:T(8,128)S(1)}, u32[]{:S(2)}, u32[]{:S(2)}) collective-permute-start(f32[48,1536]{1,0:T(8,128)S(1)} %constant_dynamic-slice_fusion), channel_id=1, source_target_pairs={{0,16},{4,20},{8,24},{12,28},{16,0},{20,4},{24,8},{28,12},{1,17},{... | collective-permute-start | bytes 884744 | tf_op jit(solution)/shard_map/ppermute | solution.py:65
  172.8 8.1 %collective-permute-start.14 = (bf16[2,15,1536]{2,1,0:T(8,128)(2,1)S(1)}, bf16[2,15,1536]{2,1,0:T(8,128)(2,1)S(1)}, u32[]{:S(2)}, u32[]{:S(2)}) collective-permute-start(bf16[2,15,1536]{2,1,0:T(8,128)(2,1)S(1)} %get-tuple-element.103), channel_id=1, source_target_pairs={{1,0},{2,1},{3,2},{5,4},{6,5},{7,6},{9,8},{10,9},{11,10},{13,12},{... | collective-permute-start | bytes 276488 | tf_op jit(solution)/shard_map/ppermute | solution.py:17
  174.1 6.8 %collective-permute-start.15 = (bf16[2,15,1536]{2,1,0:T(8,128)(2,1)S(1)}, bf16[2,15,1536]{2,1,0:T(8,128)(2,1)S(1)}, u32[]{:S(2)}, u32[]{:S(2)}) collective-permute-start(bf16[2,15,1536]{2,1,0:T(8,128)(2,1)S(1)} %get-tuple-element.104), channel_id=1, source_target_pairs={{0,1},{1,2},{2,3},{4,5},{5,6},{6,7},{8,9},{9,10},{10,11},{12,13},{... | collective-permute-start | bytes 276488 | tf_op jit(solution)/shard_map/ppermute | solution.py:16
  178.7 7.4 %collective-permute-start.24 = (f32[31,1536]{1,0:T(8,128)S(1)}, f32[31,1536]{1,0:T(8,128)S(1)}, u32[]{:S(2)}, u32[]{:S(2)}) collective-permute-start(f32[31,1536]{1,0:T(8,128)S(1)} %add.545), channel_id=1, source_target_pairs={{0,16},{4,20},{8,24},{12,28},{16,0},{20,4},{24,8},{28,12},{1,17},{... | collective-permute-start | bytes 571400 | tf_op jit(solution)/shard_map/ppermute | solution.py:34
  179.4 9.9 %collective-permute-start.19 = (f32[48,1536]{1,0:T(8,128)S(1)}, f32[48,1536]{1,0:T(8,128)S(1)}, u32[]{:S(2)}, u32[]{:S(2)}) collective-permute-start(f32[48,1536]{1,0:T(8,128)S(1)} %dynamic-slice_add_fusion.2), channel_id=1, source_target_pairs={{0,16},{4,20},{8,24},{12,28},{16,0},{20,4},{24,8},{28,12},{1,17},{... | collective-permute-start | bytes 884744 | tf_op jit(solution)/shard_map/ppermute | solution.py:69
  186.1 7.2 %collective-permute-start.25 = (f32[31,1536]{1,0:T(8,128)S(1)}, f32[31,1536]{1,0:T(8,128)S(1)}, u32[]{:S(2)}, u32[]{:S(2)}) collective-permute-start(f32[31,1536]{1,0:T(8,128)S(1)} %add.546), channel_id=1, source_target_pairs={{0,1},{1,0},{2,3},{3,2},{4,5},{5,4},{6,7},{7,6},{8,9},{9,8},{10,11... | collective-permute-start | bytes 571400 | tf_op jit(solution)/shard_map/ppermute | solution.py:34
  189.3 13.5 %collective-permute-start.20 = (f32[96,1536]{1,0:T(8,128)S(1)}, f32[96,1536]{1,0:T(8,128)S(1)}, u32[]{:S(2)}, u32[]{:S(2)}) collective-permute-start(f32[96,1536]{1,0:T(8,128)S(1)} %maximum_select_fusion.2), channel_id=1, source_target_pairs={{0,8},{4,12},{8,0},{12,4},{16,24},{20,28},{24,16},{28,20},{1,9},{5... | collective-permute-start | bytes 1769480 | tf_op jit(solution)/shard_map/ppermute | solution.py:69
  193.4 8.7 %collective-permute-start.26 = (f32[31,1536]{1,0:T(8,128)S(1)}, f32[31,1536]{1,0:T(8,128)S(1)}, u32[]{:S(2)}, u32[]{:S(2)}) collective-permute-start(f32[31,1536]{1,0:T(8,128)S(1)} %add.547), channel_id=1, source_target_pairs={{0,2},{1,3},{2,0},{3,1},{4,6},{5,7},{6,4},{7,5},{8,10},{9,11},{10,... | collective-permute-start | bytes 571400 | tf_op jit(solution)/shard_map/ppermute | solution.py:34
  202.9 2.9 %collective-permute-start.21 = (f32[192,1536]{1,0:T(8,128)S(1)}, f32[192,1536]{1,0:T(8,128)S(1)}, u32[]{:S(2)}, u32[]{:S(2)}) collective-permute-start(f32[192,1536]{1,0:T(8,128)S(1)} %maximum_select_fusion.1), channel_id=1, source_target_pairs={{0,4},{4,0},{8,12},{12,8},{16,20},{20,16},{24,28},{28,24},{1,5},{5... | collective-permute-start | bytes 3538952 | tf_op jit(solution)/shard_map/ppermute | solution.py:69
  (72 other events, 1438.3 us)
Sparse Core Ops, SparseCore 0:
  9.6 40.3 all-gather.3
  94.3 34.7 all-gather.5

commit v12 on v4

--- a/solution.py
+++ b/solution.py
@@ -71,18 +71,19 @@
     return x
 
 
-def gather_weight(block):
+def gather_weight(block, anchor):
     if lax.axis_size("dp") % 2:
-        return lax.all_gather(block, "tensor", axis=0, tiled=True)
+        return lax.all_gather(block, "tensor", axis=0, tiled=True), anchor
     peers = lax.axis_size("tensor")
     half = block.shape[0] // 2
     core = lax.rem(lax.axis_index("dp"), 2)
     mine = lax.dynamic_slice_in_dim(block, core * half, half, axis=0)
     held = lax.all_gather(mine, "tensor", axis=0, tiled=False)
+    held, anchor = lax.optimization_barrier((held, anchor))
     other = lax.ppermute(held, "dp", [(i, i ^ 1) for i in range(lax.axis_size("dp"))])
     first = jnp.where(core == 0, held, other)
     second = jnp.where(core == 0, other, held)
-    return jnp.concatenate([first, second], axis=1).reshape(peers * block.shape[0], block.shape[1])
+    return jnp.concatenate([first, second], axis=1).reshape(peers * block.shape[0], block.shape[1]), anchor
 
 
 def on_device(glu_input, depth_kernel, norm_scale, norm_shift, proj_weight, out_grad):
@@ -95,7 +96,6 @@
     me = lax.axis_index("tensor")
     local = glu_input.shape[0] * frames
     everyone = local * lax.axis_size("dp") * peers
-    full_weight = gather_weight(proj_weight)
     flat_grad = out_grad.reshape(-1, width)
     group_grad = lax.all_gather(flat_grad, "tensor", axis=0, tiled=True)
     values = glu_input[..., :width].astype(jnp.float32)
@@ -115,6 +115,7 @@
         average = lax.psum(jnp.sum(conv_out, axis=(0, 1)), ("dp", "tensor")) / everyone
         centred0 = conv_out - average
         variance = lax.psum(jnp.sum(centred0 * centred0, axis=(0, 1)), ("dp", "tensor")) / everyone
+    full_weight, average = gather_weight(proj_weight, average)
     centred = conv_out - average
     inverse = lax.rsqrt(variance + epsilon)
     normed = centred * inverse

time: 233 us -> 221 us (0.948)
  waiting for transfers between devices: 137 us -> 126 us
    all_gather x1, waiting for transfers between devices: 37.2 us -> 25.7 us  [gather_weight(): held = lax.all_gather(mine, 'tensor', axis=0, tiled=False)]
    ppermute x1, waiting for transfers between devices: 0.01 us -> 4.87 us  [gather_weight(): lax.ppermute(held, 'dp', [(i, i ^ 1) for i in range(lax.axis_size('dp'))])]
    ppermute x2, waiting for transfers between devices: 4.32 us -> 0.01 us  [extended(): after = lax.ppermute(leading, axis, down)]
    ppermute x5, waiting for transfers between devices: 15.1 us -> 11.2 us  [all_moments(): lax.ppermute(jnp.stack([mean, spread]), axis, [(i, i ^ step) for i in ran...]
    ppermute x5, starting transfers between devices: 5.02 us -> 8.55 us  [all_moments(): lax.ppermute(jnp.stack([mean, spread]), axis, [(i, i ^ step) for i in ran...]
    ppermute x10, waiting for transfers between devices: 32.2 us -> 35.2 us  [all_sum(): x = x + lax.ppermute(x, axis, [(i, i ^ step) for i in range(peers)])]
    ppermute x2, starting transfers between devices: 9.48 us -> 6.86 us  [extended(): before = lax.ppermute(last, axis, up)]
  transfers between devices with their start and end apart: 29 -> 29, of which waited for: 20 -> 20; matrix products, arithmetic and copies ran while one was open for 11% -> 12% of each run, Pallas kernels for 0% -> 0%
where the time goes in v12:
time: 221 us
  waiting for transfers between devices  126 us (57%)
  starting transfers between devices  35.1 us (16%)
  other arithmetic  26.2 us (12%)
  between operations  15.8 us (7%)
  local copies, waits for them, and re-layouts  9.15 us (4%)
  matrix products  8.83 us (4%)
    ppermute x10, waiting for transfers between devices, all_sum(): x = x + lax.ppermute(x, axis, [(i, i ^ step) for i in range(peers)])  35.2 us
    all_gather x1, waiting for transfers between devices, gather_weight(): held = lax.all_gather(mine, 'tensor', axis=0, tiled=False)  25.7 us
    ppermute x3, waiting for transfers between devices, rows_sum(): x = keep + lax.ppermute(give, axis, [(i, i ^ step) for i in range(peers)])  23.8 us
    all_gather x1, waiting for transfers between devices, on_device(): group_grad = lax.all_gather(flat_grad, 'tensor', axis=0, tiled=True)  18.5 us
    ppermute x5, waiting for transfers between devices, all_moments(): lax.ppermute(jnp.stack([mean, spread]), axis, [(i, i ^ step) for i in ran...  11.2 us
    ppermute x5, starting transfers between devices, all_moments(): lax.ppermute(jnp.stack([mean, spread]), axis, [(i, i ^ step) for i in ran...  8.55 us
    ppermute x2, starting transfers between devices, extended(): before = lax.ppermute(last, axis, up)  6.86 us
    ppermute x10, starting transfers between devices, all_sum(): x = x + lax.ppermute(x, axis, [(i, i ^ step) for i in range(peers)])  6.52 us
  transfers between devices with their start and end apart: 29, of which 20 were waited for; matrix products, arithmetic and copies ran while one was open for 12% of the time, Pallas kernels for 0%

profile of v12, /device:TPU:0, one launch (start us, length us, event | category | flops | bytes accessed | tf_op | source)
XLA Modules:
  0.0 220.6 jit_solution(464868710675443772)
XLA Ops:
  10.0 5.6 %collective-permute-start = (bf16[2,15,1536]{2,1,0:T(8,128)(2,1)S(1)}, bf16[2,15,1536]{2,1,0:T(8,128)(2,1)S(1)}, u32[]{:S(2)}, u32[]{:S(2)}) collective-permute-start(bf16[2,15,1536]{2,1,0:T(8,128)(2,1)S(1)} %get-tuple-element.102), channel_id=1, source_target_pairs={{0,1},{1,2},{2,3},{4,5},{5,6},{6,7},{8,9},{9,10},{10,11},{12,13},{... | collective-permute-start | bytes 276488 | tf_op jit(solution)/shard_map/ppermute | solution.py:16
  17.8 3.8 %fusion.144 = (f32[1536]{0:T(1024)S(1)}, f32[2,64,1536]{2,1,0:T(8,128)S(1)}) fusion(bf16[2,15,1536]{2,1,0:T(8,128)(2,1)S(1)} %collective-permute-done.1, bf16[2,64,1536]{2,1,0:T(8,128)(2,1)S(1)} %fusion.1, f32[1536]{0:T(1024)S(1)} %get-tuple-element.76, f32[1536]{0:T(1024)S(1)} %get-tuple-element.77, f32[1536]{0:T(1024)S(1)} %get-tuple-element.48, ...), kind=kLoop, calls=%fused_computation.381 | loop fusion | flops 35977728 | bytes 1560576 | tf_op jit(solution)/shard_map/reduce_sum | solution.py:108
  23.1 2.0 collective-permute-start.3
  25.1 1.8 collective-permute-done.3
  26.9 2.0 collective-permute-start.4
  29.0 1.7 collective-permute-done.4
  30.8 2.5 %collective-permute-start.5 = (f32[2,1536]{1,0:T(2,128)S(1)}, f32[2,1536]{1,0:T(2,128)S(1)}, u32[]{:S(2)}, u32[]{:S(2)}) collective-permute-start(f32[2,1536]{1,0:T(2,128)S(1)} %pad_maximum_fusion.9), channel_id=1, source_target_pairs={{0,1},{1,0},{2,3},{3,2},{4,5},{5,4},{6,7},{7,6},{8,9},{9,8},{10,11... | collective-permute-start | bytes 36872 | tf_op jit(solution)/shard_map/ppermute | solution.py:44
  33.2 3.4 %collective-permute-done.5 = f32[2,1536]{1,0:T(2,128)S(1)} collective-permute-done((f32[2,1536]{1,0:T(2,128)S(1)}, f32[2,1536]{1,0:T(2,128)S(1)}, u32[]{:S(2)}, u32[]{:S(2)}) %collective-permute-start.5) | collective-permute-done | bytes 12320 | tf_op jit(solution)/shard_map/ppermute | solution.py:44
  36.8 2.0 collective-permute-start.6
  38.8 3.1 %collective-permute-done.6 = f32[2,1536]{1,0:T(2,128)S(1)} collective-permute-done((f32[2,1536]{1,0:T(2,128)S(1)}, f32[2,1536]{1,0:T(2,128)S(1)}, u32[]{:S(2)}, u32[]{:S(2)}) %collective-permute-start.6) | collective-permute-done | bytes 12320 | tf_op jit(solution)/shard_map/ppermute | solution.py:44
  42.5 25.7 %all-gather.6.cloned.1.call-done = bf16[768,1536]{1,0:T(8,128)(2,1)} async-done(((bf16[192,1536]{1,0:T(8,128)(2,1)}), bf16[768,1536]{1,0:T(8,128)(2,1)}) %all-gather.6.cloned.1.call-update) | async-done | bytes 2359312 | tf_op jit(solution)/shard_map/all_gather | solution.py:81
  68.2 4.9 %collective-permute-done.7 = bf16[4,192,1536]{2,1,0:T(8,128)(2,1)} collective-permute-done((bf16[4,192,1536]{2,1,0:T(8,128)(2,1)}, bf16[4,192,1536]{2,1,0:T(8,128)(2,1)}, u32[]{:S(2)}, u32[]{:S(2)}) %collective-permute-start.7) | collective-permute-done | bytes 2359328 | tf_op jit(solution)/shard_map/ppermute | solution.py:83
  73.1 2.7 %broadcast_select_fusion.1 = (bf16[4,192,1536]{2,1,0:T(8,128)(2,1)S(1)}, bf16[4,192,1536]{2,1,0:T(8,128)(2,1)S(1)}) fusion(bf16[4,192,1536]{2,1,0:T(8,128)(2,1)} %bitcast.21, bf16[4,192,1536]{2,1,0:T(8,128)(2,1)} %collective-permute-done.7, pred[]{:T(512)S(6)} %eq.11), kind=kLoop, calls=%fused_computation.38 | loop fusion | flops 2359296 | bytes 9437185 | tf_op jit(solution)/shard_map/jit(_where)/select_n | solution.py:84
  77.1 2.6 %fusion.141 = (f32[1536]{0:T(1024)S(1)}, f32[1536]{0:T(1024)S(1)}, bf16[2,64,1536]{2,1,0:T(8,128)(2,1)S(1)}, f32[2,64,1536]{2,1,0:T(8,128)}) fusion(f32[1536]{0:T(1024)S(1)} %copy-done.70, f32[2,64,1536]{2,1,0:T(8,128)S(1)} %get-tuple-element.96, f32[1536]{0:T(1024)S(1)} %copy-done.71, f32[1536]{0:T(1024)S(1)} %copy-done.75, f32[1536]{0:T(1024)S(1)} %copy-done.74, ...), kind=kOutput, calls=%fused_computation.379 | convolution fusion | flops 607122432 | bytes 7114752 | tf_op jit(solution)/shard_map/btd,cd->btc/dot_general | solution.py:131
  82.6 2.2 collective-permute-done.9
  86.4 2.2 %collective-permute-done.10 = f32[2,1536]{1,0:T(2,128)S(1)} collective-permute-done((f32[2,1536]{1,0:T(2,128)S(1)}, f32[2,1536]{1,0:T(2,128)S(1)}, u32[]{:S(2)}, u32[]{:S(2)}) %collective-permute-start.10) | collective-permute-done | bytes 12320 | tf_op jit(solution)/shard_map/ppermute | solution.py:34
  88.7 4.3 %collective-permute-done.11 = f32[2,1536]{1,0:T(2,128)S(1)} collective-permute-done((f32[2,1536]{1,0:T(2,128)S(1)}, f32[2,1536]{1,0:T(2,128)S(1)}, u32[]{:S(2)}, u32[]{:S(2)}) %collective-permute-start.11) | collective-permute-done | bytes 12320 | tf_op jit(solution)/shard_map/ppermute | solution.py:34
  94.6 4.3 %all-to-all-start = ((bf16[128,4,384]{2,0,1:T(8,128)(2,1)}), bf16[128,4,384]{2,0,1:T(8,128)(2,1)}, u32[]{:S(2)}, u32[]{:S(2)}) async-start(bf16[128,4,384]{2,0,1:T(8,128)(2,1)} %copy.12), calls=%async_computation | async-start | bytes 786432 | tf_op jit(solution)/shard_map/all_to_all | solution.py:126
  99.6 2.5 %fusion.81 = (f32[1536]{0:T(1024)S(1)}, f32[1536]{0:T(1024)S(1)}, f32[1536]{0:T(1024)S(1)}, f32[1536]{0:T(1024)S(1)}, f32[1536]{0:T(1024)S(1)}, /*index=5*/f32[1...) fusion(bf16[2,15,1536]{2,1,0:T(8,128)(2,1)S(1)} %collective-permute-done, ...), kind=kLoop, calls=%fused_computation.210 | loop fusion | flops 12372480 | bytes 2537472 | tf_op jit(solution)/shard_map/reduce_sum | solution.py:149
  105.5 2.8 %stack.172 = f32[31,1536]{1,0:T(8,128)} concatenate(f32[1,1536]{1,0:T(1,128)S(1)} %stack.141, f32[1,1536]{1,0:T(1,128)S(1)} %stack.142, f32[1,1536]{1,0:T(1,128)S(1)} %stack.143, f32[1,1536]{1,0:T(1,128)S(1)} %stack.144, f32[1,1536]{1,0:T(1,128)S(1)} %stack.145, f32[1,1536]{1,0:T(1,128)S(1)} %stack.146, f32[1,1536]{1,0:T(1,128)S(1)} %stack.147, f32[1,1536]{1,0:T(1,128)S(1)} %stack.148, ...), dimensions={0} | concatenate | bytes 380928 | tf_op jit(solution)/shard_map/stack | solution.py:147
  108.2 18.5 %all-gather.4.cloned.1.call-done = bf16[512,1536]{1,0:T(8,128)(2,1)} async-done(((bf16[128,1536]{1,0:T(8,128)(2,1)}), bf16[512,1536]{1,0:T(8,128)(2,1)}) %all-gather.4.cloned.1.call-update) | async-done | bytes 1572880 | tf_op jit(solution)/shard_map/all_gather | solution.py:100
  126.7 2.3 %fusion.148 = f32[384,1536]{1,0:T(8,128)S(1)} fusion(bf16[512,384]{1,0:T(8,128)(2,1)} %bitcast.6, bf16[512,1536]{1,0:T(8,128)(2,1)} %all-gather.4.cloned.1.call-done), kind=kOutput, calls=%fused_computation.384 | convolution fusion | flops 603979776 | bytes 4325376 | tf_op jit(solution)/shard_map/fc,fd->cd/dot_general | solution.py:127
  130.2 3.2 %collective-permute-done.15 = f32[192,1536]{1,0:T(8,128)} collective-permute-done((f32[192,1536]{1,0:T(8,128)}, f32[192,1536]{1,0:T(8,128)}, u32[]{:S(2)}, u32[]{:S(2)}) %collective-permute-start.15) | collective-permute-done | bytes 1179680 | tf_op jit(solution)/shard_map/ppermute | solution.py:65
  133.4 2.4 %dynamic-slice_add_fusion = f32[192,1536]{1,0:T(8,128)} fusion(f32[192,1536]{1,0:T(8,128)} %collective-permute-done.15, f32[384,1536]{1,0:T(8,128)S(1)} %fusion.148, s32[]{:T(128)S(6)} %select_n.64), kind=kLoop, calls=%fused_computation.96 | loop fusion | flops 294912 | bytes 3538948 | tf_op jit(solution)/shard_map/add | solution.py:65
  138.5 13.9 %collective-permute-done.16 = f32[96,1536]{1,0:T(8,128)S(1)} collective-permute-done((f32[96,1536]{1,0:T(8,128)S(1)}, f32[96,1536]{1,0:T(8,128)S(1)}, u32[]{:S(2)}, u32[]{:S(2)}) %collective-permute-start.16) | collective-permute-done | bytes 589856 | tf_op jit(solution)/shard_map/ppermute | solution.py:65
  155.1 6.7 %collective-permute-done.17 = f32[48,1536]{1,0:T(8,128)S(1)} collective-permute-done((f32[48,1536]{1,0:T(8,128)S(1)}, f32[48,1536]{1,0:T(8,128)S(1)}, u32[]{:S(2)}, u32[]{:S(2)}) %collective-permute-start.17) | collective-permute-done | bytes 294944 | tf_op jit(solution)/shard_map/ppermute | solution.py:65
  163.4 5.8 %collective-permute-done.18 = f32[48,1536]{1,0:T(8,128)S(1)} collective-permute-done((f32[48,1536]{1,0:T(8,128)S(1)}, f32[48,1536]{1,0:T(8,128)S(1)}, u32[]{:S(2)}, u32[]{:S(2)}) %collective-permute-start.18) | collective-permute-done | bytes 294944 | tf_op jit(solution)/shard_map/ppermute | solution.py:69
  170.9 3.9 %convolution_convert_fusion = bf16[2,64,1536]{2,1,0:T(8,128)(2,1)} fusion(bf16[2,64,1536]{2,1,0:T(8,128)(2,1)S(1)} %copy-done.6, bf16[1536,1536,1]{1,0,2:T(8,128)(2,1)} %bitcast.19), kind=kOutput, calls=%fused_computation.35 | convolution fusion | flops 604176384 | bytes 5505024 | tf_op jit(solution)/shard_map/btc,cd->btd/dot_general | solution.py:128
  178.3 8.0 %collective-permute-done.22 = f32[31,1536]{1,0:T(8,128)S(1)} collective-permute-done((f32[31,1536]{1,0:T(8,128)S(1)}, f32[31,1536]{1,0:T(8,128)S(1)}, u32[]{:S(2)}, u32[]{:S(2)}) %collective-permute-start.22) | collective-permute-done | bytes 190496 | tf_op jit(solution)/shard_map/ppermute | solution.py:34
  188.4 4.1 %multiply_convert_fusion = (bf16[2,64,1536]{2,1,0:T(8,128)(2,1)S(1)}, f32[2,64,1536]{2,1,0:T(8,128)S(1)}) fusion(bf16[2,64,3072]{2,1,0:T(8,128)(2,1)S(1)} %copy-done.4, bf16[2,64,1536]{2,1,0:T(8,128)(2,1)S(1)} %copy-done.3, bf16[2,15,1536]{2,1,0:T(8,128)(2,1)S(1)} %collective-permute-done.14, f32[1536]{0:T(1024)S(1)} %copy-done.65, f32[1536]{0:T(1024)S(1)} %copy-done.67, ...), kind=kLoop, calls=%fused_computation.212 | loop fusion | flops 36962304 | bytes 2340864 | tf_op jit(solution)/shard_map/convert
  192.8 7.0 %collective-permute-done.24 = f32[31,1536]{1,0:T(8,128)S(1)} collective-permute-done((f32[31,1536]{1,0:T(8,128)S(1)}, f32[31,1536]{1,0:T(8,128)S(1)}, u32[]{:S(2)}, u32[]{:S(2)}) %collective-permute-start.24) | collective-permute-done | bytes 190496 | tf_op jit(solution)/shard_map/ppermute | solution.py:34
  200.9 10.5 %collective-permute-done.25 = f32[31,1536]{1,0:T(8,128)S(1)} collective-permute-done((f32[31,1536]{1,0:T(8,128)S(1)}, f32[31,1536]{1,0:T(8,128)S(1)}, u32[]{:S(2)}, u32[]{:S(2)}) %collective-permute-start.25) | collective-permute-done | bytes 190496 | tf_op jit(solution)/shard_map/ppermute | solution.py:34
  (272 shorter events, 36.4 us)
Async XLA Ops:
  7.2 61.1 %all-gather.6.cloned.1.call-start = ((), (), s32[]{:S(2)}) async-start(), calls=%async_computation.2 | async-start | bytes 2949120 | tf_op jit(solution)/shard_map/all_gather | solution.py:81
  8.7 8.7 %collective-permute-start.1 = (bf16[2,15,1536]{2,1,0:T(8,128)(2,1)S(1)}, bf16[2,15,1536]{2,1,0:T(8,128)(2,1)S(1)}, u32[]{:S(2)}, u32[]{:S(2)}) collective-permute-start(bf16[2,15,1536]{2,1,0:T(8,128)(2,1)S(1)} %get-tuple-element.103), channel_id=1, source_target_pairs={{1,0},{2,1},{3,2},{5,4},{6,5},{7,6},{9,8},{10,9},{11,10},{13,12},{... | collective-permute-start | bytes 276488 | tf_op jit(solution)/shard_map/ppermute | solution.py:17
  10.0 7.8 %collective-permute-start = (bf16[2,15,1536]{2,1,0:T(8,128)(2,1)S(1)}, bf16[2,15,1536]{2,1,0:T(8,128)(2,1)S(1)}, u32[]{:S(2)}, u32[]{:S(2)}) collective-permute-start(bf16[2,15,1536]{2,1,0:T(8,128)(2,1)S(1)} %get-tuple-element.102), channel_id=1, source_target_pairs={{0,1},{1,2},{2,3},{4,5},{5,6},{6,7},{8,9},{9,10},{10,11},{12,13},{... | collective-permute-start | bytes 276488 | tf_op jit(solution)/shard_map/ppermute | solution.py:16
  16.5 110.3 %all-gather.4.cloned.1.call-start = ((), (), s32[]{:S(2)}) async-start(), calls=%async_computation.1 | async-start | bytes 1966080 | tf_op jit(solution)/shard_map/all_gather | solution.py:100
  16.9 58.9 %copy-start.10 = (f32[1536]{0:T(1024)}, f32[1536]{0:T(1024)S(1)}, u32[]{:S(2)}) copy-start(f32[1536]{0:T(1024)S(1)} %get-tuple-element.49) | copy-start | bytes 18436
  16.9 58.9 %copy-start.12 = (f32[1536]{0:T(1024)}, f32[1536]{0:T(1024)S(1)}, u32[]{:S(2)}) copy-start(f32[1536]{0:T(1024)S(1)} %get-tuple-element.50) | copy-start | bytes 18436
  16.9 58.9 %copy-start.14 = (f32[1536]{0:T(1024)}, f32[1536]{0:T(1024)S(1)}, u32[]{:S(2)}) copy-start(f32[1536]{0:T(1024)S(1)} %get-tuple-element.51) | copy-start | bytes 18436
  21.8 1.2 collective-permute-start.2
  23.1 3.8 %collective-permute-start.3 = (f32[2,1536]{1,0:T(2,128)S(1)}, f32[2,1536]{1,0:T(2,128)S(1)}, u32[]{:S(2)}, u32[]{:S(2)}) collective-permute-start(f32[2,1536]{1,0:T(2,128)S(1)} %pad_maximum_fusion.7), channel_id=1, source_target_pairs={{0,8},{4,12},{8,0},{12,4},{16,24},{20,28},{24,16},{28,20},{1,9},{5... | collective-permute-start | bytes 36872 | tf_op jit(solution)/shard_map/ppermute | solution.py:44
  26.9 3.8 %collective-permute-start.4 = (f32[2,1536]{1,0:T(2,128)S(1)}, f32[2,1536]{1,0:T(2,128)S(1)}, u32[]{:S(2)}, u32[]{:S(2)}) collective-permute-start(f32[2,1536]{1,0:T(2,128)S(1)} %pad_maximum_fusion.8), channel_id=1, source_target_pairs={{0,16},{4,20},{8,24},{12,28},{16,0},{20,4},{24,8},{28,12},{1,17},{... | collective-permute-start | bytes 36872 | tf_op jit(solution)/shard_map/ppermute | solution.py:44
  30.8 5.9 %collective-permute-start.5 = (f32[2,1536]{1,0:T(2,128)S(1)}, f32[2,1536]{1,0:T(2,128)S(1)}, u32[]{:S(2)}, u32[]{:S(2)}) collective-permute-start(f32[2,1536]{1,0:T(2,128)S(1)} %pad_maximum_fusion.9), channel_id=1, source_target_pairs={{0,1},{1,0},{2,3},{3,2},{4,5},{5,4},{6,7},{7,6},{8,9},{9,8},{10,11... | collective-permute-start | bytes 36872 | tf_op jit(solution)/shard_map/ppermute | solution.py:44
  36.8 5.1 %collective-permute-start.6 = (f32[2,1536]{1,0:T(2,128)S(1)}, f32[2,1536]{1,0:T(2,128)S(1)}, u32[]{:S(2)}, u32[]{:S(2)}) collective-permute-start(f32[2,1536]{1,0:T(2,128)S(1)} %pad_maximum_fusion.10), channel_id=1, source_target_pairs={{0,2},{1,3},{2,0},{3,1},{4,6},{5,7},{6,4},{7,5},{8,10},{9,11},{10,... | collective-permute-start | bytes 36872 | tf_op jit(solution)/shard_map/ppermute | solution.py:44
  68.2 4.9 %collective-permute-start.7 = (bf16[4,192,1536]{2,1,0:T(8,128)(2,1)}, bf16[4,192,1536]{2,1,0:T(8,128)(2,1)}, u32[]{:S(2)}, u32[]{:S(2)}) collective-permute-start(bf16[4,192,1536]{2,1,0:T(8,128)(2,1)} %bitcast.20), channel_id=1, source_target_pairs={{0,4},{4,0},{8,12},{12,8},{16,20},{20,16},{24,28},{28,24},{1,5},{5... | collective-permute-start | bytes 7077896 | tf_op jit(solution)/shard_map/ppermute | solution.py:83
  79.8 1.2 collective-permute-start.8
  81.0 3.8 %collective-permute-start.9 = (f32[2,1536]{1,0:T(2,128)S(1)}, f32[2,1536]{1,0:T(2,128)S(1)}, u32[]{:S(2)}, u32[]{:S(2)}) collective-permute-start(f32[2,1536]{1,0:T(2,128)S(1)} %fusion.140), channel_id=1, source_target_pairs={{0,8},{4,12},{8,0},{12,4},{16,24},{20,28},{24,16},{28,20},{1,9},{5... | collective-permute-start | bytes 36872 | tf_op jit(solution)/shard_map/ppermute | solution.py:34
  84.8 3.8 %collective-permute-start.10 = (f32[2,1536]{1,0:T(2,128)S(1)}, f32[2,1536]{1,0:T(2,128)S(1)}, u32[]{:S(2)}, u32[]{:S(2)}) collective-permute-start(f32[2,1536]{1,0:T(2,128)S(1)} %fusion.155), channel_id=1, source_target_pairs={{0,16},{4,20},{8,24},{12,28},{16,0},{20,4},{24,8},{28,12},{1,17},{... | collective-permute-start | bytes 36872 | tf_op jit(solution)/shard_map/ppermute | solution.py:34
  88.6 4.3 %collective-permute-start.11 = (f32[2,1536]{1,0:T(2,128)S(1)}, f32[2,1536]{1,0:T(2,128)S(1)}, u32[]{:S(2)}, u32[]{:S(2)}) collective-permute-start(f32[2,1536]{1,0:T(2,128)S(1)} %add.496), channel_id=1, source_target_pairs={{0,1},{1,0},{2,3},{3,2},{4,5},{5,4},{6,7},{7,6},{8,9},{9,8},{10,11... | collective-permute-start | bytes 36872 | tf_op jit(solution)/shard_map/ppermute | solution.py:34
  92.9 6.0 %collective-permute-start.12 = (f32[2,1536]{1,0:T(2,128)S(1)}, f32[2,1536]{1,0:T(2,128)S(1)}, u32[]{:S(2)}, u32[]{:S(2)}) collective-permute-start(f32[2,1536]{1,0:T(2,128)S(1)} %add.497), channel_id=1, source_target_pairs={{0,2},{1,3},{2,0},{3,1},{4,6},{5,7},{6,4},{7,5},{8,10},{9,11},{10,... | collective-permute-start | bytes 36872 | tf_op jit(solution)/shard_map/ppermute | solution.py:34
  94.6 32.1 %all-to-all-start = ((bf16[128,4,384]{2,0,1:T(8,128)(2,1)}), bf16[128,4,384]{2,0,1:T(8,128)(2,1)}, u32[]{:S(2)}, u32[]{:S(2)}) async-start(bf16[128,4,384]{2,0,1:T(8,128)(2,1)} %copy.12), calls=%async_computation | async-start | bytes 786432 | tf_op jit(solution)/shard_map/all_to_all | solution.py:126
  130.2 3.2 %collective-permute-start.15 = (f32[192,1536]{1,0:T(8,128)}, f32[192,1536]{1,0:T(8,128)}, u32[]{:S(2)}, u32[]{:S(2)}) collective-permute-start(f32[192,1536]{1,0:T(8,128)} %constant_dynamic-slice_fusion.2), channel_id=1, source_target_pairs={{0,4},{4,0},{8,12},{12,8},{16,20},{20,16},{24,28},{28,24},{1,5},{5... | collective-permute-start | bytes 3538952 | tf_op jit(solution)/shard_map/ppermute | solution.py:65
  137.0 15.4 %collective-permute-start.16 = (f32[96,1536]{1,0:T(8,128)S(1)}, f32[96,1536]{1,0:T(8,128)S(1)}, u32[]{:S(2)}, u32[]{:S(2)}) collective-permute-start(f32[96,1536]{1,0:T(8,128)S(1)} %constant_dynamic-slice_fusion.1), channel_id=1, source_target_pairs={{0,8},{4,12},{8,0},{12,4},{16,24},{20,28},{24,16},{28,20},{1,9},{5... | collective-permute-start | bytes 1769480 | tf_op jit(solution)/shard_map/ppermute | solution.py:65
  153.6 8.3 %collective-permute-start.17 = (f32[48,1536]{1,0:T(8,128)S(1)}, f32[48,1536]{1,0:T(8,128)S(1)}, u32[]{:S(2)}, u32[]{:S(2)}) collective-permute-start(f32[48,1536]{1,0:T(8,128)S(1)} %constant_dynamic-slice_fusion), channel_id=1, source_target_pairs={{0,16},{4,20},{8,24},{12,28},{16,0},{20,4},{24,8},{28,12},{1,17},{... | collective-permute-start | bytes 884744 | tf_op jit(solution)/shard_map/ppermute | solution.py:65
  161.9 7.4 %collective-permute-start.18 = (f32[48,1536]{1,0:T(8,128)S(1)}, f32[48,1536]{1,0:T(8,128)S(1)}, u32[]{:S(2)}, u32[]{:S(2)}) collective-permute-start(f32[48,1536]{1,0:T(8,128)S(1)} %dynamic-slice_add_fusion.2), channel_id=1, source_target_pairs={{0,16},{4,20},{8,24},{12,28},{16,0},{20,4},{24,8},{28,12},{1,17},{... | collective-permute-start | bytes 884744 | tf_op jit(solution)/shard_map/ppermute | solution.py:69
  163.4 11.6 %collective-permute-start.21 = (f32[31,1536]{1,0:T(8,128)S(1)}, f32[31,1536]{1,0:T(8,128)S(1)}, u32[]{:S(2)}, u32[]{:S(2)}) collective-permute-start(f32[31,1536]{1,0:T(8,128)S(1)} %copy-done.7), channel_id=1, source_target_pairs={{0,4},{4,0},{8,12},{12,8},{16,20},{20,16},{24,28},{28,24},{1,5},{5... | collective-permute-start | bytes 571400 | tf_op jit(solution)/shard_map/ppermute | solution.py:34
  169.3 18.5 %collective-permute-start.19 = (f32[96,1536]{1,0:T(8,128)S(1)}, f32[96,1536]{1,0:T(8,128)S(1)}, u32[]{:S(2)}, u32[]{:S(2)}) collective-permute-start(f32[96,1536]{1,0:T(8,128)S(1)} %maximum_select_fusion.2), channel_id=1, source_target_pairs={{0,8},{4,12},{8,0},{12,4},{16,24},{20,28},{24,16},{28,20},{1,9},{5... | collective-permute-start | bytes 1769480 | tf_op jit(solution)/shard_map/ppermute | solution.py:69
  175.0 11.3 %collective-permute-start.22 = (f32[31,1536]{1,0:T(8,128)S(1)}, f32[31,1536]{1,0:T(8,128)S(1)}, u32[]{:S(2)}, u32[]{:S(2)}) collective-permute-start(f32[31,1536]{1,0:T(8,128)S(1)} %add.537), channel_id=1, source_target_pairs={{0,8},{4,12},{8,0},{12,4},{16,24},{20,28},{24,16},{28,20},{1,9},{5... | collective-permute-start | bytes 571400 | tf_op jit(solution)/shard_map/ppermute | solution.py:34
  175.7 12.3 %collective-permute-start.14 = (bf16[2,15,1536]{2,1,0:T(8,128)(2,1)S(1)}, bf16[2,15,1536]{2,1,0:T(8,128)(2,1)S(1)}, u32[]{:S(2)}, u32[]{:S(2)}) collective-permute-start(bf16[2,15,1536]{2,1,0:T(8,128)(2,1)S(1)} %get-tuple-element.101), channel_id=1, source_target_pairs={{0,1},{1,2},{2,3},{4,5},{5,6},{6,7},{8,9},{9,10},{10,11},{12,13},{... | collective-permute-start | bytes 276488 | tf_op jit(solution)/shard_map/ppermute | solution.py:16
  177.0 11.1 %collective-permute-start.13 = (bf16[2,15,1536]{2,1,0:T(8,128)(2,1)S(1)}, bf16[2,15,1536]{2,1,0:T(8,128)(2,1)S(1)}, u32[]{:S(2)}, u32[]{:S(2)}) collective-permute-start(bf16[2,15,1536]{2,1,0:T(8,128)(2,1)S(1)} %get-tuple-element.100), channel_id=1, source_target_pairs={{1,0},{2,1},{3,2},{5,4},{6,5},{7,6},{9,8},{10,9},{11,10},{13,12},{... | collective-permute-start | bytes 276488 | tf_op jit(solution)/shard_map/ppermute | solution.py:17
  186.3 6.1 %collective-permute-start.23 = (f32[31,1536]{1,0:T(8,128)S(1)}, f32[31,1536]{1,0:T(8,128)S(1)}, u32[]{:S(2)}, u32[]{:S(2)}) collective-permute-start(f32[31,1536]{1,0:T(8,128)S(1)} %add.538), channel_id=1, source_target_pairs={{0,16},{4,20},{8,24},{12,28},{16,0},{20,4},{24,8},{28,12},{1,17},{... | collective-permute-start | bytes 571400 | tf_op jit(solution)/shard_map/ppermute | solution.py:34
  188.0 24.2 %collective-permute-start.20 = (f32[192,1536]{1,0:T(8,128)S(1)}, f32[192,1536]{1,0:T(8,128)S(1)}, u32[]{:S(2)}, u32[]{:S(2)}) collective-permute-start(f32[192,1536]{1,0:T(8,128)S(1)} %maximum_select_fusion.1), channel_id=1, source_target_pairs={{0,4},{4,0},{8,12},{12,8},{16,20},{20,16},{24,28},{28,24},{1,5},{5... | collective-permute-start | bytes 3538952 | tf_op jit(solution)/shard_map/ppermute | solution.py:69
  192.5 7.3 %collective-permute-start.24 = (f32[31,1536]{1,0:T(8,128)S(1)}, f32[31,1536]{1,0:T(8,128)S(1)}, u32[]{:S(2)}, u32[]{:S(2)}) collective-permute-start(f32[31,1536]{1,0:T(8,128)S(1)} %add.539), channel_id=1, source_target_pairs={{0,1},{1,0},{2,3},{3,2},{4,5},{5,4},{6,7},{7,6},{8,9},{9,8},{10,11... | collective-permute-start | bytes 571400 | tf_op jit(solution)/shard_map/ppermute | solution.py:34
  199.9 11.6 %collective-permute-start.25 = (f32[31,1536]{1,0:T(8,128)S(1)}, f32[31,1536]{1,0:T(8,128)S(1)}, u32[]{:S(2)}, u32[]{:S(2)}) collective-permute-start(f32[31,1536]{1,0:T(8,128)S(1)} %add.540), channel_id=1, source_target_pairs={{0,2},{1,3},{2,0},{3,1},{4,6},{5,7},{6,4},{7,5},{8,10},{9,11},{10,... | collective-permute-start | bytes 571400 | tf_op jit(solution)/shard_map/ppermute | solution.py:34
  (73 other events, 1993.6 us)
Sparse Core Ops, SparseCore 0:
  16.6 51.5 all-gather.5
  82.7 43.9 all-gather.3

commit v13 on v9

--- a/solution.py
+++ b/solution.py
@@ -150,7 +150,6 @@
             for offset in range(taps)
         ]
     )
-    local_grad, kernel_terms = lax.optimization_barrier((local_grad, kernel_terms))
     weight_grad = rows_sum(local_grad, "dp")
     kernel_grad = all_sum(kernel_terms, ("dp", "tensor"))
     input_grad = jnp.concatenate(

time: 199 us -> 187 us (0.940)
  waiting for transfers between devices: 75.9 us -> 63.3 us
  other arithmetic: 28.3 us -> 22.9 us
  starting transfers between devices: 35.7 us -> 40.8 us
    another operation x32, local copies, waits for them, and re-layouts: 2.96 us -> 7.97 us  [on_device(): jnp.stack([jnp.sum(padded[:, offset:offset + frames, :].astype(jnp.float3...]
    ppermute x10, starting transfers between devices: 7.11 us -> 11.8 us  [all_sum(): x = x + lax.ppermute(x, axis, [(i, i ^ step) for i in range(peers)])]
    all_to_all x1, waiting for transfers between devices: 4.62 us -> 0.01 us  [on_device(): lax.all_to_all(flat_act, 'tensor', split_axis=1, concat_axis=0, tiled=True)]
    all_gather x1, waiting for transfers between devices: 21.6 us -> 17.2 us  [gather_weight(): held = lax.all_gather(mine, 'tensor', axis=0, tiled=False)]
    add x10, other arithmetic: 4.48 us -> 0.86 us  [all_sum(): x = x + lax.ppermute(x, axis, [(i, i ^ step) for i in range(peers)])]
    ppermute x3, waiting for transfers between devices: 4.29 us -> 1.12 us  [rows_sum(): x = keep + lax.ppermute(give, axis, [(i, i ^ step) for i in range(peers)])]
    ppermute x5, waiting for transfers between devices: 13.1 us -> 10.9 us  [all_moments(): lax.ppermute(jnp.stack([mean, spread]), axis, [(i, i ^ step) for i in ran...]
    all_gather x1, waiting for transfers between devices: 3.67 us -> 5.77 us  [on_device(): group_grad = lax.all_gather(flat_grad, 'tensor', axis=0, tiled=True)]
  transfers between devices with their start and end apart: 29 -> 29, of which waited for: 20 -> 19; matrix products, arithmetic and copies ran while one was open for 17% -> 18% of each run, Pallas kernels for 0% -> 0%
where the time goes in v13:
time: 187 us
  waiting for transfers between devices  63.3 us (34%)
  starting transfers between devices  40.8 us (22%)
  other arithmetic  22.9 us (12%)
  blocking collectives  22.6 us (12%)
  between operations  15.7 us (8%)
  local copies, waits for them, and re-layouts  15.2 us (8%)
  matrix products  6.15 us (3%)
    all_to_all x1, blocking collectives, on_device(): lax.all_to_all(own_columns, 'tensor', split_axis=0, concat_axis=1, tiled=...  22.6 us
    all_gather x1, waiting for transfers between devices, gather_weight(): held = lax.all_gather(mine, 'tensor', axis=0, tiled=False)  17.2 us
    ppermute x10, waiting for transfers between devices, all_sum(): x = x + lax.ppermute(x, axis, [(i, i ^ step) for i in range(peers)])  17.1 us
    ppermute x10, starting transfers between devices, all_sum(): x = x + lax.ppermute(x, axis, [(i, i ^ step) for i in range(peers)])  11.8 us
    ppermute x5, waiting for transfers between devices, all_moments(): lax.ppermute(jnp.stack([mean, spread]), axis, [(i, i ^ step) for i in ran...  10.9 us
    ppermute x2, starting transfers between devices, extended(): before = lax.ppermute(last, axis, up)  9.48 us
    another operation x32, local copies, waits for them, and re-layouts, on_device(): jnp.stack([jnp.sum(padded[:, offset:offset + frames, :].astype(jnp.float3...  7.97 us
    ppermute x5, starting transfers between devices, all_moments(): lax.ppermute(jnp.stack([mean, spread]), axis, [(i, i ^ step) for i in ran...  7.35 us
  transfers between devices with their start and end apart: 29, of which 19 were waited for; matrix products, arithmetic and copies ran while one was open for 18% of the time, Pallas kernels for 0%

profile of v13, /device:TPU:0, one launch (start us, length us, event | category | flops | bytes accessed | tf_op | source)
XLA Modules:
  0.0 186.7 jit_solution(4153986865869758958)
XLA Ops:
  9.3 4.9 %collective-permute-start = (bf16[2,15,1536]{2,1,0:T(8,128)(2,1)S(1)}, bf16[2,15,1536]{2,1,0:T(8,128)(2,1)S(1)}, u32[]{:S(2)}, u32[]{:S(2)}) collective-permute-start(bf16[2,15,1536]{2,1,0:T(8,128)(2,1)S(1)} %get-tuple-element.99), channel_id=1, source_target_pairs={{0,1},{1,2},{2,3},{4,5},{5,6},{6,7},{8,9},{9,10},{10,11},{12,13},{... | collective-permute-start | bytes 276488 | tf_op jit(solution)/shard_map/ppermute | solution.py:16
  16.4 4.3 %collective-permute-done.1 = bf16[2,15,1536]{2,1,0:T(8,128)(2,1)S(1)} collective-permute-done((bf16[2,15,1536]{2,1,0:T(8,128)(2,1)S(1)}, bf16[2,15,1536]{2,1,0:T(8,128)(2,1)S(1)}, u32[]{:S(2)}, u32[]{:S(2)}) %collective-permute-start.1) | collective-permute-done | bytes 92192 | tf_op jit(solution)/shard_map/ppermute | solution.py:17
  20.7 3.8 %fusion.143 = (f32[1536]{0:T(1024)S(1)}, f32[2,64,1536]{2,1,0:T(8,128)S(1)}) fusion(bf16[2,15,1536]{2,1,0:T(8,128)(2,1)S(1)} %collective-permute-done.1, bf16[2,64,1536]{2,1,0:T(8,128)(2,1)S(1)} %fusion, f32[1536]{0:T(1024)S(1)} %get-tuple-element.72, f32[1536]{0:T(1024)S(1)} %get-tuple-element.73, f32[1536]{0:T(1024)S(1)} %get-tuple-element.44, ...), kind=kLoop, calls=%fused_computation.380 | loop fusion | flops 35977728 | bytes 1560576 | tf_op jit(solution)/shard_map/reduce_sum | solution.py:107
  26.1 1.6 collective-permute-start.3
  27.7 2.2 %collective-permute-done.3 = f32[2,1536]{1,0:T(2,128)S(1)} collective-permute-done((f32[2,1536]{1,0:T(2,128)S(1)}, f32[2,1536]{1,0:T(2,128)S(1)}, u32[]{:S(2)}, u32[]{:S(2)}) %collective-permute-start.3) | collective-permute-done | bytes 12320 | tf_op jit(solution)/shard_map/ppermute | solution.py:44
  29.9 1.6 collective-permute-start.4
  31.5 2.2 %collective-permute-done.4 = f32[2,1536]{1,0:T(2,128)S(1)} collective-permute-done((f32[2,1536]{1,0:T(2,128)S(1)}, f32[2,1536]{1,0:T(2,128)S(1)}, u32[]{:S(2)}, u32[]{:S(2)}) %collective-permute-start.4) | collective-permute-done | bytes 12320 | tf_op jit(solution)/shard_map/ppermute | solution.py:44
  33.8 1.6 collective-permute-start.5
  35.4 2.5 %collective-permute-done.5 = f32[2,1536]{1,0:T(2,128)S(1)} collective-permute-done((f32[2,1536]{1,0:T(2,128)S(1)}, f32[2,1536]{1,0:T(2,128)S(1)}, u32[]{:S(2)}, u32[]{:S(2)}) %collective-permute-start.5) | collective-permute-done | bytes 12320 | tf_op jit(solution)/shard_map/ppermute | solution.py:44
  38.0 2.5 %collective-permute-start.6 = (f32[2,1536]{1,0:T(2,128)S(1)}, f32[2,1536]{1,0:T(2,128)S(1)}, u32[]{:S(2)}, u32[]{:S(2)}) collective-permute-start(f32[2,1536]{1,0:T(2,128)S(1)} %pad_maximum_fusion.10), channel_id=1, source_target_pairs={{0,2},{1,3},{2,0},{3,1},{4,6},{5,7},{6,4},{7,5},{8,10},{9,11},{10,... | collective-permute-start | bytes 36872 | tf_op jit(solution)/shard_map/ppermute | solution.py:44
  40.5 2.9 %collective-permute-done.6 = f32[2,1536]{1,0:T(2,128)S(1)} collective-permute-done((f32[2,1536]{1,0:T(2,128)S(1)}, f32[2,1536]{1,0:T(2,128)S(1)}, u32[]{:S(2)}, u32[]{:S(2)}) %collective-permute-start.6) | collective-permute-done | bytes 12320 | tf_op jit(solution)/shard_map/ppermute | solution.py:44
  44.2 5.8 %all-gather.4.cloned.1.call-done = bf16[512,1536]{1,0:T(8,128)(2,1)} async-done(((bf16[128,1536]{1,0:T(8,128)(2,1)}), bf16[512,1536]{1,0:T(8,128)(2,1)}) %all-gather.4.cloned.1.call-update) | async-done | bytes 1572880 | tf_op jit(solution)/shard_map/all_gather | solution.py:99
  50.0 2.4 %fusion.147 = f32[512,384]{1,0:T(8,128)S(1)} fusion(bf16[512,1536]{1,0:T(8,128)(2,1)} %all-gather.4.cloned.1.call-done, bf16[384,1536]{1,0:T(8,128)(2,1)S(1)} %copy-done), kind=kOutput, calls=%fused_computation.383 | convolution fusion | flops 603979776 | bytes 3538944 | tf_op jit(solution)/shard_map/fd,cd->fc/dot_general | solution.py:118
  52.4 22.6 %all_to_all.35 = f32[4,128,384]{2,1,0:T(8,128)S(1)} all-to-all(f32[4,128,384]{2,1,0:T(8,128)S(1)} %bitcast.21), channel_id=1, replica_groups=mesh['dp'=8,'tensor'=4] {'tensor'}, dimensions={0} | all-to-all | bytes 1572864 | tf_op jit(solution)/shard_map/all_to_all | solution.py:119
  76.8 2.4 %fusion.140 = (f32[1536]{0:T(1024)S(1)}, f32[1536]{0:T(1024)S(1)}, f32[2,64,1536]{2,1,0:T(8,128)}, bf16[2,64,1536]{2,1,0:T(8,128)(2,1)S(1)}) fusion(f32[1536]{0:T(1024)S(1)} %get-tuple-element.90, f32[2,64,1536]{2,1,0:T(8,128)S(1)} %get-tuple-element.93, f32[1536]{0:T(1024)S(1)} %get-tuple-element.8, f32[2,64,1536]{2,1,0:T(8,128)} %reshape.189, ...), kind=kLoop, calls=%fused_computation.378 | loop fusion | flops 3142656 | bytes 2789376 | tf_op jit(solution)/shard_map/reduce_sum | solution.py:131
  80.2 3.5 %all-to-all-start.1 = ((bf16[128,4,384]{2,0,1:T(8,128)(2,1)}), bf16[128,4,384]{2,0,1:T(8,128)(2,1)S(1)}, u32[]{:S(2)}, u32[]{:S(2)}) async-start(bf16[128,4,384]{2,0,1:T(8,128)(2,1)} %copy.17), calls=%async_computation.1 | async-start | bytes 786432 | tf_op jit(solution)/shard_map/all_to_all | solution.py:128
  89.3 2.2 %collective-permute-done.10 = f32[2,1536]{1,0:T(2,128)S(1)} collective-permute-done((f32[2,1536]{1,0:T(2,128)S(1)}, f32[2,1536]{1,0:T(2,128)S(1)}, u32[]{:S(2)}, u32[]{:S(2)}) %collective-permute-start.10) | collective-permute-done | bytes 12320 | tf_op jit(solution)/shard_map/ppermute | solution.py:34
  91.5 1.8 collective-permute-start.11
  93.3 1.9 %collective-permute-done.11 = f32[2,1536]{1,0:T(2,128)S(1)} collective-permute-done((f32[2,1536]{1,0:T(2,128)S(1)}, f32[2,1536]{1,0:T(2,128)S(1)}, u32[]{:S(2)}, u32[]{:S(2)}) %collective-permute-start.11) | collective-permute-done | bytes 12320 | tf_op jit(solution)/shard_map/ppermute | solution.py:34
  95.3 2.7 %collective-permute-start.12 = (f32[2,1536]{1,0:T(2,128)S(1)}, f32[2,1536]{1,0:T(2,128)S(1)}, u32[]{:S(2)}, u32[]{:S(2)}) collective-permute-start(f32[2,1536]{1,0:T(2,128)S(1)} %add.497), channel_id=1, source_target_pairs={{0,2},{1,3},{2,0},{3,1},{4,6},{5,7},{6,4},{7,5},{8,10},{9,11},{10,... | collective-permute-start | bytes 36872 | tf_op jit(solution)/shard_map/ppermute | solution.py:34
  98.0 3.5 %collective-permute-done.12 = f32[2,1536]{1,0:T(2,128)S(1)} collective-permute-done((f32[2,1536]{1,0:T(2,128)S(1)}, f32[2,1536]{1,0:T(2,128)S(1)}, u32[]{:S(2)}, u32[]{:S(2)}) %collective-permute-start.12) | collective-permute-done | bytes 12320 | tf_op jit(solution)/shard_map/ppermute | solution.py:34
  101.6 2.2 %fusion.148 = f32[384,1536]{1,0:T(8,128)S(1)} fusion(bf16[512,384]{1,0:T(8,128)(2,1)S(1)} %bitcast.20, bf16[512,1536]{1,0:T(8,128)(2,1)} %all-gather.4.cloned.1.call-done), kind=kOutput, calls=%fused_computation.384 | convolution fusion | flops 603979776 | bytes 4325376 | tf_op jit(solution)/shard_map/fc,fd->cd/dot_general | solution.py:129
  118.5 2.5 %stack.172 = f32[31,1536]{1,0:T(8,128)S(1)} concatenate(f32[1,1536]{1,0:T(1,128)} %stack.141, f32[1,1536]{1,0:T(1,128)} %stack.142, f32[1,1536]{1,0:T(1,128)} %stack.143, f32[1,1536]{1,0:T(1,128)} %stack.144, f32[1,1536]{1,0:T(1,128)} %stack.145, f32[1,1536]{1,0:T(1,128)S(1)} %stack.146, f32[1,1536]{1,0:T(1,128)S(1)} %stack.147, f32[1,1536]{1,0:T(1,128)S(1)} %stack.148, ...), dimensions={0} | concatenate | bytes 380928 | tf_op jit(solution)/shard_map/stack | solution.py:145
  121.1 17.2 %all-gather.6.cloned.1.call-done = bf16[768,1536]{1,0:T(8,128)(2,1)} async-done(((bf16[192,1536]{1,0:T(8,128)(2,1)}), bf16[768,1536]{1,0:T(8,128)(2,1)}) %all-gather.6.cloned.1.call-update) | async-done | bytes 2359312 | tf_op jit(solution)/shard_map/all_gather | solution.py:81
  144.2 4.6 %collective-permute-start.14 = (bf16[2,15,1536]{2,1,0:T(8,128)(2,1)S(1)}, bf16[2,15,1536]{2,1,0:T(8,128)(2,1)S(1)}, u32[]{:S(2)}, u32[]{:S(2)}) collective-permute-start(bf16[2,15,1536]{2,1,0:T(8,128)(2,1)S(1)} %get-tuple-element.98), channel_id=1, source_target_pairs={{0,1},{1,2},{2,3},{4,5},{5,6},{6,7},{8,9},{9,10},{10,11},{12,13},{... | collective-permute-start | bytes 276488 | tf_op jit(solution)/shard_map/ppermute | solution.py:16
  150.6 2.1 %collective-permute-start.18 = (f32[48,1536]{1,0:T(8,128)S(1)}, f32[48,1536]{1,0:T(8,128)S(1)}, u32[]{:S(2)}, u32[]{:S(2)}) collective-permute-start(f32[48,1536]{1,0:T(8,128)S(1)} %dynamic-slice_add_fusion.2), channel_id=1, source_target_pairs={{0,16},{4,20},{8,24},{12,28},{16,0},{20,4},{24,8},{28,12},{1,17},{... | collective-permute-start | bytes 884744 | tf_op jit(solution)/shard_map/ppermute | solution.py:69
  152.9 4.1 %multiply_convert_fusion = (bf16[2,64,1536]{2,1,0:T(8,128)(2,1)S(1)}, f32[2,64,1536]{2,1,0:T(8,128)S(1)}) fusion(bf16[2,64,3072]{2,1,0:T(8,128)(2,1)S(1)} %copy-done.1, bf16[2,64,1536]{2,1,0:T(8,128)(2,1)S(1)} %get-tuple-element.86, bf16[2,15,1536]{2,1,0:T(8,128)(2,1)S(1)} %collective-permute-done.14, f32[1536]{0:T(1024)S(1)} %copy-done.62, ...), kind=kLoop, calls=%fused_computation.210 | loop fusion | flops 36962304 | bytes 2340864 | tf_op jit(solution)/shard_map/convert
  157.8 3.6 %collective-permute-done.18 = f32[48,1536]{1,0:T(8,128)S(1)} collective-permute-done((f32[48,1536]{1,0:T(8,128)S(1)}, f32[48,1536]{1,0:T(8,128)S(1)}, u32[]{:S(2)}, u32[]{:S(2)}) %collective-permute-start.18) | collective-permute-done | bytes 294944 | tf_op jit(solution)/shard_map/ppermute | solution.py:69
  164.9 7.6 %collective-permute-done.25 = f32[31,1536]{1,0:T(8,128)S(1)} collective-permute-done((f32[31,1536]{1,0:T(8,128)S(1)}, f32[31,1536]{1,0:T(8,128)S(1)}, u32[]{:S(2)}, u32[]{:S(2)}) %collective-permute-start.25) | collective-permute-done | bytes 190496 | tf_op jit(solution)/shard_map/ppermute | solution.py:34
  173.2 1.9 %collective-permute-done.19 = f32[96,1536]{1,0:T(8,128)S(1)} collective-permute-done((f32[96,1536]{1,0:T(8,128)S(1)}, f32[96,1536]{1,0:T(8,128)S(1)}, u32[]{:S(2)}, u32[]{:S(2)}) %collective-permute-start.19) | collective-permute-done | bytes 589856 | tf_op jit(solution)/shard_map/ppermute | solution.py:69
  176.0 1.5 convolution_convert_fusion
  178.2 1.6 maximum_select_fusion
  (266 shorter events, 43.1 us)
Async XLA Ops:
  7.2 42.8 %copy-start = (bf16[384,1536]{1,0:T(8,128)(2,1)S(1)}, bf16[384,1536]{1,0:T(8,128)(2,1)}, u32[]{:S(2)}) copy-start(bf16[384,1536]{1,0:T(8,128)(2,1)} %param.10) | copy-start | bytes 3538948
  7.2 42.8 %all-gather.4.cloned.1.call-start = ((), (), s32[]{:S(2)}) async-start(), calls=%async_computation.2 | async-start | bytes 1966080 | tf_op jit(solution)/shard_map/all_gather | solution.py:99
  9.3 7.1 %collective-permute-start = (bf16[2,15,1536]{2,1,0:T(8,128)(2,1)S(1)}, bf16[2,15,1536]{2,1,0:T(8,128)(2,1)S(1)}, u32[]{:S(2)}, u32[]{:S(2)}) collective-permute-start(bf16[2,15,1536]{2,1,0:T(8,128)(2,1)S(1)} %get-tuple-element.99), channel_id=1, source_target_pairs={{0,1},{1,2},{2,3},{4,5},{5,6},{6,7},{8,9},{9,10},{10,11},{12,13},{... | collective-permute-start | bytes 276488 | tf_op jit(solution)/shard_map/ppermute | solution.py:16
  14.2 6.5 %collective-permute-start.1 = (bf16[2,15,1536]{2,1,0:T(8,128)(2,1)S(1)}, bf16[2,15,1536]{2,1,0:T(8,128)(2,1)S(1)}, u32[]{:S(2)}, u32[]{:S(2)}) collective-permute-start(bf16[2,15,1536]{2,1,0:T(8,128)(2,1)S(1)} %get-tuple-element.100), channel_id=1, source_target_pairs={{1,0},{2,1},{3,2},{5,4},{6,5},{7,6},{9,8},{10,9},{11,10},{13,12},{... | collective-permute-start | bytes 276488 | tf_op jit(solution)/shard_map/ppermute | solution.py:17
  16.3 36.0 %copy-start.45 = (f32[1536]{0:T(1024)}, f32[1536]{0:T(1024)S(1)}, u32[]{:S(2)}) copy-start(f32[1536]{0:T(1024)S(1)} %get-tuple-element.64) | copy-start | bytes 18436
  16.3 36.0 %copy-start.47 = (f32[1536]{0:T(1024)}, f32[1536]{0:T(1024)S(1)}, u32[]{:S(2)}) copy-start(f32[1536]{0:T(1024)S(1)} %get-tuple-element.65) | copy-start | bytes 18436
  24.8 1.2 collective-permute-start.2
  26.1 3.8 %collective-permute-start.3 = (f32[2,1536]{1,0:T(2,128)S(1)}, f32[2,1536]{1,0:T(2,128)S(1)}, u32[]{:S(2)}, u32[]{:S(2)}) collective-permute-start(f32[2,1536]{1,0:T(2,128)S(1)} %pad_maximum_fusion.7), channel_id=1, source_target_pairs={{0,8},{4,12},{8,0},{12,4},{16,24},{20,28},{24,16},{28,20},{1,9},{5... | collective-permute-start | bytes 36872 | tf_op jit(solution)/shard_map/ppermute | solution.py:44
  29.9 3.8 %collective-permute-start.4 = (f32[2,1536]{1,0:T(2,128)S(1)}, f32[2,1536]{1,0:T(2,128)S(1)}, u32[]{:S(2)}, u32[]{:S(2)}) collective-permute-start(f32[2,1536]{1,0:T(2,128)S(1)} %pad_maximum_fusion.8), channel_id=1, source_target_pairs={{0,16},{4,20},{8,24},{12,28},{16,0},{20,4},{24,8},{28,12},{1,17},{... | collective-permute-start | bytes 36872 | tf_op jit(solution)/shard_map/ppermute | solution.py:44
  33.8 4.2 %collective-permute-start.5 = (f32[2,1536]{1,0:T(2,128)S(1)}, f32[2,1536]{1,0:T(2,128)S(1)}, u32[]{:S(2)}, u32[]{:S(2)}) collective-permute-start(f32[2,1536]{1,0:T(2,128)S(1)} %pad_maximum_fusion.9), channel_id=1, source_target_pairs={{0,1},{1,0},{2,3},{3,2},{4,5},{5,4},{6,7},{7,6},{8,9},{9,8},{10,11... | collective-permute-start | bytes 36872 | tf_op jit(solution)/shard_map/ppermute | solution.py:44
  38.0 5.4 %collective-permute-start.6 = (f32[2,1536]{1,0:T(2,128)S(1)}, f32[2,1536]{1,0:T(2,128)S(1)}, u32[]{:S(2)}, u32[]{:S(2)}) collective-permute-start(f32[2,1536]{1,0:T(2,128)S(1)} %pad_maximum_fusion.10), channel_id=1, source_target_pairs={{0,2},{1,3},{2,0},{3,1},{4,6},{5,7},{6,4},{7,5},{8,10},{9,11},{10,... | collective-permute-start | bytes 36872 | tf_op jit(solution)/shard_map/ppermute | solution.py:44
  79.3 4.7 %collective-permute-start.8 = (f32[2,1536]{1,0:T(2,128)S(1)}, f32[2,1536]{1,0:T(2,128)S(1)}, u32[]{:S(2)}, u32[]{:S(2)}) collective-permute-start(f32[2,1536]{1,0:T(2,128)S(1)} %pad_maximum_fusion.11), channel_id=1, source_target_pairs={{0,4},{4,0},{8,12},{12,8},{16,20},{20,16},{24,28},{28,24},{1,5},{5... | collective-permute-start | bytes 36872 | tf_op jit(solution)/shard_map/ppermute | solution.py:34
  80.2 21.3 %all-to-all-start.1 = ((bf16[128,4,384]{2,0,1:T(8,128)(2,1)}), bf16[128,4,384]{2,0,1:T(8,128)(2,1)S(1)}, u32[]{:S(2)}, u32[]{:S(2)}) async-start(bf16[128,4,384]{2,0,1:T(8,128)(2,1)} %copy.17), calls=%async_computation.1 | async-start | bytes 786432 | tf_op jit(solution)/shard_map/all_to_all | solution.py:128
  83.7 54.5 %all-gather.6.cloned.1.call-start = ((), (), s32[]{:S(2)}) async-start(), calls=%async_computation.3 | async-start | bytes 2949120 | tf_op jit(solution)/shard_map/all_gather | solution.py:81
  84.0 3.8 %collective-permute-start.9 = (f32[2,1536]{1,0:T(2,128)S(1)}, f32[2,1536]{1,0:T(2,128)S(1)}, u32[]{:S(2)}, u32[]{:S(2)}) collective-permute-start(f32[2,1536]{1,0:T(2,128)S(1)} %fusion.139), channel_id=1, source_target_pairs={{0,8},{4,12},{8,0},{12,4},{16,24},{20,28},{24,16},{28,20},{1,9},{5... | collective-permute-start | bytes 36872 | tf_op jit(solution)/shard_map/ppermute | solution.py:34
  87.8 3.8 %collective-permute-start.10 = (f32[2,1536]{1,0:T(2,128)S(1)}, f32[2,1536]{1,0:T(2,128)S(1)}, u32[]{:S(2)}, u32[]{:S(2)}) collective-permute-start(f32[2,1536]{1,0:T(2,128)S(1)} %fusion.155), channel_id=1, source_target_pairs={{0,16},{4,20},{8,24},{12,28},{16,0},{20,4},{24,8},{28,12},{1,17},{... | collective-permute-start | bytes 36872 | tf_op jit(solution)/shard_map/ppermute | solution.py:34
  91.5 3.8 %collective-permute-start.11 = (f32[2,1536]{1,0:T(2,128)S(1)}, f32[2,1536]{1,0:T(2,128)S(1)}, u32[]{:S(2)}, u32[]{:S(2)}) collective-permute-start(f32[2,1536]{1,0:T(2,128)S(1)} %add.496), channel_id=1, source_target_pairs={{0,1},{1,0},{2,3},{3,2},{4,5},{5,4},{6,7},{7,6},{8,9},{9,8},{10,11... | collective-permute-start | bytes 36872 | tf_op jit(solution)/shard_map/ppermute | solution.py:34
  95.3 6.2 %collective-permute-start.12 = (f32[2,1536]{1,0:T(2,128)S(1)}, f32[2,1536]{1,0:T(2,128)S(1)}, u32[]{:S(2)}, u32[]{:S(2)}) collective-permute-start(f32[2,1536]{1,0:T(2,128)S(1)} %add.497), channel_id=1, source_target_pairs={{0,2},{1,3},{2,0},{3,1},{4,6},{5,7},{6,4},{7,5},{8,10},{9,11},{10,... | collective-permute-start | bytes 36872 | tf_op jit(solution)/shard_map/ppermute | solution.py:34
  103.9 3.8 %collective-permute-start.15 = (f32[192,1536]{1,0:T(8,128)S(1)}, f32[192,1536]{1,0:T(8,128)S(1)}, u32[]{:S(2)}, u32[]{:S(2)}) collective-permute-start(f32[192,1536]{1,0:T(8,128)S(1)} %constant_dynamic-slice_fusion.2), channel_id=1, source_target_pairs={{0,4},{4,0},{8,12},{12,8},{16,20},{20,16},{24,28},{28,24},{1,5},{5... | collective-permute-start | bytes 3538952 | tf_op jit(solution)/shard_map/ppermute | solution.py:65
  109.7 30.1 %collective-permute-start.16 = (f32[96,1536]{1,0:T(8,128)}, f32[96,1536]{1,0:T(8,128)}, u32[]{:S(2)}, u32[]{:S(2)}) collective-permute-start(f32[96,1536]{1,0:T(8,128)} %constant_dynamic-slice_fusion.1), channel_id=1, source_target_pairs={{0,8},{4,12},{8,0},{12,4},{16,24},{20,28},{24,16},{28,20},{1,9},{5... | collective-permute-start | bytes 1769480 | tf_op jit(solution)/shard_map/ppermute | solution.py:65
  121.0 17.3 %collective-permute-start.21 = (f32[31,1536]{1,0:T(8,128)S(1)}, f32[31,1536]{1,0:T(8,128)S(1)}, u32[]{:S(2)}, u32[]{:S(2)}) collective-permute-start(f32[31,1536]{1,0:T(8,128)S(1)} %stack.172), channel_id=1, source_target_pairs={{0,4},{4,0},{8,12},{12,8},{16,20},{20,16},{24,28},{28,24},{1,5},{5... | collective-permute-start | bytes 571400 | tf_op jit(solution)/shard_map/ppermute | solution.py:34
  138.3 37.1 %collective-permute-start.7 = (bf16[4,192,1536]{2,1,0:T(8,128)(2,1)}, bf16[4,192,1536]{2,1,0:T(8,128)(2,1)S(1)}, u32[]{:S(2)}, u32[]{:S(2)}) collective-permute-start(bf16[4,192,1536]{2,1,0:T(8,128)(2,1)} %bitcast.18), channel_id=1, source_target_pairs={{0,4},{4,0},{8,12},{12,8},{16,20},{20,16},{24,28},{28,24},{1,5},{5... | collective-permute-start | bytes 7077896 | tf_op jit(solution)/shard_map/ppermute | solution.py:82
  138.3 10.4 %collective-permute-start.22 = (f32[31,1536]{1,0:T(8,128)S(1)}, f32[31,1536]{1,0:T(8,128)S(1)}, u32[]{:S(2)}, u32[]{:S(2)}) collective-permute-start(f32[31,1536]{1,0:T(8,128)S(1)} %add.537), channel_id=1, source_target_pairs={{0,8},{4,12},{8,0},{12,4},{16,24},{20,28},{24,16},{28,20},{1,9},{5... | collective-permute-start | bytes 571400 | tf_op jit(solution)/shard_map/ppermute | solution.py:34
  141.3 9.2 %collective-permute-start.17 = (f32[48,1536]{1,0:T(8,128)S(1)}, f32[48,1536]{1,0:T(8,128)S(1)}, u32[]{:S(2)}, u32[]{:S(2)}) collective-permute-start(f32[48,1536]{1,0:T(8,128)S(1)} %constant_dynamic-slice_fusion), channel_id=1, source_target_pairs={{0,16},{4,20},{8,24},{12,28},{16,0},{20,4},{24,8},{28,12},{1,17},{... | collective-permute-start | bytes 884744 | tf_op jit(solution)/shard_map/ppermute | solution.py:65
  142.9 9.8 %collective-permute-start.13 = (bf16[2,15,1536]{2,1,0:T(8,128)(2,1)S(1)}, bf16[2,15,1536]{2,1,0:T(8,128)(2,1)S(1)}, u32[]{:S(2)}, u32[]{:S(2)}) collective-permute-start(bf16[2,15,1536]{2,1,0:T(8,128)(2,1)S(1)} %get-tuple-element.97), channel_id=1, source_target_pairs={{1,0},{2,1},{3,2},{5,4},{6,5},{7,6},{9,8},{10,9},{11,10},{13,12},{... | collective-permute-start | bytes 276488 | tf_op jit(solution)/shard_map/ppermute | solution.py:17
  144.2 8.5 %collective-permute-start.14 = (bf16[2,15,1536]{2,1,0:T(8,128)(2,1)S(1)}, bf16[2,15,1536]{2,1,0:T(8,128)(2,1)S(1)}, u32[]{:S(2)}, u32[]{:S(2)}) collective-permute-start(bf16[2,15,1536]{2,1,0:T(8,128)(2,1)S(1)} %get-tuple-element.98), channel_id=1, source_target_pairs={{0,1},{1,2},{2,3},{4,5},{5,6},{6,7},{8,9},{9,10},{10,11},{12,13},{... | collective-permute-start | bytes 276488 | tf_op jit(solution)/shard_map/ppermute | solution.py:16
  148.8 8.2 %collective-permute-start.23 = (f32[31,1536]{1,0:T(8,128)S(1)}, f32[31,1536]{1,0:T(8,128)S(1)}, u32[]{:S(2)}, u32[]{:S(2)}) collective-permute-start(f32[31,1536]{1,0:T(8,128)S(1)} %add.538), channel_id=1, source_target_pairs={{0,16},{4,20},{8,24},{12,28},{16,0},{20,4},{24,8},{28,12},{1,17},{... | collective-permute-start | bytes 571400 | tf_op jit(solution)/shard_map/ppermute | solution.py:34
  150.6 10.8 %collective-permute-start.18 = (f32[48,1536]{1,0:T(8,128)S(1)}, f32[48,1536]{1,0:T(8,128)S(1)}, u32[]{:S(2)}, u32[]{:S(2)}) collective-permute-start(f32[48,1536]{1,0:T(8,128)S(1)} %dynamic-slice_add_fusion.2), channel_id=1, source_target_pairs={{0,16},{4,20},{8,24},{12,28},{16,0},{20,4},{24,8},{28,12},{1,17},{... | collective-permute-start | bytes 884744 | tf_op jit(solution)/shard_map/ppermute | solution.py:69
  157.1 5.7 %collective-permute-start.24 = (f32[31,1536]{1,0:T(8,128)S(1)}, f32[31,1536]{1,0:T(8,128)S(1)}, u32[]{:S(2)}, u32[]{:S(2)}) collective-permute-start(f32[31,1536]{1,0:T(8,128)S(1)} %add.539), channel_id=1, source_target_pairs={{0,1},{1,0},{2,3},{3,2},{4,5},{5,4},{6,7},{7,6},{8,9},{9,8},{10,11... | collective-permute-start | bytes 571400 | tf_op jit(solution)/shard_map/ppermute | solution.py:34
  161.4 13.8 %collective-permute-start.19 = (f32[96,1536]{1,0:T(8,128)S(1)}, f32[96,1536]{1,0:T(8,128)S(1)}, u32[]{:S(2)}, u32[]{:S(2)}) collective-permute-start(f32[96,1536]{1,0:T(8,128)S(1)} %maximum_select_fusion.2), channel_id=1, source_target_pairs={{0,8},{4,12},{8,0},{12,4},{16,24},{20,28},{24,16},{28,20},{1,9},{5... | collective-permute-start | bytes 1769480 | tf_op jit(solution)/shard_map/ppermute | solution.py:69
  162.8 9.7 %collective-permute-start.25 = (f32[31,1536]{1,0:T(8,128)S(1)}, f32[31,1536]{1,0:T(8,128)S(1)}, u32[]{:S(2)}, u32[]{:S(2)}) collective-permute-start(f32[31,1536]{1,0:T(8,128)S(1)} %add.540), channel_id=1, source_target_pairs={{0,2},{1,3},{2,0},{3,1},{4,6},{5,7},{6,4},{7,5},{8,10},{9,11},{10,... | collective-permute-start | bytes 571400 | tf_op jit(solution)/shard_map/ppermute | solution.py:34
  175.3 2.9 %collective-permute-start.20 = (f32[192,1536]{1,0:T(8,128)S(1)}, f32[192,1536]{1,0:T(8,128)S(1)}, u32[]{:S(2)}, u32[]{:S(2)}) collective-permute-start(f32[192,1536]{1,0:T(8,128)S(1)} %maximum_select_fusion.1), channel_id=1, source_target_pairs={{0,4},{4,0},{8,12},{12,8},{16,20},{20,16},{24,28},{28,24},{1,5},{5... | collective-permute-start | bytes 3538952 | tf_op jit(solution)/shard_map/ppermute | solution.py:69
  (68 other events, 1192.8 us)
Sparse Core Ops, SparseCore 0:
  9.6 40.3 all-gather.3
  86.5 51.7 all-gather.5

commit v14 on v13

--- a/solution.py
+++ b/solution.py
@@ -114,7 +114,6 @@
         average = lax.psum(jnp.sum(conv_out, axis=(0, 1)), ("dp", "tensor")) / everyone
         centred0 = conv_out - average
         variance = lax.psum(jnp.sum(centred0 * centred0, axis=(0, 1)), ("dp", "tensor")) / everyone
-    group_grad, average = lax.optimization_barrier((group_grad, average))
     own_columns = jnp.einsum("fd,cd->fc", group_grad, proj_weight, preferred_element_type=jnp.float32)
     grad_act = lax.all_to_all(own_columns, "tensor", split_axis=0, concat_axis=1, tiled=True)
     grad_act = grad_act.reshape(out_grad.shape)

time: 187 us -> 192 us (1.027)
  blocking collectives: 22.6 us -> 0 us
  waiting for transfers between devices: 63.3 us -> 79.9 us
  starting transfers between devices: 40.8 us -> 46.9 us
    all_to_all x1 -> x0, blocking collectives: 22.6 us -> none  [on_device(): lax.all_to_all(own_columns, 'tensor', split_axis=0, concat_axis=1, tiled=...]
    all_gather x1, waiting for transfers between devices: 5.77 us -> 16.2 us  [on_device(): group_grad = lax.all_gather(flat_grad, 'tensor', axis=0, tiled=True)]
    ppermute x5, waiting for transfers between devices: 10.9 us -> 16.5 us  [all_moments(): lax.ppermute(jnp.stack([mean, spread]), axis, [(i, i ^ step) for i in ran...]
    all_to_all x0 -> x1, starting transfers between devices: none -> 3.64 us  [on_device(): lax.all_to_all(own_columns, 'tensor', split_axis=0, concat_axis=1, tiled=...]
    ppermute x5, starting transfers between devices: 7.35 us -> 9.84 us  [all_moments(): lax.ppermute(jnp.stack([mean, spread]), axis, [(i, i ^ step) for i in ran...]
    slice x4, other arithmetic: 0.18 us -> 2.16 us  [all_moments(): spread = spread + other[1] + delta * delta * (count * 0.5)]
  transfers between devices with their start and end apart: 29 -> 30, of which waited for: 19 -> 18; matrix products, arithmetic and copies ran while one was open for 18% -> 20% of each run, Pallas kernels for 0% -> 0%
where the time goes in v14:
time: 192 us; the launch traced here: 191 us
  waiting for transfers between devices  79.9 us (42%)
  starting transfers between devices  46.9 us (24%)
  other arithmetic  24.8 us (13%)
  local copies, waits for them, and re-layouts  16.7 us (9%)
  between operations  15.9 us (8%)
  matrix products  7.03 us (4%)
    all_gather x1, waiting for transfers between devices, gather_weight(): held = lax.all_gather(mine, 'tensor', axis=0, tiled=False)  17.8 us
    ppermute x10, waiting for transfers between devices, all_sum(): x = x + lax.ppermute(x, axis, [(i, i ^ step) for i in range(peers)])  17.1 us
    ppermute x5, waiting for transfers between devices, all_moments(): lax.ppermute(jnp.stack([mean, spread]), axis, [(i, i ^ step) for i in ran...  16.5 us
    all_gather x1, waiting for transfers between devices, on_device(): group_grad = lax.all_gather(flat_grad, 'tensor', axis=0, tiled=True)  16.2 us
    ppermute x10, starting transfers between devices, all_sum(): x = x + lax.ppermute(x, axis, [(i, i ^ step) for i in range(peers)])  11.8 us
    ppermute x5, starting transfers between devices, all_moments(): lax.ppermute(jnp.stack([mean, spread]), axis, [(i, i ^ step) for i in ran...  9.84 us
    ppermute x2, starting transfers between devices, extended(): before = lax.ppermute(last, axis, up)  9.48 us
    another operation x32, local copies, waits for them, and re-layouts, on_device(): jnp.stack([jnp.sum(padded[:, offset:offset + frames, :].astype(jnp.float3...  7.37 us
  transfers between devices with their start and end apart: 30, of which 18 were waited for; matrix products, arithmetic and copies ran while one was open for 20% of the time, Pallas kernels for 0%

profile of v14, /device:TPU:0, one launch (start us, length us, event | category | flops | bytes accessed | tf_op | source)
XLA Modules:
  0.0 191.2 jit_solution(11649947982885963120)
XLA Ops:
  9.3 4.9 %collective-permute-start = (bf16[2,15,1536]{2,1,0:T(8,128)(2,1)S(1)}, bf16[2,15,1536]{2,1,0:T(8,128)(2,1)S(1)}, u32[]{:S(2)}, u32[]{:S(2)}) collective-permute-start(bf16[2,15,1536]{2,1,0:T(8,128)(2,1)S(1)} %get-tuple-element.95), channel_id=1, source_target_pairs={{0,1},{1,2},{2,3},{4,5},{5,6},{6,7},{8,9},{9,10},{10,11},{12,13},{... | collective-permute-start | bytes 276488 | tf_op jit(solution)/shard_map/ppermute | solution.py:16
  16.4 4.3 %collective-permute-done.1 = bf16[2,15,1536]{2,1,0:T(8,128)(2,1)S(1)} collective-permute-done((bf16[2,15,1536]{2,1,0:T(8,128)(2,1)S(1)}, bf16[2,15,1536]{2,1,0:T(8,128)(2,1)S(1)}, u32[]{:S(2)}, u32[]{:S(2)}) %collective-permute-start.1) | collective-permute-done | bytes 92192 | tf_op jit(solution)/shard_map/ppermute | solution.py:17
  20.7 3.8 %fusion.143 = (f32[1536]{0:T(1024)S(1)}, f32[2,64,1536]{2,1,0:T(8,128)S(1)}) fusion(bf16[2,15,1536]{2,1,0:T(8,128)(2,1)S(1)} %collective-permute-done.1, bf16[2,64,1536]{2,1,0:T(8,128)(2,1)S(1)} %fusion, f32[1536]{0:T(1024)S(1)} %get-tuple-element.68, f32[1536]{0:T(1024)S(1)} %get-tuple-element.69, f32[1536]{0:T(1024)S(1)} %get-tuple-element.40, ...), kind=kLoop, calls=%fused_computation.380 | loop fusion | flops 35977728 | bytes 1560576 | tf_op jit(solution)/shard_map/reduce_sum | solution.py:107
  26.7 1.6 collective-permute-start.3
  28.3 2.2 %collective-permute-done.3 = f32[2,1536]{1,0:T(2,128)S(1)} collective-permute-done((f32[2,1536]{1,0:T(2,128)S(1)}, f32[2,1536]{1,0:T(2,128)S(1)}, u32[]{:S(2)}, u32[]{:S(2)}) %collective-permute-start.3) | collective-permute-done | bytes 12320 | tf_op jit(solution)/shard_map/ppermute | solution.py:44
  33.2 16.2 %all-gather.4.cloned.1.call-done = bf16[512,1536]{1,0:T(8,128)(2,1)} async-done(((bf16[128,1536]{1,0:T(8,128)(2,1)}), bf16[512,1536]{1,0:T(8,128)(2,1)}) %all-gather.4.cloned.1.call-update) | async-done | bytes 1572880 | tf_op jit(solution)/shard_map/all_gather | solution.py:99
  49.4 3.3 %fusion.147 = f32[512,384]{1,0:T(8,128)} fusion(bf16[512,1536]{1,0:T(8,128)(2,1)} %all-gather.4.cloned.1.call-done, bf16[384,1536]{1,0:T(8,128)(2,1)S(1)} %copy-done), kind=kOutput, calls=%fused_computation.383 | convolution fusion | flops 603979776 | bytes 3538944 | tf_op jit(solution)/shard_map/fd,cd->fc/dot_general | solution.py:117
  53.1 3.6 %all-to-all-start = ((f32[4,128,384]{2,1,0:T(8,128)}), f32[4,128,384]{2,1,0:T(8,128)S(1)}, u32[]{:S(2)}, u32[]{:S(2)}) async-start(f32[4,128,384]{2,1,0:T(8,128)} %bitcast.21), calls=%async_computation | async-start | bytes 1572864 | tf_op jit(solution)/shard_map/all_to_all | solution.py:118
  57.6 2.0 %collective-permute-start.5 = (f32[2,1536]{1,0:T(2,128)S(1)}, f32[2,1536]{1,0:T(2,128)S(1)}, u32[]{:S(2)}, u32[]{:S(2)}) collective-permute-start(f32[2,1536]{1,0:T(2,128)S(1)} %pad_maximum_fusion.9), channel_id=1, source_target_pairs={{0,1},{1,0},{2,3},{3,2},{4,5},{5,4},{6,7},{7,6},{8,9},{9,8},{10,11... | collective-permute-start | bytes 36872 | tf_op jit(solution)/shard_map/ppermute | solution.py:44
  59.6 10.3 %collective-permute-done.5 = f32[2,1536]{1,0:T(2,128)S(1)} collective-permute-done((f32[2,1536]{1,0:T(2,128)S(1)}, f32[2,1536]{1,0:T(2,128)S(1)}, u32[]{:S(2)}, u32[]{:S(2)}) %collective-permute-start.5) | collective-permute-done | bytes 12320 | tf_op jit(solution)/shard_map/ppermute | solution.py:44
  70.0 4.7 %collective-permute-start.6 = (f32[2,1536]{1,0:T(2,128)S(1)}, f32[2,1536]{1,0:T(2,128)S(1)}, u32[]{:S(2)}, u32[]{:S(2)}) collective-permute-start(f32[2,1536]{1,0:T(2,128)S(1)} %pad_maximum_fusion.10), channel_id=1, source_target_pairs={{0,2},{1,3},{2,0},{3,1},{4,6},{5,7},{6,4},{7,5},{8,10},{9,11},{10,... | collective-permute-start | bytes 36872 | tf_op jit(solution)/shard_map/ppermute | solution.py:44
  74.7 2.8 %collective-permute-done.6 = f32[2,1536]{1,0:T(2,128)S(1)} collective-permute-done((f32[2,1536]{1,0:T(2,128)S(1)}, f32[2,1536]{1,0:T(2,128)S(1)}, u32[]{:S(2)}, u32[]{:S(2)}) %collective-permute-start.6) | collective-permute-done | bytes 12320 | tf_op jit(solution)/shard_map/ppermute | solution.py:44
  79.0 2.3 %reshape.208 = f32[2,64,1536]{2,1,0:T(8,128)} reshape(f32[128,4,384]{2,1,0:T(4,128)} %copy.16) | data formatting | bytes 1572864 | tf_op jit(solution)/shard_map/reshape | solution.py:119
  81.4 2.4 %fusion.140 = (f32[1536]{0:T(1024)S(1)}, f32[1536]{0:T(1024)S(1)}, f32[2,64,1536]{2,1,0:T(8,128)}, bf16[2,64,1536]{2,1,0:T(8,128)(2,1)S(1)}) fusion(f32[1536]{0:T(1024)S(1)} %get-tuple-element.86, f32[2,64,1536]{2,1,0:T(8,128)S(1)} %get-tuple-element.89, f32[1536]{0:T(1024)S(1)} %get-tuple-element.97, f32[2,64,1536]{2,1,0:T(8,128)} %reshape.208, ...), kind=kLoop, calls=%fused_computation.378 | loop fusion | flops 3142656 | bytes 2789376 | tf_op jit(solution)/shard_map/reduce_sum | solution.py:130
  84.8 3.5 %all-to-all-start.1 = ((bf16[128,4,384]{2,0,1:T(8,128)(2,1)}), bf16[128,4,384]{2,0,1:T(8,128)(2,1)S(1)}, u32[]{:S(2)}, u32[]{:S(2)}) async-start(bf16[128,4,384]{2,0,1:T(8,128)(2,1)} %copy.17), calls=%async_computation.1 | async-start | bytes 786432 | tf_op jit(solution)/shard_map/all_to_all | solution.py:127
  93.9 2.2 %collective-permute-done.10 = f32[2,1536]{1,0:T(2,128)S(1)} collective-permute-done((f32[2,1536]{1,0:T(2,128)S(1)}, f32[2,1536]{1,0:T(2,128)S(1)}, u32[]{:S(2)}, u32[]{:S(2)}) %collective-permute-start.10) | collective-permute-done | bytes 12320 | tf_op jit(solution)/shard_map/ppermute | solution.py:34
  96.1 1.8 collective-permute-start.11
  97.9 1.9 %collective-permute-done.11 = f32[2,1536]{1,0:T(2,128)S(1)} collective-permute-done((f32[2,1536]{1,0:T(2,128)S(1)}, f32[2,1536]{1,0:T(2,128)S(1)}, u32[]{:S(2)}, u32[]{:S(2)}) %collective-permute-start.11) | collective-permute-done | bytes 12320 | tf_op jit(solution)/shard_map/ppermute | solution.py:34
  99.9 2.7 %collective-permute-start.12 = (f32[2,1536]{1,0:T(2,128)S(1)}, f32[2,1536]{1,0:T(2,128)S(1)}, u32[]{:S(2)}, u32[]{:S(2)}) collective-permute-start(f32[2,1536]{1,0:T(2,128)S(1)} %add.513), channel_id=1, source_target_pairs={{0,2},{1,3},{2,0},{3,1},{4,6},{5,7},{6,4},{7,5},{8,10},{9,11},{10,... | collective-permute-start | bytes 36872 | tf_op jit(solution)/shard_map/ppermute | solution.py:34
  102.6 3.5 %collective-permute-done.12 = f32[2,1536]{1,0:T(2,128)S(1)} collective-permute-done((f32[2,1536]{1,0:T(2,128)S(1)}, f32[2,1536]{1,0:T(2,128)S(1)}, u32[]{:S(2)}, u32[]{:S(2)}) %collective-permute-start.12) | collective-permute-done | bytes 12320 | tf_op jit(solution)/shard_map/ppermute | solution.py:34
  106.1 2.2 %fusion.148 = f32[384,1536]{1,0:T(8,128)S(1)} fusion(bf16[512,384]{1,0:T(8,128)(2,1)S(1)} %bitcast.20, bf16[512,1536]{1,0:T(8,128)(2,1)} %all-gather.4.cloned.1.call-done), kind=kOutput, calls=%fused_computation.384 | convolution fusion | flops 603979776 | bytes 4325376 | tf_op jit(solution)/shard_map/fc,fd->cd/dot_general | solution.py:128
  122.5 2.5 %stack.172 = f32[31,1536]{1,0:T(8,128)S(1)} concatenate(f32[1,1536]{1,0:T(1,128)} %stack.141, f32[1,1536]{1,0:T(1,128)} %stack.142, f32[1,1536]{1,0:T(1,128)} %stack.143, f32[1,1536]{1,0:T(1,128)} %stack.144, f32[1,1536]{1,0:T(1,128)S(1)} %stack.145, f32[1,1536]{1,0:T(1,128)S(1)} %stack.146, f32[1,1536]{1,0:T(1,128)S(1)} %stack.147, f32[1,1536]{1,0:T(1,128)S(1)} %stack.148, ...), dimensions={0} | concatenate | bytes 380928 | tf_op jit(solution)/shard_map/stack | solution.py:144
  125.1 17.8 %all-gather.6.cloned.1.call-done = bf16[768,1536]{1,0:T(8,128)(2,1)} async-done(((bf16[192,1536]{1,0:T(8,128)(2,1)}), bf16[768,1536]{1,0:T(8,128)(2,1)}) %all-gather.6.cloned.1.call-update) | async-done | bytes 2359312 | tf_op jit(solution)/shard_map/all_gather | solution.py:81
  145.9 1.5 collective-permute-start.17
  148.8 4.6 %collective-permute-start.14 = (bf16[2,15,1536]{2,1,0:T(8,128)(2,1)S(1)}, bf16[2,15,1536]{2,1,0:T(8,128)(2,1)S(1)}, u32[]{:S(2)}, u32[]{:S(2)}) collective-permute-start(bf16[2,15,1536]{2,1,0:T(8,128)(2,1)S(1)} %get-tuple-element.94), channel_id=1, source_target_pairs={{0,1},{1,2},{2,3},{4,5},{5,6},{6,7},{8,9},{9,10},{10,11},{12,13},{... | collective-permute-start | bytes 276488 | tf_op jit(solution)/shard_map/ppermute | solution.py:16
  155.1 2.1 %collective-permute-start.18 = (f32[48,1536]{1,0:T(8,128)S(1)}, f32[48,1536]{1,0:T(8,128)S(1)}, u32[]{:S(2)}, u32[]{:S(2)}) collective-permute-start(f32[48,1536]{1,0:T(8,128)S(1)} %dynamic-slice_add_fusion.2), channel_id=1, source_target_pairs={{0,16},{4,20},{8,24},{12,28},{16,0},{20,4},{24,8},{28,12},{1,17},{... | collective-permute-start | bytes 884744 | tf_op jit(solution)/shard_map/ppermute | solution.py:69
  157.5 4.1 %multiply_convert_fusion = (bf16[2,64,1536]{2,1,0:T(8,128)(2,1)S(1)}, f32[2,64,1536]{2,1,0:T(8,128)S(1)}) fusion(bf16[2,64,3072]{2,1,0:T(8,128)(2,1)S(1)} %copy-done.1, bf16[2,64,1536]{2,1,0:T(8,128)(2,1)S(1)} %get-tuple-element.82, bf16[2,15,1536]{2,1,0:T(8,128)(2,1)S(1)} %collective-permute-done.14, f32[1536]{0:T(1024)S(1)} %copy-done.62, ...), kind=kLoop, calls=%fused_computation.210 | loop fusion | flops 36962304 | bytes 2340864 | tf_op jit(solution)/shard_map/convert
  162.4 3.6 %collective-permute-done.18 = f32[48,1536]{1,0:T(8,128)S(1)} collective-permute-done((f32[48,1536]{1,0:T(8,128)S(1)}, f32[48,1536]{1,0:T(8,128)S(1)}, u32[]{:S(2)}, u32[]{:S(2)}) %collective-permute-start.18) | collective-permute-done | bytes 294944 | tf_op jit(solution)/shard_map/ppermute | solution.py:69
  169.5 7.6 %collective-permute-done.25 = f32[31,1536]{1,0:T(8,128)S(1)} collective-permute-done((f32[31,1536]{1,0:T(8,128)S(1)}, f32[31,1536]{1,0:T(8,128)S(1)}, u32[]{:S(2)}, u32[]{:S(2)}) %collective-permute-start.25) | collective-permute-done | bytes 190496 | tf_op jit(solution)/shard_map/ppermute | solution.py:34
  177.8 1.9 %collective-permute-done.19 = f32[96,1536]{1,0:T(8,128)S(1)} collective-permute-done((f32[96,1536]{1,0:T(8,128)S(1)}, f32[96,1536]{1,0:T(8,128)S(1)}, u32[]{:S(2)}, u32[]{:S(2)}) %collective-permute-start.19) | collective-permute-done | bytes 589856 | tf_op jit(solution)/shard_map/ppermute | solution.py:69
  180.6 1.5 convolution_convert_fusion
  182.8 1.6 maximum_select_fusion
  (283 shorter events, 44.2 us)
Async XLA Ops:
  7.2 42.3 %copy-start = (bf16[384,1536]{1,0:T(8,128)(2,1)S(1)}, bf16[384,1536]{1,0:T(8,128)(2,1)}, u32[]{:S(2)}) copy-start(bf16[384,1536]{1,0:T(8,128)(2,1)} %param.10) | copy-start | bytes 3538948
  7.2 42.2 %all-gather.4.cloned.1.call-start = ((), (), s32[]{:S(2)}) async-start(), calls=%async_computation.2 | async-start | bytes 1966080 | tf_op jit(solution)/shard_map/all_gather | solution.py:99
  9.3 7.1 %collective-permute-start = (bf16[2,15,1536]{2,1,0:T(8,128)(2,1)S(1)}, bf16[2,15,1536]{2,1,0:T(8,128)(2,1)S(1)}, u32[]{:S(2)}, u32[]{:S(2)}) collective-permute-start(bf16[2,15,1536]{2,1,0:T(8,128)(2,1)S(1)} %get-tuple-element.95), channel_id=1, source_target_pairs={{0,1},{1,2},{2,3},{4,5},{5,6},{6,7},{8,9},{9,10},{10,11},{12,13},{... | collective-permute-start | bytes 276488 | tf_op jit(solution)/shard_map/ppermute | solution.py:16
  14.2 6.5 %collective-permute-start.1 = (bf16[2,15,1536]{2,1,0:T(8,128)(2,1)S(1)}, bf16[2,15,1536]{2,1,0:T(8,128)(2,1)S(1)}, u32[]{:S(2)}, u32[]{:S(2)}) collective-permute-start(bf16[2,15,1536]{2,1,0:T(8,128)(2,1)S(1)} %get-tuple-element.96), channel_id=1, source_target_pairs={{1,0},{2,1},{3,2},{5,4},{6,5},{7,6},{9,8},{10,9},{11,10},{13,12},{... | collective-permute-start | bytes 276488 | tf_op jit(solution)/shard_map/ppermute | solution.py:17
  15.9 36.8 %copy-start.9 = (f32[1536]{0:T(1024)}, f32[1536]{0:T(1024)S(1)}, u32[]{:S(2)}) copy-start(f32[1536]{0:T(1024)S(1)} %get-tuple-element.42) | copy-start | bytes 18436
  24.8 1.2 collective-permute-start.2
  26.7 3.8 %collective-permute-start.3 = (f32[2,1536]{1,0:T(2,128)S(1)}, f32[2,1536]{1,0:T(2,128)S(1)}, u32[]{:S(2)}, u32[]{:S(2)}) collective-permute-start(f32[2,1536]{1,0:T(2,128)S(1)} %pad_maximum_fusion.7), channel_id=1, source_target_pairs={{0,8},{4,12},{8,0},{12,4},{16,24},{20,28},{24,16},{28,20},{1,9},{5... | collective-permute-start | bytes 36872 | tf_op jit(solution)/shard_map/ppermute | solution.py:44
  31.7 25.0 %collective-permute-start.4 = (f32[2,1536]{1,0:T(2,128)}, f32[2,1536]{1,0:T(2,128)}, u32[]{:S(2)}, u32[]{:S(2)}) collective-permute-start(f32[2,1536]{1,0:T(2,128)} %pad_maximum_fusion.8), channel_id=1, source_target_pairs={{0,16},{4,20},{8,24},{12,28},{16,0},{20,4},{24,8},{28,12},{1,17},{... | collective-permute-start | bytes 36872 | tf_op jit(solution)/shard_map/ppermute | solution.py:44
  53.1 24.5 %all-to-all-start = ((f32[4,128,384]{2,1,0:T(8,128)}), f32[4,128,384]{2,1,0:T(8,128)S(1)}, u32[]{:S(2)}, u32[]{:S(2)}) async-start(f32[4,128,384]{2,1,0:T(8,128)} %bitcast.21), calls=%async_computation | async-start | bytes 1572864 | tf_op jit(solution)/shard_map/all_to_all | solution.py:118
  57.6 12.4 %collective-permute-start.5 = (f32[2,1536]{1,0:T(2,128)S(1)}, f32[2,1536]{1,0:T(2,128)S(1)}, u32[]{:S(2)}, u32[]{:S(2)}) collective-permute-start(f32[2,1536]{1,0:T(2,128)S(1)} %pad_maximum_fusion.9), channel_id=1, source_target_pairs={{0,1},{1,0},{2,3},{3,2},{4,5},{5,4},{6,7},{7,6},{8,9},{9,8},{10,11... | collective-permute-start | bytes 36872 | tf_op jit(solution)/shard_map/ppermute | solution.py:44
  70.0 7.4 %collective-permute-start.6 = (f32[2,1536]{1,0:T(2,128)S(1)}, f32[2,1536]{1,0:T(2,128)S(1)}, u32[]{:S(2)}, u32[]{:S(2)}) collective-permute-start(f32[2,1536]{1,0:T(2,128)S(1)} %pad_maximum_fusion.10), channel_id=1, source_target_pairs={{0,2},{1,3},{2,0},{3,1},{4,6},{5,7},{6,4},{7,5},{8,10},{9,11},{10,... | collective-permute-start | bytes 36872 | tf_op jit(solution)/shard_map/ppermute | solution.py:44
  83.8 4.7 %collective-permute-start.8 = (f32[2,1536]{1,0:T(2,128)S(1)}, f32[2,1536]{1,0:T(2,128)S(1)}, u32[]{:S(2)}, u32[]{:S(2)}) collective-permute-start(f32[2,1536]{1,0:T(2,128)S(1)} %pad_maximum_fusion.11), channel_id=1, source_target_pairs={{0,4},{4,0},{8,12},{12,8},{16,20},{20,16},{24,28},{28,24},{1,5},{5... | collective-permute-start | bytes 36872 | tf_op jit(solution)/shard_map/ppermute | solution.py:34
  84.8 21.3 %all-to-all-start.1 = ((bf16[128,4,384]{2,0,1:T(8,128)(2,1)}), bf16[128,4,384]{2,0,1:T(8,128)(2,1)S(1)}, u32[]{:S(2)}, u32[]{:S(2)}) async-start(bf16[128,4,384]{2,0,1:T(8,128)(2,1)} %copy.17), calls=%async_computation.1 | async-start | bytes 786432 | tf_op jit(solution)/shard_map/all_to_all | solution.py:127
  88.3 54.6 %all-gather.6.cloned.1.call-start = ((), (), s32[]{:S(2)}) async-start(), calls=%async_computation.3 | async-start | bytes 2949120 | tf_op jit(solution)/shard_map/all_gather | solution.py:81
  88.6 3.8 %collective-permute-start.9 = (f32[2,1536]{1,0:T(2,128)S(1)}, f32[2,1536]{1,0:T(2,128)S(1)}, u32[]{:S(2)}, u32[]{:S(2)}) collective-permute-start(f32[2,1536]{1,0:T(2,128)S(1)} %fusion.139), channel_id=1, source_target_pairs={{0,8},{4,12},{8,0},{12,4},{16,24},{20,28},{24,16},{28,20},{1,9},{5... | collective-permute-start | bytes 36872 | tf_op jit(solution)/shard_map/ppermute | solution.py:34
  92.3 3.8 %collective-permute-start.10 = (f32[2,1536]{1,0:T(2,128)S(1)}, f32[2,1536]{1,0:T(2,128)S(1)}, u32[]{:S(2)}, u32[]{:S(2)}) collective-permute-start(f32[2,1536]{1,0:T(2,128)S(1)} %fusion.155), channel_id=1, source_target_pairs={{0,16},{4,20},{8,24},{12,28},{16,0},{20,4},{24,8},{28,12},{1,17},{... | collective-permute-start | bytes 36872 | tf_op jit(solution)/shard_map/ppermute | solution.py:34
  96.1 3.8 %collective-permute-start.11 = (f32[2,1536]{1,0:T(2,128)S(1)}, f32[2,1536]{1,0:T(2,128)S(1)}, u32[]{:S(2)}, u32[]{:S(2)}) collective-permute-start(f32[2,1536]{1,0:T(2,128)S(1)} %add.512), channel_id=1, source_target_pairs={{0,1},{1,0},{2,3},{3,2},{4,5},{5,4},{6,7},{7,6},{8,9},{9,8},{10,11... | collective-permute-start | bytes 36872 | tf_op jit(solution)/shard_map/ppermute | solution.py:34
  99.9 6.2 %collective-permute-start.12 = (f32[2,1536]{1,0:T(2,128)S(1)}, f32[2,1536]{1,0:T(2,128)S(1)}, u32[]{:S(2)}, u32[]{:S(2)}) collective-permute-start(f32[2,1536]{1,0:T(2,128)S(1)} %add.513), channel_id=1, source_target_pairs={{0,2},{1,3},{2,0},{3,1},{4,6},{5,7},{6,4},{7,5},{8,10},{9,11},{10,... | collective-permute-start | bytes 36872 | tf_op jit(solution)/shard_map/ppermute | solution.py:34
  108.5 3.8 %collective-permute-start.15 = (f32[192,1536]{1,0:T(8,128)S(1)}, f32[192,1536]{1,0:T(8,128)S(1)}, u32[]{:S(2)}, u32[]{:S(2)}) collective-permute-start(f32[192,1536]{1,0:T(8,128)S(1)} %constant_dynamic-slice_fusion.2), channel_id=1, source_target_pairs={{0,4},{4,0},{8,12},{12,8},{16,20},{20,16},{24,28},{28,24},{1,5},{5... | collective-permute-start | bytes 3538952 | tf_op jit(solution)/shard_map/ppermute | solution.py:65
  114.3 30.1 %collective-permute-start.16 = (f32[96,1536]{1,0:T(8,128)}, f32[96,1536]{1,0:T(8,128)}, u32[]{:S(2)}, u32[]{:S(2)}) collective-permute-start(f32[96,1536]{1,0:T(8,128)} %constant_dynamic-slice_fusion.1), channel_id=1, source_target_pairs={{0,8},{4,12},{8,0},{12,4},{16,24},{20,28},{24,16},{28,20},{1,9},{5... | collective-permute-start | bytes 1769480 | tf_op jit(solution)/shard_map/ppermute | solution.py:65
  124.9 17.9 %collective-permute-start.21 = (f32[31,1536]{1,0:T(8,128)S(1)}, f32[31,1536]{1,0:T(8,128)S(1)}, u32[]{:S(2)}, u32[]{:S(2)}) collective-permute-start(f32[31,1536]{1,0:T(8,128)S(1)} %stack.172), channel_id=1, source_target_pairs={{0,4},{4,0},{8,12},{12,8},{16,20},{20,16},{24,28},{28,24},{1,5},{5... | collective-permute-start | bytes 571400 | tf_op jit(solution)/shard_map/ppermute | solution.py:34
  142.8 37.1 %collective-permute-start.7 = (bf16[4,192,1536]{2,1,0:T(8,128)(2,1)}, bf16[4,192,1536]{2,1,0:T(8,128)(2,1)S(1)}, u32[]{:S(2)}, u32[]{:S(2)}) collective-permute-start(bf16[4,192,1536]{2,1,0:T(8,128)(2,1)} %bitcast.18), channel_id=1, source_target_pairs={{0,4},{4,0},{8,12},{12,8},{16,20},{20,16},{24,28},{28,24},{1,5},{5... | collective-permute-start | bytes 7077896 | tf_op jit(solution)/shard_map/ppermute | solution.py:82
  142.9 10.4 %collective-permute-start.22 = (f32[31,1536]{1,0:T(8,128)S(1)}, f32[31,1536]{1,0:T(8,128)S(1)}, u32[]{:S(2)}, u32[]{:S(2)}) collective-permute-start(f32[31,1536]{1,0:T(8,128)S(1)} %add.553), channel_id=1, source_target_pairs={{0,8},{4,12},{8,0},{12,4},{16,24},{20,28},{24,16},{28,20},{1,9},{5... | collective-permute-start | bytes 571400 | tf_op jit(solution)/shard_map/ppermute | solution.py:34
  145.9 9.2 %collective-permute-start.17 = (f32[48,1536]{1,0:T(8,128)S(1)}, f32[48,1536]{1,0:T(8,128)S(1)}, u32[]{:S(2)}, u32[]{:S(2)}) collective-permute-start(f32[48,1536]{1,0:T(8,128)S(1)} %constant_dynamic-slice_fusion), channel_id=1, source_target_pairs={{0,16},{4,20},{8,24},{12,28},{16,0},{20,4},{24,8},{28,12},{1,17},{... | collective-permute-start | bytes 884744 | tf_op jit(solution)/shard_map/ppermute | solution.py:65
  147.5 9.8 %collective-permute-start.13 = (bf16[2,15,1536]{2,1,0:T(8,128)(2,1)S(1)}, bf16[2,15,1536]{2,1,0:T(8,128)(2,1)S(1)}, u32[]{:S(2)}, u32[]{:S(2)}) collective-permute-start(bf16[2,15,1536]{2,1,0:T(8,128)(2,1)S(1)} %get-tuple-element.93), channel_id=1, source_target_pairs={{1,0},{2,1},{3,2},{5,4},{6,5},{7,6},{9,8},{10,9},{11,10},{13,12},{... | collective-permute-start | bytes 276488 | tf_op jit(solution)/shard_map/ppermute | solution.py:17
  148.8 8.5 %collective-permute-start.14 = (bf16[2,15,1536]{2,1,0:T(8,128)(2,1)S(1)}, bf16[2,15,1536]{2,1,0:T(8,128)(2,1)S(1)}, u32[]{:S(2)}, u32[]{:S(2)}) collective-permute-start(bf16[2,15,1536]{2,1,0:T(8,128)(2,1)S(1)} %get-tuple-element.94), channel_id=1, source_target_pairs={{0,1},{1,2},{2,3},{4,5},{5,6},{6,7},{8,9},{9,10},{10,11},{12,13},{... | collective-permute-start | bytes 276488 | tf_op jit(solution)/shard_map/ppermute | solution.py:16
  153.4 8.2 %collective-permute-start.23 = (f32[31,1536]{1,0:T(8,128)S(1)}, f32[31,1536]{1,0:T(8,128)S(1)}, u32[]{:S(2)}, u32[]{:S(2)}) collective-permute-start(f32[31,1536]{1,0:T(8,128)S(1)} %add.554), channel_id=1, source_target_pairs={{0,16},{4,20},{8,24},{12,28},{16,0},{20,4},{24,8},{28,12},{1,17},{... | collective-permute-start | bytes 571400 | tf_op jit(solution)/shard_map/ppermute | solution.py:34
  155.1 10.8 %collective-permute-start.18 = (f32[48,1536]{1,0:T(8,128)S(1)}, f32[48,1536]{1,0:T(8,128)S(1)}, u32[]{:S(2)}, u32[]{:S(2)}) collective-permute-start(f32[48,1536]{1,0:T(8,128)S(1)} %dynamic-slice_add_fusion.2), channel_id=1, source_target_pairs={{0,16},{4,20},{8,24},{12,28},{16,0},{20,4},{24,8},{28,12},{1,17},{... | collective-permute-start | bytes 884744 | tf_op jit(solution)/shard_map/ppermute | solution.py:69
  161.6 5.7 %collective-permute-start.24 = (f32[31,1536]{1,0:T(8,128)S(1)}, f32[31,1536]{1,0:T(8,128)S(1)}, u32[]{:S(2)}, u32[]{:S(2)}) collective-permute-start(f32[31,1536]{1,0:T(8,128)S(1)} %add.555), channel_id=1, source_target_pairs={{0,1},{1,0},{2,3},{3,2},{4,5},{5,4},{6,7},{7,6},{8,9},{9,8},{10,11... | collective-permute-start | bytes 571400 | tf_op jit(solution)/shard_map/ppermute | solution.py:34
  166.0 13.8 %collective-permute-start.19 = (f32[96,1536]{1,0:T(8,128)S(1)}, f32[96,1536]{1,0:T(8,128)S(1)}, u32[]{:S(2)}, u32[]{:S(2)}) collective-permute-start(f32[96,1536]{1,0:T(8,128)S(1)} %maximum_select_fusion.2), channel_id=1, source_target_pairs={{0,8},{4,12},{8,0},{12,4},{16,24},{20,28},{24,16},{28,20},{1,9},{5... | collective-permute-start | bytes 1769480 | tf_op jit(solution)/shard_map/ppermute | solution.py:69
  167.4 9.7 %collective-permute-start.25 = (f32[31,1536]{1,0:T(8,128)S(1)}, f32[31,1536]{1,0:T(8,128)S(1)}, u32[]{:S(2)}, u32[]{:S(2)}) collective-permute-start(f32[31,1536]{1,0:T(8,128)S(1)} %add.556), channel_id=1, source_target_pairs={{0,2},{1,3},{2,0},{3,1},{4,6},{5,7},{6,4},{7,5},{8,10},{9,11},{10,... | collective-permute-start | bytes 571400 | tf_op jit(solution)/shard_map/ppermute | solution.py:34
  179.9 2.9 %collective-permute-start.20 = (f32[192,1536]{1,0:T(8,128)S(1)}, f32[192,1536]{1,0:T(8,128)S(1)}, u32[]{:S(2)}, u32[]{:S(2)}) collective-permute-start(f32[192,1536]{1,0:T(8,128)S(1)} %maximum_select_fusion.1), channel_id=1, source_target_pairs={{0,4},{4,0},{8,12},{12,8},{16,20},{20,16},{24,28},{28,24},{1,5},{5... | collective-permute-start | bytes 3538952 | tf_op jit(solution)/shard_map/ppermute | solution.py:69
  (77 other events, 1604.6 us)
Sparse Core Ops, SparseCore 0:
  9.6 39.7 all-gather.3
  91.1 51.7 all-gather.5

commit v15 on v13

--- a/solution.py
+++ b/solution.py
@@ -101,9 +101,25 @@
     gates = jax.nn.sigmoid(glu_input[..., width:].astype(jnp.float32))
     gated = (values * gates).astype(jnp.bfloat16)
     padded = extended(gated, (("tensor", 1),), radius)
-    conv_out = jnp.zeros(gated.shape, jnp.float32)
-    for offset in range(taps):
-        conv_out = conv_out + depth_kernel[offset] * padded[:, offset : offset + frames, :]
+    if frames >= 2 * radius:
+        own = jnp.pad(gated, ((0, 0), (radius, radius), (0, 0)))
+        conv_out = jnp.zeros(gated.shape, jnp.float32)
+        for offset in range(taps):
+            conv_out = conv_out + depth_kernel[offset] * own[:, offset : offset + frames, :]
+        blank = jnp.zeros((gated.shape[0], 2 * radius, gated.shape[2]), gated.dtype)
+        left = jnp.concatenate([padded[:, :radius], blank], axis=1)
+        right = jnp.concatenate([blank, padded[:, frames + radius :]], axis=1)
+        head = jnp.zeros((gated.shape[0], radius, gated.shape[2]), jnp.float32)
+        tail = jnp.zeros((gated.shape[0], radius, gated.shape[2]), jnp.float32)
+        for offset in range(taps):
+            head = head + depth_kernel[offset] * left[:, offset : offset + radius, :]
+            tail = tail + depth_kernel[offset] * right[:, offset : offset + radius, :]
+        middle = jnp.zeros((gated.shape[0], frames - 2 * radius, gated.shape[2]), jnp.float32)
+        conv_out = conv_out + jnp.concatenate([head, middle, tail], axis=1)
+    else:
+        conv_out = jnp.zeros(gated.shape, jnp.float32)
+        for offset in range(taps):
+            conv_out = conv_out + depth_kernel[offset] * padded[:, offset : offset + frames, :]
     mean_local = jnp.sum(conv_out, axis=(0, 1)) / local
     dev_local = conv_out - mean_local
     spread_local = jnp.sum(dev_local * dev_local, axis=(0, 1))

time: 187 us -> 189 us (1.011)
  waiting for transfers between devices: 63.3 us -> 43.9 us
  local copies, waits for them, and re-layouts: 15.2 us -> 29.2 us
  other arithmetic: 22.9 us -> 28.7 us
  starting transfers between devices: 40.8 us -> 42.9 us
    all_gather x1, waiting for transfers between devices: 17.2 us -> 0.54 us  [gather_weight(): held = lax.all_gather(mine, 'tensor', axis=0, tiled=False)]
    another operation x32, local copies, waits for them, and re-layouts: 7.97 us -> 21.9 us  [on_device(): jnp.stack([jnp.sum(padded[:, offset:offset + frames, :].astype(jnp.float3...]
    add x10, other arithmetic: 0.86 us -> 5.79 us  [all_sum(): x = x + lax.ppermute(x, axis, [(i, i ^ step) for i in range(peers)])]
  transfers between devices with their start and end apart: 29 -> 29, of which waited for: 19 -> 18; matrix products, arithmetic and copies ran while one was open for 18% -> 28% of each run, Pallas kernels for 0% -> 0%
where the time goes in v15:
time: 189 us; the launch traced here: 188 us
  waiting for transfers between devices  43.9 us (23%)
  starting transfers between devices  42.9 us (23%)
  local copies, waits for them, and re-layouts  29.2 us (15%)
  other arithmetic  28.7 us (15%)
  blocking collectives  22.6 us (12%)
  between operations  14.9 us (8%)
  matrix products  6.15 us (3%)
    all_to_all x1, blocking collectives, on_device(): lax.all_to_all(own_columns, 'tensor', split_axis=0, concat_axis=1, tiled=...  22.6 us
    another operation x32, local copies, waits for them, and re-layouts, on_device(): jnp.stack([jnp.sum(padded[:, offset:offset + frames, :].astype(jnp.float3...  21.9 us
    ppermute x10, waiting for transfers between devices, all_sum(): x = x + lax.ppermute(x, axis, [(i, i ^ step) for i in range(peers)])  15.7 us
    ppermute x10, starting transfers between devices, all_sum(): x = x + lax.ppermute(x, axis, [(i, i ^ step) for i in range(peers)])  13.2 us
    ppermute x5, waiting for transfers between devices, all_moments(): lax.ppermute(jnp.stack([mean, spread]), axis, [(i, i ^ step) for i in ran...  10.5 us
    ppermute x2, starting transfers between devices, extended(): before = lax.ppermute(last, axis, up)  9.48 us
    ppermute x5, starting transfers between devices, all_moments(): lax.ppermute(jnp.stack([mean, spread]), axis, [(i, i ^ step) for i in ran...  7.51 us
    all_gather x1, waiting for transfers between devices, on_device(): group_grad = lax.all_gather(flat_grad, 'tensor', axis=0, tiled=True)  5.93 us
  transfers between devices with their start and end apart: 29, of which 18 were waited for; matrix products, arithmetic and copies ran while one was open for 28% of the time, Pallas kernels for 0%

profile of v15, /device:TPU:0, one launch (start us, length us, event | category | flops | bytes accessed | tf_op | source)
XLA Modules:
  0.0 188.4 jit_solution(690415956204647870)
XLA Ops:
  9.3 4.9 %collective-permute-start = (bf16[2,15,1536]{2,1,0:T(8,128)(2,1)S(1)}, bf16[2,15,1536]{2,1,0:T(8,128)(2,1)S(1)}, u32[]{:S(2)}, u32[]{:S(2)}) collective-permute-start(bf16[2,15,1536]{2,1,0:T(8,128)(2,1)S(1)} %get-tuple-element.99), channel_id=1, source_target_pairs={{0,1},{1,2},{2,3},{4,5},{5,6},{6,7},{8,9},{9,10},{10,11},{12,13},{... | collective-permute-start | bytes 276488 | tf_op jit(solution)/shard_map/ppermute | solution.py:16
  16.3 4.4 %collective-permute-done.1 = bf16[2,15,1536]{2,1,0:T(8,128)(2,1)S(1)} collective-permute-done((bf16[2,15,1536]{2,1,0:T(8,128)(2,1)S(1)}, bf16[2,15,1536]{2,1,0:T(8,128)(2,1)S(1)}, u32[]{:S(2)}, u32[]{:S(2)}) %collective-permute-start.1) | collective-permute-done | bytes 92192 | tf_op jit(solution)/shard_map/ppermute | solution.py:17
  21.5 3.3 %fusion.130 = (f32[1536]{0:T(1024)S(1)}, f32[2,64,1536]{2,1,0:T(8,128)S(1)}) fusion(f32[2,15,1536]{2,1,0:T(8,128)S(1)} %multiply_add_fusion.1, f32[64]{0:T(128)S(1)} %pad.44.clone, f32[2,15,1536]{2,1,0:T(8,128)S(1)} %add_add_fusion, f32[1536]{0:T(1024)S(1)} %get-tuple-element.72, f32[1536]{0:T(1024)S(1)} %get-tuple-element.73, ...), kind=kLoop, calls=%fused_computation.414 | loop fusion | flops 18872832 | bytes 1745152 | tf_op jit(solution)/shard_map/reduce_sum | solution.py:123
  27.9 2.2 %collective-permute-done.3 = f32[2,1536]{1,0:T(2,128)S(1)} collective-permute-done((f32[2,1536]{1,0:T(2,128)S(1)}, f32[2,1536]{1,0:T(2,128)S(1)}, u32[]{:S(2)}, u32[]{:S(2)}) %collective-permute-start.3) | collective-permute-done | bytes 12320 | tf_op jit(solution)/shard_map/ppermute | solution.py:44
  30.2 1.6 collective-permute-start.4
  31.7 2.2 %collective-permute-done.4 = f32[2,1536]{1,0:T(2,128)S(1)} collective-permute-done((f32[2,1536]{1,0:T(2,128)S(1)}, f32[2,1536]{1,0:T(2,128)S(1)}, u32[]{:S(2)}, u32[]{:S(2)}) %collective-permute-start.4) | collective-permute-done | bytes 12320 | tf_op jit(solution)/shard_map/ppermute | solution.py:44
  34.0 1.6 collective-permute-start.5
  35.6 2.4 %collective-permute-done.5 = f32[2,1536]{1,0:T(2,128)S(1)} collective-permute-done((f32[2,1536]{1,0:T(2,128)S(1)}, f32[2,1536]{1,0:T(2,128)S(1)}, u32[]{:S(2)}, u32[]{:S(2)}) %collective-permute-start.5) | collective-permute-done | bytes 12320 | tf_op jit(solution)/shard_map/ppermute | solution.py:44
  38.0 2.7 %collective-permute-start.6 = (f32[2,1536]{1,0:T(2,128)S(1)}, f32[2,1536]{1,0:T(2,128)S(1)}, u32[]{:S(2)}, u32[]{:S(2)}) collective-permute-start(f32[2,1536]{1,0:T(2,128)S(1)} %pad_maximum_fusion.10), channel_id=1, source_target_pairs={{0,2},{1,3},{2,0},{3,1},{4,6},{5,7},{6,4},{7,5},{8,10},{9,11},{10,... | collective-permute-start | bytes 36872 | tf_op jit(solution)/shard_map/ppermute | solution.py:44
  40.7 2.6 %collective-permute-done.6 = f32[2,1536]{1,0:T(2,128)S(1)} collective-permute-done((f32[2,1536]{1,0:T(2,128)S(1)}, f32[2,1536]{1,0:T(2,128)S(1)}, u32[]{:S(2)}, u32[]{:S(2)}) %collective-permute-start.6) | collective-permute-done | bytes 12320 | tf_op jit(solution)/shard_map/ppermute | solution.py:44
  44.0 5.9 %all-gather.4.cloned.1.call-done = bf16[512,1536]{1,0:T(8,128)(2,1)} async-done(((bf16[128,1536]{1,0:T(8,128)(2,1)}), bf16[512,1536]{1,0:T(8,128)(2,1)}) %all-gather.4.cloned.1.call-update) | async-done | bytes 1572880 | tf_op jit(solution)/shard_map/all_gather | solution.py:99
  50.0 2.4 %fusion.134 = f32[512,384]{1,0:T(8,128)S(1)} fusion(bf16[512,1536]{1,0:T(8,128)(2,1)} %all-gather.4.cloned.1.call-done, bf16[384,1536]{1,0:T(8,128)(2,1)S(1)} %copy-done), kind=kOutput, calls=%fused_computation.417 | convolution fusion | flops 603979776 | bytes 3538944 | tf_op jit(solution)/shard_map/fd,cd->fc/dot_general | solution.py:134
  52.4 22.6 %all_to_all.35 = f32[4,128,384]{2,1,0:T(8,128)S(1)} all-to-all(f32[4,128,384]{2,1,0:T(8,128)S(1)} %bitcast.21), channel_id=1, replica_groups=mesh['dp'=8,'tensor'=4] {'tensor'}, dimensions={0} | all-to-all | bytes 1572864 | tf_op jit(solution)/shard_map/all_to_all | solution.py:135
  76.7 2.5 %fusion.127 = (f32[1536]{0:T(1024)S(1)}, f32[1536]{0:T(1024)S(1)}, f32[2,64,1536]{2,1,0:T(8,128)}, bf16[2,64,1536]{2,1,0:T(8,128)(2,1)S(1)}) fusion(f32[1536]{0:T(1024)} %get-tuple-element.90, f32[2,64,1536]{2,1,0:T(8,128)S(1)} %get-tuple-element.93, f32[1536]{0:T(1024)} %get-tuple-element.8, f32[2,64,1536]{2,1,0:T(8,128)} %reshape.189, f32[1536]{0:T(1024)} %param.9, ...), kind=kLoop, calls=%fused_computation.412 | loop fusion | flops 3142656 | bytes 2789376 | tf_op jit(solution)/shard_map/reduce_sum | solution.py:147
  80.8 3.5 %all-to-all-start.1 = ((bf16[128,4,384]{2,0,1:T(8,128)(2,1)}), bf16[128,4,384]{2,0,1:T(8,128)(2,1)S(1)}, u32[]{:S(2)}, u32[]{:S(2)}) async-start(bf16[128,4,384]{2,0,1:T(8,128)(2,1)} %copy.17), calls=%async_computation.1 | async-start | bytes 786432 | tf_op jit(solution)/shard_map/all_to_all | solution.py:144
  88.2 1.7 collective-permute-done.9
  92.1 2.2 %collective-permute-done.10 = f32[2,1536]{1,0:T(2,128)S(1)} collective-permute-done((f32[2,1536]{1,0:T(2,128)S(1)}, f32[2,1536]{1,0:T(2,128)S(1)}, u32[]{:S(2)}, u32[]{:S(2)}) %collective-permute-start.10) | collective-permute-done | bytes 12320 | tf_op jit(solution)/shard_map/ppermute | solution.py:34
  94.4 1.8 collective-permute-start.11
  96.2 1.9 %collective-permute-done.11 = f32[2,1536]{1,0:T(2,128)S(1)} collective-permute-done((f32[2,1536]{1,0:T(2,128)S(1)}, f32[2,1536]{1,0:T(2,128)S(1)}, u32[]{:S(2)}, u32[]{:S(2)}) %collective-permute-start.11) | collective-permute-done | bytes 12320 | tf_op jit(solution)/shard_map/ppermute | solution.py:34
  98.7 2.7 %collective-permute-start.12 = (f32[2,1536]{1,0:T(2,128)}, f32[2,1536]{1,0:T(2,128)}, u32[]{:S(2)}, u32[]{:S(2)}) collective-permute-start(f32[2,1536]{1,0:T(2,128)} %add.762), channel_id=1, source_target_pairs={{0,2},{1,3},{2,0},{3,1},{4,6},{5,7},{6,4},{7,5},{8,10},{9,11},{10,... | collective-permute-start | bytes 36872 | tf_op jit(solution)/shard_map/ppermute | solution.py:34
  101.4 2.6 %collective-permute-done.12 = f32[2,1536]{1,0:T(2,128)} collective-permute-done((f32[2,1536]{1,0:T(2,128)}, f32[2,1536]{1,0:T(2,128)}, u32[]{:S(2)}, u32[]{:S(2)}) %collective-permute-start.12) | collective-permute-done | bytes 12320 | tf_op jit(solution)/shard_map/ppermute | solution.py:34
  105.3 2.2 %fusion.135 = f32[384,1536]{1,0:T(8,128)S(1)} fusion(bf16[512,384]{1,0:T(8,128)(2,1)S(1)} %bitcast.20, bf16[512,1536]{1,0:T(8,128)(2,1)} %all-gather.4.cloned.1.call-done), kind=kOutput, calls=%fused_computation.418 | convolution fusion | flops 603979776 | bytes 4325376 | tf_op jit(solution)/shard_map/fc,fd->cd/dot_general | solution.py:145
  135.2 3.5 %stack.172 = f32[31,1536]{1,0:T(8,128)S(1)} concatenate(f32[1,1536]{1,0:T(1,128)} %stack.141, f32[1,1536]{1,0:T(1,128)} %stack.142, f32[1,1536]{1,0:T(1,128)} %stack.143, f32[1,1536]{1,0:T(1,128)} %stack.144, f32[1,1536]{1,0:T(1,128)} %stack.145, f32[1,1536]{1,0:T(1,128)} %stack.146, f32[1,1536]{1,0:T(1,128)} %stack.147, f32[1,1536]{1,0:T(1,128)} %stack.148, f32[1,1536]{1,0:T(1,128)} %stack.149, ...), dimensions={0} | concatenate | bytes 380928 | tf_op jit(solution)/shard_map/stack | solution.py:161
  146.1 4.6 %collective-permute-start.14 = (bf16[2,15,1536]{2,1,0:T(8,128)(2,1)S(1)}, bf16[2,15,1536]{2,1,0:T(8,128)(2,1)S(1)}, u32[]{:S(2)}, u32[]{:S(2)}) collective-permute-start(bf16[2,15,1536]{2,1,0:T(8,128)(2,1)S(1)} %get-tuple-element.98), channel_id=1, source_target_pairs={{0,1},{1,2},{2,3},{4,5},{5,6},{6,7},{8,9},{9,10},{10,11},{12,13},{... | collective-permute-start | bytes 276488 | tf_op jit(solution)/shard_map/ppermute | solution.py:16
  152.4 2.1 %collective-permute-start.18 = (f32[48,1536]{1,0:T(8,128)S(1)}, f32[48,1536]{1,0:T(8,128)S(1)}, u32[]{:S(2)}, u32[]{:S(2)}) collective-permute-start(f32[48,1536]{1,0:T(8,128)S(1)} %dynamic-slice_add_fusion.2), channel_id=1, source_target_pairs={{0,16},{4,20},{8,24},{12,28},{16,0},{20,4},{24,8},{28,12},{1,17},{... | collective-permute-start | bytes 884744 | tf_op jit(solution)/shard_map/ppermute | solution.py:69
  154.5 4.1 %multiply_convert_fusion = (bf16[2,64,1536]{2,1,0:T(8,128)(2,1)S(1)}, f32[2,64,1536]{2,1,0:T(8,128)S(1)}) fusion(bf16[2,64,3072]{2,1,0:T(8,128)(2,1)S(1)} %copy-done.1, bf16[2,64,1536]{2,1,0:T(8,128)(2,1)S(1)} %get-tuple-element.86, bf16[2,15,1536]{2,1,0:T(8,128)(2,1)S(1)} %collective-permute-done.14, f32[1536]{0:T(1024)S(1)} %copy-done.11, ...), kind=kLoop, calls=%fused_computation.225 | loop fusion | flops 36962304 | bytes 2340864 | tf_op jit(solution)/shard_map/convert
  158.7 1.8 collective-permute-start.24
  160.5 2.7 %collective-permute-done.18 = f32[48,1536]{1,0:T(8,128)S(1)} collective-permute-done((f32[48,1536]{1,0:T(8,128)S(1)}, f32[48,1536]{1,0:T(8,128)S(1)}, u32[]{:S(2)}, u32[]{:S(2)}) %collective-permute-start.18) | collective-permute-done | bytes 294944 | tf_op jit(solution)/shard_map/ppermute | solution.py:69
  164.8 2.6 %collective-permute-start.25 = (f32[31,1536]{1,0:T(8,128)S(1)}, f32[31,1536]{1,0:T(8,128)S(1)}, u32[]{:S(2)}, u32[]{:S(2)}) collective-permute-start(f32[31,1536]{1,0:T(8,128)S(1)} %add.805), channel_id=1, source_target_pairs={{0,2},{1,3},{2,0},{3,1},{4,6},{5,7},{6,4},{7,5},{8,10},{9,11},{10,... | collective-permute-start | bytes 571400 | tf_op jit(solution)/shard_map/ppermute | solution.py:34
  168.4 6.3 %collective-permute-done.25 = f32[31,1536]{1,0:T(8,128)S(1)} collective-permute-done((f32[31,1536]{1,0:T(8,128)S(1)}, f32[31,1536]{1,0:T(8,128)S(1)}, u32[]{:S(2)}, u32[]{:S(2)}) %collective-permute-start.25) | collective-permute-done | bytes 190496 | tf_op jit(solution)/shard_map/ppermute | solution.py:34
  175.4 1.6 collective-permute-done.19
  180.0 1.6 maximum_select_fusion
  (188 shorter events, 62.8 us)
Async XLA Ops:
  7.2 42.8 %copy-start = (bf16[384,1536]{1,0:T(8,128)(2,1)S(1)}, bf16[384,1536]{1,0:T(8,128)(2,1)}, u32[]{:S(2)}) copy-start(bf16[384,1536]{1,0:T(8,128)(2,1)} %param.10) | copy-start | bytes 3538948
  7.2 42.8 %all-gather.4.cloned.1.call-start = ((), (), s32[]{:S(2)}) async-start(), calls=%async_computation.2 | async-start | bytes 1966080 | tf_op jit(solution)/shard_map/all_gather | solution.py:99
  9.3 11.7 %collective-permute-start = (bf16[2,15,1536]{2,1,0:T(8,128)(2,1)S(1)}, bf16[2,15,1536]{2,1,0:T(8,128)(2,1)S(1)}, u32[]{:S(2)}, u32[]{:S(2)}) collective-permute-start(bf16[2,15,1536]{2,1,0:T(8,128)(2,1)S(1)} %get-tuple-element.99), channel_id=1, source_target_pairs={{0,1},{1,2},{2,3},{4,5},{5,6},{6,7},{8,9},{9,10},{10,11},{12,13},{... | collective-permute-start | bytes 276488 | tf_op jit(solution)/shard_map/ppermute | solution.py:16
  14.2 6.5 %collective-permute-start.1 = (bf16[2,15,1536]{2,1,0:T(8,128)(2,1)S(1)}, bf16[2,15,1536]{2,1,0:T(8,128)(2,1)S(1)}, u32[]{:S(2)}, u32[]{:S(2)}) collective-permute-start(bf16[2,15,1536]{2,1,0:T(8,128)(2,1)S(1)} %get-tuple-element.100), channel_id=1, source_target_pairs={{1,0},{2,1},{3,2},{5,4},{6,5},{7,6},{9,8},{10,9},{11,10},{13,12},{... | collective-permute-start | bytes 276488 | tf_op jit(solution)/shard_map/ppermute | solution.py:17
  21.5 21.9 %copy-start.22 = (f32[1536]{0:T(1024)S(1)}, f32[1536]{0:T(1024)}, u32[]{:S(2)}) copy-start(f32[1536]{0:T(1024)} %param.8) | copy-start | bytes 18436
  25.0 1.2 collective-permute-start.2
  26.3 3.8 %collective-permute-start.3 = (f32[2,1536]{1,0:T(2,128)S(1)}, f32[2,1536]{1,0:T(2,128)S(1)}, u32[]{:S(2)}, u32[]{:S(2)}) collective-permute-start(f32[2,1536]{1,0:T(2,128)S(1)} %pad_maximum_fusion.7), channel_id=1, source_target_pairs={{0,8},{4,12},{8,0},{12,4},{16,24},{20,28},{24,16},{28,20},{1,9},{5... | collective-permute-start | bytes 36872 | tf_op jit(solution)/shard_map/ppermute | solution.py:44
  30.2 3.8 %collective-permute-start.4 = (f32[2,1536]{1,0:T(2,128)S(1)}, f32[2,1536]{1,0:T(2,128)S(1)}, u32[]{:S(2)}, u32[]{:S(2)}) collective-permute-start(f32[2,1536]{1,0:T(2,128)S(1)} %pad_maximum_fusion.8), channel_id=1, source_target_pairs={{0,16},{4,20},{8,24},{12,28},{16,0},{20,4},{24,8},{28,12},{1,17},{... | collective-permute-start | bytes 36872 | tf_op jit(solution)/shard_map/ppermute | solution.py:44
  34.0 4.0 %collective-permute-start.5 = (f32[2,1536]{1,0:T(2,128)S(1)}, f32[2,1536]{1,0:T(2,128)S(1)}, u32[]{:S(2)}, u32[]{:S(2)}) collective-permute-start(f32[2,1536]{1,0:T(2,128)S(1)} %pad_maximum_fusion.9), channel_id=1, source_target_pairs={{0,1},{1,0},{2,3},{3,2},{4,5},{5,4},{6,7},{7,6},{8,9},{9,8},{10,11... | collective-permute-start | bytes 36872 | tf_op jit(solution)/shard_map/ppermute | solution.py:44
  38.0 5.3 %collective-permute-start.6 = (f32[2,1536]{1,0:T(2,128)S(1)}, f32[2,1536]{1,0:T(2,128)S(1)}, u32[]{:S(2)}, u32[]{:S(2)}) collective-permute-start(f32[2,1536]{1,0:T(2,128)S(1)} %pad_maximum_fusion.10), channel_id=1, source_target_pairs={{0,2},{1,3},{2,0},{3,1},{4,6},{5,7},{6,4},{7,5},{8,10},{9,11},{10,... | collective-permute-start | bytes 36872 | tf_op jit(solution)/shard_map/ppermute | solution.py:44
  79.8 4.6 %collective-permute-start.8 = (f32[2,1536]{1,0:T(2,128)}, f32[2,1536]{1,0:T(2,128)}, u32[]{:S(2)}, u32[]{:S(2)}) collective-permute-start(f32[2,1536]{1,0:T(2,128)} %pad_maximum_fusion.11), channel_id=1, source_target_pairs={{0,4},{4,0},{8,12},{12,8},{16,20},{20,16},{24,28},{28,24},{1,5},{5... | collective-permute-start | bytes 36872 | tf_op jit(solution)/shard_map/ppermute | solution.py:34
  80.8 24.6 %all-to-all-start.1 = ((bf16[128,4,384]{2,0,1:T(8,128)(2,1)}), bf16[128,4,384]{2,0,1:T(8,128)(2,1)S(1)}, u32[]{:S(2)}, u32[]{:S(2)}) async-start(bf16[128,4,384]{2,0,1:T(8,128)(2,1)} %copy.17), calls=%async_computation.1 | async-start | bytes 786432 | tf_op jit(solution)/shard_map/all_to_all | solution.py:144
  84.2 55.2 %all-gather.6.cloned.1.call-start = ((), (), s32[]{:S(2)}) async-start(), calls=%async_computation.3 | async-start | bytes 2949120 | tf_op jit(solution)/shard_map/all_gather | solution.py:81
  85.8 4.0 %collective-permute-start.9 = (f32[2,1536]{1,0:T(2,128)}, f32[2,1536]{1,0:T(2,128)}, u32[]{:S(2)}, u32[]{:S(2)}) collective-permute-start(f32[2,1536]{1,0:T(2,128)} %fusion.126), channel_id=1, source_target_pairs={{0,8},{4,12},{8,0},{12,4},{16,24},{20,28},{24,16},{28,20},{1,9},{5... | collective-permute-start | bytes 36872 | tf_op jit(solution)/shard_map/ppermute | solution.py:34
  90.6 3.8 %collective-permute-start.10 = (f32[2,1536]{1,0:T(2,128)S(1)}, f32[2,1536]{1,0:T(2,128)S(1)}, u32[]{:S(2)}, u32[]{:S(2)}) collective-permute-start(f32[2,1536]{1,0:T(2,128)S(1)} %fusion.142), channel_id=1, source_target_pairs={{0,16},{4,20},{8,24},{12,28},{16,0},{20,4},{24,8},{28,12},{1,17},{... | collective-permute-start | bytes 36872 | tf_op jit(solution)/shard_map/ppermute | solution.py:34
  94.4 3.8 %collective-permute-start.11 = (f32[2,1536]{1,0:T(2,128)S(1)}, f32[2,1536]{1,0:T(2,128)S(1)}, u32[]{:S(2)}, u32[]{:S(2)}) collective-permute-start(f32[2,1536]{1,0:T(2,128)S(1)} %add.761), channel_id=1, source_target_pairs={{0,1},{1,0},{2,3},{3,2},{4,5},{5,4},{6,7},{7,6},{8,9},{9,8},{10,11... | collective-permute-start | bytes 36872 | tf_op jit(solution)/shard_map/ppermute | solution.py:34
  98.7 5.3 %collective-permute-start.12 = (f32[2,1536]{1,0:T(2,128)}, f32[2,1536]{1,0:T(2,128)}, u32[]{:S(2)}, u32[]{:S(2)}) collective-permute-start(f32[2,1536]{1,0:T(2,128)} %add.762), channel_id=1, source_target_pairs={{0,2},{1,3},{2,0},{3,1},{4,6},{5,7},{6,4},{7,5},{8,10},{9,11},{10,... | collective-permute-start | bytes 36872 | tf_op jit(solution)/shard_map/ppermute | solution.py:34
  107.7 4.0 %collective-permute-start.15 = (f32[192,1536]{1,0:T(8,128)S(1)}, f32[192,1536]{1,0:T(8,128)S(1)}, u32[]{:S(2)}, u32[]{:S(2)}) collective-permute-start(f32[192,1536]{1,0:T(8,128)S(1)} %constant_dynamic-slice_fusion.2), channel_id=1, source_target_pairs={{0,4},{4,0},{8,12},{12,8},{16,20},{20,16},{24,28},{28,24},{1,5},{5... | collective-permute-start | bytes 3538952 | tf_op jit(solution)/shard_map/ppermute | solution.py:65
  113.7 28.3 %collective-permute-start.16 = (f32[96,1536]{1,0:T(8,128)}, f32[96,1536]{1,0:T(8,128)}, u32[]{:S(2)}, u32[]{:S(2)}) collective-permute-start(f32[96,1536]{1,0:T(8,128)} %constant_dynamic-slice_fusion.1), channel_id=1, source_target_pairs={{0,8},{4,12},{8,0},{12,4},{16,24},{20,28},{24,16},{28,20},{1,9},{5... | collective-permute-start | bytes 1769480 | tf_op jit(solution)/shard_map/ppermute | solution.py:65
  126.9 15.1 %copy-start.3 = (f32[192,1536]{1,0:T(8,128)S(1)}, f32[192,1536]{1,0:T(8,128)}, u32[]{:S(2)}) copy-start(f32[192,1536]{1,0:T(8,128)} %copy-done.2) | copy-start | bytes 3538948
  138.8 1.6 collective-permute-start.21
  139.4 37.7 %collective-permute-start.7 = (bf16[4,192,1536]{2,1,0:T(8,128)(2,1)}, bf16[4,192,1536]{2,1,0:T(8,128)(2,1)S(1)}, u32[]{:S(2)}, u32[]{:S(2)}) collective-permute-start(bf16[4,192,1536]{2,1,0:T(8,128)(2,1)} %bitcast.18), channel_id=1, source_target_pairs={{0,4},{4,0},{8,12},{12,8},{16,20},{20,16},{24,28},{28,24},{1,5},{5... | collective-permute-start | bytes 7077896 | tf_op jit(solution)/shard_map/ppermute | solution.py:82
  141.3 9.3 %collective-permute-start.22 = (f32[31,1536]{1,0:T(8,128)S(1)}, f32[31,1536]{1,0:T(8,128)S(1)}, u32[]{:S(2)}, u32[]{:S(2)}) collective-permute-start(f32[31,1536]{1,0:T(8,128)S(1)} %add.802), channel_id=1, source_target_pairs={{0,8},{4,12},{8,0},{12,4},{16,24},{20,28},{24,16},{28,20},{1,9},{5... | collective-permute-start | bytes 571400 | tf_op jit(solution)/shard_map/ppermute | solution.py:34
  143.2 9.2 %collective-permute-start.17 = (f32[48,1536]{1,0:T(8,128)S(1)}, f32[48,1536]{1,0:T(8,128)S(1)}, u32[]{:S(2)}, u32[]{:S(2)}) collective-permute-start(f32[48,1536]{1,0:T(8,128)S(1)} %constant_dynamic-slice_fusion), channel_id=1, source_target_pairs={{0,16},{4,20},{8,24},{12,28},{16,0},{20,4},{24,8},{28,12},{1,17},{... | collective-permute-start | bytes 884744 | tf_op jit(solution)/shard_map/ppermute | solution.py:65
  144.8 9.7 %collective-permute-start.13 = (bf16[2,15,1536]{2,1,0:T(8,128)(2,1)S(1)}, bf16[2,15,1536]{2,1,0:T(8,128)(2,1)S(1)}, u32[]{:S(2)}, u32[]{:S(2)}) collective-permute-start(bf16[2,15,1536]{2,1,0:T(8,128)(2,1)S(1)} %get-tuple-element.97), channel_id=1, source_target_pairs={{1,0},{2,1},{3,2},{5,4},{6,5},{7,6},{9,8},{10,9},{11,10},{13,12},{... | collective-permute-start | bytes 276488 | tf_op jit(solution)/shard_map/ppermute | solution.py:17
  146.1 8.4 %collective-permute-start.14 = (bf16[2,15,1536]{2,1,0:T(8,128)(2,1)S(1)}, bf16[2,15,1536]{2,1,0:T(8,128)(2,1)S(1)}, u32[]{:S(2)}, u32[]{:S(2)}) collective-permute-start(bf16[2,15,1536]{2,1,0:T(8,128)(2,1)S(1)} %get-tuple-element.98), channel_id=1, source_target_pairs={{0,1},{1,2},{2,3},{4,5},{5,6},{6,7},{8,9},{9,10},{10,11},{12,13},{... | collective-permute-start | bytes 276488 | tf_op jit(solution)/shard_map/ppermute | solution.py:16
  150.7 7.9 %collective-permute-start.23 = (f32[31,1536]{1,0:T(8,128)S(1)}, f32[31,1536]{1,0:T(8,128)S(1)}, u32[]{:S(2)}, u32[]{:S(2)}) collective-permute-start(f32[31,1536]{1,0:T(8,128)S(1)} %add.803), channel_id=1, source_target_pairs={{0,16},{4,20},{8,24},{12,28},{16,0},{20,4},{24,8},{28,12},{1,17},{... | collective-permute-start | bytes 571400 | tf_op jit(solution)/shard_map/ppermute | solution.py:34
  152.4 10.8 %collective-permute-start.18 = (f32[48,1536]{1,0:T(8,128)S(1)}, f32[48,1536]{1,0:T(8,128)S(1)}, u32[]{:S(2)}, u32[]{:S(2)}) collective-permute-start(f32[48,1536]{1,0:T(8,128)S(1)} %dynamic-slice_add_fusion.2), channel_id=1, source_target_pairs={{0,16},{4,20},{8,24},{12,28},{16,0},{20,4},{24,8},{28,12},{1,17},{... | collective-permute-start | bytes 884744 | tf_op jit(solution)/shard_map/ppermute | solution.py:69
  158.7 6.1 %collective-permute-start.24 = (f32[31,1536]{1,0:T(8,128)S(1)}, f32[31,1536]{1,0:T(8,128)S(1)}, u32[]{:S(2)}, u32[]{:S(2)}) collective-permute-start(f32[31,1536]{1,0:T(8,128)S(1)} %add.804), channel_id=1, source_target_pairs={{0,1},{1,0},{2,3},{3,2},{4,5},{5,4},{6,7},{7,6},{8,9},{9,8},{10,11... | collective-permute-start | bytes 571400 | tf_op jit(solution)/shard_map/ppermute | solution.py:34
  163.3 13.7 %collective-permute-start.19 = (f32[96,1536]{1,0:T(8,128)S(1)}, f32[96,1536]{1,0:T(8,128)S(1)}, u32[]{:S(2)}, u32[]{:S(2)}) collective-permute-start(f32[96,1536]{1,0:T(8,128)S(1)} %maximum_select_fusion.2), channel_id=1, source_target_pairs={{0,8},{4,12},{8,0},{12,4},{16,24},{20,28},{24,16},{28,20},{1,9},{5... | collective-permute-start | bytes 1769480 | tf_op jit(solution)/shard_map/ppermute | solution.py:69
  164.8 9.8 %collective-permute-start.25 = (f32[31,1536]{1,0:T(8,128)S(1)}, f32[31,1536]{1,0:T(8,128)S(1)}, u32[]{:S(2)}, u32[]{:S(2)}) collective-permute-start(f32[31,1536]{1,0:T(8,128)S(1)} %add.805), channel_id=1, source_target_pairs={{0,2},{1,3},{2,0},{3,1},{4,6},{5,7},{6,4},{7,5},{8,10},{9,11},{10,... | collective-permute-start | bytes 571400 | tf_op jit(solution)/shard_map/ppermute | solution.py:34
  177.1 2.9 %collective-permute-start.20 = (f32[192,1536]{1,0:T(8,128)S(1)}, f32[192,1536]{1,0:T(8,128)S(1)}, u32[]{:S(2)}, u32[]{:S(2)}) collective-permute-start(f32[192,1536]{1,0:T(8,128)S(1)} %maximum_select_fusion.1), channel_id=1, source_target_pairs={{0,4},{4,0},{8,12},{12,8},{16,20},{20,16},{24,28},{28,24},{1,5},{5... | collective-permute-start | bytes 3538952 | tf_op jit(solution)/shard_map/ppermute | solution.py:69
  (23 other events, 142.0 us)
Sparse Core Ops, SparseCore 0:
  9.6 40.3 all-gather.3
  88.3 51.0 all-gather.5

commit v16 on v10

--- a/solution.py
+++ b/solution.py
@@ -151,13 +151,12 @@
             for offset in range(taps)
         ]
     )
-    local_grad, kernel_terms = lax.optimization_barrier((local_grad, kernel_terms))
     weight_grad = rows_sum(local_grad, "dp")
     kernel_grad = all_sum(kernel_terms, ("dp", "tensor"))
-    full_weight, kernel_grad = gather_weight(proj_weight, kernel_grad)
     input_grad = jnp.concatenate(
         [grad_gated * gates, grad_gated * values * gates * (1.0 - gates)], axis=-1
     ).astype(jnp.bfloat16)
+    full_weight, kernel_grad = gather_weight(proj_weight, kernel_grad)
     conv_output = jnp.einsum(
         "btc,cd->btd", activated, full_weight, preferred_element_type=jnp.float32
     ).astype(jnp.bfloat16)

time: 219 us -> 204 us (0.932)
  waiting for transfers between devices: 89.6 us -> 76.9 us
    ppermute x10, waiting for transfers between devices: 52.4 us -> 41.1 us  [all_sum(): x = x + lax.ppermute(x, axis, [(i, i ^ step) for i in range(peers)])]
    unnamed x92 -> x94, local copies, waits for them, and re-layouts: 1.45 us -> 4.31 us
    ppermute x2, starting transfers between devices: 10.6 us -> 7.95 us  [extended(): before = lax.ppermute(last, axis, up)]
    another operation x32, local copies, waits for them, and re-layouts: 2.96 us -> 0.52 us  [on_device(): jnp.stack([jnp.sum(padded[:, offset:offset + frames, :].astype(jnp.float3...]
  transfers between devices with their start and end apart: 29 -> 29, of which waited for: 18 -> 18; matrix products, arithmetic and copies ran while one was open for 15% -> 16% of each run, Pallas kernels for 0% -> 0%
where the time goes in v16:
time: 204 us; the launch traced here: 202 us
  waiting for transfers between devices  76.9 us (38%)
  starting transfers between devices  40.8 us (20%)
  other arithmetic  28.1 us (14%)
  blocking collectives  22.7 us (11%)
  between operations  15.4 us (8%)
  local copies, waits for them, and re-layouts  11.5 us (6%)
  matrix products  6.22 us (3%)
    ppermute x10, waiting for transfers between devices, all_sum(): x = x + lax.ppermute(x, axis, [(i, i ^ step) for i in range(peers)])  41.1 us
    all_to_all x1, blocking collectives, on_device(): lax.all_to_all(own_columns, 'tensor', split_axis=0, concat_axis=1, tiled=...  22.7 us
    all_gather x1, waiting for transfers between devices, on_device(): group_grad = lax.all_gather(flat_grad, 'tensor', axis=0, tiled=True)  12.2 us
    ppermute x3, waiting for transfers between devices, rows_sum(): other = lax.ppermute(x, axis, [(i, i ^ step) for i in range(peers)])  10.8 us
    ppermute x10, starting transfers between devices, all_sum(): x = x + lax.ppermute(x, axis, [(i, i ^ step) for i in range(peers)])  10.6 us
    ppermute x5, starting transfers between devices, all_moments(): lax.ppermute(jnp.stack([mean, spread]), axis, [(i, i ^ step) for i in ran...  9.76 us
    ppermute x5, waiting for transfers between devices, all_moments(): lax.ppermute(jnp.stack([mean, spread]), axis, [(i, i ^ step) for i in ran...  9.19 us
    ppermute x2, starting transfers between devices, extended(): before = lax.ppermute(last, axis, up)  7.95 us
  transfers between devices with their start and end apart: 29, of which 18 were waited for; matrix products, arithmetic and copies ran while one was open for 16% of the time, Pallas kernels for 0%

profile of v16, /device:TPU:0, one launch (start us, length us, event | category | flops | bytes accessed | tf_op | source)
XLA Modules:
  0.0 201.6 jit_solution(8356097516181955668)
XLA Ops:
  10.0 5.6 %collective-permute-start = (bf16[2,15,1536]{2,1,0:T(8,128)(2,1)S(1)}, bf16[2,15,1536]{2,1,0:T(8,128)(2,1)S(1)}, u32[]{:S(2)}, u32[]{:S(2)}) collective-permute-start(bf16[2,15,1536]{2,1,0:T(8,128)(2,1)S(1)} %get-tuple-element.103), channel_id=1, source_target_pairs={{0,1},{1,2},{2,3},{4,5},{5,6},{6,7},{8,9},{9,10},{10,11},{12,13},{... | collective-permute-start | bytes 276488 | tf_op jit(solution)/shard_map/ppermute | solution.py:16
  17.8 3.8 %fusion.143 = (f32[1536]{0:T(1024)S(1)}, f32[2,64,1536]{2,1,0:T(8,128)S(1)}) fusion(bf16[2,15,1536]{2,1,0:T(8,128)(2,1)S(1)} %collective-permute-done.1, bf16[2,64,1536]{2,1,0:T(8,128)(2,1)S(1)} %fusion, f32[1536]{0:T(1024)S(1)} %get-tuple-element.76, f32[1536]{0:T(1024)S(1)} %get-tuple-element.77, f32[1536]{0:T(1024)S(1)} %get-tuple-element.48, ...), kind=kLoop, calls=%fused_computation.380 | loop fusion | flops 35977728 | bytes 1560576 | tf_op jit(solution)/shard_map/reduce_sum | solution.py:108
  23.1 2.0 collective-permute-start.3
  25.1 1.8 collective-permute-done.3
  27.0 2.0 %collective-permute-start.4 = (f32[2,1536]{1,0:T(2,128)S(1)}, f32[2,1536]{1,0:T(2,128)S(1)}, u32[]{:S(2)}, u32[]{:S(2)}) collective-permute-start(f32[2,1536]{1,0:T(2,128)S(1)} %pad_maximum_fusion.8), channel_id=1, source_target_pairs={{0,16},{4,20},{8,24},{12,28},{16,0},{20,4},{24,8},{28,12},{1,17},{... | collective-permute-start | bytes 36872 | tf_op jit(solution)/shard_map/ppermute | solution.py:44
  29.0 1.7 collective-permute-done.4
  30.8 2.5 %collective-permute-start.5 = (f32[2,1536]{1,0:T(2,128)S(1)}, f32[2,1536]{1,0:T(2,128)S(1)}, u32[]{:S(2)}, u32[]{:S(2)}) collective-permute-start(f32[2,1536]{1,0:T(2,128)S(1)} %pad_maximum_fusion.9), channel_id=1, source_target_pairs={{0,1},{1,0},{2,3},{3,2},{4,5},{5,4},{6,7},{7,6},{8,9},{9,8},{10,11... | collective-permute-start | bytes 36872 | tf_op jit(solution)/shard_map/ppermute | solution.py:44
  33.3 2.2 %collective-permute-done.5 = f32[2,1536]{1,0:T(2,128)S(1)} collective-permute-done((f32[2,1536]{1,0:T(2,128)S(1)}, f32[2,1536]{1,0:T(2,128)S(1)}, u32[]{:S(2)}, u32[]{:S(2)}) %collective-permute-start.5) | collective-permute-done | bytes 12320 | tf_op jit(solution)/shard_map/ppermute | solution.py:44
  35.6 3.2 %collective-permute-start.6 = (f32[2,1536]{1,0:T(2,128)S(1)}, f32[2,1536]{1,0:T(2,128)S(1)}, u32[]{:S(2)}, u32[]{:S(2)}) collective-permute-start(f32[2,1536]{1,0:T(2,128)S(1)} %pad_maximum_fusion.10), channel_id=1, source_target_pairs={{0,2},{1,3},{2,0},{3,1},{4,6},{5,7},{6,4},{7,5},{8,10},{9,11},{10,... | collective-permute-start | bytes 36872 | tf_op jit(solution)/shard_map/ppermute | solution.py:44
  38.8 2.3 %collective-permute-done.6 = f32[2,1536]{1,0:T(2,128)S(1)} collective-permute-done((f32[2,1536]{1,0:T(2,128)S(1)}, f32[2,1536]{1,0:T(2,128)S(1)}, u32[]{:S(2)}, u32[]{:S(2)}) %collective-permute-start.6) | collective-permute-done | bytes 12320 | tf_op jit(solution)/shard_map/ppermute | solution.py:44
  41.9 12.2 %all-gather.4.cloned.1.call-done = bf16[512,1536]{1,0:T(8,128)(2,1)} async-done(((bf16[128,1536]{1,0:T(8,128)(2,1)}), bf16[512,1536]{1,0:T(8,128)(2,1)}) %all-gather.4.cloned.1.call-update) | async-done | bytes 1572880 | tf_op jit(solution)/shard_map/all_gather | solution.py:100
  54.1 2.4 %fusion.147 = f32[512,384]{1,0:T(8,128)S(1)} fusion(bf16[512,1536]{1,0:T(8,128)(2,1)} %all-gather.4.cloned.1.call-done, bf16[384,1536]{1,0:T(8,128)(2,1)S(1)} %copy-done), kind=kOutput, calls=%fused_computation.383 | convolution fusion | flops 603979776 | bytes 3538944 | tf_op jit(solution)/shard_map/fd,cd->fc/dot_general | solution.py:119
  56.6 22.7 %all_to_all.35 = f32[4,128,384]{2,1,0:T(8,128)S(1)} all-to-all(f32[4,128,384]{2,1,0:T(8,128)S(1)} %bitcast.21), channel_id=1, replica_groups=mesh['dp'=8,'tensor'=4] {'tensor'}, dimensions={0} | all-to-all | bytes 1572864 | tf_op jit(solution)/shard_map/all_to_all | solution.py:120
  81.0 2.5 %fusion.140 = (f32[1536]{0:T(1024)S(1)}, f32[1536]{0:T(1024)S(1)}, f32[2,64,1536]{2,1,0:T(8,128)}, bf16[2,64,1536]{2,1,0:T(8,128)(2,1)S(1)}) fusion(f32[1536]{0:T(1024)} %get-tuple-element.94, f32[2,64,1536]{2,1,0:T(8,128)S(1)} %get-tuple-element.97, f32[1536]{0:T(1024)} %get-tuple-element.10, f32[2,64,1536]{2,1,0:T(8,128)} %reshape.188, f32[1536]{0:T(1024)} %param.9, ...), kind=kLoop, calls=%fused_computation.378 | loop fusion | flops 3142656 | bytes 2789376 | tf_op jit(solution)/shard_map/reduce_sum | solution.py:132
  86.3 2.2 %collective-permute-done.8 = f32[2,1536]{1,0:T(2,128)S(1)} collective-permute-done((f32[2,1536]{1,0:T(2,128)S(1)}, f32[2,1536]{1,0:T(2,128)S(1)}, u32[]{:S(2)}, u32[]{:S(2)}) %collective-permute-start.8) | collective-permute-done | bytes 12320 | tf_op jit(solution)/shard_map/ppermute | solution.py:34
  90.1 2.2 %collective-permute-done.9 = f32[2,1536]{1,0:T(2,128)S(1)} collective-permute-done((f32[2,1536]{1,0:T(2,128)S(1)}, f32[2,1536]{1,0:T(2,128)S(1)}, u32[]{:S(2)}, u32[]{:S(2)}) %collective-permute-start.9) | collective-permute-done | bytes 12320 | tf_op jit(solution)/shard_map/ppermute | solution.py:34
  93.5 3.5 %all-to-all-start.1 = ((bf16[128,4,384]{2,0,1:T(8,128)(2,1)}), bf16[128,4,384]{2,0,1:T(8,128)(2,1)S(1)}, u32[]{:S(2)}, u32[]{:S(2)}) async-start(bf16[128,4,384]{2,0,1:T(8,128)(2,1)} %copy.17), calls=%async_computation.1 | async-start | bytes 786432 | tf_op jit(solution)/shard_map/all_to_all | solution.py:129
  97.3 2.7 %collective-permute-start.11 = (f32[2,1536]{1,0:T(2,128)S(1)}, f32[2,1536]{1,0:T(2,128)S(1)}, u32[]{:S(2)}, u32[]{:S(2)}) collective-permute-start(f32[2,1536]{1,0:T(2,128)S(1)} %add.497), channel_id=1, source_target_pairs={{0,2},{1,3},{2,0},{3,1},{4,6},{5,7},{6,4},{7,5},{8,10},{9,11},{10,... | collective-permute-start | bytes 36872 | tf_op jit(solution)/shard_map/ppermute | solution.py:34
  100.9 6.4 %collective-permute-done.11 = f32[2,1536]{1,0:T(2,128)S(1)} collective-permute-done((f32[2,1536]{1,0:T(2,128)S(1)}, f32[2,1536]{1,0:T(2,128)S(1)}, u32[]{:S(2)}, u32[]{:S(2)}) %collective-permute-start.11) | collective-permute-done | bytes 12320 | tf_op jit(solution)/shard_map/ppermute | solution.py:34
  107.9 2.3 %fusion.148 = f32[384,1536]{1,0:T(8,128)S(1)} fusion(bf16[512,384]{1,0:T(8,128)(2,1)S(1)} %bitcast.20, bf16[512,1536]{1,0:T(8,128)(2,1)} %all-gather.4.cloned.1.call-done), kind=kOutput, calls=%fused_computation.384 | convolution fusion | flops 603979776 | bytes 4325376 | tf_op jit(solution)/shard_map/fc,fd->cd/dot_general | solution.py:130
  118.5 1.8 dynamic-slice_add_fusion
  121.4 1.6 collective-permute-start.21
  123.6 17.7 %collective-permute-done.13 = f32[31,1536]{1,0:T(8,128)S(1)} collective-permute-done((f32[31,1536]{1,0:T(8,128)S(1)}, f32[31,1536]{1,0:T(8,128)S(1)}, u32[]{:S(2)}, u32[]{:S(2)}) %collective-permute-start.13) | collective-permute-done | bytes 190496 | tf_op jit(solution)/shard_map/ppermute | solution.py:34
  141.3 1.6 collective-permute-start.14
  142.9 4.9 %collective-permute-done.14 = f32[31,1536]{1,0:T(8,128)S(1)} collective-permute-done((f32[31,1536]{1,0:T(8,128)S(1)}, f32[31,1536]{1,0:T(8,128)S(1)}, u32[]{:S(2)}, u32[]{:S(2)}) %collective-permute-start.14) | collective-permute-done | bytes 190496 | tf_op jit(solution)/shard_map/ppermute | solution.py:34
  147.9 6.5 %collective-permute-done.15 = f32[31,1536]{1,0:T(8,128)S(1)} collective-permute-done((f32[31,1536]{1,0:T(8,128)S(1)}, f32[31,1536]{1,0:T(8,128)S(1)}, u32[]{:S(2)}, u32[]{:S(2)}) %collective-permute-start.15) | collective-permute-done | bytes 190496 | tf_op jit(solution)/shard_map/ppermute | solution.py:34
  154.4 2.0 collective-permute-start.16
  161.4 2.4 %collective-permute-start.19 = (bf16[2,15,1536]{2,1,0:T(8,128)(2,1)}, bf16[2,15,1536]{2,1,0:T(8,128)(2,1)S(1)}, u32[]{:S(2)}, u32[]{:S(2)}) collective-permute-start(bf16[2,15,1536]{2,1,0:T(8,128)(2,1)} %get-tuple-element.102), channel_id=1, source_target_pairs={{0,1},{1,2},{2,3},{4,5},{5,6},{6,7},{8,9},{9,10},{10,11},{12,13},{... | collective-permute-start | bytes 276488 | tf_op jit(solution)/shard_map/ppermute | solution.py:16
  165.8 1.8 collective-permute-done.22
  170.6 6.4 %multiply_convert_fusion = (bf16[2,64,1536]{2,1,0:T(8,128)(2,1)S(1)}, f32[2,64,1536]{2,1,0:T(8,128)S(1)}) fusion(bf16[2,64,3072]{2,1,0:T(8,128)(2,1)S(1)} %copy-done.2, bf16[2,64,1536]{2,1,0:T(8,128)(2,1)S(1)} %get-tuple-element.92, bf16[2,15,1536]{2,1,0:T(8,128)(2,1)S(1)} %collective-permute-done.19, f32[1536]{0:T(1024)} %copy-done.41, ...), kind=kLoop, calls=%fused_computation.210 | loop fusion | flops 36962304 | bytes 2340864 | tf_op jit(solution)/shard_map/convert
  179.9 10.2 %collective-permute-done.24 = f32[96,1536]{1,0:T(8,128)S(1)} collective-permute-done((f32[96,1536]{1,0:T(8,128)S(1)}, f32[96,1536]{1,0:T(8,128)S(1)}, u32[]{:S(2)}, u32[]{:S(2)}) %collective-permute-start.24) | collective-permute-done | bytes 589856 | tf_op jit(solution)/shard_map/ppermute | solution.py:69
  193.1 1.6 maximum_select_fusion
  (218 shorter events, 41.7 us)
Async XLA Ops:
  7.2 46.9 %copy-start = (bf16[384,1536]{1,0:T(8,128)(2,1)S(1)}, bf16[384,1536]{1,0:T(8,128)(2,1)}, u32[]{:S(2)}) copy-start(bf16[384,1536]{1,0:T(8,128)(2,1)} %param.10) | copy-start | bytes 3538948
  7.2 46.9 %all-gather.4.cloned.1.call-start = ((), (), s32[]{:S(2)}) async-start(), calls=%async_computation.2 | async-start | bytes 1966080 | tf_op jit(solution)/shard_map/all_gather | solution.py:100
  8.7 7.7 %collective-permute-start.1 = (bf16[2,15,1536]{2,1,0:T(8,128)(2,1)S(1)}, bf16[2,15,1536]{2,1,0:T(8,128)(2,1)S(1)}, u32[]{:S(2)}, u32[]{:S(2)}) collective-permute-start(bf16[2,15,1536]{2,1,0:T(8,128)(2,1)S(1)} %get-tuple-element.104), channel_id=1, source_target_pairs={{1,0},{2,1},{3,2},{5,4},{6,5},{7,6},{9,8},{10,9},{11,10},{13,12},{... | collective-permute-start | bytes 276488 | tf_op jit(solution)/shard_map/ppermute | solution.py:17
  10.0 7.8 %collective-permute-start = (bf16[2,15,1536]{2,1,0:T(8,128)(2,1)S(1)}, bf16[2,15,1536]{2,1,0:T(8,128)(2,1)S(1)}, u32[]{:S(2)}, u32[]{:S(2)}) collective-permute-start(bf16[2,15,1536]{2,1,0:T(8,128)(2,1)S(1)} %get-tuple-element.103), channel_id=1, source_target_pairs={{0,1},{1,2},{2,3},{4,5},{5,6},{6,7},{8,9},{9,10},{10,11},{12,13},{... | collective-permute-start | bytes 276488 | tf_op jit(solution)/shard_map/ppermute | solution.py:16
  16.3 40.1 %copy-start.31 = (f32[1536]{0:T(1024)}, f32[1536]{0:T(1024)S(1)}, u32[]{:S(2)}) copy-start(f32[1536]{0:T(1024)S(1)} %get-tuple-element.66) | copy-start | bytes 18436
  16.4 40.1 %copy-start.32 = (f32[1536]{0:T(1024)}, f32[1536]{0:T(1024)S(1)}, u32[]{:S(2)}) copy-start(f32[1536]{0:T(1024)S(1)} %get-tuple-element.67) | copy-start | bytes 18436
  21.8 1.2 collective-permute-start.2
  23.1 3.8 %collective-permute-start.3 = (f32[2,1536]{1,0:T(2,128)S(1)}, f32[2,1536]{1,0:T(2,128)S(1)}, u32[]{:S(2)}, u32[]{:S(2)}) collective-permute-start(f32[2,1536]{1,0:T(2,128)S(1)} %pad_maximum_fusion.7), channel_id=1, source_target_pairs={{0,8},{4,12},{8,0},{12,4},{16,24},{20,28},{24,16},{28,20},{1,9},{5... | collective-permute-start | bytes 36872 | tf_op jit(solution)/shard_map/ppermute | solution.py:44
  27.0 3.8 %collective-permute-start.4 = (f32[2,1536]{1,0:T(2,128)S(1)}, f32[2,1536]{1,0:T(2,128)S(1)}, u32[]{:S(2)}, u32[]{:S(2)}) collective-permute-start(f32[2,1536]{1,0:T(2,128)S(1)} %pad_maximum_fusion.8), channel_id=1, source_target_pairs={{0,16},{4,20},{8,24},{12,28},{16,0},{20,4},{24,8},{28,12},{1,17},{... | collective-permute-start | bytes 36872 | tf_op jit(solution)/shard_map/ppermute | solution.py:44
  30.8 4.7 %collective-permute-start.5 = (f32[2,1536]{1,0:T(2,128)S(1)}, f32[2,1536]{1,0:T(2,128)S(1)}, u32[]{:S(2)}, u32[]{:S(2)}) collective-permute-start(f32[2,1536]{1,0:T(2,128)S(1)} %pad_maximum_fusion.9), channel_id=1, source_target_pairs={{0,1},{1,0},{2,3},{3,2},{4,5},{5,4},{6,7},{7,6},{8,9},{9,8},{10,11... | collective-permute-start | bytes 36872 | tf_op jit(solution)/shard_map/ppermute | solution.py:44
  35.6 5.5 %collective-permute-start.6 = (f32[2,1536]{1,0:T(2,128)S(1)}, f32[2,1536]{1,0:T(2,128)S(1)}, u32[]{:S(2)}, u32[]{:S(2)}) collective-permute-start(f32[2,1536]{1,0:T(2,128)S(1)} %pad_maximum_fusion.10), channel_id=1, source_target_pairs={{0,2},{1,3},{2,0},{3,1},{4,6},{5,7},{6,4},{7,5},{8,10},{9,11},{10,... | collective-permute-start | bytes 36872 | tf_op jit(solution)/shard_map/ppermute | solution.py:44
  83.5 1.2 collective-permute-start.7
  84.8 3.8 %collective-permute-start.8 = (f32[2,1536]{1,0:T(2,128)S(1)}, f32[2,1536]{1,0:T(2,128)S(1)}, u32[]{:S(2)}, u32[]{:S(2)}) collective-permute-start(f32[2,1536]{1,0:T(2,128)S(1)} %fusion.139), channel_id=1, source_target_pairs={{0,8},{4,12},{8,0},{12,4},{16,24},{20,28},{24,16},{28,20},{1,9},{5... | collective-permute-start | bytes 36872 | tf_op jit(solution)/shard_map/ppermute | solution.py:34
  88.6 3.8 %collective-permute-start.9 = (f32[2,1536]{1,0:T(2,128)S(1)}, f32[2,1536]{1,0:T(2,128)S(1)}, u32[]{:S(2)}, u32[]{:S(2)}) collective-permute-start(f32[2,1536]{1,0:T(2,128)S(1)} %fusion.155), channel_id=1, source_target_pairs={{0,16},{4,20},{8,24},{12,28},{16,0},{20,4},{24,8},{28,12},{1,17},{... | collective-permute-start | bytes 36872 | tf_op jit(solution)/shard_map/ppermute | solution.py:34
  92.4 4.9 %collective-permute-start.10 = (f32[2,1536]{1,0:T(2,128)S(1)}, f32[2,1536]{1,0:T(2,128)S(1)}, u32[]{:S(2)}, u32[]{:S(2)}) collective-permute-start(f32[2,1536]{1,0:T(2,128)S(1)} %add.496), channel_id=1, source_target_pairs={{0,1},{1,0},{2,3},{3,2},{4,5},{5,4},{6,7},{7,6},{8,9},{9,8},{10,11... | collective-permute-start | bytes 36872 | tf_op jit(solution)/shard_map/ppermute | solution.py:34
  93.5 13.8 %all-to-all-start.1 = ((bf16[128,4,384]{2,0,1:T(8,128)(2,1)}), bf16[128,4,384]{2,0,1:T(8,128)(2,1)S(1)}, u32[]{:S(2)}, u32[]{:S(2)}) async-start(bf16[128,4,384]{2,0,1:T(8,128)(2,1)} %copy.17), calls=%async_computation.1 | async-start | bytes 786432 | tf_op jit(solution)/shard_map/all_to_all | solution.py:129
  97.0 68.8 %all-gather.6.cloned.1.call-start = ((), (), s32[]{:S(2)}) async-start(), calls=%async_computation.3 | async-start | bytes 2949120 | tf_op jit(solution)/shard_map/all_gather | solution.py:81
  97.3 10.0 %collective-permute-start.11 = (f32[2,1536]{1,0:T(2,128)S(1)}, f32[2,1536]{1,0:T(2,128)S(1)}, u32[]{:S(2)}, u32[]{:S(2)}) collective-permute-start(f32[2,1536]{1,0:T(2,128)S(1)} %add.497), channel_id=1, source_target_pairs={{0,2},{1,3},{2,0},{3,1},{4,6},{5,7},{6,4},{7,5},{8,10},{9,11},{10,... | collective-permute-start | bytes 36872 | tf_op jit(solution)/shard_map/ppermute | solution.py:34
  112.8 5.8 %collective-permute-start.20 = (f32[192,1536]{1,0:T(8,128)}, f32[192,1536]{1,0:T(8,128)}, u32[]{:S(2)}, u32[]{:S(2)}) collective-permute-start(f32[192,1536]{1,0:T(8,128)} %constant_dynamic-slice_fusion.2), channel_id=1, source_target_pairs={{0,4},{4,0},{8,12},{12,8},{16,20},{20,16},{24,28},{28,24},{1,5},{5... | collective-permute-start | bytes 3538952 | tf_op jit(solution)/shard_map/ppermute | solution.py:65
  118.3 4.7 %collective-permute-start.12 = (f32[31,1536]{1,0:T(8,128)S(1)}, f32[31,1536]{1,0:T(8,128)S(1)}, u32[]{:S(2)}, u32[]{:S(2)}) collective-permute-start(f32[31,1536]{1,0:T(8,128)S(1)} %stack.172), channel_id=1, source_target_pairs={{0,4},{4,0},{8,12},{12,8},{16,20},{20,16},{24,28},{28,24},{1,5},{5... | collective-permute-start | bytes 571400 | tf_op jit(solution)/shard_map/ppermute | solution.py:34
  121.4 35.0 %collective-permute-start.21 = (f32[96,1536]{1,0:T(8,128)S(1)}, f32[96,1536]{1,0:T(8,128)}, u32[]{:S(2)}, u32[]{:S(2)}) collective-permute-start(f32[96,1536]{1,0:T(8,128)S(1)} %constant_dynamic-slice_fusion.1), channel_id=1, source_target_pairs={{0,8},{4,12},{8,0},{12,4},{16,24},{20,28},{24,16},{28,20},{1,9},{5... | collective-permute-start | bytes 1769480 | tf_op jit(solution)/shard_map/ppermute | solution.py:65
  123.0 18.2 %collective-permute-start.13 = (f32[31,1536]{1,0:T(8,128)S(1)}, f32[31,1536]{1,0:T(8,128)S(1)}, u32[]{:S(2)}, u32[]{:S(2)}) collective-permute-start(f32[31,1536]{1,0:T(8,128)S(1)} %add.499), channel_id=1, source_target_pairs={{0,8},{4,12},{8,0},{12,4},{16,24},{20,28},{24,16},{28,20},{1,9},{5... | collective-permute-start | bytes 571400 | tf_op jit(solution)/shard_map/ppermute | solution.py:34
  141.3 6.5 %collective-permute-start.14 = (f32[31,1536]{1,0:T(8,128)S(1)}, f32[31,1536]{1,0:T(8,128)S(1)}, u32[]{:S(2)}, u32[]{:S(2)}) collective-permute-start(f32[31,1536]{1,0:T(8,128)S(1)} %add.500), channel_id=1, source_target_pairs={{0,16},{4,20},{8,24},{12,28},{16,0},{20,4},{24,8},{28,12},{1,17},{... | collective-permute-start | bytes 571400 | tf_op jit(solution)/shard_map/ppermute | solution.py:34
  147.8 6.6 %collective-permute-start.15 = (f32[31,1536]{1,0:T(8,128)S(1)}, f32[31,1536]{1,0:T(8,128)S(1)}, u32[]{:S(2)}, u32[]{:S(2)}) collective-permute-start(f32[31,1536]{1,0:T(8,128)S(1)} %add.501), channel_id=1, source_target_pairs={{0,1},{1,0},{2,3},{3,2},{4,5},{5,4},{6,7},{7,6},{8,9},{9,8},{10,11... | collective-permute-start | bytes 571400 | tf_op jit(solution)/shard_map/ppermute | solution.py:34
  154.4 10.7 %collective-permute-start.16 = (f32[31,1536]{1,0:T(8,128)S(1)}, f32[31,1536]{1,0:T(8,128)S(1)}, u32[]{:S(2)}, u32[]{:S(2)}) collective-permute-start(f32[31,1536]{1,0:T(8,128)S(1)} %add.502), channel_id=1, source_target_pairs={{0,2},{1,3},{2,0},{3,1},{4,6},{5,7},{6,4},{7,5},{8,10},{9,11},{10,... | collective-permute-start | bytes 571400 | tf_op jit(solution)/shard_map/ppermute | solution.py:34
  159.3 8.4 %collective-permute-start.22 = (f32[48,1536]{1,0:T(8,128)}, f32[48,1536]{1,0:T(8,128)S(1)}, u32[]{:S(2)}, u32[]{:S(2)}) collective-permute-start(f32[48,1536]{1,0:T(8,128)} %constant_dynamic-slice_fusion), channel_id=1, source_target_pairs={{0,16},{4,20},{8,24},{12,28},{16,0},{20,4},{24,8},{28,12},{1,17},{... | collective-permute-start | bytes 884744 | tf_op jit(solution)/shard_map/ppermute | solution.py:65
  161.4 8.8 %collective-permute-start.19 = (bf16[2,15,1536]{2,1,0:T(8,128)(2,1)}, bf16[2,15,1536]{2,1,0:T(8,128)(2,1)S(1)}, u32[]{:S(2)}, u32[]{:S(2)}) collective-permute-start(bf16[2,15,1536]{2,1,0:T(8,128)(2,1)} %get-tuple-element.102), channel_id=1, source_target_pairs={{0,1},{1,2},{2,3},{4,5},{5,6},{6,7},{8,9},{9,10},{10,11},{12,13},{... | collective-permute-start | bytes 276488 | tf_op jit(solution)/shard_map/ppermute | solution.py:16
  163.8 6.8 %collective-permute-start.18 = (bf16[2,15,1536]{2,1,0:T(8,128)(2,1)}, bf16[2,15,1536]{2,1,0:T(8,128)(2,1)}, u32[]{:S(2)}, u32[]{:S(2)}) collective-permute-start(bf16[2,15,1536]{2,1,0:T(8,128)(2,1)} %get-tuple-element.101), channel_id=1, source_target_pairs={{1,0},{2,1},{3,2},{5,4},{6,5},{7,6},{9,8},{10,9},{11,10},{13,12},{... | collective-permute-start | bytes 276488 | tf_op jit(solution)/shard_map/ppermute | solution.py:17
  165.8 24.4 %collective-permute-start.17 = (bf16[4,192,1536]{2,1,0:T(8,128)(2,1)}, bf16[4,192,1536]{2,1,0:T(8,128)(2,1)S(1)}, u32[]{:S(2)}, u32[]{:S(2)}) collective-permute-start(bf16[4,192,1536]{2,1,0:T(8,128)(2,1)} %bitcast.18), channel_id=1, source_target_pairs={{0,4},{4,0},{8,12},{12,8},{16,20},{20,16},{24,28},{28,24},{1,5},{5... | collective-permute-start | bytes 7077896 | tf_op jit(solution)/shard_map/ppermute | solution.py:83
  168.7 8.4 %collective-permute-start.23 = (f32[48,1536]{1,0:T(8,128)S(1)}, f32[48,1536]{1,0:T(8,128)S(1)}, u32[]{:S(2)}, u32[]{:S(2)}) collective-permute-start(f32[48,1536]{1,0:T(8,128)S(1)} %dynamic-slice_add_fusion.2), channel_id=1, source_target_pairs={{0,16},{4,20},{8,24},{12,28},{16,0},{20,4},{24,8},{28,12},{1,17},{... | collective-permute-start | bytes 884744 | tf_op jit(solution)/shard_map/ppermute | solution.py:69
  177.1 13.0 %collective-permute-start.24 = (f32[96,1536]{1,0:T(8,128)S(1)}, f32[96,1536]{1,0:T(8,128)S(1)}, u32[]{:S(2)}, u32[]{:S(2)}) collective-permute-start(f32[96,1536]{1,0:T(8,128)S(1)} %maximum_select_fusion.2), channel_id=1, source_target_pairs={{0,8},{4,12},{8,0},{12,4},{16,24},{20,28},{24,16},{28,20},{1,9},{5... | collective-permute-start | bytes 1769480 | tf_op jit(solution)/shard_map/ppermute | solution.py:69
  190.2 2.9 %collective-permute-start.25 = (f32[192,1536]{1,0:T(8,128)S(1)}, f32[192,1536]{1,0:T(8,128)S(1)}, u32[]{:S(2)}, u32[]{:S(2)}) collective-permute-start(f32[192,1536]{1,0:T(8,128)S(1)} %maximum_select_fusion.1), channel_id=1, source_target_pairs={{0,4},{4,0},{8,12},{12,8},{16,20},{20,16},{24,28},{28,24},{1,5},{5... | collective-permute-start | bytes 3538952 | tf_op jit(solution)/shard_map/ppermute | solution.py:69
  (44 other events, 993.0 us)
Sparse Core Ops, SparseCore 0:
  15.8 38.2 all-gather.3
  101.0 50.2 all-gather.5

commit v17 on v16

--- a/solution.py
+++ b/solution.py
@@ -131,6 +131,7 @@
     grad_affine = grad_act * (sig_affine + affine * sig_affine * (1.0 - sig_affine))
     sums = jnp.stack([jnp.sum(grad_affine, axis=(0, 1)), jnp.sum(grad_affine * normed, axis=(0, 1))])
     sums = all_sum(sums, ("dp", "tensor"))
+    full_weight, sums = gather_weight(proj_weight, sums)
     shift_grad, scale_grad = sums[0], sums[1]
     grad_conv = (
         norm_scale
@@ -156,7 +157,6 @@
     input_grad = jnp.concatenate(
         [grad_gated * gates, grad_gated * values * gates * (1.0 - gates)], axis=-1
     ).astype(jnp.bfloat16)
-    full_weight, kernel_grad = gather_weight(proj_weight, kernel_grad)
     conv_output = jnp.einsum(
         "btc,cd->btd", activated, full_weight, preferred_element_type=jnp.float32
     ).astype(jnp.bfloat16)

time: 204 us -> 196 us (0.961); the launches traced: 202 us -> 196 us
  waiting for transfers between devices: 76.9 us -> 53.1 us
  blocking collectives: 22.7 us -> 41.1 us
  other arithmetic: 28.1 us -> 22.2 us
  local copies, waits for them, and re-layouts: 11.5 us -> 14.6 us
  starting transfers between devices: 40.8 us -> 43 us
    ppermute x10, waiting for transfers between devices: 41.1 us -> 21.9 us  [all_sum(): x = x + lax.ppermute(x, axis, [(i, i ^ step) for i in range(peers)])]
    all_to_all x1, blocking collectives: 22.7 us -> 41.1 us  [on_device(): lax.all_to_all(own_columns, 'tensor', split_axis=0, concat_axis=1, tiled=...]
    another operation x32, local copies, waits for them, and re-layouts: 0.52 us -> 7.36 us  [on_device(): jnp.stack([jnp.sum(padded[:, offset:offset + frames, :].astype(jnp.float3...]
    all_gather x1, waiting for transfers between devices: 12.2 us -> 6.52 us  [on_device(): group_grad = lax.all_gather(flat_grad, 'tensor', axis=0, tiled=True)]
    ppermute x3, waiting for transfers between devices: 10.8 us -> 6.15 us  [rows_sum(): other = lax.ppermute(x, axis, [(i, i ^ step) for i in range(peers)])]
    ppermute x2, waiting for transfers between devices: 0.45 us -> 4.32 us  [extended(): after = lax.ppermute(leading, axis, down)]
    add x3, other arithmetic: 4.06 us -> 1.31 us  [rows_sum(): x = keep + lax.ppermute(give, axis, [(i, i ^ step) for i in range(peers)])]
    ppermute x5, starting transfers between devices: 9.76 us -> 7.39 us  [all_moments(): lax.ppermute(jnp.stack([mean, spread]), axis, [(i, i ^ step) for i in ran...]
  transfers between devices with their start and end apart: 29 -> 29, of which waited for: 18 -> 20; matrix products, arithmetic and copies ran while one was open for 16% -> 18% of each run, Pallas kernels for 0% -> 0%
where the time goes in v17:
time: 196 us
  waiting for transfers between devices  53.1 us (27%)
  starting transfers between devices  43 us (22%)
  blocking collectives  41.1 us (21%)
  other arithmetic  22.2 us (11%)
  between operations  15.7 us (8%)
  local copies, waits for them, and re-layouts  14.6 us (7%)
  matrix products  6.14 us (3%)
    all_to_all x1, blocking collectives, on_device(): lax.all_to_all(own_columns, 'tensor', split_axis=0, concat_axis=1, tiled=...  41.1 us
    ppermute x10, waiting for transfers between devices, all_sum(): x = x + lax.ppermute(x, axis, [(i, i ^ step) for i in range(peers)])  21.9 us
    ppermute x10, starting transfers between devices, all_sum(): x = x + lax.ppermute(x, axis, [(i, i ^ step) for i in range(peers)])  12.3 us
    ppermute x5, waiting for transfers between devices, all_moments(): lax.ppermute(jnp.stack([mean, spread]), axis, [(i, i ^ step) for i in ran...  9.7 us
    ppermute x2, starting transfers between devices, extended(): before = lax.ppermute(last, axis, up)  9.48 us
    ppermute x5, starting transfers between devices, all_moments(): lax.ppermute(jnp.stack([mean, spread]), axis, [(i, i ^ step) for i in ran...  7.39 us
    another operation x32, local copies, waits for them, and re-layouts, on_device(): jnp.stack([jnp.sum(padded[:, offset:offset + frames, :].astype(jnp.float3...  7.36 us
    all_gather x1, waiting for transfers between devices, on_device(): group_grad = lax.all_gather(flat_grad, 'tensor', axis=0, tiled=True)  6.52 us
  transfers between devices with their start and end apart: 29, of which 20 were waited for; matrix products, arithmetic and copies ran while one was open for 18% of the time, Pallas kernels for 0%

profile of v17, /device:TPU:0, one launch (start us, length us, event | category | flops | bytes accessed | tf_op | source)
XLA Modules:
  0.0 195.9 jit_solution(10785781669787028285)
XLA Ops:
  9.3 4.9 %collective-permute-start = (bf16[2,15,1536]{2,1,0:T(8,128)(2,1)S(1)}, bf16[2,15,1536]{2,1,0:T(8,128)(2,1)S(1)}, u32[]{:S(2)}, u32[]{:S(2)}) collective-permute-start(bf16[2,15,1536]{2,1,0:T(8,128)(2,1)S(1)} %get-tuple-element.103), channel_id=1, source_target_pairs={{0,1},{1,2},{2,3},{4,5},{5,6},{6,7},{8,9},{9,10},{10,11},{12,13},{... | collective-permute-start | bytes 276488 | tf_op jit(solution)/shard_map/ppermute | solution.py:16
  16.5 4.3 %collective-permute-done.1 = bf16[2,15,1536]{2,1,0:T(8,128)(2,1)S(1)} collective-permute-done((bf16[2,15,1536]{2,1,0:T(8,128)(2,1)S(1)}, bf16[2,15,1536]{2,1,0:T(8,128)(2,1)S(1)}, u32[]{:S(2)}, u32[]{:S(2)}) %collective-permute-start.1) | collective-permute-done | bytes 92192 | tf_op jit(solution)/shard_map/ppermute | solution.py:17
  20.8 3.8 %fusion.143 = (f32[1536]{0:T(1024)S(1)}, f32[2,64,1536]{2,1,0:T(8,128)S(1)}) fusion(bf16[2,15,1536]{2,1,0:T(8,128)(2,1)S(1)} %collective-permute-done.1, bf16[2,64,1536]{2,1,0:T(8,128)(2,1)S(1)} %fusion, f32[1536]{0:T(1024)S(1)} %get-tuple-element.76, f32[1536]{0:T(1024)S(1)} %get-tuple-element.77, f32[1536]{0:T(1024)S(1)} %get-tuple-element.48, ...), kind=kLoop, calls=%fused_computation.380 | loop fusion | flops 35977728 | bytes 1560576 | tf_op jit(solution)/shard_map/reduce_sum | solution.py:108
  26.2 1.6 collective-permute-start.3
  27.7 2.2 %collective-permute-done.3 = f32[2,1536]{1,0:T(2,128)S(1)} collective-permute-done((f32[2,1536]{1,0:T(2,128)S(1)}, f32[2,1536]{1,0:T(2,128)S(1)}, u32[]{:S(2)}, u32[]{:S(2)}) %collective-permute-start.3) | collective-permute-done | bytes 12320 | tf_op jit(solution)/shard_map/ppermute | solution.py:44
  30.0 1.6 collective-permute-start.4
  31.6 2.2 %collective-permute-done.4 = f32[2,1536]{1,0:T(2,128)S(1)} collective-permute-done((f32[2,1536]{1,0:T(2,128)S(1)}, f32[2,1536]{1,0:T(2,128)S(1)}, u32[]{:S(2)}, u32[]{:S(2)}) %collective-permute-start.4) | collective-permute-done | bytes 12320 | tf_op jit(solution)/shard_map/ppermute | solution.py:44
  33.8 1.6 collective-permute-start.5
  38.0 2.5 %collective-permute-start.6 = (f32[2,1536]{1,0:T(2,128)S(1)}, f32[2,1536]{1,0:T(2,128)S(1)}, u32[]{:S(2)}, u32[]{:S(2)}) collective-permute-start(f32[2,1536]{1,0:T(2,128)S(1)} %pad_maximum_fusion.10), channel_id=1, source_target_pairs={{0,2},{1,3},{2,0},{3,1},{4,6},{5,7},{6,4},{7,5},{8,10},{9,11},{10,... | collective-permute-start | bytes 36872 | tf_op jit(solution)/shard_map/ppermute | solution.py:44
  40.5 2.8 %collective-permute-done.6 = f32[2,1536]{1,0:T(2,128)S(1)} collective-permute-done((f32[2,1536]{1,0:T(2,128)S(1)}, f32[2,1536]{1,0:T(2,128)S(1)}, u32[]{:S(2)}, u32[]{:S(2)}) %collective-permute-start.6) | collective-permute-done | bytes 12320 | tf_op jit(solution)/shard_map/ppermute | solution.py:44
  43.4 6.5 %all-gather.4.cloned.1.call-done = bf16[512,1536]{1,0:T(8,128)(2,1)} async-done(((bf16[128,1536]{1,0:T(8,128)(2,1)}), bf16[512,1536]{1,0:T(8,128)(2,1)}) %all-gather.4.cloned.1.call-update) | async-done | bytes 1572880 | tf_op jit(solution)/shard_map/all_gather | solution.py:100
  49.9 2.4 %fusion.147 = f32[512,384]{1,0:T(8,128)S(1)} fusion(bf16[512,1536]{1,0:T(8,128)(2,1)} %all-gather.4.cloned.1.call-done, bf16[384,1536]{1,0:T(8,128)(2,1)S(1)} %copy-done), kind=kOutput, calls=%fused_computation.383 | convolution fusion | flops 603979776 | bytes 3538944 | tf_op jit(solution)/shard_map/fd,cd->fc/dot_general | solution.py:119
  52.3 41.1 %all_to_all.35 = f32[4,128,384]{2,1,0:T(8,128)S(1)} all-to-all(f32[4,128,384]{2,1,0:T(8,128)S(1)} %bitcast.21), channel_id=1, replica_groups=mesh['dp'=8,'tensor'=4] {'tensor'}, dimensions={0} | all-to-all | bytes 1572864 | tf_op jit(solution)/shard_map/all_to_all | solution.py:120
  95.2 2.4 %fusion.140 = (f32[1536]{0:T(1024)S(1)}, f32[1536]{0:T(1024)S(1)}, f32[2,64,1536]{2,1,0:T(8,128)}, bf16[2,64,1536]{2,1,0:T(8,128)(2,1)S(1)}) fusion(f32[1536]{0:T(1024)S(1)} %get-tuple-element.94, f32[2,64,1536]{2,1,0:T(8,128)S(1)} %get-tuple-element.97, f32[1536]{0:T(1024)S(1)} %get-tuple-element.10, f32[2,64,1536]{2,1,0:T(8,128)} %reshape.188, ...), kind=kLoop, calls=%fused_computation.378 | loop fusion | flops 3142656 | bytes 2789376 | tf_op jit(solution)/shard_map/reduce_sum | solution.py:132
  98.6 4.3 %all-to-all-start.1 = ((bf16[128,4,384]{2,0,1:T(8,128)(2,1)}), bf16[128,4,384]{2,0,1:T(8,128)(2,1)S(1)}, u32[]{:S(2)}, u32[]{:S(2)}) async-start(bf16[128,4,384]{2,0,1:T(8,128)(2,1)} %copy.17), calls=%async_computation.1 | async-start | bytes 786432 | tf_op jit(solution)/shard_map/all_to_all | solution.py:129
  104.5 2.3 %collective-permute-done.8 = f32[2,1536]{1,0:T(2,128)S(1)} collective-permute-done((f32[2,1536]{1,0:T(2,128)S(1)}, f32[2,1536]{1,0:T(2,128)S(1)}, u32[]{:S(2)}, u32[]{:S(2)}) %collective-permute-start.8) | collective-permute-done | bytes 12320 | tf_op jit(solution)/shard_map/ppermute | solution.py:34
  108.3 2.3 %collective-permute-done.9 = f32[2,1536]{1,0:T(2,128)S(1)} collective-permute-done((f32[2,1536]{1,0:T(2,128)S(1)}, f32[2,1536]{1,0:T(2,128)S(1)}, u32[]{:S(2)}, u32[]{:S(2)}) %collective-permute-start.9) | collective-permute-done | bytes 12320 | tf_op jit(solution)/shard_map/ppermute | solution.py:34
  110.5 2.1 %collective-permute-start.10 = (f32[2,1536]{1,0:T(2,128)S(1)}, f32[2,1536]{1,0:T(2,128)S(1)}, u32[]{:S(2)}, u32[]{:S(2)}) collective-permute-start(f32[2,1536]{1,0:T(2,128)S(1)} %add.496), channel_id=1, source_target_pairs={{0,1},{1,0},{2,3},{3,2},{4,5},{5,4},{6,7},{7,6},{8,9},{9,8},{10,11... | collective-permute-start | bytes 36872 | tf_op jit(solution)/shard_map/ppermute | solution.py:34
  112.6 1.7 collective-permute-done.10
  114.4 2.9 %collective-permute-start.11 = (f32[2,1536]{1,0:T(2,128)S(1)}, f32[2,1536]{1,0:T(2,128)S(1)}, u32[]{:S(2)}, u32[]{:S(2)}) collective-permute-start(f32[2,1536]{1,0:T(2,128)S(1)} %add.497), channel_id=1, source_target_pairs={{0,2},{1,3},{2,0},{3,1},{4,6},{5,7},{6,4},{7,5},{8,10},{9,11},{10,... | collective-permute-start | bytes 36872 | tf_op jit(solution)/shard_map/ppermute | solution.py:34
  117.3 4.4 %collective-permute-done.11 = f32[2,1536]{1,0:T(2,128)S(1)} collective-permute-done((f32[2,1536]{1,0:T(2,128)S(1)}, f32[2,1536]{1,0:T(2,128)S(1)}, u32[]{:S(2)}, u32[]{:S(2)}) %collective-permute-start.11) | collective-permute-done | bytes 12320 | tf_op jit(solution)/shard_map/ppermute | solution.py:34
  122.2 2.2 %fusion.148 = f32[384,1536]{1,0:T(8,128)S(1)} fusion(bf16[512,384]{1,0:T(8,128)(2,1)S(1)} %bitcast.20, bf16[512,1536]{1,0:T(8,128)(2,1)} %all-gather.4.cloned.1.call-done), kind=kOutput, calls=%fused_computation.384 | convolution fusion | flops 603979776 | bytes 4325376 | tf_op jit(solution)/shard_map/fc,fd->cd/dot_general | solution.py:130
  138.5 2.5 %stack.172 = f32[31,1536]{1,0:T(8,128)S(1)} concatenate(f32[1,1536]{1,0:T(1,128)} %stack.141, f32[1,1536]{1,0:T(1,128)} %stack.142, f32[1,1536]{1,0:T(1,128)} %stack.143, f32[1,1536]{1,0:T(1,128)} %stack.144, f32[1,1536]{1,0:T(1,128)S(1)} %stack.145, f32[1,1536]{1,0:T(1,128)S(1)} %stack.146, f32[1,1536]{1,0:T(1,128)S(1)} %stack.147, f32[1,1536]{1,0:T(1,128)S(1)} %stack.148, ...), dimensions={0} | concatenate | bytes 380928 | tf_op jit(solution)/shard_map/stack | solution.py:147
  143.2 3.2 %collective-permute-done.16 = f32[96,1536]{1,0:T(8,128)} collective-permute-done((f32[96,1536]{1,0:T(8,128)}, f32[96,1536]{1,0:T(8,128)}, u32[]{:S(2)}, u32[]{:S(2)}) %collective-permute-start.16) | collective-permute-done | bytes 589856 | tf_op jit(solution)/shard_map/ppermute | solution.py:65
  147.8 1.6 collective-permute-start.17
  150.7 4.6 %collective-permute-start.14 = (bf16[2,15,1536]{2,1,0:T(8,128)(2,1)S(1)}, bf16[2,15,1536]{2,1,0:T(8,128)(2,1)S(1)}, u32[]{:S(2)}, u32[]{:S(2)}) collective-permute-start(bf16[2,15,1536]{2,1,0:T(8,128)(2,1)S(1)} %get-tuple-element.102), channel_id=1, source_target_pairs={{0,1},{1,2},{2,3},{4,5},{5,6},{6,7},{8,9},{9,10},{10,11},{12,13},{... | collective-permute-start | bytes 276488 | tf_op jit(solution)/shard_map/ppermute | solution.py:16
  157.9 4.1 %multiply_convert_fusion = (bf16[2,64,1536]{2,1,0:T(8,128)(2,1)S(1)}, f32[2,64,1536]{2,1,0:T(8,128)S(1)}) fusion(bf16[2,64,3072]{2,1,0:T(8,128)(2,1)S(1)} %copy-done.1, bf16[2,64,1536]{2,1,0:T(8,128)(2,1)S(1)} %get-tuple-element.90, bf16[2,15,1536]{2,1,0:T(8,128)(2,1)S(1)} %collective-permute-done.14, f32[1536]{0:T(1024)S(1)} %copy-done.62, ...), kind=kLoop, calls=%fused_computation.210 | loop fusion | flops 36962304 | bytes 2340864 | tf_op jit(solution)/shard_map/convert
  164.3 4.7 %collective-permute-done.18 = f32[48,1536]{1,0:T(8,128)S(1)} collective-permute-done((f32[48,1536]{1,0:T(8,128)S(1)}, f32[48,1536]{1,0:T(8,128)S(1)}, u32[]{:S(2)}, u32[]{:S(2)}) %collective-permute-start.18) | collective-permute-done | bytes 294944 | tf_op jit(solution)/shard_map/ppermute | solution.py:69
  169.1 2.1 %collective-permute-start.19 = (f32[96,1536]{1,0:T(8,128)S(1)}, f32[96,1536]{1,0:T(8,128)S(1)}, u32[]{:S(2)}, u32[]{:S(2)}) collective-permute-start(f32[96,1536]{1,0:T(8,128)S(1)} %maximum_select_fusion.2), channel_id=1, source_target_pairs={{0,8},{4,12},{8,0},{12,4},{16,24},{20,28},{24,16},{28,20},{1,9},{5... | collective-permute-start | bytes 1769480 | tf_op jit(solution)/shard_map/ppermute | solution.py:69
  171.5 1.7 collective-permute-start.25
  174.2 8.7 %collective-permute-done.25 = f32[31,1536]{1,0:T(8,128)S(1)} collective-permute-done((f32[31,1536]{1,0:T(8,128)S(1)}, f32[31,1536]{1,0:T(8,128)S(1)}, u32[]{:S(2)}, u32[]{:S(2)}) %collective-permute-start.25) | collective-permute-done | bytes 190496 | tf_op jit(solution)/shard_map/ppermute | solution.py:34
  187.4 1.6 maximum_select_fusion
  (264 shorter events, 43.2 us)
Async XLA Ops:
  7.2 28.3 %copy-start = (bf16[384,1536]{1,0:T(8,128)(2,1)S(1)}, bf16[384,1536]{1,0:T(8,128)(2,1)}, u32[]{:S(2)}) copy-start(bf16[384,1536]{1,0:T(8,128)(2,1)} %param.10) | copy-start | bytes 3538948
  7.2 42.8 %all-gather.4.cloned.1.call-start = ((), (), s32[]{:S(2)}) async-start(), calls=%async_computation.2 | async-start | bytes 1966080 | tf_op jit(solution)/shard_map/all_gather | solution.py:100
  7.9 114.3 %all-gather.6.cloned.1.call-start = ((), (), s32[]{:S(2)}) async-start(), calls=%async_computation.3 | async-start | bytes 2949120 | tf_op jit(solution)/shard_map/all_gather | solution.py:81
  9.3 7.1 %collective-permute-start = (bf16[2,15,1536]{2,1,0:T(8,128)(2,1)S(1)}, bf16[2,15,1536]{2,1,0:T(8,128)(2,1)S(1)}, u32[]{:S(2)}, u32[]{:S(2)}) collective-permute-start(bf16[2,15,1536]{2,1,0:T(8,128)(2,1)S(1)} %get-tuple-element.103), channel_id=1, source_target_pairs={{0,1},{1,2},{2,3},{4,5},{5,6},{6,7},{8,9},{9,10},{10,11},{12,13},{... | collective-permute-start | bytes 276488 | tf_op jit(solution)/shard_map/ppermute | solution.py:16
  14.3 6.5 %collective-permute-start.1 = (bf16[2,15,1536]{2,1,0:T(8,128)(2,1)S(1)}, bf16[2,15,1536]{2,1,0:T(8,128)(2,1)S(1)}, u32[]{:S(2)}, u32[]{:S(2)}) collective-permute-start(bf16[2,15,1536]{2,1,0:T(8,128)(2,1)S(1)} %get-tuple-element.104), channel_id=1, source_target_pairs={{1,0},{2,1},{3,2},{5,4},{6,5},{7,6},{9,8},{10,9},{11,10},{13,12},{... | collective-permute-start | bytes 276488 | tf_op jit(solution)/shard_map/ppermute | solution.py:17
  15.9 20.4 %copy-start.7 = (f32[1536]{0:T(1024)}, f32[1536]{0:T(1024)S(1)}, u32[]{:S(2)}) copy-start(f32[1536]{0:T(1024)S(1)} %get-tuple-element.49) | copy-start | bytes 18436
  15.9 20.4 %copy-start.9 = (f32[1536]{0:T(1024)}, f32[1536]{0:T(1024)S(1)}, u32[]{:S(2)}) copy-start(f32[1536]{0:T(1024)S(1)} %get-tuple-element.50) | copy-start | bytes 18436
  24.8 1.2 collective-permute-start.2
  26.2 3.8 %collective-permute-start.3 = (f32[2,1536]{1,0:T(2,128)S(1)}, f32[2,1536]{1,0:T(2,128)S(1)}, u32[]{:S(2)}, u32[]{:S(2)}) collective-permute-start(f32[2,1536]{1,0:T(2,128)S(1)} %pad_maximum_fusion.7), channel_id=1, source_target_pairs={{0,8},{4,12},{8,0},{12,4},{16,24},{20,28},{24,16},{28,20},{1,9},{5... | collective-permute-start | bytes 36872 | tf_op jit(solution)/shard_map/ppermute | solution.py:44
  30.0 3.8 %collective-permute-start.4 = (f32[2,1536]{1,0:T(2,128)S(1)}, f32[2,1536]{1,0:T(2,128)S(1)}, u32[]{:S(2)}, u32[]{:S(2)}) collective-permute-start(f32[2,1536]{1,0:T(2,128)S(1)} %pad_maximum_fusion.8), channel_id=1, source_target_pairs={{0,16},{4,20},{8,24},{12,28},{16,0},{20,4},{24,8},{28,12},{1,17},{... | collective-permute-start | bytes 36872 | tf_op jit(solution)/shard_map/ppermute | solution.py:44
  33.8 4.1 %collective-permute-start.5 = (f32[2,1536]{1,0:T(2,128)S(1)}, f32[2,1536]{1,0:T(2,128)S(1)}, u32[]{:S(2)}, u32[]{:S(2)}) collective-permute-start(f32[2,1536]{1,0:T(2,128)S(1)} %pad_maximum_fusion.9), channel_id=1, source_target_pairs={{0,1},{1,0},{2,3},{3,2},{4,5},{5,4},{6,7},{7,6},{8,9},{9,8},{10,11... | collective-permute-start | bytes 36872 | tf_op jit(solution)/shard_map/ppermute | solution.py:44
  38.0 5.4 %collective-permute-start.6 = (f32[2,1536]{1,0:T(2,128)S(1)}, f32[2,1536]{1,0:T(2,128)S(1)}, u32[]{:S(2)}, u32[]{:S(2)}) collective-permute-start(f32[2,1536]{1,0:T(2,128)S(1)} %pad_maximum_fusion.10), channel_id=1, source_target_pairs={{0,2},{1,3},{2,0},{3,1},{4,6},{5,7},{6,4},{7,5},{8,10},{9,11},{10,... | collective-permute-start | bytes 36872 | tf_op jit(solution)/shard_map/ppermute | solution.py:44
  97.7 5.3 %collective-permute-start.7 = (f32[2,1536]{1,0:T(2,128)S(1)}, f32[2,1536]{1,0:T(2,128)S(1)}, u32[]{:S(2)}, u32[]{:S(2)}) collective-permute-start(f32[2,1536]{1,0:T(2,128)S(1)} %pad_maximum_fusion.11), channel_id=1, source_target_pairs={{0,4},{4,0},{8,12},{12,8},{16,20},{20,16},{24,28},{28,24},{1,5},{5... | collective-permute-start | bytes 36872 | tf_op jit(solution)/shard_map/ppermute | solution.py:34
  98.6 23.6 %all-to-all-start.1 = ((bf16[128,4,384]{2,0,1:T(8,128)(2,1)}), bf16[128,4,384]{2,0,1:T(8,128)(2,1)S(1)}, u32[]{:S(2)}, u32[]{:S(2)}) async-start(bf16[128,4,384]{2,0,1:T(8,128)(2,1)} %copy.17), calls=%async_computation.1 | async-start | bytes 786432 | tf_op jit(solution)/shard_map/all_to_all | solution.py:129
  103.0 3.8 %collective-permute-start.8 = (f32[2,1536]{1,0:T(2,128)S(1)}, f32[2,1536]{1,0:T(2,128)S(1)}, u32[]{:S(2)}, u32[]{:S(2)}) collective-permute-start(f32[2,1536]{1,0:T(2,128)S(1)} %fusion.139), channel_id=1, source_target_pairs={{0,8},{4,12},{8,0},{12,4},{16,24},{20,28},{24,16},{28,20},{1,9},{5... | collective-permute-start | bytes 36872 | tf_op jit(solution)/shard_map/ppermute | solution.py:34
  106.8 3.8 %collective-permute-start.9 = (f32[2,1536]{1,0:T(2,128)S(1)}, f32[2,1536]{1,0:T(2,128)S(1)}, u32[]{:S(2)}, u32[]{:S(2)}) collective-permute-start(f32[2,1536]{1,0:T(2,128)S(1)} %fusion.155), channel_id=1, source_target_pairs={{0,16},{4,20},{8,24},{12,28},{16,0},{20,4},{24,8},{28,12},{1,17},{... | collective-permute-start | bytes 36872 | tf_op jit(solution)/shard_map/ppermute | solution.py:34
  110.5 3.8 %collective-permute-start.10 = (f32[2,1536]{1,0:T(2,128)S(1)}, f32[2,1536]{1,0:T(2,128)S(1)}, u32[]{:S(2)}, u32[]{:S(2)}) collective-permute-start(f32[2,1536]{1,0:T(2,128)S(1)} %add.496), channel_id=1, source_target_pairs={{0,1},{1,0},{2,3},{3,2},{4,5},{5,4},{6,7},{7,6},{8,9},{9,8},{10,11... | collective-permute-start | bytes 36872 | tf_op jit(solution)/shard_map/ppermute | solution.py:34
  114.4 7.3 %collective-permute-start.11 = (f32[2,1536]{1,0:T(2,128)S(1)}, f32[2,1536]{1,0:T(2,128)S(1)}, u32[]{:S(2)}, u32[]{:S(2)}) collective-permute-start(f32[2,1536]{1,0:T(2,128)S(1)} %add.497), channel_id=1, source_target_pairs={{0,2},{1,3},{2,0},{3,1},{4,6},{5,7},{6,4},{7,5},{8,10},{9,11},{10,... | collective-permute-start | bytes 36872 | tf_op jit(solution)/shard_map/ppermute | solution.py:34
  124.6 3.8 %collective-permute-start.15 = (f32[192,1536]{1,0:T(8,128)S(1)}, f32[192,1536]{1,0:T(8,128)S(1)}, u32[]{:S(2)}, u32[]{:S(2)}) collective-permute-start(f32[192,1536]{1,0:T(8,128)S(1)} %constant_dynamic-slice_fusion.2), channel_id=1, source_target_pairs={{0,4},{4,0},{8,12},{12,8},{16,20},{20,16},{24,28},{28,24},{1,5},{5... | collective-permute-start | bytes 3538952 | tf_op jit(solution)/shard_map/ppermute | solution.py:65
  130.4 16.0 %collective-permute-start.16 = (f32[96,1536]{1,0:T(8,128)}, f32[96,1536]{1,0:T(8,128)}, u32[]{:S(2)}, u32[]{:S(2)}) collective-permute-start(f32[96,1536]{1,0:T(8,128)} %constant_dynamic-slice_fusion.1), channel_id=1, source_target_pairs={{0,8},{4,12},{8,0},{12,4},{16,24},{20,28},{24,16},{28,20},{1,9},{5... | collective-permute-start | bytes 1769480 | tf_op jit(solution)/shard_map/ppermute | solution.py:65
  141.0 1.5 collective-permute-start.21
  142.5 12.8 %collective-permute-start.22 = (f32[31,1536]{1,0:T(8,128)S(1)}, f32[31,1536]{1,0:T(8,128)S(1)}, u32[]{:S(2)}, u32[]{:S(2)}) collective-permute-start(f32[31,1536]{1,0:T(8,128)S(1)} %add.537), channel_id=1, source_target_pairs={{0,8},{4,12},{8,0},{12,4},{16,24},{20,28},{24,16},{28,20},{1,9},{5... | collective-permute-start | bytes 571400 | tf_op jit(solution)/shard_map/ppermute | solution.py:34
  147.8 8.2 %collective-permute-start.17 = (f32[48,1536]{1,0:T(8,128)S(1)}, f32[48,1536]{1,0:T(8,128)S(1)}, u32[]{:S(2)}, u32[]{:S(2)}) collective-permute-start(f32[48,1536]{1,0:T(8,128)S(1)} %constant_dynamic-slice_fusion), channel_id=1, source_target_pairs={{0,16},{4,20},{8,24},{12,28},{16,0},{20,4},{24,8},{28,12},{1,17},{... | collective-permute-start | bytes 884744 | tf_op jit(solution)/shard_map/ppermute | solution.py:65
  149.4 8.2 %collective-permute-start.13 = (bf16[2,15,1536]{2,1,0:T(8,128)(2,1)S(1)}, bf16[2,15,1536]{2,1,0:T(8,128)(2,1)S(1)}, u32[]{:S(2)}, u32[]{:S(2)}) collective-permute-start(bf16[2,15,1536]{2,1,0:T(8,128)(2,1)S(1)} %get-tuple-element.101), channel_id=1, source_target_pairs={{1,0},{2,1},{3,2},{5,4},{6,5},{7,6},{9,8},{10,9},{11,10},{13,12},{... | collective-permute-start | bytes 276488 | tf_op jit(solution)/shard_map/ppermute | solution.py:17
  150.7 6.9 %collective-permute-start.14 = (bf16[2,15,1536]{2,1,0:T(8,128)(2,1)S(1)}, bf16[2,15,1536]{2,1,0:T(8,128)(2,1)S(1)}, u32[]{:S(2)}, u32[]{:S(2)}) collective-permute-start(bf16[2,15,1536]{2,1,0:T(8,128)(2,1)S(1)} %get-tuple-element.102), channel_id=1, source_target_pairs={{0,1},{1,2},{2,3},{4,5},{5,6},{6,7},{8,9},{9,10},{10,11},{12,13},{... | collective-permute-start | bytes 276488 | tf_op jit(solution)/shard_map/ppermute | solution.py:16
  155.3 29.3 %collective-permute-start.12 = (bf16[4,192,1536]{2,1,0:T(8,128)(2,1)S(1)}, bf16[4,192,1536]{2,1,0:T(8,128)(2,1)S(1)}, u32[]{:S(2)}, u32[]{:S(2)}) collective-permute-start(bf16[4,192,1536]{2,1,0:T(8,128)(2,1)S(1)} %bitcast.18), channel_id=1, source_target_pairs={{0,4},{4,0},{8,12},{12,8},{16,20},{20,16},{24,28},{28,24},{1,5},{5... | collective-permute-start | bytes 7077896 | tf_op jit(solution)/shard_map/ppermute | solution.py:83
  155.4 7.8 %collective-permute-start.23 = (f32[31,1536]{1,0:T(8,128)S(1)}, f32[31,1536]{1,0:T(8,128)S(1)}, u32[]{:S(2)}, u32[]{:S(2)}) collective-permute-start(f32[31,1536]{1,0:T(8,128)S(1)} %add.538), channel_id=1, source_target_pairs={{0,16},{4,20},{8,24},{12,28},{16,0},{20,4},{24,8},{28,12},{1,17},{... | collective-permute-start | bytes 571400 | tf_op jit(solution)/shard_map/ppermute | solution.py:34
  156.0 13.0 %collective-permute-start.18 = (f32[48,1536]{1,0:T(8,128)S(1)}, f32[48,1536]{1,0:T(8,128)S(1)}, u32[]{:S(2)}, u32[]{:S(2)}) collective-permute-start(f32[48,1536]{1,0:T(8,128)S(1)} %dynamic-slice_add_fusion.2), channel_id=1, source_target_pairs={{0,16},{4,20},{8,24},{12,28},{16,0},{20,4},{24,8},{28,12},{1,17},{... | collective-permute-start | bytes 884744 | tf_op jit(solution)/shard_map/ppermute | solution.py:69
  163.2 8.3 %collective-permute-start.24 = (f32[31,1536]{1,0:T(8,128)S(1)}, f32[31,1536]{1,0:T(8,128)S(1)}, u32[]{:S(2)}, u32[]{:S(2)}) collective-permute-start(f32[31,1536]{1,0:T(8,128)S(1)} %add.539), channel_id=1, source_target_pairs={{0,1},{1,0},{2,3},{3,2},{4,5},{5,4},{6,7},{7,6},{8,9},{9,8},{10,11... | collective-permute-start | bytes 571400 | tf_op jit(solution)/shard_map/ppermute | solution.py:34
  169.1 15.3 %collective-permute-start.19 = (f32[96,1536]{1,0:T(8,128)S(1)}, f32[96,1536]{1,0:T(8,128)S(1)}, u32[]{:S(2)}, u32[]{:S(2)}) collective-permute-start(f32[96,1536]{1,0:T(8,128)S(1)} %maximum_select_fusion.2), channel_id=1, source_target_pairs={{0,8},{4,12},{8,0},{12,4},{16,24},{20,28},{24,16},{28,20},{1,9},{5... | collective-permute-start | bytes 1769480 | tf_op jit(solution)/shard_map/ppermute | solution.py:69
  171.5 11.4 %collective-permute-start.25 = (f32[31,1536]{1,0:T(8,128)S(1)}, f32[31,1536]{1,0:T(8,128)S(1)}, u32[]{:S(2)}, u32[]{:S(2)}) collective-permute-start(f32[31,1536]{1,0:T(8,128)S(1)} %add.540), channel_id=1, source_target_pairs={{0,2},{1,3},{2,0},{3,1},{4,6},{5,7},{6,4},{7,5},{8,10},{9,11},{10,... | collective-permute-start | bytes 571400 | tf_op jit(solution)/shard_map/ppermute | solution.py:34
  184.5 2.9 %collective-permute-start.20 = (f32[192,1536]{1,0:T(8,128)S(1)}, f32[192,1536]{1,0:T(8,128)S(1)}, u32[]{:S(2)}, u32[]{:S(2)}) collective-permute-start(f32[192,1536]{1,0:T(8,128)S(1)} %maximum_select_fusion.1), channel_id=1, source_target_pairs={{0,4},{4,0},{8,12},{12,8},{16,20},{20,16},{24,28},{28,24},{1,5},{5... | collective-permute-start | bytes 3538952 | tf_op jit(solution)/shard_map/ppermute | solution.py:69
  (67 other events, 891.4 us)
Sparse Core Ops, SparseCore 0:
  9.6 40.3 all-gather.3
  52.1 70.1 all-gather.5

commit v18 on v13

--- a/solution.py
+++ b/solution.py
@@ -151,7 +151,7 @@
         ]
     )
     weight_grad = rows_sum(local_grad, "dp")
-    kernel_grad = all_sum(kernel_terms, ("dp", "tensor"))
+    kernel_grad = all_sum(kernel_terms, ("tensor", "dp"))
     input_grad = jnp.concatenate(
         [grad_gated * gates, grad_gated * values * gates * (1.0 - gates)], axis=-1
     ).astype(jnp.bfloat16)

time: 187 us -> 192 us (1.027)
  starting transfers between devices: 40.8 us -> 43.7 us
    ppermute x10, starting transfers between devices: 11.8 us -> 14.3 us  [all_sum(): x = x + lax.ppermute(x, axis, [(i, i ^ step) for i in range(peers)])]
  transfers between devices with their start and end apart: 29 -> 29, of which waited for: 19 -> 20; matrix products, arithmetic and copies ran while one was open for 18% -> 18% of each run, Pallas kernels for 0% -> 0%
where the time goes in v18:
time: 192 us; the launch traced here: 191 us
  waiting for transfers between devices  64.7 us (34%)
  starting transfers between devices  43.7 us (23%)
  other arithmetic  22.9 us (12%)
  blocking collectives  22.6 us (12%)
  between operations  15.6 us (8%)
  local copies, waits for them, and re-layouts  15.2 us (8%)
  matrix products  6.15 us (3%)
    all_to_all x1, blocking collectives, on_device(): lax.all_to_all(own_columns, 'tensor', split_axis=0, concat_axis=1, tiled=...  22.6 us
    all_gather x1, waiting for transfers between devices, gather_weight(): held = lax.all_gather(mine, 'tensor', axis=0, tiled=False)  18.5 us
    ppermute x10, waiting for transfers between devices, all_sum(): x = x + lax.ppermute(x, axis, [(i, i ^ step) for i in range(peers)])  16.9 us
    ppermute x10, starting transfers between devices, all_sum(): x = x + lax.ppermute(x, axis, [(i, i ^ step) for i in range(peers)])  14.3 us
    ppermute x5, waiting for transfers between devices, all_moments(): lax.ppermute(jnp.stack([mean, spread]), axis, [(i, i ^ step) for i in ran...  10.9 us
    ppermute x2, starting transfers between devices, extended(): before = lax.ppermute(last, axis, up)  9.48 us
    another operation x32, local copies, waits for them, and re-layouts, on_device(): jnp.stack([jnp.sum(padded[:, offset:offset + frames, :].astype(jnp.float3...  7.97 us
    ppermute x5, starting transfers between devices, all_moments(): lax.ppermute(jnp.stack([mean, spread]), axis, [(i, i ^ step) for i in ran...  7.35 us
  transfers between devices with their start and end apart: 29, of which 20 were waited for; matrix products, arithmetic and copies ran while one was open for 18% of the time, Pallas kernels for 0%

profile of v18, /device:TPU:0, one launch (start us, length us, event | category | flops | bytes accessed | tf_op | source)
XLA Modules:
  0.0 190.9 jit_solution(6249980351350756969)
XLA Ops:
  9.3 4.9 %collective-permute-start = (bf16[2,15,1536]{2,1,0:T(8,128)(2,1)S(1)}, bf16[2,15,1536]{2,1,0:T(8,128)(2,1)S(1)}, u32[]{:S(2)}, u32[]{:S(2)}) collective-permute-start(bf16[2,15,1536]{2,1,0:T(8,128)(2,1)S(1)} %get-tuple-element.99), channel_id=1, source_target_pairs={{0,1},{1,2},{2,3},{4,5},{5,6},{6,7},{8,9},{9,10},{10,11},{12,13},{... | collective-permute-start | bytes 276488 | tf_op jit(solution)/shard_map/ppermute | solution.py:16
  16.4 4.3 %collective-permute-done.1 = bf16[2,15,1536]{2,1,0:T(8,128)(2,1)S(1)} collective-permute-done((bf16[2,15,1536]{2,1,0:T(8,128)(2,1)S(1)}, bf16[2,15,1536]{2,1,0:T(8,128)(2,1)S(1)}, u32[]{:S(2)}, u32[]{:S(2)}) %collective-permute-start.1) | collective-permute-done | bytes 92192 | tf_op jit(solution)/shard_map/ppermute | solution.py:17
  20.7 3.8 %fusion.143 = (f32[1536]{0:T(1024)S(1)}, f32[2,64,1536]{2,1,0:T(8,128)S(1)}) fusion(bf16[2,15,1536]{2,1,0:T(8,128)(2,1)S(1)} %collective-permute-done.1, bf16[2,64,1536]{2,1,0:T(8,128)(2,1)S(1)} %fusion, f32[1536]{0:T(1024)S(1)} %get-tuple-element.72, f32[1536]{0:T(1024)S(1)} %get-tuple-element.73, f32[1536]{0:T(1024)S(1)} %get-tuple-element.44, ...), kind=kLoop, calls=%fused_computation.380 | loop fusion | flops 35977728 | bytes 1560576 | tf_op jit(solution)/shard_map/reduce_sum | solution.py:107
  26.1 1.6 collective-permute-start.3
  27.7 2.2 %collective-permute-done.3 = f32[2,1536]{1,0:T(2,128)S(1)} collective-permute-done((f32[2,1536]{1,0:T(2,128)S(1)}, f32[2,1536]{1,0:T(2,128)S(1)}, u32[]{:S(2)}, u32[]{:S(2)}) %collective-permute-start.3) | collective-permute-done | bytes 12320 | tf_op jit(solution)/shard_map/ppermute | solution.py:44
  29.9 1.6 collective-permute-start.4
  31.5 2.2 %collective-permute-done.4 = f32[2,1536]{1,0:T(2,128)S(1)} collective-permute-done((f32[2,1536]{1,0:T(2,128)S(1)}, f32[2,1536]{1,0:T(2,128)S(1)}, u32[]{:S(2)}, u32[]{:S(2)}) %collective-permute-start.4) | collective-permute-done | bytes 12320 | tf_op jit(solution)/shard_map/ppermute | solution.py:44
  33.8 1.6 collective-permute-start.5
  35.4 2.5 %collective-permute-done.5 = f32[2,1536]{1,0:T(2,128)S(1)} collective-permute-done((f32[2,1536]{1,0:T(2,128)S(1)}, f32[2,1536]{1,0:T(2,128)S(1)}, u32[]{:S(2)}, u32[]{:S(2)}) %collective-permute-start.5) | collective-permute-done | bytes 12320 | tf_op jit(solution)/shard_map/ppermute | solution.py:44
  38.0 2.5 %collective-permute-start.6 = (f32[2,1536]{1,0:T(2,128)S(1)}, f32[2,1536]{1,0:T(2,128)S(1)}, u32[]{:S(2)}, u32[]{:S(2)}) collective-permute-start(f32[2,1536]{1,0:T(2,128)S(1)} %pad_maximum_fusion.10), channel_id=1, source_target_pairs={{0,2},{1,3},{2,0},{3,1},{4,6},{5,7},{6,4},{7,5},{8,10},{9,11},{10,... | collective-permute-start | bytes 36872 | tf_op jit(solution)/shard_map/ppermute | solution.py:44
  40.5 2.9 %collective-permute-done.6 = f32[2,1536]{1,0:T(2,128)S(1)} collective-permute-done((f32[2,1536]{1,0:T(2,128)S(1)}, f32[2,1536]{1,0:T(2,128)S(1)}, u32[]{:S(2)}, u32[]{:S(2)}) %collective-permute-start.6) | collective-permute-done | bytes 12320 | tf_op jit(solution)/shard_map/ppermute | solution.py:44
  44.2 5.8 %all-gather.4.cloned.1.call-done = bf16[512,1536]{1,0:T(8,128)(2,1)} async-done(((bf16[128,1536]{1,0:T(8,128)(2,1)}), bf16[512,1536]{1,0:T(8,128)(2,1)}) %all-gather.4.cloned.1.call-update) | async-done | bytes 1572880 | tf_op jit(solution)/shard_map/all_gather | solution.py:99
  50.0 2.4 %fusion.147 = f32[512,384]{1,0:T(8,128)S(1)} fusion(bf16[512,1536]{1,0:T(8,128)(2,1)} %all-gather.4.cloned.1.call-done, bf16[384,1536]{1,0:T(8,128)(2,1)S(1)} %copy-done), kind=kOutput, calls=%fused_computation.383 | convolution fusion | flops 603979776 | bytes 3538944 | tf_op jit(solution)/shard_map/fd,cd->fc/dot_general | solution.py:118
  52.4 22.6 %all_to_all.35 = f32[4,128,384]{2,1,0:T(8,128)S(1)} all-to-all(f32[4,128,384]{2,1,0:T(8,128)S(1)} %bitcast.21), channel_id=1, replica_groups=mesh['dp'=8,'tensor'=4] {'tensor'}, dimensions={0} | all-to-all | bytes 1572864 | tf_op jit(solution)/shard_map/all_to_all | solution.py:119
  76.8 2.4 %fusion.140 = (f32[1536]{0:T(1024)S(1)}, f32[1536]{0:T(1024)S(1)}, f32[2,64,1536]{2,1,0:T(8,128)}, bf16[2,64,1536]{2,1,0:T(8,128)(2,1)S(1)}) fusion(f32[1536]{0:T(1024)S(1)} %get-tuple-element.90, f32[2,64,1536]{2,1,0:T(8,128)S(1)} %get-tuple-element.93, f32[1536]{0:T(1024)S(1)} %get-tuple-element.8, f32[2,64,1536]{2,1,0:T(8,128)} %reshape.189, ...), kind=kLoop, calls=%fused_computation.378 | loop fusion | flops 3142656 | bytes 2789376 | tf_op jit(solution)/shard_map/reduce_sum | solution.py:131
  80.2 3.5 %all-to-all-start.1 = ((bf16[128,4,384]{2,0,1:T(8,128)(2,1)}), bf16[128,4,384]{2,0,1:T(8,128)(2,1)S(1)}, u32[]{:S(2)}, u32[]{:S(2)}) async-start(bf16[128,4,384]{2,0,1:T(8,128)(2,1)} %copy.17), calls=%async_computation.1 | async-start | bytes 786432 | tf_op jit(solution)/shard_map/all_to_all | solution.py:128
  89.3 2.2 %collective-permute-done.10 = f32[2,1536]{1,0:T(2,128)S(1)} collective-permute-done((f32[2,1536]{1,0:T(2,128)S(1)}, f32[2,1536]{1,0:T(2,128)S(1)}, u32[]{:S(2)}, u32[]{:S(2)}) %collective-permute-start.10) | collective-permute-done | bytes 12320 | tf_op jit(solution)/shard_map/ppermute | solution.py:34
  91.5 1.8 collective-permute-start.11
  93.3 1.9 %collective-permute-done.11 = f32[2,1536]{1,0:T(2,128)S(1)} collective-permute-done((f32[2,1536]{1,0:T(2,128)S(1)}, f32[2,1536]{1,0:T(2,128)S(1)}, u32[]{:S(2)}, u32[]{:S(2)}) %collective-permute-start.11) | collective-permute-done | bytes 12320 | tf_op jit(solution)/shard_map/ppermute | solution.py:34
  95.3 2.7 %collective-permute-start.12 = (f32[2,1536]{1,0:T(2,128)S(1)}, f32[2,1536]{1,0:T(2,128)S(1)}, u32[]{:S(2)}, u32[]{:S(2)}) collective-permute-start(f32[2,1536]{1,0:T(2,128)S(1)} %add.497), channel_id=1, source_target_pairs={{0,2},{1,3},{2,0},{3,1},{4,6},{5,7},{6,4},{7,5},{8,10},{9,11},{10,... | collective-permute-start | bytes 36872 | tf_op jit(solution)/shard_map/ppermute | solution.py:34
  98.0 3.5 %collective-permute-done.12 = f32[2,1536]{1,0:T(2,128)S(1)} collective-permute-done((f32[2,1536]{1,0:T(2,128)S(1)}, f32[2,1536]{1,0:T(2,128)S(1)}, u32[]{:S(2)}, u32[]{:S(2)}) %collective-permute-start.12) | collective-permute-done | bytes 12320 | tf_op jit(solution)/shard_map/ppermute | solution.py:34
  101.6 2.2 %fusion.148 = f32[384,1536]{1,0:T(8,128)S(1)} fusion(bf16[512,384]{1,0:T(8,128)(2,1)S(1)} %bitcast.20, bf16[512,1536]{1,0:T(8,128)(2,1)} %all-gather.4.cloned.1.call-done), kind=kOutput, calls=%fused_computation.384 | convolution fusion | flops 603979776 | bytes 4325376 | tf_op jit(solution)/shard_map/fc,fd->cd/dot_general | solution.py:129
  118.5 2.5 %stack.172 = f32[31,1536]{1,0:T(8,128)S(1)} concatenate(f32[1,1536]{1,0:T(1,128)} %stack.141, f32[1,1536]{1,0:T(1,128)} %stack.142, f32[1,1536]{1,0:T(1,128)} %stack.143, f32[1,1536]{1,0:T(1,128)} %stack.144, f32[1,1536]{1,0:T(1,128)} %stack.145, f32[1,1536]{1,0:T(1,128)S(1)} %stack.146, f32[1,1536]{1,0:T(1,128)S(1)} %stack.147, f32[1,1536]{1,0:T(1,128)S(1)} %stack.148, ...), dimensions={0} | concatenate | bytes 380928 | tf_op jit(solution)/shard_map/stack | solution.py:145
  122.1 18.5 %all-gather.6.cloned.1.call-done = bf16[768,1536]{1,0:T(8,128)(2,1)} async-done(((bf16[192,1536]{1,0:T(8,128)(2,1)}), bf16[768,1536]{1,0:T(8,128)(2,1)}) %all-gather.6.cloned.1.call-update) | async-done | bytes 2359312 | tf_op jit(solution)/shard_map/all_gather | solution.py:81
  140.7 2.8 %collective-permute-start.22 = (f32[31,1536]{1,0:T(8,128)S(1)}, f32[31,1536]{1,0:T(8,128)S(1)}, u32[]{:S(2)}, u32[]{:S(2)}) collective-permute-start(f32[31,1536]{1,0:T(8,128)S(1)} %add.537), channel_id=1, source_target_pairs={{0,2},{1,3},{2,0},{3,1},{4,6},{5,7},{6,4},{7,5},{8,10},{9,11},{10,... | collective-permute-start | bytes 571400 | tf_op jit(solution)/shard_map/ppermute | solution.py:34
  147.8 4.6 %collective-permute-start.14 = (bf16[2,15,1536]{2,1,0:T(8,128)(2,1)S(1)}, bf16[2,15,1536]{2,1,0:T(8,128)(2,1)S(1)}, u32[]{:S(2)}, u32[]{:S(2)}) collective-permute-start(bf16[2,15,1536]{2,1,0:T(8,128)(2,1)S(1)} %get-tuple-element.98), channel_id=1, source_target_pairs={{0,1},{1,2},{2,3},{4,5},{5,6},{6,7},{8,9},{9,10},{10,11},{12,13},{... | collective-permute-start | bytes 276488 | tf_op jit(solution)/shard_map/ppermute | solution.py:16
  156.1 4.1 %multiply_convert_fusion = (bf16[2,64,1536]{2,1,0:T(8,128)(2,1)S(1)}, f32[2,64,1536]{2,1,0:T(8,128)S(1)}) fusion(bf16[2,64,3072]{2,1,0:T(8,128)(2,1)S(1)} %copy-done.1, bf16[2,64,1536]{2,1,0:T(8,128)(2,1)S(1)} %get-tuple-element.86, bf16[2,15,1536]{2,1,0:T(8,128)(2,1)S(1)} %collective-permute-done.14, f32[1536]{0:T(1024)S(1)} %copy-done.62, ...), kind=kLoop, calls=%fused_computation.210 | loop fusion | flops 36962304 | bytes 2340864 | tf_op jit(solution)/shard_map/convert
  165.1 3.0 %collective-permute-done.24 = f32[31,1536]{1,0:T(8,128)S(1)} collective-permute-done((f32[31,1536]{1,0:T(8,128)S(1)}, f32[31,1536]{1,0:T(8,128)S(1)}, u32[]{:S(2)}, u32[]{:S(2)}) %collective-permute-start.24) | collective-permute-done | bytes 190496 | tf_op jit(solution)/shard_map/ppermute | solution.py:34
  170.2 3.7 %collective-permute-done.25 = f32[31,1536]{1,0:T(8,128)S(1)} collective-permute-done((f32[31,1536]{1,0:T(8,128)S(1)}, f32[31,1536]{1,0:T(8,128)S(1)}, u32[]{:S(2)}, u32[]{:S(2)}) %collective-permute-start.25) | collective-permute-done | bytes 190496 | tf_op jit(solution)/shard_map/ppermute | solution.py:34
  174.5 4.9 %collective-permute-done.19 = f32[96,1536]{1,0:T(8,128)S(1)} collective-permute-done((f32[96,1536]{1,0:T(8,128)S(1)}, f32[96,1536]{1,0:T(8,128)S(1)}, u32[]{:S(2)}, u32[]{:S(2)}) %collective-permute-start.19) | collective-permute-done | bytes 589856 | tf_op jit(solution)/shard_map/ppermute | solution.py:69
  180.3 1.5 convolution_convert_fusion
  182.4 1.6 maximum_select_fusion
  (266 shorter events, 46.9 us)
Async XLA Ops:
  7.2 42.8 %copy-start = (bf16[384,1536]{1,0:T(8,128)(2,1)S(1)}, bf16[384,1536]{1,0:T(8,128)(2,1)}, u32[]{:S(2)}) copy-start(bf16[384,1536]{1,0:T(8,128)(2,1)} %param.10) | copy-start | bytes 3538948
  7.2 42.8 %all-gather.4.cloned.1.call-start = ((), (), s32[]{:S(2)}) async-start(), calls=%async_computation.2 | async-start | bytes 1966080 | tf_op jit(solution)/shard_map/all_gather | solution.py:99
  9.3 7.1 %collective-permute-start = (bf16[2,15,1536]{2,1,0:T(8,128)(2,1)S(1)}, bf16[2,15,1536]{2,1,0:T(8,128)(2,1)S(1)}, u32[]{:S(2)}, u32[]{:S(2)}) collective-permute-start(bf16[2,15,1536]{2,1,0:T(8,128)(2,1)S(1)} %get-tuple-element.99), channel_id=1, source_target_pairs={{0,1},{1,2},{2,3},{4,5},{5,6},{6,7},{8,9},{9,10},{10,11},{12,13},{... | collective-permute-start | bytes 276488 | tf_op jit(solution)/shard_map/ppermute | solution.py:16
  14.2 6.5 %collective-permute-start.1 = (bf16[2,15,1536]{2,1,0:T(8,128)(2,1)S(1)}, bf16[2,15,1536]{2,1,0:T(8,128)(2,1)S(1)}, u32[]{:S(2)}, u32[]{:S(2)}) collective-permute-start(bf16[2,15,1536]{2,1,0:T(8,128)(2,1)S(1)} %get-tuple-element.100), channel_id=1, source_target_pairs={{1,0},{2,1},{3,2},{5,4},{6,5},{7,6},{9,8},{10,9},{11,10},{13,12},{... | collective-permute-start | bytes 276488 | tf_op jit(solution)/shard_map/ppermute | solution.py:17
  16.3 36.0 %copy-start.45 = (f32[1536]{0:T(1024)}, f32[1536]{0:T(1024)S(1)}, u32[]{:S(2)}) copy-start(f32[1536]{0:T(1024)S(1)} %get-tuple-element.64) | copy-start | bytes 18436
  16.3 36.0 %copy-start.47 = (f32[1536]{0:T(1024)}, f32[1536]{0:T(1024)S(1)}, u32[]{:S(2)}) copy-start(f32[1536]{0:T(1024)S(1)} %get-tuple-element.65) | copy-start | bytes 18436
  24.8 1.2 collective-permute-start.2
  26.1 3.8 %collective-permute-start.3 = (f32[2,1536]{1,0:T(2,128)S(1)}, f32[2,1536]{1,0:T(2,128)S(1)}, u32[]{:S(2)}, u32[]{:S(2)}) collective-permute-start(f32[2,1536]{1,0:T(2,128)S(1)} %pad_maximum_fusion.7), channel_id=1, source_target_pairs={{0,8},{4,12},{8,0},{12,4},{16,24},{20,28},{24,16},{28,20},{1,9},{5... | collective-permute-start | bytes 36872 | tf_op jit(solution)/shard_map/ppermute | solution.py:44
  29.9 3.8 %collective-permute-start.4 = (f32[2,1536]{1,0:T(2,128)S(1)}, f32[2,1536]{1,0:T(2,128)S(1)}, u32[]{:S(2)}, u32[]{:S(2)}) collective-permute-start(f32[2,1536]{1,0:T(2,128)S(1)} %pad_maximum_fusion.8), channel_id=1, source_target_pairs={{0,16},{4,20},{8,24},{12,28},{16,0},{20,4},{24,8},{28,12},{1,17},{... | collective-permute-start | bytes 36872 | tf_op jit(solution)/shard_map/ppermute | solution.py:44
  33.8 4.2 %collective-permute-start.5 = (f32[2,1536]{1,0:T(2,128)S(1)}, f32[2,1536]{1,0:T(2,128)S(1)}, u32[]{:S(2)}, u32[]{:S(2)}) collective-permute-start(f32[2,1536]{1,0:T(2,128)S(1)} %pad_maximum_fusion.9), channel_id=1, source_target_pairs={{0,1},{1,0},{2,3},{3,2},{4,5},{5,4},{6,7},{7,6},{8,9},{9,8},{10,11... | collective-permute-start | bytes 36872 | tf_op jit(solution)/shard_map/ppermute | solution.py:44
  38.0 5.4 %collective-permute-start.6 = (f32[2,1536]{1,0:T(2,128)S(1)}, f32[2,1536]{1,0:T(2,128)S(1)}, u32[]{:S(2)}, u32[]{:S(2)}) collective-permute-start(f32[2,1536]{1,0:T(2,128)S(1)} %pad_maximum_fusion.10), channel_id=1, source_target_pairs={{0,2},{1,3},{2,0},{3,1},{4,6},{5,7},{6,4},{7,5},{8,10},{9,11},{10,... | collective-permute-start | bytes 36872 | tf_op jit(solution)/shard_map/ppermute | solution.py:44
  79.3 4.7 %collective-permute-start.8 = (f32[2,1536]{1,0:T(2,128)S(1)}, f32[2,1536]{1,0:T(2,128)S(1)}, u32[]{:S(2)}, u32[]{:S(2)}) collective-permute-start(f32[2,1536]{1,0:T(2,128)S(1)} %pad_maximum_fusion.11), channel_id=1, source_target_pairs={{0,4},{4,0},{8,12},{12,8},{16,20},{20,16},{24,28},{28,24},{1,5},{5... | collective-permute-start | bytes 36872 | tf_op jit(solution)/shard_map/ppermute | solution.py:34
  80.2 21.3 %all-to-all-start.1 = ((bf16[128,4,384]{2,0,1:T(8,128)(2,1)}), bf16[128,4,384]{2,0,1:T(8,128)(2,1)S(1)}, u32[]{:S(2)}, u32[]{:S(2)}) async-start(bf16[128,4,384]{2,0,1:T(8,128)(2,1)} %copy.17), calls=%async_computation.1 | async-start | bytes 786432 | tf_op jit(solution)/shard_map/all_to_all | solution.py:128
  83.7 56.9 %all-gather.6.cloned.1.call-start = ((), (), s32[]{:S(2)}) async-start(), calls=%async_computation.3 | async-start | bytes 2949120 | tf_op jit(solution)/shard_map/all_gather | solution.py:81
  84.0 3.8 %collective-permute-start.9 = (f32[2,1536]{1,0:T(2,128)S(1)}, f32[2,1536]{1,0:T(2,128)S(1)}, u32[]{:S(2)}, u32[]{:S(2)}) collective-permute-start(f32[2,1536]{1,0:T(2,128)S(1)} %fusion.139), channel_id=1, source_target_pairs={{0,8},{4,12},{8,0},{12,4},{16,24},{20,28},{24,16},{28,20},{1,9},{5... | collective-permute-start | bytes 36872 | tf_op jit(solution)/shard_map/ppermute | solution.py:34
  87.8 3.8 %collective-permute-start.10 = (f32[2,1536]{1,0:T(2,128)S(1)}, f32[2,1536]{1,0:T(2,128)S(1)}, u32[]{:S(2)}, u32[]{:S(2)}) collective-permute-start(f32[2,1536]{1,0:T(2,128)S(1)} %fusion.155), channel_id=1, source_target_pairs={{0,16},{4,20},{8,24},{12,28},{16,0},{20,4},{24,8},{28,12},{1,17},{... | collective-permute-start | bytes 36872 | tf_op jit(solution)/shard_map/ppermute | solution.py:34
  91.5 3.8 %collective-permute-start.11 = (f32[2,1536]{1,0:T(2,128)S(1)}, f32[2,1536]{1,0:T(2,128)S(1)}, u32[]{:S(2)}, u32[]{:S(2)}) collective-permute-start(f32[2,1536]{1,0:T(2,128)S(1)} %add.496), channel_id=1, source_target_pairs={{0,1},{1,0},{2,3},{3,2},{4,5},{5,4},{6,7},{7,6},{8,9},{9,8},{10,11... | collective-permute-start | bytes 36872 | tf_op jit(solution)/shard_map/ppermute | solution.py:34
  95.3 6.2 %collective-permute-start.12 = (f32[2,1536]{1,0:T(2,128)S(1)}, f32[2,1536]{1,0:T(2,128)S(1)}, u32[]{:S(2)}, u32[]{:S(2)}) collective-permute-start(f32[2,1536]{1,0:T(2,128)S(1)} %add.497), channel_id=1, source_target_pairs={{0,2},{1,3},{2,0},{3,1},{4,6},{5,7},{6,4},{7,5},{8,10},{9,11},{10,... | collective-permute-start | bytes 36872 | tf_op jit(solution)/shard_map/ppermute | solution.py:34
  103.9 3.8 %collective-permute-start.15 = (f32[192,1536]{1,0:T(8,128)S(1)}, f32[192,1536]{1,0:T(8,128)S(1)}, u32[]{:S(2)}, u32[]{:S(2)}) collective-permute-start(f32[192,1536]{1,0:T(8,128)S(1)} %constant_dynamic-slice_fusion.2), channel_id=1, source_target_pairs={{0,4},{4,0},{8,12},{12,8},{16,20},{20,16},{24,28},{28,24},{1,5},{5... | collective-permute-start | bytes 3538952 | tf_op jit(solution)/shard_map/ppermute | solution.py:65
  109.7 33.8 %collective-permute-start.16 = (f32[96,1536]{1,0:T(8,128)}, f32[96,1536]{1,0:T(8,128)}, u32[]{:S(2)}, u32[]{:S(2)}) collective-permute-start(f32[96,1536]{1,0:T(8,128)} %constant_dynamic-slice_fusion.1), channel_id=1, source_target_pairs={{0,8},{4,12},{8,0},{12,4},{16,24},{20,28},{24,16},{28,20},{1,9},{5... | collective-permute-start | bytes 1769480 | tf_op jit(solution)/shard_map/ppermute | solution.py:65
  121.0 19.7 %collective-permute-start.21 = (f32[31,1536]{1,0:T(8,128)S(1)}, f32[31,1536]{1,0:T(8,128)S(1)}, u32[]{:S(2)}, u32[]{:S(2)}) collective-permute-start(f32[31,1536]{1,0:T(8,128)S(1)} %stack.172), channel_id=1, source_target_pairs={{0,1},{1,0},{2,3},{3,2},{4,5},{5,4},{6,7},{7,6},{8,9},{9,8},{10,11... | collective-permute-start | bytes 571400 | tf_op jit(solution)/shard_map/ppermute | solution.py:34
  140.7 39.0 %collective-permute-start.7 = (bf16[4,192,1536]{2,1,0:T(8,128)(2,1)}, bf16[4,192,1536]{2,1,0:T(8,128)(2,1)S(1)}, u32[]{:S(2)}, u32[]{:S(2)}) collective-permute-start(bf16[4,192,1536]{2,1,0:T(8,128)(2,1)} %bitcast.18), channel_id=1, source_target_pairs={{0,4},{4,0},{8,12},{12,8},{16,20},{20,16},{24,28},{28,24},{1,5},{5... | collective-permute-start | bytes 7077896 | tf_op jit(solution)/shard_map/ppermute | solution.py:82
  140.7 12.9 %collective-permute-start.22 = (f32[31,1536]{1,0:T(8,128)S(1)}, f32[31,1536]{1,0:T(8,128)S(1)}, u32[]{:S(2)}, u32[]{:S(2)}) collective-permute-start(f32[31,1536]{1,0:T(8,128)S(1)} %add.537), channel_id=1, source_target_pairs={{0,2},{1,3},{2,0},{3,1},{4,6},{5,7},{6,4},{7,5},{8,10},{9,11},{10,... | collective-permute-start | bytes 571400 | tf_op jit(solution)/shard_map/ppermute | solution.py:34
  145.0 9.2 %collective-permute-start.17 = (f32[48,1536]{1,0:T(8,128)S(1)}, f32[48,1536]{1,0:T(8,128)S(1)}, u32[]{:S(2)}, u32[]{:S(2)}) collective-permute-start(f32[48,1536]{1,0:T(8,128)S(1)} %constant_dynamic-slice_fusion), channel_id=1, source_target_pairs={{0,16},{4,20},{8,24},{12,28},{16,0},{20,4},{24,8},{28,12},{1,17},{... | collective-permute-start | bytes 884744 | tf_op jit(solution)/shard_map/ppermute | solution.py:65
  146.5 9.2 %collective-permute-start.13 = (bf16[2,15,1536]{2,1,0:T(8,128)(2,1)S(1)}, bf16[2,15,1536]{2,1,0:T(8,128)(2,1)S(1)}, u32[]{:S(2)}, u32[]{:S(2)}) collective-permute-start(bf16[2,15,1536]{2,1,0:T(8,128)(2,1)S(1)} %get-tuple-element.97), channel_id=1, source_target_pairs={{1,0},{2,1},{3,2},{5,4},{6,5},{7,6},{9,8},{10,9},{11,10},{13,12},{... | collective-permute-start | bytes 276488 | tf_op jit(solution)/shard_map/ppermute | solution.py:17
  147.8 7.9 %collective-permute-start.14 = (bf16[2,15,1536]{2,1,0:T(8,128)(2,1)S(1)}, bf16[2,15,1536]{2,1,0:T(8,128)(2,1)S(1)}, u32[]{:S(2)}, u32[]{:S(2)}) collective-permute-start(bf16[2,15,1536]{2,1,0:T(8,128)(2,1)S(1)} %get-tuple-element.98), channel_id=1, source_target_pairs={{0,1},{1,2},{2,3},{4,5},{5,6},{6,7},{8,9},{9,10},{10,11},{12,13},{... | collective-permute-start | bytes 276488 | tf_op jit(solution)/shard_map/ppermute | solution.py:16
  153.6 6.5 %collective-permute-start.23 = (f32[31,1536]{1,0:T(8,128)S(1)}, f32[31,1536]{1,0:T(8,128)S(1)}, u32[]{:S(2)}, u32[]{:S(2)}) collective-permute-start(f32[31,1536]{1,0:T(8,128)S(1)} %add.538), channel_id=1, source_target_pairs={{0,4},{4,0},{8,12},{12,8},{16,20},{20,16},{24,28},{28,24},{1,5},{5... | collective-permute-start | bytes 571400 | tf_op jit(solution)/shard_map/ppermute | solution.py:34
  154.2 9.0 %collective-permute-start.18 = (f32[48,1536]{1,0:T(8,128)S(1)}, f32[48,1536]{1,0:T(8,128)S(1)}, u32[]{:S(2)}, u32[]{:S(2)}) collective-permute-start(f32[48,1536]{1,0:T(8,128)S(1)} %dynamic-slice_add_fusion.2), channel_id=1, source_target_pairs={{0,16},{4,20},{8,24},{12,28},{16,0},{20,4},{24,8},{28,12},{1,17},{... | collective-permute-start | bytes 884744 | tf_op jit(solution)/shard_map/ppermute | solution.py:69
  160.2 7.9 %collective-permute-start.24 = (f32[31,1536]{1,0:T(8,128)S(1)}, f32[31,1536]{1,0:T(8,128)S(1)}, u32[]{:S(2)}, u32[]{:S(2)}) collective-permute-start(f32[31,1536]{1,0:T(8,128)S(1)} %add.539), channel_id=1, source_target_pairs={{0,8},{4,12},{8,0},{12,4},{16,24},{20,28},{24,16},{28,20},{1,9},{5... | collective-permute-start | bytes 571400 | tf_op jit(solution)/shard_map/ppermute | solution.py:34
  163.3 16.2 %collective-permute-start.19 = (f32[96,1536]{1,0:T(8,128)S(1)}, f32[96,1536]{1,0:T(8,128)S(1)}, u32[]{:S(2)}, u32[]{:S(2)}) collective-permute-start(f32[96,1536]{1,0:T(8,128)S(1)} %maximum_select_fusion.2), channel_id=1, source_target_pairs={{0,8},{4,12},{8,0},{12,4},{16,24},{20,28},{24,16},{28,20},{1,9},{5... | collective-permute-start | bytes 1769480 | tf_op jit(solution)/shard_map/ppermute | solution.py:69
  168.1 5.7 %collective-permute-start.25 = (f32[31,1536]{1,0:T(8,128)S(1)}, f32[31,1536]{1,0:T(8,128)S(1)}, u32[]{:S(2)}, u32[]{:S(2)}) collective-permute-start(f32[31,1536]{1,0:T(8,128)S(1)} %add.540), channel_id=1, source_target_pairs={{0,16},{4,20},{8,24},{12,28},{16,0},{20,4},{24,8},{28,12},{1,17},{... | collective-permute-start | bytes 571400 | tf_op jit(solution)/shard_map/ppermute | solution.py:34
  179.5 2.9 %collective-permute-start.20 = (f32[192,1536]{1,0:T(8,128)S(1)}, f32[192,1536]{1,0:T(8,128)S(1)}, u32[]{:S(2)}, u32[]{:S(2)}) collective-permute-start(f32[192,1536]{1,0:T(8,128)S(1)} %maximum_select_fusion.1), channel_id=1, source_target_pairs={{0,4},{4,0},{8,12},{12,8},{16,20},{20,16},{24,28},{28,24},{1,5},{5... | collective-permute-start | bytes 3538952 | tf_op jit(solution)/shard_map/ppermute | solution.py:69
  (68 other events, 1179.2 us)
Sparse Core Ops, SparseCore 0:
  9.6 40.3 all-gather.3
  86.5 54.1 all-gather.5

commit v19 on v13

--- a/solution.py
+++ b/solution.py
@@ -56,15 +56,15 @@
         return lax.psum(x, axis)
     me = lax.axis_index(axis)
     bits = []
-    step = 1
-    while step < peers:
+    step = peers // 2
+    while step >= 1:
         bit = lax.rem(me // step, 2)
         half = x.shape[0] // 2
         keep = lax.dynamic_slice_in_dim(x, bit * half, half, axis=0)
         give = lax.dynamic_slice_in_dim(x, (1 - bit) * half, half, axis=0)
         x = keep + lax.ppermute(give, axis, [(i, i ^ step) for i in range(peers)])
         bits.append((step, bit))
-        step *= 2
+        step //= 2
     for step, bit in reversed(bits):
         other = lax.ppermute(x, axis, [(i, i ^ step) for i in range(peers)])
         x = jnp.where(bit == 0, jnp.concatenate([x, other]), jnp.concatenate([other, x]))

time: 187 us -> 213 us (1.14)
  waiting for transfers between devices: 63.3 us -> 84.5 us
  starting transfers between devices: 40.8 us -> 46.3 us
    ppermute x3, waiting for transfers between devices: 1.12 us -> 18.6 us  [rows_sum(): x = keep + lax.ppermute(give, axis, [(i, i ^ step) for i in range(peers)])]
    all_gather x1, waiting for transfers between devices: 17.2 us -> 0.02 us  [gather_weight(): held = lax.all_gather(mine, 'tensor', axis=0, tiled=False)]
    ppermute x3, waiting for transfers between devices: 6.13 us -> 23 us  [rows_sum(): other = lax.ppermute(x, axis, [(i, i ^ step) for i in range(peers)])]
    ppermute x10, starting transfers between devices: 11.8 us -> 15.3 us  [all_sum(): x = x + lax.ppermute(x, axis, [(i, i ^ step) for i in range(peers)])]
    ppermute x10, waiting for transfers between devices: 17.1 us -> 20.1 us  [all_sum(): x = x + lax.ppermute(x, axis, [(i, i ^ step) for i in range(peers)])]
  transfers between devices with their start and end apart: 29 -> 29, of which waited for: 19 -> 19; matrix products, arithmetic and copies ran while one was open for 18% -> 16% of each run, Pallas kernels for 0% -> 0%
where the time goes in v19:
time: 213 us
  waiting for transfers between devices  84.5 us (40%)
  starting transfers between devices  46.3 us (22%)
  other arithmetic  22.9 us (11%)
  blocking collectives  22.6 us (11%)
  between operations  15.6 us (7%)
  local copies, waits for them, and re-layouts  14.4 us (7%)
  matrix products  6.15 us (3%)
    ppermute x3, waiting for transfers between devices, rows_sum(): other = lax.ppermute(x, axis, [(i, i ^ step) for i in range(peers)])  23 us
    all_to_all x1, blocking collectives, on_device(): lax.all_to_all(own_columns, 'tensor', split_axis=0, concat_axis=1, tiled=...  22.6 us
    ppermute x10, waiting for transfers between devices, all_sum(): x = x + lax.ppermute(x, axis, [(i, i ^ step) for i in range(peers)])  20.1 us
    ppermute x3, waiting for transfers between devices, rows_sum(): x = keep + lax.ppermute(give, axis, [(i, i ^ step) for i in range(peers)])  18.6 us
    ppermute x10, starting transfers between devices, all_sum(): x = x + lax.ppermute(x, axis, [(i, i ^ step) for i in range(peers)])  15.3 us
    ppermute x5, waiting for transfers between devices, all_moments(): lax.ppermute(jnp.stack([mean, spread]), axis, [(i, i ^ step) for i in ran...  10.9 us
    ppermute x2, starting transfers between devices, extended(): before = lax.ppermute(last, axis, up)  10.2 us
    another operation x32, local copies, waits for them, and re-layouts, on_device(): jnp.stack([jnp.sum(padded[:, offset:offset + frames, :].astype(jnp.float3...  7.97 us
  transfers between devices with their start and end apart: 29, of which 19 were waited for; matrix products, arithmetic and copies ran while one was open for 16% of the time, Pallas kernels for 0%

profile of v19, /device:TPU:0, one launch (start us, length us, event | category | flops | bytes accessed | tf_op | source)
XLA Modules:
  0.0 212.5 jit_solution(14823030980121296749)
XLA Ops:
  9.3 4.9 %collective-permute-start = (bf16[2,15,1536]{2,1,0:T(8,128)(2,1)S(1)}, bf16[2,15,1536]{2,1,0:T(8,128)(2,1)S(1)}, u32[]{:S(2)}, u32[]{:S(2)}) collective-permute-start(bf16[2,15,1536]{2,1,0:T(8,128)(2,1)S(1)} %get-tuple-element.99), channel_id=1, source_target_pairs={{0,1},{1,2},{2,3},{4,5},{5,6},{6,7},{8,9},{9,10},{10,11},{12,13},{... | collective-permute-start | bytes 276488 | tf_op jit(solution)/shard_map/ppermute | solution.py:16
  16.4 4.3 %collective-permute-done.1 = bf16[2,15,1536]{2,1,0:T(8,128)(2,1)S(1)} collective-permute-done((bf16[2,15,1536]{2,1,0:T(8,128)(2,1)S(1)}, bf16[2,15,1536]{2,1,0:T(8,128)(2,1)S(1)}, u32[]{:S(2)}, u32[]{:S(2)}) %collective-permute-start.1) | collective-permute-done | bytes 92192 | tf_op jit(solution)/shard_map/ppermute | solution.py:17
  20.7 3.8 %fusion.143 = (f32[1536]{0:T(1024)S(1)}, f32[2,64,1536]{2,1,0:T(8,128)S(1)}) fusion(bf16[2,15,1536]{2,1,0:T(8,128)(2,1)S(1)} %collective-permute-done.1, bf16[2,64,1536]{2,1,0:T(8,128)(2,1)S(1)} %fusion, f32[1536]{0:T(1024)S(1)} %get-tuple-element.72, f32[1536]{0:T(1024)S(1)} %get-tuple-element.73, f32[1536]{0:T(1024)S(1)} %get-tuple-element.44, ...), kind=kLoop, calls=%fused_computation.380 | loop fusion | flops 35977728 | bytes 1560576 | tf_op jit(solution)/shard_map/reduce_sum | solution.py:107
  27.7 2.2 %collective-permute-done.3 = f32[2,1536]{1,0:T(2,128)S(1)} collective-permute-done((f32[2,1536]{1,0:T(2,128)S(1)}, f32[2,1536]{1,0:T(2,128)S(1)}, u32[]{:S(2)}, u32[]{:S(2)}) %collective-permute-start.3) | collective-permute-done | bytes 12320 | tf_op jit(solution)/shard_map/ppermute | solution.py:44
  29.9 1.6 collective-permute-start.4
  31.5 2.2 %collective-permute-done.4 = f32[2,1536]{1,0:T(2,128)S(1)} collective-permute-done((f32[2,1536]{1,0:T(2,128)S(1)}, f32[2,1536]{1,0:T(2,128)S(1)}, u32[]{:S(2)}, u32[]{:S(2)}) %collective-permute-start.4) | collective-permute-done | bytes 12320 | tf_op jit(solution)/shard_map/ppermute | solution.py:44
  33.8 1.6 collective-permute-start.5
  35.4 2.5 %collective-permute-done.5 = f32[2,1536]{1,0:T(2,128)S(1)} collective-permute-done((f32[2,1536]{1,0:T(2,128)S(1)}, f32[2,1536]{1,0:T(2,128)S(1)}, u32[]{:S(2)}, u32[]{:S(2)}) %collective-permute-start.5) | collective-permute-done | bytes 12320 | tf_op jit(solution)/shard_map/ppermute | solution.py:44
  38.0 2.5 %collective-permute-start.6 = (f32[2,1536]{1,0:T(2,128)S(1)}, f32[2,1536]{1,0:T(2,128)S(1)}, u32[]{:S(2)}, u32[]{:S(2)}) collective-permute-start(f32[2,1536]{1,0:T(2,128)S(1)} %pad_maximum_fusion.10), channel_id=1, source_target_pairs={{0,2},{1,3},{2,0},{3,1},{4,6},{5,7},{6,4},{7,5},{8,10},{9,11},{10,... | collective-permute-start | bytes 36872 | tf_op jit(solution)/shard_map/ppermute | solution.py:44
  40.5 2.9 %collective-permute-done.6 = f32[2,1536]{1,0:T(2,128)S(1)} collective-permute-done((f32[2,1536]{1,0:T(2,128)S(1)}, f32[2,1536]{1,0:T(2,128)S(1)}, u32[]{:S(2)}, u32[]{:S(2)}) %collective-permute-start.6) | collective-permute-done | bytes 12320 | tf_op jit(solution)/shard_map/ppermute | solution.py:44
  44.2 5.8 %all-gather.4.cloned.1.call-done = bf16[512,1536]{1,0:T(8,128)(2,1)} async-done(((bf16[128,1536]{1,0:T(8,128)(2,1)}), bf16[512,1536]{1,0:T(8,128)(2,1)}) %all-gather.4.cloned.1.call-update) | async-done | bytes 1572880 | tf_op jit(solution)/shard_map/all_gather | solution.py:99
  50.0 2.4 %fusion.147 = f32[512,384]{1,0:T(8,128)S(1)} fusion(bf16[512,1536]{1,0:T(8,128)(2,1)} %all-gather.4.cloned.1.call-done, bf16[384,1536]{1,0:T(8,128)(2,1)S(1)} %copy-done), kind=kOutput, calls=%fused_computation.383 | convolution fusion | flops 603979776 | bytes 3538944 | tf_op jit(solution)/shard_map/fd,cd->fc/dot_general | solution.py:118
  52.4 22.6 %all_to_all.35 = f32[4,128,384]{2,1,0:T(8,128)S(1)} all-to-all(f32[4,128,384]{2,1,0:T(8,128)S(1)} %bitcast.21), channel_id=1, replica_groups=mesh['dp'=8,'tensor'=4] {'tensor'}, dimensions={0} | all-to-all | bytes 1572864 | tf_op jit(solution)/shard_map/all_to_all | solution.py:119
  76.8 2.4 %fusion.140 = (f32[1536]{0:T(1024)S(1)}, f32[1536]{0:T(1024)S(1)}, f32[2,64,1536]{2,1,0:T(8,128)}, bf16[2,64,1536]{2,1,0:T(8,128)(2,1)S(1)}) fusion(f32[1536]{0:T(1024)S(1)} %get-tuple-element.90, f32[2,64,1536]{2,1,0:T(8,128)S(1)} %get-tuple-element.93, f32[1536]{0:T(1024)S(1)} %get-tuple-element.8, f32[2,64,1536]{2,1,0:T(8,128)} %reshape.189, ...), kind=kLoop, calls=%fused_computation.378 | loop fusion | flops 3142656 | bytes 2789376 | tf_op jit(solution)/shard_map/reduce_sum | solution.py:131
  80.2 3.5 %all-to-all-start.1 = ((bf16[128,4,384]{2,0,1:T(8,128)(2,1)}), bf16[128,4,384]{2,0,1:T(8,128)(2,1)S(1)}, u32[]{:S(2)}, u32[]{:S(2)}) async-start(bf16[128,4,384]{2,0,1:T(8,128)(2,1)} %copy.17), calls=%async_computation.1 | async-start | bytes 786432 | tf_op jit(solution)/shard_map/all_to_all | solution.py:128
  89.3 2.2 %collective-permute-done.10 = f32[2,1536]{1,0:T(2,128)S(1)} collective-permute-done((f32[2,1536]{1,0:T(2,128)S(1)}, f32[2,1536]{1,0:T(2,128)S(1)}, u32[]{:S(2)}, u32[]{:S(2)}) %collective-permute-start.10) | collective-permute-done | bytes 12320 | tf_op jit(solution)/shard_map/ppermute | solution.py:34
  91.5 1.8 collective-permute-start.11
  93.3 1.9 collective-permute-done.11
  95.3 2.7 %collective-permute-start.12 = (f32[2,1536]{1,0:T(2,128)S(1)}, f32[2,1536]{1,0:T(2,128)S(1)}, u32[]{:S(2)}, u32[]{:S(2)}) collective-permute-start(f32[2,1536]{1,0:T(2,128)S(1)} %add.499), channel_id=1, source_target_pairs={{0,2},{1,3},{2,0},{3,1},{4,6},{5,7},{6,4},{7,5},{8,10},{9,11},{10,... | collective-permute-start | bytes 36872 | tf_op jit(solution)/shard_map/ppermute | solution.py:34
  98.0 3.5 %collective-permute-done.12 = f32[2,1536]{1,0:T(2,128)S(1)} collective-permute-done((f32[2,1536]{1,0:T(2,128)S(1)}, f32[2,1536]{1,0:T(2,128)S(1)}, u32[]{:S(2)}, u32[]{:S(2)}) %collective-permute-start.12) | collective-permute-done | bytes 12320 | tf_op jit(solution)/shard_map/ppermute | solution.py:34
  101.6 2.2 %fusion.148 = f32[384,1536]{1,0:T(8,128)S(1)} fusion(bf16[512,384]{1,0:T(8,128)(2,1)S(1)} %bitcast.20, bf16[512,1536]{1,0:T(8,128)(2,1)} %all-gather.4.cloned.1.call-done), kind=kOutput, calls=%fused_computation.384 | convolution fusion | flops 603979776 | bytes 4325376 | tf_op jit(solution)/shard_map/fc,fd->cd/dot_general | solution.py:129
  108.3 18.6 %collective-permute-done.15 = f32[192,1536]{1,0:T(8,128)S(1)} collective-permute-done((f32[192,1536]{1,0:T(8,128)S(1)}, f32[192,1536]{1,0:T(8,128)S(1)}, u32[]{:S(2)}, u32[]{:S(2)}) %collective-permute-start.15) | collective-permute-done | bytes 1179680 | tf_op jit(solution)/shard_map/ppermute | solution.py:65
  137.7 2.5 %stack.172 = f32[31,1536]{1,0:T(8,128)S(1)} concatenate(f32[1,1536]{1,0:T(1,128)} %stack.141, f32[1,1536]{1,0:T(1,128)} %stack.142, f32[1,1536]{1,0:T(1,128)} %stack.143, f32[1,1536]{1,0:T(1,128)} %stack.144, f32[1,1536]{1,0:T(1,128)} %stack.145, f32[1,1536]{1,0:T(1,128)S(1)} %stack.146, f32[1,1536]{1,0:T(1,128)S(1)} %stack.147, f32[1,1536]{1,0:T(1,128)S(1)} %stack.148, ...), dimensions={0} | concatenate | bytes 380928 | tf_op jit(solution)/shard_map/stack | solution.py:145
  145.2 5.3 %collective-permute-start.14 = (bf16[2,15,1536]{2,1,0:T(8,128)(2,1)S(1)}, bf16[2,15,1536]{2,1,0:T(8,128)(2,1)S(1)}, u32[]{:S(2)}, u32[]{:S(2)}) collective-permute-start(bf16[2,15,1536]{2,1,0:T(8,128)(2,1)S(1)} %get-tuple-element.98), channel_id=1, source_target_pairs={{0,1},{1,2},{2,3},{4,5},{5,6},{6,7},{8,9},{9,10},{10,11},{12,13},{... | collective-permute-start | bytes 276488 | tf_op jit(solution)/shard_map/ppermute | solution.py:16
  153.4 4.1 %multiply_convert_fusion = (bf16[2,64,1536]{2,1,0:T(8,128)(2,1)S(1)}, f32[2,64,1536]{2,1,0:T(8,128)S(1)}) fusion(bf16[2,64,3072]{2,1,0:T(8,128)(2,1)S(1)} %copy-done.1, bf16[2,64,1536]{2,1,0:T(8,128)(2,1)S(1)} %get-tuple-element.86, bf16[2,15,1536]{2,1,0:T(8,128)(2,1)S(1)} %collective-permute-done.14, f32[1536]{0:T(1024)S(1)} %copy-done.62, ...), kind=kLoop, calls=%fused_computation.210 | loop fusion | flops 36962304 | bytes 2340864 | tf_op jit(solution)/shard_map/convert
  157.6 2.5 %collective-permute-start.24 = (f32[31,1536]{1,0:T(8,128)S(1)}, f32[31,1536]{1,0:T(8,128)S(1)}, u32[]{:S(2)}, u32[]{:S(2)}) collective-permute-start(f32[31,1536]{1,0:T(8,128)S(1)} %add.542), channel_id=1, source_target_pairs={{0,1},{1,0},{2,3},{3,2},{4,5},{5,4},{6,7},{7,6},{8,9},{9,8},{10,11... | collective-permute-start | bytes 571400 | tf_op jit(solution)/shard_map/ppermute | solution.py:34
  161.9 2.9 %collective-permute-done.24 = f32[31,1536]{1,0:T(8,128)S(1)} collective-permute-done((f32[31,1536]{1,0:T(8,128)S(1)}, f32[31,1536]{1,0:T(8,128)S(1)}, u32[]{:S(2)}, u32[]{:S(2)}) %collective-permute-start.24) | collective-permute-done | bytes 190496 | tf_op jit(solution)/shard_map/ppermute | solution.py:34
  164.9 3.0 %collective-permute-start.25 = (f32[31,1536]{1,0:T(8,128)S(1)}, f32[31,1536]{1,0:T(8,128)S(1)}, u32[]{:S(2)}, u32[]{:S(2)}) collective-permute-start(f32[31,1536]{1,0:T(8,128)S(1)} %add.543), channel_id=1, source_target_pairs={{0,2},{1,3},{2,0},{3,1},{4,6},{5,7},{6,4},{7,5},{8,10},{9,11},{10,... | collective-permute-start | bytes 571400 | tf_op jit(solution)/shard_map/ppermute | solution.py:34
  168.8 7.2 %collective-permute-done.25 = f32[31,1536]{1,0:T(8,128)S(1)} collective-permute-done((f32[31,1536]{1,0:T(8,128)S(1)}, f32[31,1536]{1,0:T(8,128)S(1)}, u32[]{:S(2)}, u32[]{:S(2)}) %collective-permute-start.25) | collective-permute-done | bytes 190496 | tf_op jit(solution)/shard_map/ppermute | solution.py:34
  176.8 2.0 collective-permute-start.20
  181.0 23.0 %collective-permute-done.20 = f32[192,1536]{1,0:T(8,128)S(1)} collective-permute-done((f32[192,1536]{1,0:T(8,128)S(1)}, f32[192,1536]{1,0:T(8,128)S(1)}, u32[]{:S(2)}, u32[]{:S(2)}) %collective-permute-start.20) | collective-permute-done | bytes 1179680 | tf_op jit(solution)/shard_map/ppermute | solution.py:69
  204.0 1.6 maximum_select_fusion
  (266 shorter events, 44.5 us)
Async XLA Ops:
  7.2 42.8 %copy-start = (bf16[384,1536]{1,0:T(8,128)(2,1)S(1)}, bf16[384,1536]{1,0:T(8,128)(2,1)}, u32[]{:S(2)}) copy-start(bf16[384,1536]{1,0:T(8,128)(2,1)} %param.10) | copy-start | bytes 3538948
  7.2 42.8 %all-gather.4.cloned.1.call-start = ((), (), s32[]{:S(2)}) async-start(), calls=%async_computation.2 | async-start | bytes 1966080 | tf_op jit(solution)/shard_map/all_gather | solution.py:99
  9.3 7.1 %collective-permute-start = (bf16[2,15,1536]{2,1,0:T(8,128)(2,1)S(1)}, bf16[2,15,1536]{2,1,0:T(8,128)(2,1)S(1)}, u32[]{:S(2)}, u32[]{:S(2)}) collective-permute-start(bf16[2,15,1536]{2,1,0:T(8,128)(2,1)S(1)} %get-tuple-element.99), channel_id=1, source_target_pairs={{0,1},{1,2},{2,3},{4,5},{5,6},{6,7},{8,9},{9,10},{10,11},{12,13},{... | collective-permute-start | bytes 276488 | tf_op jit(solution)/shard_map/ppermute | solution.py:16
  14.2 6.5 %collective-permute-start.1 = (bf16[2,15,1536]{2,1,0:T(8,128)(2,1)S(1)}, bf16[2,15,1536]{2,1,0:T(8,128)(2,1)S(1)}, u32[]{:S(2)}, u32[]{:S(2)}) collective-permute-start(bf16[2,15,1536]{2,1,0:T(8,128)(2,1)S(1)} %get-tuple-element.100), channel_id=1, source_target_pairs={{1,0},{2,1},{3,2},{5,4},{6,5},{7,6},{9,8},{10,9},{11,10},{13,12},{... | collective-permute-start | bytes 276488 | tf_op jit(solution)/shard_map/ppermute | solution.py:17
  16.3 36.0 %copy-start.45 = (f32[1536]{0:T(1024)}, f32[1536]{0:T(1024)S(1)}, u32[]{:S(2)}) copy-start(f32[1536]{0:T(1024)S(1)} %get-tuple-element.64) | copy-start | bytes 18436
  16.3 36.0 %copy-start.47 = (f32[1536]{0:T(1024)}, f32[1536]{0:T(1024)S(1)}, u32[]{:S(2)}) copy-start(f32[1536]{0:T(1024)S(1)} %get-tuple-element.65) | copy-start | bytes 18436
  24.8 1.2 collective-permute-start.2
  26.1 3.8 %collective-permute-start.3 = (f32[2,1536]{1,0:T(2,128)S(1)}, f32[2,1536]{1,0:T(2,128)S(1)}, u32[]{:S(2)}, u32[]{:S(2)}) collective-permute-start(f32[2,1536]{1,0:T(2,128)S(1)} %pad_maximum_fusion.7), channel_id=1, source_target_pairs={{0,8},{4,12},{8,0},{12,4},{16,24},{20,28},{24,16},{28,20},{1,9},{5... | collective-permute-start | bytes 36872 | tf_op jit(solution)/shard_map/ppermute | solution.py:44
  29.9 3.8 %collective-permute-start.4 = (f32[2,1536]{1,0:T(2,128)S(1)}, f32[2,1536]{1,0:T(2,128)S(1)}, u32[]{:S(2)}, u32[]{:S(2)}) collective-permute-start(f32[2,1536]{1,0:T(2,128)S(1)} %pad_maximum_fusion.8), channel_id=1, source_target_pairs={{0,16},{4,20},{8,24},{12,28},{16,0},{20,4},{24,8},{28,12},{1,17},{... | collective-permute-start | bytes 36872 | tf_op jit(solution)/shard_map/ppermute | solution.py:44
  33.8 4.2 %collective-permute-start.5 = (f32[2,1536]{1,0:T(2,128)S(1)}, f32[2,1536]{1,0:T(2,128)S(1)}, u32[]{:S(2)}, u32[]{:S(2)}) collective-permute-start(f32[2,1536]{1,0:T(2,128)S(1)} %pad_maximum_fusion.9), channel_id=1, source_target_pairs={{0,1},{1,0},{2,3},{3,2},{4,5},{5,4},{6,7},{7,6},{8,9},{9,8},{10,11... | collective-permute-start | bytes 36872 | tf_op jit(solution)/shard_map/ppermute | solution.py:44
  38.0 5.4 %collective-permute-start.6 = (f32[2,1536]{1,0:T(2,128)S(1)}, f32[2,1536]{1,0:T(2,128)S(1)}, u32[]{:S(2)}, u32[]{:S(2)}) collective-permute-start(f32[2,1536]{1,0:T(2,128)S(1)} %pad_maximum_fusion.10), channel_id=1, source_target_pairs={{0,2},{1,3},{2,0},{3,1},{4,6},{5,7},{6,4},{7,5},{8,10},{9,11},{10,... | collective-permute-start | bytes 36872 | tf_op jit(solution)/shard_map/ppermute | solution.py:44
  79.3 4.7 %collective-permute-start.8 = (f32[2,1536]{1,0:T(2,128)S(1)}, f32[2,1536]{1,0:T(2,128)S(1)}, u32[]{:S(2)}, u32[]{:S(2)}) collective-permute-start(f32[2,1536]{1,0:T(2,128)S(1)} %pad_maximum_fusion.11), channel_id=1, source_target_pairs={{0,4},{4,0},{8,12},{12,8},{16,20},{20,16},{24,28},{28,24},{1,5},{5... | collective-permute-start | bytes 36872 | tf_op jit(solution)/shard_map/ppermute | solution.py:34
  80.2 21.3 %all-to-all-start.1 = ((bf16[128,4,384]{2,0,1:T(8,128)(2,1)}), bf16[128,4,384]{2,0,1:T(8,128)(2,1)S(1)}, u32[]{:S(2)}, u32[]{:S(2)}) async-start(bf16[128,4,384]{2,0,1:T(8,128)(2,1)} %copy.17), calls=%async_computation.1 | async-start | bytes 786432 | tf_op jit(solution)/shard_map/all_to_all | solution.py:128
  83.7 56.6 %all-gather.6.cloned.1.call-start = ((), (), s32[]{:S(2)}) async-start(), calls=%async_computation.3 | async-start | bytes 2949120 | tf_op jit(solution)/shard_map/all_gather | solution.py:81
  84.0 3.8 %collective-permute-start.9 = (f32[2,1536]{1,0:T(2,128)S(1)}, f32[2,1536]{1,0:T(2,128)S(1)}, u32[]{:S(2)}, u32[]{:S(2)}) collective-permute-start(f32[2,1536]{1,0:T(2,128)S(1)} %fusion.139), channel_id=1, source_target_pairs={{0,8},{4,12},{8,0},{12,4},{16,24},{20,28},{24,16},{28,20},{1,9},{5... | collective-permute-start | bytes 36872 | tf_op jit(solution)/shard_map/ppermute | solution.py:34
  87.8 3.8 %collective-permute-start.10 = (f32[2,1536]{1,0:T(2,128)S(1)}, f32[2,1536]{1,0:T(2,128)S(1)}, u32[]{:S(2)}, u32[]{:S(2)}) collective-permute-start(f32[2,1536]{1,0:T(2,128)S(1)} %fusion.155), channel_id=1, source_target_pairs={{0,16},{4,20},{8,24},{12,28},{16,0},{20,4},{24,8},{28,12},{1,17},{... | collective-permute-start | bytes 36872 | tf_op jit(solution)/shard_map/ppermute | solution.py:34
  91.5 3.8 %collective-permute-start.11 = (f32[2,1536]{1,0:T(2,128)S(1)}, f32[2,1536]{1,0:T(2,128)S(1)}, u32[]{:S(2)}, u32[]{:S(2)}) collective-permute-start(f32[2,1536]{1,0:T(2,128)S(1)} %add.498), channel_id=1, source_target_pairs={{0,1},{1,0},{2,3},{3,2},{4,5},{5,4},{6,7},{7,6},{8,9},{9,8},{10,11... | collective-permute-start | bytes 36872 | tf_op jit(solution)/shard_map/ppermute | solution.py:34
  95.3 6.2 %collective-permute-start.12 = (f32[2,1536]{1,0:T(2,128)S(1)}, f32[2,1536]{1,0:T(2,128)S(1)}, u32[]{:S(2)}, u32[]{:S(2)}) collective-permute-start(f32[2,1536]{1,0:T(2,128)S(1)} %add.499), channel_id=1, source_target_pairs={{0,2},{1,3},{2,0},{3,1},{4,6},{5,7},{6,4},{7,5},{8,10},{9,11},{10,... | collective-permute-start | bytes 36872 | tf_op jit(solution)/shard_map/ppermute | solution.py:34
  103.9 23.0 %collective-permute-start.15 = (f32[192,1536]{1,0:T(8,128)S(1)}, f32[192,1536]{1,0:T(8,128)S(1)}, u32[]{:S(2)}, u32[]{:S(2)}) collective-permute-start(f32[192,1536]{1,0:T(8,128)S(1)} %constant_dynamic-slice_fusion.2), channel_id=1, source_target_pairs={{0,16},{4,20},{8,24},{12,28},{16,0},{20,4},{24,8},{28,12},{1,17},{... | collective-permute-start | bytes 3538952 | tf_op jit(solution)/shard_map/ppermute | solution.py:65
  128.9 13.4 %collective-permute-start.16 = (f32[96,1536]{1,0:T(8,128)}, f32[96,1536]{1,0:T(8,128)}, u32[]{:S(2)}, u32[]{:S(2)}) collective-permute-start(f32[96,1536]{1,0:T(8,128)} %constant_dynamic-slice_fusion.1), channel_id=1, source_target_pairs={{0,8},{4,12},{8,0},{12,4},{16,24},{20,28},{24,16},{28,20},{1,9},{5... | collective-permute-start | bytes 1769480 | tf_op jit(solution)/shard_map/ppermute | solution.py:65
  140.2 1.5 collective-permute-start.21
  140.3 38.5 %collective-permute-start.7 = (bf16[4,192,1536]{2,1,0:T(8,128)(2,1)}, bf16[4,192,1536]{2,1,0:T(8,128)(2,1)S(1)}, u32[]{:S(2)}, u32[]{:S(2)}) collective-permute-start(bf16[4,192,1536]{2,1,0:T(8,128)(2,1)} %bitcast.18), channel_id=1, source_target_pairs={{0,4},{4,0},{8,12},{12,8},{16,20},{20,16},{24,28},{28,24},{1,5},{5... | collective-permute-start | bytes 7077896 | tf_op jit(solution)/shard_map/ppermute | solution.py:82
  141.7 8.7 %collective-permute-start.22 = (f32[31,1536]{1,0:T(8,128)S(1)}, f32[31,1536]{1,0:T(8,128)S(1)}, u32[]{:S(2)}, u32[]{:S(2)}) collective-permute-start(f32[31,1536]{1,0:T(8,128)S(1)} %add.540), channel_id=1, source_target_pairs={{0,8},{4,12},{8,0},{12,4},{16,24},{20,28},{24,16},{28,20},{1,9},{5... | collective-permute-start | bytes 571400 | tf_op jit(solution)/shard_map/ppermute | solution.py:34
  143.8 8.3 %collective-permute-start.17 = (f32[48,1536]{1,0:T(8,128)S(1)}, f32[48,1536]{1,0:T(8,128)S(1)}, u32[]{:S(2)}, u32[]{:S(2)}) collective-permute-start(f32[48,1536]{1,0:T(8,128)S(1)} %constant_dynamic-slice_fusion), channel_id=1, source_target_pairs={{0,4},{4,0},{8,12},{12,8},{16,20},{20,16},{24,28},{28,24},{1,5},{5... | collective-permute-start | bytes 884744 | tf_op jit(solution)/shard_map/ppermute | solution.py:65
  143.9 8.3 %collective-permute-start.13 = (bf16[2,15,1536]{2,1,0:T(8,128)(2,1)S(1)}, bf16[2,15,1536]{2,1,0:T(8,128)(2,1)S(1)}, u32[]{:S(2)}, u32[]{:S(2)}) collective-permute-start(bf16[2,15,1536]{2,1,0:T(8,128)(2,1)S(1)} %get-tuple-element.97), channel_id=1, source_target_pairs={{1,0},{2,1},{3,2},{5,4},{6,5},{7,6},{9,8},{10,9},{11,10},{13,12},{... | collective-permute-start | bytes 276488 | tf_op jit(solution)/shard_map/ppermute | solution.py:17
  145.2 8.0 %collective-permute-start.14 = (bf16[2,15,1536]{2,1,0:T(8,128)(2,1)S(1)}, bf16[2,15,1536]{2,1,0:T(8,128)(2,1)S(1)}, u32[]{:S(2)}, u32[]{:S(2)}) collective-permute-start(bf16[2,15,1536]{2,1,0:T(8,128)(2,1)S(1)} %get-tuple-element.98), channel_id=1, source_target_pairs={{0,1},{1,2},{2,3},{4,5},{5,6},{6,7},{8,9},{9,10},{10,11},{12,13},{... | collective-permute-start | bytes 276488 | tf_op jit(solution)/shard_map/ppermute | solution.py:16
  150.5 7.1 %collective-permute-start.23 = (f32[31,1536]{1,0:T(8,128)S(1)}, f32[31,1536]{1,0:T(8,128)S(1)}, u32[]{:S(2)}, u32[]{:S(2)}) collective-permute-start(f32[31,1536]{1,0:T(8,128)S(1)} %add.541), channel_id=1, source_target_pairs={{0,16},{4,20},{8,24},{12,28},{16,0},{20,4},{24,8},{28,12},{1,17},{... | collective-permute-start | bytes 571400 | tf_op jit(solution)/shard_map/ppermute | solution.py:34
  152.1 8.0 %collective-permute-start.18 = (f32[48,1536]{1,0:T(8,128)S(1)}, f32[48,1536]{1,0:T(8,128)S(1)}, u32[]{:S(2)}, u32[]{:S(2)}) collective-permute-start(f32[48,1536]{1,0:T(8,128)S(1)} %dynamic-slice_add_fusion.2), channel_id=1, source_target_pairs={{0,4},{4,0},{8,12},{12,8},{16,20},{20,16},{24,28},{28,24},{1,5},{5... | collective-permute-start | bytes 884744 | tf_op jit(solution)/shard_map/ppermute | solution.py:69
  157.6 7.3 %collective-permute-start.24 = (f32[31,1536]{1,0:T(8,128)S(1)}, f32[31,1536]{1,0:T(8,128)S(1)}, u32[]{:S(2)}, u32[]{:S(2)}) collective-permute-start(f32[31,1536]{1,0:T(8,128)S(1)} %add.542), channel_id=1, source_target_pairs={{0,1},{1,0},{2,3},{3,2},{4,5},{5,4},{6,7},{7,6},{8,9},{9,8},{10,11... | collective-permute-start | bytes 571400 | tf_op jit(solution)/shard_map/ppermute | solution.py:34
  160.1 16.6 %collective-permute-start.19 = (f32[96,1536]{1,0:T(8,128)S(1)}, f32[96,1536]{1,0:T(8,128)S(1)}, u32[]{:S(2)}, u32[]{:S(2)}) collective-permute-start(f32[96,1536]{1,0:T(8,128)S(1)} %maximum_select_fusion.2), channel_id=1, source_target_pairs={{0,8},{4,12},{8,0},{12,4},{16,24},{20,28},{24,16},{28,20},{1,9},{5... | collective-permute-start | bytes 1769480 | tf_op jit(solution)/shard_map/ppermute | solution.py:69
  164.9 11.1 %collective-permute-start.25 = (f32[31,1536]{1,0:T(8,128)S(1)}, f32[31,1536]{1,0:T(8,128)S(1)}, u32[]{:S(2)}, u32[]{:S(2)}) collective-permute-start(f32[31,1536]{1,0:T(8,128)S(1)} %add.543), channel_id=1, source_target_pairs={{0,2},{1,3},{2,0},{3,1},{4,6},{5,7},{6,4},{7,5},{8,10},{9,11},{10,... | collective-permute-start | bytes 571400 | tf_op jit(solution)/shard_map/ppermute | solution.py:34
  176.8 27.2 %collective-permute-start.20 = (f32[192,1536]{1,0:T(8,128)S(1)}, f32[192,1536]{1,0:T(8,128)S(1)}, u32[]{:S(2)}, u32[]{:S(2)}) collective-permute-start(f32[192,1536]{1,0:T(8,128)S(1)} %maximum_select_fusion.1), channel_id=1, source_target_pairs={{0,16},{4,20},{8,24},{12,28},{16,0},{20,4},{24,8},{28,12},{1,17},{... | collective-permute-start | bytes 3538952 | tf_op jit(solution)/shard_map/ppermute | solution.py:69
  (68 other events, 1115.5 us)
Sparse Core Ops, SparseCore 0:
  9.6 40.3 all-gather.3
  86.5 51.7 all-gather.5

commit v20 on v13

--- a/solution.py
+++ b/solution.py
@@ -129,7 +129,7 @@
     local_grad = jnp.einsum("fc,fd->cd", group_act, group_grad, preferred_element_type=jnp.float32)
     grad_affine = grad_act * (sig_affine + affine * sig_affine * (1.0 - sig_affine))
     sums = jnp.stack([jnp.sum(grad_affine, axis=(0, 1)), jnp.sum(grad_affine * normed, axis=(0, 1))])
-    sums = all_sum(sums, ("dp", "tensor"))
+    sums = all_sum(sums, ("tensor", "dp"))
     shift_grad, scale_grad = sums[0], sums[1]
     grad_conv = (
         norm_scale

time: 187 us -> 187 us (level)
    ppermute x10, waiting for transfers between devices: 17.1 us -> 21.2 us  [all_sum(): x = x + lax.ppermute(x, axis, [(i, i ^ step) for i in range(peers)])]
    all_gather x1, waiting for transfers between devices: 17.2 us -> 14.4 us  [gather_weight(): held = lax.all_gather(mine, 'tensor', axis=0, tiled=False)]
where the time goes in v20:
time: 187 us
  waiting for transfers between devices  64.7 us (35%)
  starting transfers between devices  39.4 us (21%)
  other arithmetic  22.9 us (12%)
  blocking collectives  22.6 us (12%)
  between operations  15.7 us (8%)
  local copies, waits for them, and re-layouts  15.2 us (8%)
  matrix products  6.16 us (3%)
    all_to_all x1, blocking collectives, on_device(): lax.all_to_all(own_columns, 'tensor', split_axis=0, concat_axis=1, tiled=...  22.6 us
    ppermute x10, waiting for transfers between devices, all_sum(): x = x + lax.ppermute(x, axis, [(i, i ^ step) for i in range(peers)])  21.2 us
    all_gather x1, waiting for transfers between devices, gather_weight(): held = lax.all_gather(mine, 'tensor', axis=0, tiled=False)  14.4 us
    ppermute x5, waiting for transfers between devices, all_moments(): lax.ppermute(jnp.stack([mean, spread]), axis, [(i, i ^ step) for i in ran...  10.9 us
    ppermute x10, starting transfers between devices, all_sum(): x = x + lax.ppermute(x, axis, [(i, i ^ step) for i in range(peers)])  10.4 us
    ppermute x2, starting transfers between devices, extended(): before = lax.ppermute(last, axis, up)  9.48 us
    another operation x32, local copies, waits for them, and re-layouts, on_device(): jnp.stack([jnp.sum(padded[:, offset:offset + frames, :].astype(jnp.float3...  7.97 us
    ppermute x5, starting transfers between devices, all_moments(): lax.ppermute(jnp.stack([mean, spread]), axis, [(i, i ^ step) for i in ran...  7.35 us
  transfers between devices with their start and end apart: 29, of which 19 were waited for; matrix products, arithmetic and copies ran while one was open for 18% of the time, Pallas kernels for 0%

profile of v20, /device:TPU:0, one launch (start us, length us, event | category | flops | bytes accessed | tf_op | source)
XLA Modules:
  0.0 186.6 jit_solution(8996814178643198088)
XLA Ops:
  9.3 4.9 %collective-permute-start = (bf16[2,15,1536]{2,1,0:T(8,128)(2,1)S(1)}, bf16[2,15,1536]{2,1,0:T(8,128)(2,1)S(1)}, u32[]{:S(2)}, u32[]{:S(2)}) collective-permute-start(bf16[2,15,1536]{2,1,0:T(8,128)(2,1)S(1)} %get-tuple-element.99), channel_id=1, source_target_pairs={{0,1},{1,2},{2,3},{4,5},{5,6},{6,7},{8,9},{9,10},{10,11},{12,13},{... | collective-permute-start | bytes 276488 | tf_op jit(solution)/shard_map/ppermute | solution.py:16
  16.4 4.3 %collective-permute-done.1 = bf16[2,15,1536]{2,1,0:T(8,128)(2,1)S(1)} collective-permute-done((bf16[2,15,1536]{2,1,0:T(8,128)(2,1)S(1)}, bf16[2,15,1536]{2,1,0:T(8,128)(2,1)S(1)}, u32[]{:S(2)}, u32[]{:S(2)}) %collective-permute-start.1) | collective-permute-done | bytes 92192 | tf_op jit(solution)/shard_map/ppermute | solution.py:17
  20.7 3.8 %fusion.143 = (f32[1536]{0:T(1024)S(1)}, f32[2,64,1536]{2,1,0:T(8,128)S(1)}) fusion(bf16[2,15,1536]{2,1,0:T(8,128)(2,1)S(1)} %collective-permute-done.1, bf16[2,64,1536]{2,1,0:T(8,128)(2,1)S(1)} %fusion, f32[1536]{0:T(1024)S(1)} %get-tuple-element.72, f32[1536]{0:T(1024)S(1)} %get-tuple-element.73, f32[1536]{0:T(1024)S(1)} %get-tuple-element.44, ...), kind=kLoop, calls=%fused_computation.380 | loop fusion | flops 35977728 | bytes 1560576 | tf_op jit(solution)/shard_map/reduce_sum | solution.py:107
  26.1 1.6 collective-permute-start.3
  27.7 2.2 %collective-permute-done.3 = f32[2,1536]{1,0:T(2,128)S(1)} collective-permute-done((f32[2,1536]{1,0:T(2,128)S(1)}, f32[2,1536]{1,0:T(2,128)S(1)}, u32[]{:S(2)}, u32[]{:S(2)}) %collective-permute-start.3) | collective-permute-done | bytes 12320 | tf_op jit(solution)/shard_map/ppermute | solution.py:44
  29.9 1.6 collective-permute-start.4
  31.5 2.2 %collective-permute-done.4 = f32[2,1536]{1,0:T(2,128)S(1)} collective-permute-done((f32[2,1536]{1,0:T(2,128)S(1)}, f32[2,1536]{1,0:T(2,128)S(1)}, u32[]{:S(2)}, u32[]{:S(2)}) %collective-permute-start.4) | collective-permute-done | bytes 12320 | tf_op jit(solution)/shard_map/ppermute | solution.py:44
  33.8 1.6 collective-permute-start.5
  35.4 2.5 %collective-permute-done.5 = f32[2,1536]{1,0:T(2,128)S(1)} collective-permute-done((f32[2,1536]{1,0:T(2,128)S(1)}, f32[2,1536]{1,0:T(2,128)S(1)}, u32[]{:S(2)}, u32[]{:S(2)}) %collective-permute-start.5) | collective-permute-done | bytes 12320 | tf_op jit(solution)/shard_map/ppermute | solution.py:44
  38.0 2.5 %collective-permute-start.6 = (f32[2,1536]{1,0:T(2,128)S(1)}, f32[2,1536]{1,0:T(2,128)S(1)}, u32[]{:S(2)}, u32[]{:S(2)}) collective-permute-start(f32[2,1536]{1,0:T(2,128)S(1)} %pad_maximum_fusion.10), channel_id=1, source_target_pairs={{0,2},{1,3},{2,0},{3,1},{4,6},{5,7},{6,4},{7,5},{8,10},{9,11},{10,... | collective-permute-start | bytes 36872 | tf_op jit(solution)/shard_map/ppermute | solution.py:44
  40.5 2.9 %collective-permute-done.6 = f32[2,1536]{1,0:T(2,128)S(1)} collective-permute-done((f32[2,1536]{1,0:T(2,128)S(1)}, f32[2,1536]{1,0:T(2,128)S(1)}, u32[]{:S(2)}, u32[]{:S(2)}) %collective-permute-start.6) | collective-permute-done | bytes 12320 | tf_op jit(solution)/shard_map/ppermute | solution.py:44
  44.2 5.8 %all-gather.4.cloned.1.call-done = bf16[512,1536]{1,0:T(8,128)(2,1)} async-done(((bf16[128,1536]{1,0:T(8,128)(2,1)}), bf16[512,1536]{1,0:T(8,128)(2,1)}) %all-gather.4.cloned.1.call-update) | async-done | bytes 1572880 | tf_op jit(solution)/shard_map/all_gather | solution.py:99
  50.0 2.4 %fusion.147 = f32[512,384]{1,0:T(8,128)S(1)} fusion(bf16[512,1536]{1,0:T(8,128)(2,1)} %all-gather.4.cloned.1.call-done, bf16[384,1536]{1,0:T(8,128)(2,1)S(1)} %copy-done), kind=kOutput, calls=%fused_computation.383 | convolution fusion | flops 603979776 | bytes 3538944 | tf_op jit(solution)/shard_map/fd,cd->fc/dot_general | solution.py:118
  52.4 22.6 %all_to_all.35 = f32[4,128,384]{2,1,0:T(8,128)S(1)} all-to-all(f32[4,128,384]{2,1,0:T(8,128)S(1)} %bitcast.21), channel_id=1, replica_groups=mesh['dp'=8,'tensor'=4] {'tensor'}, dimensions={0} | all-to-all | bytes 1572864 | tf_op jit(solution)/shard_map/all_to_all | solution.py:119
  76.8 2.4 %fusion.140 = (f32[1536]{0:T(1024)S(1)}, f32[1536]{0:T(1024)S(1)}, f32[2,64,1536]{2,1,0:T(8,128)}, bf16[2,64,1536]{2,1,0:T(8,128)(2,1)S(1)}) fusion(f32[1536]{0:T(1024)S(1)} %get-tuple-element.90, f32[2,64,1536]{2,1,0:T(8,128)S(1)} %get-tuple-element.93, f32[1536]{0:T(1024)S(1)} %get-tuple-element.8, f32[2,64,1536]{2,1,0:T(8,128)} %reshape.189, ...), kind=kLoop, calls=%fused_computation.378 | loop fusion | flops 3142656 | bytes 2789376 | tf_op jit(solution)/shard_map/reduce_sum | solution.py:131
  80.4 3.5 %all-to-all-start.1 = ((bf16[128,4,384]{2,0,1:T(8,128)(2,1)}), bf16[128,4,384]{2,0,1:T(8,128)(2,1)S(1)}, u32[]{:S(2)}, u32[]{:S(2)}) async-start(bf16[128,4,384]{2,0,1:T(8,128)(2,1)} %copy.17), calls=%async_computation.1 | async-start | bytes 786432 | tf_op jit(solution)/shard_map/all_to_all | solution.py:128
  84.2 2.7 %collective-permute-start.9 = (f32[2,1536]{1,0:T(2,128)S(1)}, f32[2,1536]{1,0:T(2,128)S(1)}, u32[]{:S(2)}, u32[]{:S(2)}) collective-permute-start(f32[2,1536]{1,0:T(2,128)S(1)} %fusion.139), channel_id=1, source_target_pairs={{0,2},{1,3},{2,0},{3,1},{4,6},{5,7},{6,4},{7,5},{8,10},{9,11},{10,... | collective-permute-start | bytes 36872 | tf_op jit(solution)/shard_map/ppermute | solution.py:34
  87.8 7.6 %collective-permute-done.9 = f32[2,1536]{1,0:T(2,128)S(1)} collective-permute-done((f32[2,1536]{1,0:T(2,128)S(1)}, f32[2,1536]{1,0:T(2,128)S(1)}, u32[]{:S(2)}, u32[]{:S(2)}) %collective-permute-start.9) | collective-permute-done | bytes 12320 | tf_op jit(solution)/shard_map/ppermute | solution.py:34
  98.2 2.2 %collective-permute-done.11 = f32[2,1536]{1,0:T(2,128)S(1)} collective-permute-done((f32[2,1536]{1,0:T(2,128)S(1)}, f32[2,1536]{1,0:T(2,128)S(1)}, u32[]{:S(2)}, u32[]{:S(2)}) %collective-permute-start.11) | collective-permute-done | bytes 12320 | tf_op jit(solution)/shard_map/ppermute | solution.py:34
  102.0 2.2 %collective-permute-done.12 = f32[2,1536]{1,0:T(2,128)S(1)} collective-permute-done((f32[2,1536]{1,0:T(2,128)S(1)}, f32[2,1536]{1,0:T(2,128)S(1)}, u32[]{:S(2)}, u32[]{:S(2)}) %collective-permute-start.12) | collective-permute-done | bytes 12320 | tf_op jit(solution)/shard_map/ppermute | solution.py:34
  104.2 2.2 %fusion.148 = f32[384,1536]{1,0:T(8,128)S(1)} fusion(bf16[512,384]{1,0:T(8,128)(2,1)S(1)} %bitcast.20, bf16[512,1536]{1,0:T(8,128)(2,1)} %all-gather.4.cloned.1.call-done), kind=kOutput, calls=%fused_computation.384 | convolution fusion | flops 603979776 | bytes 4325376 | tf_op jit(solution)/shard_map/fc,fd->cd/dot_general | solution.py:129
  107.6 1.5 fusion.80
  121.1 2.5 %stack.172 = f32[31,1536]{1,0:T(8,128)S(1)} concatenate(f32[1,1536]{1,0:T(1,128)} %stack.141, f32[1,1536]{1,0:T(1,128)} %stack.142, f32[1,1536]{1,0:T(1,128)} %stack.143, f32[1,1536]{1,0:T(1,128)} %stack.144, f32[1,1536]{1,0:T(1,128)} %stack.145, f32[1,1536]{1,0:T(1,128)S(1)} %stack.146, f32[1,1536]{1,0:T(1,128)S(1)} %stack.147, f32[1,1536]{1,0:T(1,128)S(1)} %stack.148, ...), dimensions={0} | concatenate | bytes 380928 | tf_op jit(solution)/shard_map/stack | solution.py:145
  123.8 14.4 %all-gather.6.cloned.1.call-done = bf16[768,1536]{1,0:T(8,128)(2,1)} async-done(((bf16[192,1536]{1,0:T(8,128)(2,1)}), bf16[768,1536]{1,0:T(8,128)(2,1)}) %all-gather.6.cloned.1.call-update) | async-done | bytes 2359312 | tf_op jit(solution)/shard_map/all_gather | solution.py:81
  144.1 4.6 %collective-permute-start.14 = (bf16[2,15,1536]{2,1,0:T(8,128)(2,1)S(1)}, bf16[2,15,1536]{2,1,0:T(8,128)(2,1)S(1)}, u32[]{:S(2)}, u32[]{:S(2)}) collective-permute-start(bf16[2,15,1536]{2,1,0:T(8,128)(2,1)S(1)} %get-tuple-element.98), channel_id=1, source_target_pairs={{0,1},{1,2},{2,3},{4,5},{5,6},{6,7},{8,9},{9,10},{10,11},{12,13},{... | collective-permute-start | bytes 276488 | tf_op jit(solution)/shard_map/ppermute | solution.py:16
  150.5 2.1 %collective-permute-start.18 = (f32[48,1536]{1,0:T(8,128)S(1)}, f32[48,1536]{1,0:T(8,128)S(1)}, u32[]{:S(2)}, u32[]{:S(2)}) collective-permute-start(f32[48,1536]{1,0:T(8,128)S(1)} %dynamic-slice_add_fusion.2), channel_id=1, source_target_pairs={{0,16},{4,20},{8,24},{12,28},{16,0},{20,4},{24,8},{28,12},{1,17},{... | collective-permute-start | bytes 884744 | tf_op jit(solution)/shard_map/ppermute | solution.py:69
  152.9 4.1 %multiply_convert_fusion = (bf16[2,64,1536]{2,1,0:T(8,128)(2,1)S(1)}, f32[2,64,1536]{2,1,0:T(8,128)S(1)}) fusion(bf16[2,64,3072]{2,1,0:T(8,128)(2,1)S(1)} %copy-done.1, bf16[2,64,1536]{2,1,0:T(8,128)(2,1)S(1)} %get-tuple-element.86, bf16[2,15,1536]{2,1,0:T(8,128)(2,1)S(1)} %collective-permute-done.14, f32[1536]{0:T(1024)S(1)} %copy-done.62, ...), kind=kLoop, calls=%fused_computation.210 | loop fusion | flops 36962304 | bytes 2340864 | tf_op jit(solution)/shard_map/convert
  157.7 3.6 %collective-permute-done.18 = f32[48,1536]{1,0:T(8,128)S(1)} collective-permute-done((f32[48,1536]{1,0:T(8,128)S(1)}, f32[48,1536]{1,0:T(8,128)S(1)}, u32[]{:S(2)}, u32[]{:S(2)}) %collective-permute-start.18) | collective-permute-done | bytes 294944 | tf_op jit(solution)/shard_map/ppermute | solution.py:69
  165.0 7.5 %collective-permute-done.25 = f32[31,1536]{1,0:T(8,128)S(1)} collective-permute-done((f32[31,1536]{1,0:T(8,128)S(1)}, f32[31,1536]{1,0:T(8,128)S(1)}, u32[]{:S(2)}, u32[]{:S(2)}) %collective-permute-start.25) | collective-permute-done | bytes 190496 | tf_op jit(solution)/shard_map/ppermute | solution.py:34
  173.2 1.9 %collective-permute-done.19 = f32[96,1536]{1,0:T(8,128)S(1)} collective-permute-done((f32[96,1536]{1,0:T(8,128)S(1)}, f32[96,1536]{1,0:T(8,128)S(1)}, u32[]{:S(2)}, u32[]{:S(2)}) %collective-permute-start.19) | collective-permute-done | bytes 589856 | tf_op jit(solution)/shard_map/ppermute | solution.py:69
  175.9 1.5 convolution_convert_fusion
  178.1 1.6 maximum_select_fusion
  (266 shorter events, 41.7 us)
Async XLA Ops:
  7.2 42.8 %copy-start = (bf16[384,1536]{1,0:T(8,128)(2,1)S(1)}, bf16[384,1536]{1,0:T(8,128)(2,1)}, u32[]{:S(2)}) copy-start(bf16[384,1536]{1,0:T(8,128)(2,1)} %param.10) | copy-start | bytes 3538948
  7.2 42.8 %all-gather.4.cloned.1.call-start = ((), (), s32[]{:S(2)}) async-start(), calls=%async_computation.2 | async-start | bytes 1966080 | tf_op jit(solution)/shard_map/all_gather | solution.py:99
  9.3 7.1 %collective-permute-start = (bf16[2,15,1536]{2,1,0:T(8,128)(2,1)S(1)}, bf16[2,15,1536]{2,1,0:T(8,128)(2,1)S(1)}, u32[]{:S(2)}, u32[]{:S(2)}) collective-permute-start(bf16[2,15,1536]{2,1,0:T(8,128)(2,1)S(1)} %get-tuple-element.99), channel_id=1, source_target_pairs={{0,1},{1,2},{2,3},{4,5},{5,6},{6,7},{8,9},{9,10},{10,11},{12,13},{... | collective-permute-start | bytes 276488 | tf_op jit(solution)/shard_map/ppermute | solution.py:16
  14.2 6.5 %collective-permute-start.1 = (bf16[2,15,1536]{2,1,0:T(8,128)(2,1)S(1)}, bf16[2,15,1536]{2,1,0:T(8,128)(2,1)S(1)}, u32[]{:S(2)}, u32[]{:S(2)}) collective-permute-start(bf16[2,15,1536]{2,1,0:T(8,128)(2,1)S(1)} %get-tuple-element.100), channel_id=1, source_target_pairs={{1,0},{2,1},{3,2},{5,4},{6,5},{7,6},{9,8},{10,9},{11,10},{13,12},{... | collective-permute-start | bytes 276488 | tf_op jit(solution)/shard_map/ppermute | solution.py:17
  16.3 36.0 %copy-start.45 = (f32[1536]{0:T(1024)}, f32[1536]{0:T(1024)S(1)}, u32[]{:S(2)}) copy-start(f32[1536]{0:T(1024)S(1)} %get-tuple-element.64) | copy-start | bytes 18436
  16.3 36.0 %copy-start.47 = (f32[1536]{0:T(1024)}, f32[1536]{0:T(1024)S(1)}, u32[]{:S(2)}) copy-start(f32[1536]{0:T(1024)S(1)} %get-tuple-element.65) | copy-start | bytes 18436
  24.8 1.2 collective-permute-start.2
  26.1 3.8 %collective-permute-start.3 = (f32[2,1536]{1,0:T(2,128)S(1)}, f32[2,1536]{1,0:T(2,128)S(1)}, u32[]{:S(2)}, u32[]{:S(2)}) collective-permute-start(f32[2,1536]{1,0:T(2,128)S(1)} %pad_maximum_fusion.7), channel_id=1, source_target_pairs={{0,8},{4,12},{8,0},{12,4},{16,24},{20,28},{24,16},{28,20},{1,9},{5... | collective-permute-start | bytes 36872 | tf_op jit(solution)/shard_map/ppermute | solution.py:44
  29.9 3.8 %collective-permute-start.4 = (f32[2,1536]{1,0:T(2,128)S(1)}, f32[2,1536]{1,0:T(2,128)S(1)}, u32[]{:S(2)}, u32[]{:S(2)}) collective-permute-start(f32[2,1536]{1,0:T(2,128)S(1)} %pad_maximum_fusion.8), channel_id=1, source_target_pairs={{0,16},{4,20},{8,24},{12,28},{16,0},{20,4},{24,8},{28,12},{1,17},{... | collective-permute-start | bytes 36872 | tf_op jit(solution)/shard_map/ppermute | solution.py:44
  33.8 4.2 %collective-permute-start.5 = (f32[2,1536]{1,0:T(2,128)S(1)}, f32[2,1536]{1,0:T(2,128)S(1)}, u32[]{:S(2)}, u32[]{:S(2)}) collective-permute-start(f32[2,1536]{1,0:T(2,128)S(1)} %pad_maximum_fusion.9), channel_id=1, source_target_pairs={{0,1},{1,0},{2,3},{3,2},{4,5},{5,4},{6,7},{7,6},{8,9},{9,8},{10,11... | collective-permute-start | bytes 36872 | tf_op jit(solution)/shard_map/ppermute | solution.py:44
  38.0 5.4 %collective-permute-start.6 = (f32[2,1536]{1,0:T(2,128)S(1)}, f32[2,1536]{1,0:T(2,128)S(1)}, u32[]{:S(2)}, u32[]{:S(2)}) collective-permute-start(f32[2,1536]{1,0:T(2,128)S(1)} %pad_maximum_fusion.10), channel_id=1, source_target_pairs={{0,2},{1,3},{2,0},{3,1},{4,6},{5,7},{6,4},{7,5},{8,10},{9,11},{10,... | collective-permute-start | bytes 36872 | tf_op jit(solution)/shard_map/ppermute | solution.py:44
  79.3 4.9 %collective-permute-start.8 = (f32[2,1536]{1,0:T(2,128)S(1)}, f32[2,1536]{1,0:T(2,128)S(1)}, u32[]{:S(2)}, u32[]{:S(2)}) collective-permute-start(f32[2,1536]{1,0:T(2,128)S(1)} %pad_maximum_fusion.11), channel_id=1, source_target_pairs={{0,1},{1,0},{2,3},{3,2},{4,5},{5,4},{6,7},{7,6},{8,9},{9,8},{10,11... | collective-permute-start | bytes 36872 | tf_op jit(solution)/shard_map/ppermute | solution.py:34
  80.4 23.8 %all-to-all-start.1 = ((bf16[128,4,384]{2,0,1:T(8,128)(2,1)}), bf16[128,4,384]{2,0,1:T(8,128)(2,1)S(1)}, u32[]{:S(2)}, u32[]{:S(2)}) async-start(bf16[128,4,384]{2,0,1:T(8,128)(2,1)} %copy.17), calls=%async_computation.1 | async-start | bytes 786432 | tf_op jit(solution)/shard_map/all_to_all | solution.py:128
  83.9 54.3 %all-gather.6.cloned.1.call-start = ((), (), s32[]{:S(2)}) async-start(), calls=%async_computation.3 | async-start | bytes 2949120 | tf_op jit(solution)/shard_map/all_gather | solution.py:81
  84.2 11.2 %collective-permute-start.9 = (f32[2,1536]{1,0:T(2,128)S(1)}, f32[2,1536]{1,0:T(2,128)S(1)}, u32[]{:S(2)}, u32[]{:S(2)}) collective-permute-start(f32[2,1536]{1,0:T(2,128)S(1)} %fusion.139), channel_id=1, source_target_pairs={{0,2},{1,3},{2,0},{3,1},{4,6},{5,7},{6,4},{7,5},{8,10},{9,11},{10,... | collective-permute-start | bytes 36872 | tf_op jit(solution)/shard_map/ppermute | solution.py:34
  95.4 1.2 collective-permute-start.10
  96.7 3.8 %collective-permute-start.11 = (f32[2,1536]{1,0:T(2,128)S(1)}, f32[2,1536]{1,0:T(2,128)S(1)}, u32[]{:S(2)}, u32[]{:S(2)}) collective-permute-start(f32[2,1536]{1,0:T(2,128)S(1)} %add.496), channel_id=1, source_target_pairs={{0,8},{4,12},{8,0},{12,4},{16,24},{20,28},{24,16},{28,20},{1,9},{5... | collective-permute-start | bytes 36872 | tf_op jit(solution)/shard_map/ppermute | solution.py:34
  100.5 3.8 %collective-permute-start.12 = (f32[2,1536]{1,0:T(2,128)S(1)}, f32[2,1536]{1,0:T(2,128)S(1)}, u32[]{:S(2)}, u32[]{:S(2)}) collective-permute-start(f32[2,1536]{1,0:T(2,128)S(1)} %add.497), channel_id=1, source_target_pairs={{0,16},{4,20},{8,24},{12,28},{16,0},{20,4},{24,8},{28,12},{1,17},{... | collective-permute-start | bytes 36872 | tf_op jit(solution)/shard_map/ppermute | solution.py:34
  106.6 3.8 %collective-permute-start.15 = (f32[192,1536]{1,0:T(8,128)S(1)}, f32[192,1536]{1,0:T(8,128)S(1)}, u32[]{:S(2)}, u32[]{:S(2)}) collective-permute-start(f32[192,1536]{1,0:T(8,128)S(1)} %constant_dynamic-slice_fusion.2), channel_id=1, source_target_pairs={{0,4},{4,0},{8,12},{12,8},{16,20},{20,16},{24,28},{28,24},{1,5},{5... | collective-permute-start | bytes 3538952 | tf_op jit(solution)/shard_map/ppermute | solution.py:65
  112.4 27.4 %collective-permute-start.16 = (f32[96,1536]{1,0:T(8,128)}, f32[96,1536]{1,0:T(8,128)}, u32[]{:S(2)}, u32[]{:S(2)}) collective-permute-start(f32[96,1536]{1,0:T(8,128)} %constant_dynamic-slice_fusion.1), channel_id=1, source_target_pairs={{0,8},{4,12},{8,0},{12,4},{16,24},{20,28},{24,16},{28,20},{1,9},{5... | collective-permute-start | bytes 1769480 | tf_op jit(solution)/shard_map/ppermute | solution.py:65
  123.6 14.6 %collective-permute-start.21 = (f32[31,1536]{1,0:T(8,128)S(1)}, f32[31,1536]{1,0:T(8,128)S(1)}, u32[]{:S(2)}, u32[]{:S(2)}) collective-permute-start(f32[31,1536]{1,0:T(8,128)S(1)} %stack.172), channel_id=1, source_target_pairs={{0,4},{4,0},{8,12},{12,8},{16,20},{20,16},{24,28},{28,24},{1,5},{5... | collective-permute-start | bytes 571400 | tf_op jit(solution)/shard_map/ppermute | solution.py:34
  138.2 37.1 %collective-permute-start.7 = (bf16[4,192,1536]{2,1,0:T(8,128)(2,1)}, bf16[4,192,1536]{2,1,0:T(8,128)(2,1)S(1)}, u32[]{:S(2)}, u32[]{:S(2)}) collective-permute-start(bf16[4,192,1536]{2,1,0:T(8,128)(2,1)} %bitcast.18), channel_id=1, source_target_pairs={{0,4},{4,0},{8,12},{12,8},{16,20},{20,16},{24,28},{28,24},{1,5},{5... | collective-permute-start | bytes 7077896 | tf_op jit(solution)/shard_map/ppermute | solution.py:82
  138.2 10.4 %collective-permute-start.22 = (f32[31,1536]{1,0:T(8,128)S(1)}, f32[31,1536]{1,0:T(8,128)S(1)}, u32[]{:S(2)}, u32[]{:S(2)}) collective-permute-start(f32[31,1536]{1,0:T(8,128)S(1)} %add.537), channel_id=1, source_target_pairs={{0,8},{4,12},{8,0},{12,4},{16,24},{20,28},{24,16},{28,20},{1,9},{5... | collective-permute-start | bytes 571400 | tf_op jit(solution)/shard_map/ppermute | solution.py:34
  141.2 9.2 %collective-permute-start.17 = (f32[48,1536]{1,0:T(8,128)S(1)}, f32[48,1536]{1,0:T(8,128)S(1)}, u32[]{:S(2)}, u32[]{:S(2)}) collective-permute-start(f32[48,1536]{1,0:T(8,128)S(1)} %constant_dynamic-slice_fusion), channel_id=1, source_target_pairs={{0,16},{4,20},{8,24},{12,28},{16,0},{20,4},{24,8},{28,12},{1,17},{... | collective-permute-start | bytes 884744 | tf_op jit(solution)/shard_map/ppermute | solution.py:65
  142.8 9.8 %collective-permute-start.13 = (bf16[2,15,1536]{2,1,0:T(8,128)(2,1)S(1)}, bf16[2,15,1536]{2,1,0:T(8,128)(2,1)S(1)}, u32[]{:S(2)}, u32[]{:S(2)}) collective-permute-start(bf16[2,15,1536]{2,1,0:T(8,128)(2,1)S(1)} %get-tuple-element.97), channel_id=1, source_target_pairs={{1,0},{2,1},{3,2},{5,4},{6,5},{7,6},{9,8},{10,9},{11,10},{13,12},{... | collective-permute-start | bytes 276488 | tf_op jit(solution)/shard_map/ppermute | solution.py:17
  144.1 8.5 %collective-permute-start.14 = (bf16[2,15,1536]{2,1,0:T(8,128)(2,1)S(1)}, bf16[2,15,1536]{2,1,0:T(8,128)(2,1)S(1)}, u32[]{:S(2)}, u32[]{:S(2)}) collective-permute-start(bf16[2,15,1536]{2,1,0:T(8,128)(2,1)S(1)} %get-tuple-element.98), channel_id=1, source_target_pairs={{0,1},{1,2},{2,3},{4,5},{5,6},{6,7},{8,9},{9,10},{10,11},{12,13},{... | collective-permute-start | bytes 276488 | tf_op jit(solution)/shard_map/ppermute | solution.py:16
  148.7 8.2 %collective-permute-start.23 = (f32[31,1536]{1,0:T(8,128)S(1)}, f32[31,1536]{1,0:T(8,128)S(1)}, u32[]{:S(2)}, u32[]{:S(2)}) collective-permute-start(f32[31,1536]{1,0:T(8,128)S(1)} %add.538), channel_id=1, source_target_pairs={{0,16},{4,20},{8,24},{12,28},{16,0},{20,4},{24,8},{28,12},{1,17},{... | collective-permute-start | bytes 571400 | tf_op jit(solution)/shard_map/ppermute | solution.py:34
  150.5 10.8 %collective-permute-start.18 = (f32[48,1536]{1,0:T(8,128)S(1)}, f32[48,1536]{1,0:T(8,128)S(1)}, u32[]{:S(2)}, u32[]{:S(2)}) collective-permute-start(f32[48,1536]{1,0:T(8,128)S(1)} %dynamic-slice_add_fusion.2), channel_id=1, source_target_pairs={{0,16},{4,20},{8,24},{12,28},{16,0},{20,4},{24,8},{28,12},{1,17},{... | collective-permute-start | bytes 884744 | tf_op jit(solution)/shard_map/ppermute | solution.py:69
  157.0 5.7 %collective-permute-start.24 = (f32[31,1536]{1,0:T(8,128)S(1)}, f32[31,1536]{1,0:T(8,128)S(1)}, u32[]{:S(2)}, u32[]{:S(2)}) collective-permute-start(f32[31,1536]{1,0:T(8,128)S(1)} %add.539), channel_id=1, source_target_pairs={{0,1},{1,0},{2,3},{3,2},{4,5},{5,4},{6,7},{7,6},{8,9},{9,8},{10,11... | collective-permute-start | bytes 571400 | tf_op jit(solution)/shard_map/ppermute | solution.py:34
  161.3 13.8 %collective-permute-start.19 = (f32[96,1536]{1,0:T(8,128)S(1)}, f32[96,1536]{1,0:T(8,128)S(1)}, u32[]{:S(2)}, u32[]{:S(2)}) collective-permute-start(f32[96,1536]{1,0:T(8,128)S(1)} %maximum_select_fusion.2), channel_id=1, source_target_pairs={{0,8},{4,12},{8,0},{12,4},{16,24},{20,28},{24,16},{28,20},{1,9},{5... | collective-permute-start | bytes 1769480 | tf_op jit(solution)/shard_map/ppermute | solution.py:69
  162.7 9.7 %collective-permute-start.25 = (f32[31,1536]{1,0:T(8,128)S(1)}, f32[31,1536]{1,0:T(8,128)S(1)}, u32[]{:S(2)}, u32[]{:S(2)}) collective-permute-start(f32[31,1536]{1,0:T(8,128)S(1)} %add.540), channel_id=1, source_target_pairs={{0,2},{1,3},{2,0},{3,1},{4,6},{5,7},{6,4},{7,5},{8,10},{9,11},{10,... | collective-permute-start | bytes 571400 | tf_op jit(solution)/shard_map/ppermute | solution.py:34
  175.2 2.9 %collective-permute-start.20 = (f32[192,1536]{1,0:T(8,128)S(1)}, f32[192,1536]{1,0:T(8,128)S(1)}, u32[]{:S(2)}, u32[]{:S(2)}) collective-permute-start(f32[192,1536]{1,0:T(8,128)S(1)} %maximum_select_fusion.1), channel_id=1, source_target_pairs={{0,4},{4,0},{8,12},{12,8},{16,20},{20,16},{24,28},{28,24},{1,5},{5... | collective-permute-start | bytes 3538952 | tf_op jit(solution)/shard_map/ppermute | solution.py:69
  (68 other events, 1189.9 us)
Sparse Core Ops, SparseCore 0:
  9.6 40.3 all-gather.3
  87.9 50.2 all-gather.5
